TPU v7x, 512 devices: a whole 4x4x16 slice. The times are simulated.
512 devices in a mesh: ctx: 16 (over z), head: 32 (over x, y, core).
Axes of the slice: x: 4, y: 4, z: 16, core: 2. Of those that a mesh axis runs over, the one named last changes fastest.
Arguments:
- tokens_in: bfloat16 [4096, 4096], P('ctx', 'head'), may hold values from -6 to 6
- w_qkv: bfloat16 [4096, 32, 384], P(None, 'head'), may hold values from -0.125 to 0.125
- w_out: bfloat16 [32, 128, 4096], P('head'), may hold values from -0.375 to 0.375
- codebook: bfloat16 [32, 512, 128], P('head'), may hold values from -184 to 184
- codes: int32 [32, 4096], P('head', 'ctx'), may hold values from 0 to 511
- reach: int32 [16], P('ctx'), may hold values from 1 to 256, as said below
Outputs:
- mixed: bfloat16 [4096, 4096], P(('ctx', 'head'))
Inputs may be any that keep to these rules, and one draw needn't show every extreme that they name: reach[g] is how many of the last positions of block g - 1 block g sees with exact keys; reach[0] has no effect.
All inputs are finite; a program needn't handle non-finite values.
Results may differ from a plain program's by a relative error of at most 0.015.
Values may be sent and summed in bfloat16 or wider, within the bound.
No kernel may reach another device: no remote copies, remote signals or barrier semaphores. Data moves between devices by JAX's collectives and lax.ppermute only.
A program may use at most 64 MiB of HBM per device.

v0:
```python
import math

import jax
import jax.numpy as jnp
from jax import lax
from jax.sharding import PartitionSpec as P

BLK = 256


def from_behind(block, axis, distance):
    devices = range(lax.axis_size(axis))
    route = [(i - distance, i) for i in devices if i - distance in devices]
    return lax.ppermute(block, axis, route)


def entering(value, axis, combine, identity):
    devices, index = (lax.axis_size(axis), lax.axis_index(axis))
    everything = jax.tree.map(
        lambda part, kind: lax.all_gather(part.astype(kind), axis),
        value,
        (jnp.bfloat16, jnp.bfloat16),
    )
    start = jax.tree.map(
        lambda part, zero: jnp.broadcast_to(jnp.asarray(zero, part.dtype), part.shape),
        value,
        identity,
    )

    def turn(k, before):
        reached = k < index
        new = combine(
            before, jax.tree.map(lambda part, own: part[k].astype(own.dtype), everything, value)
        )
        return jax.tree.map(lambda a, b: jnp.where(reached, a, b), new, before)

    return lax.fori_loop(0, devices, turn, start)


def attend_block(
    queries, keys_win, vals_win, cache_v, cache_c, book, reach_one, prev_flag, block_len, scale
):
    exact = (
        lax.dot_general(
            queries, keys_win, (((1,), (1,)), ((), ())), preferred_element_type=jnp.float32
        )
        * scale
    )
    coded = (
        lax.dot_general(queries, book, (((1,), (1,)), ((), ())), preferred_element_type=jnp.float32)
        * scale
    )
    rows = lax.broadcasted_iota(jnp.int32, exact.shape, 0)
    cols = lax.broadcasted_iota(jnp.int32, exact.shape, 1)
    prev_ok = (cols < block_len) & (cols >= block_len - reach_one) & prev_flag
    curr_ok = (cols >= block_len) & (cols - block_len <= rows)
    allowed = prev_ok | curr_ok
    valid = cache_c > 0.5
    top = jnp.maximum(
        jnp.max(jnp.where(allowed, exact, -jnp.inf), axis=1),
        jnp.max(jnp.where(valid[None, :], coded, -jnp.inf), axis=1),
    )
    probs = jnp.exp(jnp.where(allowed, exact - top[:, None], -jnp.inf))
    weights = jnp.exp(jnp.where(valid[None, :], coded - top[:, None], -jnp.inf))
    numer = jnp.dot(probs.astype(jnp.bfloat16), vals_win, preferred_element_type=jnp.float32)
    numer = numer + jnp.dot(weights, cache_v, precision=lax.Precision.HIGHEST)
    denom = jnp.sum(probs, axis=1) + jnp.dot(weights, cache_c, precision=lax.Precision.HIGHEST)
    return (numer / denom[:, None]).astype(jnp.bfloat16)


def combine(earlier, later):
    return (earlier[0] + later[0], earlier[1] + later[1])


def on_device(tokens_in, w_qkv, w_out, codebook, codes, reach):
    tok_rows = tokens_in.shape[0]
    head_dim = codebook.shape[2]
    num_codes = codebook.shape[1]
    num_blocks = tok_rows // BLK
    scale = 1.0 / math.sqrt(head_dim)
    w_local = w_qkv[:, 0, :]
    projected = jnp.dot(
        lax.all_gather(tokens_in, "head", axis=1, tiled=True),
        w_local,
        preferred_element_type=jnp.float32,
    )
    queries = projected[:, :head_dim].astype(jnp.bfloat16)
    key_vals = projected[:, head_dim:].astype(jnp.bfloat16)
    code_row = codes[0]
    book = codebook[0]
    prev_kv, prev_codes = from_behind((key_vals, code_row), "ctx", 1)
    has_prev = lax.axis_index("ctx") > 0
    code_ids = jnp.arange(num_codes, dtype=jnp.int32)
    onehot_loc = (code_row[:, None] == code_ids[None, :]).astype(jnp.bfloat16)
    local_v = jnp.einsum(
        "ts,td->sd", onehot_loc, key_vals[:, head_dim:], preferred_element_type=jnp.float32
    )
    local_c = jnp.sum(onehot_loc, axis=0, dtype=jnp.float32)
    before_v, before_c = entering(
        (local_v, local_c), "ctx", combine, (jnp.zeros_like(local_v), jnp.zeros_like(local_c))
    )
    ext_kv = jnp.concatenate([prev_kv, key_vals], axis=0)
    ext_codes = jnp.concatenate([prev_codes, code_row], axis=0)
    ext_len = BLK + tok_rows
    positions = jnp.arange(ext_len, dtype=jnp.int32)[:, None]
    thresholds = (jnp.arange(num_blocks, dtype=jnp.int32) + 1) * BLK - reach
    plus = (positions >= BLK) & (positions < thresholds[None, :])
    minus = (positions < BLK) & (positions >= thresholds[None, :]) & has_prev
    signs = (plus.astype(jnp.float32) - minus.astype(jnp.float32)).astype(jnp.bfloat16)
    signed_vals = (signs[:, :, None] * ext_kv[:, None, head_dim:]).reshape(
        ext_len, num_blocks * head_dim
    )
    onehot_ext = (ext_codes[:, None] == code_ids[None, :]).astype(jnp.bfloat16)
    part_v = jnp.einsum(
        "es,ef->sf", onehot_ext, signed_vals, preferred_element_type=jnp.float32
    ).reshape(num_codes, num_blocks, head_dim)
    part_c = jnp.einsum("es,eb->sb", onehot_ext, signs, preferred_element_type=jnp.float32)
    cache_v = before_v + part_v[:, 0, :]
    cache_c = before_c + part_c[:, 0]
    prev_flag = has_prev | (0 > 0)
    pieces_out = attend_block(
        queries,
        ext_kv[:, :head_dim],
        ext_kv[:, head_dim:],
        cache_v,
        cache_c,
        book,
        reach[0],
        prev_flag,
        BLK,
        scale,
    )
    w_proj = w_out[0]
    mixed = lax.psum_scatter(
        jnp.dot(pieces_out, w_proj, preferred_element_type=jnp.float32).astype(jnp.bfloat16),
        "head",
        scatter_dimension=0,
        tiled=True,
    )
    return mixed


def solution(mesh):
    in_specs = (
        P("ctx", "head"),
        P(None, "head", None),
        P("head", None, None),
        P("head", None, None),
        P("head", "ctx"),
        P("ctx"),
    )
    out_specs = P(("ctx", "head"), None)
    return jax.shard_map(
        on_device, mesh=mesh, in_specs=in_specs, out_specs=out_specs, check_vma=False
    )
```

profile of v0, /device:TPU:1, one launch (start us, length us, event | category | flops | bytes accessed | tf_op | source)
XLA Modules:
  0.0 295.9 jit_solution(15039246053632858118)
XLA Ops:
  6.5 0.7 all-gather.6.cloned.1.call-update
  7.3 0.0 all-gather.8.cloned.1.call-start
  7.3 68.9 %all-gather.6.cloned.1.call-done = bf16[256,4096]{1,0:T(8,128)(2,1)} async-done(((bf16[256,128]{1,0:T(8,128)(2,1)}), bf16[256,4096]{1,0:T(8,128)(2,1)}) %all-gather.6.cloned.1.call-update) | async-done | bytes 2097168 | tf_op jit(solution)/shard_map/all_gather | solution.py:83
  76.2 0.0 copy-done
  76.2 2.8 fusion.2
  79.1 0.7 copy-done.1
  79.7 1.1 convolution_convert_fusion.1
  80.8 0.0 all-gather.8.cloned.1.call-update
  80.8 0.0 reduce-scatter.2.cloned.1.call-start
  80.9 3.2 %collective-permute-start.1 = (s32[256]{0:T(256)S(1)}, s32[256]{0:T(256)S(1)}, u32[]{:S(2)}, u32[]{:S(2)}) collective-permute-start(s32[256]{0:T(256)S(1)} %bitcast.40), channel_id=1, source_target_pairs={{0,32},{32,64},{64,96},{96,128},{128,160},{160,192},{192,224},{224... | collective-permute-start | bytes 3080 | tf_op jit(solution)/shard_map/ppermute | solution.py:14
  84.1 0.1 fusion.20
  84.9 23.9 %all-gather.2 = bf16[16,1,512]{2,1,0:T(2,128)(2,1)S(1)} all-gather(bf16[1,1,512]{2,1,0:T(2,128)(2,1)S(1)} %reshape.63), channel_id=3, replica_groups=mesh['ctx'=16,'head'=32] {'ctx'}, dimensions={0}, use_global_device_ids=true | all-gather | bytes 17408 | tf_op jit(solution)/shard_map/all_gather | solution.py:20
  108.8 0.6 copy.9
  109.4 0.0 collective-permute-done.1
  109.5 0.9 slice.25
  110.4 1.3 collective-permute-start
  111.7 0.9 fusion.8
  112.6 1.0 collective-permute-done
  113.6 0.7 copy-done.2
  114.3 2.5 select_reduce_fusion.1
  116.7 28.4 %all-gather.8.cloned.1.call-done = bf16[8192,128]{1,0:T(8,128)(2,1)} async-done(((bf16[512,128]{1,0:T(8,128)(2,1)}), bf16[8192,128]{1,0:T(8,128)(2,1)}) %all-gather.8.cloned.1.call-update) | async-done | bytes 2097168 | tf_op jit(solution)/shard_map/all_gather | solution.py:20
  145.1 28.5 %while.16 = (s32[]{:T(128)}, f32[512,128]{1,0:T(8,128)S(1)}, f32[512]{0:T(512)S(1)}, s32[]{:T(128)}, bf16[16,512,128]{2,1,0:T(8,128)(2,1)}, /*index=5*/bf16[16,512]{1,0:T(8,128)(2,1)}, s32[]{:T(128)}, s32[]{:T(128)}) while((s32[]{:T(128)}, f32[512,128]{1,0:T(8,128)S(1)}, f32[512]{0:T(512)S(1)}, s32[]{:T(128)}, ...), condition=%wide.region_3.4_spmd.clone, body=%wide.region_2.3_spmd.clone.sunk | while | flops 264196 | bytes 664699 | solution.py:37
  145.1 1.0 add_select_fusion.4
  146.2 0.7 dynamic-slice_convert_fusion.2
  146.9 1.0 add_select_fusion.4
  147.9 0.7 dynamic-slice_convert_fusion.2
  148.7 1.0 add_select_fusion.4
  149.7 0.7 dynamic-slice_convert_fusion.2
  150.5 1.0 add_select_fusion.4
  151.5 0.7 dynamic-slice_convert_fusion.2
  152.2 1.0 add_select_fusion.4
  153.3 0.7 dynamic-slice_convert_fusion.2
  154.0 1.0 add_select_fusion.4
  155.1 0.7 dynamic-slice_convert_fusion.2
  155.8 1.0 add_select_fusion.4
  156.8 0.7 dynamic-slice_convert_fusion.2
  157.6 1.0 add_select_fusion.4
  158.6 0.7 dynamic-slice_convert_fusion.2
  159.4 1.0 add_select_fusion.4
  160.4 0.7 dynamic-slice_convert_fusion.2
  161.1 1.0 add_select_fusion.4
  162.2 0.7 dynamic-slice_convert_fusion.2
  162.9 1.0 add_select_fusion.4
  164.0 0.7 dynamic-slice_convert_fusion.2
  164.7 1.0 add_select_fusion.4
  165.7 0.7 dynamic-slice_convert_fusion.2
  166.5 1.0 add_select_fusion.4
  167.5 0.7 dynamic-slice_convert_fusion.2
  168.3 1.0 add_select_fusion.4
  169.3 0.7 dynamic-slice_convert_fusion.2
  170.0 1.0 add_select_fusion.4
  171.1 0.7 dynamic-slice_convert_fusion.2
  171.8 1.0 add_select_fusion.4
  172.9 0.7 dynamic-slice_convert_fusion.2
  173.6 0.7 broadcast_compare_fusion
  174.2 1.3 select_reduce_fusion
  175.5 0.7 max.7
  176.2 1.3 fusion.16
  177.5 1.5 convolution_add_fusion
  179.0 0.6 fusion.15
  179.6 0.6 fusion.14
  180.3 3.7 %convolution_convert_fusion = bf16[256,4096]{1,0:T(8,128)(2,1)} fusion(f32[256,128]{1,0:T(8,128)S(1)} %fusion.15, bf16[1,128,4096]{2,1,0:T(8,128)(2,1)} %param.10, f32[256,512]{1,0:T(8,128)} %get-tuple-element.153, f32[256]{0:T(256)S(1)} %max.7, s32[512]{0:T(512)S(1)} %iota_add_fusion, pred[512]{0:T(512)(128)(4,1)S(1)} %get-tuple-element.156, ...), kind=kOutput, calls=%fused_computation.3 | convolution fusion | flops 304185344 | bytes 4068352 | tf_op jit(solution)/shard_map/dot_general | solution.py:135
  184.0 0.0 reduce-scatter.2.cloned.1.call-update
  184.0 105.4 %reduce-scatter.2.cloned.1.call-done = bf16[8,4096]{1,0:T(8,128)(2,1)} async-done(((bf16[256,4096]{1,0:T(8,128)(2,1)}), bf16[8,4096]{1,0:T(8,128)(2,1)}) %reduce-scatter.2.cloned.1.call-update) | async-done | bytes 65552 | tf_op jit(solution)/shard_map/reduce_scatter | solution.py:134
  (35 shorter events, 0.3 us)
Async XLA Ops:
  6.5 69.7 %copy-start = (bf16[4096,1,384]{2,0,1:T(8,128)(2,1)S(1)}, bf16[4096,1,384]{2,0,1:T(8,128)(2,1)}, u32[]{:S(2)}) copy-start(bf16[4096,1,384]{2,0,1:T(8,128)(2,1)} %param.9) | copy-start | bytes 9437188
  6.5 69.7 %all-gather.6.cloned.1.call-start = ((), (), s32[]{:S(2)}) async-start(), calls=%async_computation.1 | async-start | bytes 2162688 | tf_op jit(solution)/shard_map/all_gather | solution.py:83
  7.3 72.5 %copy-start.4 = (s32[1,256]{1,0:T(1,128)S(1)}, s32[1,256]{1,0:T(1,128)}, u32[]{:S(2)}) copy-start(s32[1,256]{1,0:T(1,128)} %param.12) | copy-start | bytes 3076
  7.3 137.8 %all-gather.8.cloned.1.call-start = ((), (), s32[]{:S(2)}) async-start(), calls=%async_computation.3 | async-start | bytes 2228224 | tf_op jit(solution)/shard_map/all_gather | solution.py:20
  79.1 0.7 copy-start.1
  80.8 208.6 %reduce-scatter.2.cloned.1.call-start = ((), (), s32[]{:S(2)}) async-start(), calls=%async_computation.2 | async-start | bytes 2162688 | tf_op jit(solution)/shard_map/reduce_scatter | solution.py:134
  80.9 28.6 %collective-permute-start.1 = (s32[256]{0:T(256)S(1)}, s32[256]{0:T(256)S(1)}, u32[]{:S(2)}, u32[]{:S(2)}) collective-permute-start(s32[256]{0:T(256)S(1)} %bitcast.40), channel_id=1, source_target_pairs={{0,32},{32,64},{64,96},{96,128},{128,160},{160,192},{192,224},{224... | collective-permute-start | bytes 3080 | tf_op jit(solution)/shard_map/ppermute | solution.py:14
  84.9 24.5 %copy-start.3 = (bf16[512]{0:T(512)(128)(2,1)}, bf16[512]{0:T(512)(128)(2,1)S(1)}, u32[]{:S(2)}) copy-start(bf16[512]{0:T(512)(128)(2,1)S(1)} %subtract_convert_fusion) | copy-start | bytes 3076
  109.5 4.2 %copy-start.5 = (s32[512]{0:T(512)}, s32[512]{0:T(512)S(1)}, u32[]{:S(2)}) copy-start(s32[512]{0:T(512)S(1)} %pad_add_fusion) | copy-start | bytes 6148
  110.4 3.2 %collective-permute-start = (bf16[256,256]{1,0:T(8,128)(2,1)S(1)}, bf16[256,256]{1,0:T(8,128)(2,1)S(1)}, u32[]{:S(2)}, u32[]{:S(2)}) collective-permute-start(bf16[256,256]{1,0:T(8,128)(2,1)S(1)} %slice.25), channel_id=1, source_target_pairs={{0,32},{32,64},{64,96},{96,128},{128,160},{160,192},{192,224},{224... | collective-permute-start | bytes 393224 | tf_op jit(solution)/shard_map/ppermute | solution.py:14
  113.6 0.7 copy-start.2
Sparse Core Ops, SparseCore 0:
  10.4 65.7 all-gather.5
  81.0 64.1 all-gather.7
  184.1 105.2 reduce-scatter.1
where the time goes:
time: 298 us; the launch traced here: 296 us
  waiting for transfers between devices  204 us (68%)
  other arithmetic  31 us (10%)
  blocking collectives  23.9 us (8%)
  matrix products  15 us (5%)
  between operations  13.9 us (5%)
  starting transfers between devices  4.56 us (2%)
    reduce_scatter x1, waiting for transfers between devices, on_device(): lax.psum_scatter(jnp.dot(pieces_out, w_proj, preferred_element_type=jnp.f...  105 us
    all_gather x1, waiting for transfers between devices, on_device(): lax.all_gather(tokens_in, 'head', axis=1, tiled=True)  68.9 us
    all_gather x1, waiting for transfers between devices, entering(): lax.all_gather(part.astype(kind), axis)  28.4 us
    all_gather x1, blocking collectives, entering(): lax.all_gather(part.astype(kind), axis)  23.9 us
    select_n x32, other arithmetic, turn(): return jax.tree.map(lambda a, b: jnp.where(reached, a, b), new, before)  16.8 us
    convert_element_type x16, other arithmetic, turn(): part[k].astype(own.dtype)  11.3 us
  transfers between devices with their start and end apart: 5, of which 4 were waited for; matrix products, arithmetic and copies ran while one was open for 2% of the time, Pallas kernels for 0%

commit v1 on v0

v1 whole, which is shorter than its diff:
```python
import math

import jax
import jax.numpy as jnp
from jax import lax
from jax.sharding import Mesh
from jax.sharding import PartitionSpec as P

BLK = 256
HEAD_AXES = ("hx", "hy", "hc")


def _flat(x, y, c, ny, nc):
    return (x * ny + y) * nc + c


def _ring_perm(stage, d, nx, ny, nc):
    pairs = []
    for x in range(nx):
        for y in range(ny):
            for c in range(nc):
                along_y = (c == 0) == (stage == 0)
                if along_y:
                    tx, ty = x, (y + d) % ny
                else:
                    tx, ty = (x + d) % nx, y
                pairs.append((_flat(x, y, c, ny, nc), _flat(tx, ty, c, ny, nc)))
    return pairs


def _core_perm(nx, ny, nc):
    pairs = []
    for x in range(nx):
        for y in range(ny):
            for c in range(nc):
                pairs.append((_flat(x, y, c, ny, nc), _flat(x, y, 1 - c, ny, nc)))
    return pairs


def _send(value, perm):
    return lax.ppermute(value, HEAD_AXES, perm)


def gather_ring(blk, stage, sizes):
    p1 = _send(blk, _ring_perm(stage, 1, *sizes))
    m1 = _send(blk, _ring_perm(stage, -1, *sizes))
    h = blk.shape[0] // 2
    a = _send(p1[:h], _ring_perm(stage, 1, *sizes))
    b = _send(m1[h:], _ring_perm(stage, -1, *sizes))
    far = jnp.concatenate([a, b], axis=0)
    return jnp.stack([blk, p1, far, m1])


def reduce_ring(data, stage, sizes):
    h = data.shape[1] // 2
    rp = _send(data[2, :h].astype(jnp.bfloat16), _ring_perm(stage, 1, *sizes))
    rm = _send(data[2, h:].astype(jnp.bfloat16), _ring_perm(stage, -1, *sizes))
    ahead = jnp.concatenate([data[1, :h] + rp, data[1, h:]], axis=0)
    behind = jnp.concatenate([data[3, :h], data[3, h:] + rm], axis=0)
    gp = _send(ahead.astype(jnp.bfloat16), _ring_perm(stage, 1, *sizes))
    gm = _send(behind.astype(jnp.bfloat16), _ring_perm(stage, -1, *sizes))
    return data[0] + gp.astype(jnp.float32) + gm.astype(jnp.float32)


def attend_block(
    queries, keys_win, vals_win, cache_v, cache_c, book, reach_one, prev_flag, block_len, scale
):
    exact = (
        lax.dot_general(
            queries, keys_win, (((1,), (1,)), ((), ())), preferred_element_type=jnp.float32
        )
        * scale
    )
    coded = (
        lax.dot_general(queries, book, (((1,), (1,)), ((), ())), preferred_element_type=jnp.float32)
        * scale
    )
    rows = lax.broadcasted_iota(jnp.int32, exact.shape, 0)
    cols = lax.broadcasted_iota(jnp.int32, exact.shape, 1)
    prev_ok = (cols < block_len) & (cols >= block_len - reach_one) & prev_flag
    curr_ok = (cols >= block_len) & (cols - block_len <= rows)
    allowed = prev_ok | curr_ok
    valid = cache_c > 0.5
    top = jnp.maximum(
        jnp.max(jnp.where(allowed, exact, -jnp.inf), axis=1),
        jnp.max(jnp.where(valid[None, :], coded, -jnp.inf), axis=1),
    )
    probs = jnp.exp(jnp.where(allowed, exact - top[:, None], -jnp.inf))
    weights = jnp.exp(jnp.where(valid[None, :], coded - top[:, None], -jnp.inf))
    numer = jnp.dot(probs.astype(jnp.bfloat16), vals_win, preferred_element_type=jnp.float32)
    numer = numer + jnp.dot(weights, cache_v, precision=lax.Precision.HIGHEST)
    denom = jnp.sum(probs, axis=1) + jnp.dot(weights, cache_c, precision=lax.Precision.HIGHEST)
    return (numer / denom[:, None]).astype(jnp.bfloat16)


def on_device(tokens_in, w_qkv, w_out, codebook, codes, reach):
    nx, ny, nc = lax.axis_size("hx"), lax.axis_size("hy"), lax.axis_size("hc")
    sizes = (nx, ny, nc)
    core_perm = _core_perm(*sizes)
    me_x, me_y, me_c = lax.axis_index("hx"), lax.axis_index("hy"), lax.axis_index("hc")
    n_ctx = lax.axis_size("ctx")
    g = lax.axis_index("ctx")
    rows, width = tokens_in.shape
    head_dim = codebook.shape[2]
    num_codes = codebook.shape[1]
    scale = 1.0 / math.sqrt(head_dim)
    half = rows // 2

    code_row = codes[0]
    codes_all = lax.all_gather(code_row, "ctx").reshape(n_ctx * rows)
    limit = g * BLK - reach[0]
    cached = jnp.arange(n_ctx * rows, dtype=jnp.int32) < limit
    code_ids = jnp.arange(num_codes, dtype=jnp.int32)
    onehot = ((codes_all[:, None] == code_ids[None, :]) & cached[:, None]).astype(jnp.bfloat16)
    cache_c = jnp.sum(onehot.astype(jnp.float32), axis=0)

    projected = project(tokens_in, w_qkv, sizes)
    queries = projected[:, :head_dim].astype(jnp.bfloat16)
    key_vals = projected[:, head_dim:].astype(jnp.bfloat16)
    values = key_vals[:, head_dim:]

    route = [(i, i + 1) for i in range(n_ctx - 1)]
    prev_kv = lax.ppermute(key_vals, "ctx", route)
    vals_all = lax.all_gather(values, "ctx").reshape(n_ctx * rows, head_dim)
    cache_v = lax.dot_general(
        onehot, vals_all, (((0,), (0,)), ((), ())), preferred_element_type=jnp.float32
    )

    ext_kv = jnp.concatenate([prev_kv, key_vals], axis=0)
    attended = attend_block(
        queries,
        ext_kv[:, :head_dim],
        ext_kv[:, head_dim:],
        cache_v,
        cache_c,
        codebook[0],
        reach[0],
        g > 0,
        BLK,
        scale,
    )

    return reduce_out(attended, w_out, sizes)


def project(tokens_in, w_qkv, sizes):
    nx, ny, nc = sizes
    core_perm = _core_perm(*sizes)
    me_x, me_y, me_c = lax.axis_index("hx"), lax.axis_index("hy"), lax.axis_index("hc")
    rows, width = tokens_in.shape
    half = rows // 2
    mine = lax.dynamic_slice_in_dim(tokens_in, me_c * half, half, 0)
    other = lax.dynamic_slice_in_dim(tokens_in, (1 - me_c) * half, half, 0)
    got = _send(other, core_perm)
    chip = jnp.where(
        me_c == 0, jnp.concatenate([mine, got], axis=1), jnp.concatenate([got, mine], axis=1)
    )
    g1 = gather_ring(chip, 0, sizes)
    g2 = gather_ring(g1, 1, sizes)
    g2p = _send(g2, core_perm)

    w_local = w_qkv[:, 0, :]
    nw = w_local.shape[1]
    w16 = w_local.reshape(nx * ny, nc * width, nw)
    k2 = jnp.arange(4, dtype=jnp.int32)[:, None]
    k1 = jnp.arange(4, dtype=jnp.int32)[None, :]

    def source_rows(cc):
        xs = jnp.where(cc == 0, (me_x - k2) % nx, (me_x - k1) % nx)
        ys = jnp.where(cc == 0, (me_y - k1) % ny, (me_y - k2) % ny)
        return (xs * ny + ys).reshape(nx * ny)

    w_own = jnp.take(w16, source_rows(me_c), axis=0, mode="clip")
    w_oth = jnp.take(w16, source_rows(1 - me_c), axis=0, mode="clip")
    dims = (((0, 2), (0, 1)), ((), ()))
    proj_own = lax.dot_general(
        g2.reshape(nx * ny, half, nc * width), w_own, dims, preferred_element_type=jnp.float32
    )
    proj_oth = lax.dot_general(
        g2p.reshape(nx * ny, half, nc * width), w_oth, dims, preferred_element_type=jnp.float32
    )
    projected = jnp.where(
        me_c == 0,
        jnp.concatenate([proj_own, proj_oth], axis=0),
        jnp.concatenate([proj_oth, proj_own], axis=0),
    )
    return projected


def reduce_out(attended, w_out, sizes):
    nx, ny, nc = sizes
    core_perm = _core_perm(*sizes)
    me_x, me_y, me_c = lax.axis_index("hx"), lax.axis_index("hy"), lax.axis_index("hc")
    rows = attended.shape[0]
    e1 = jnp.arange(4, dtype=jnp.int32)[:, None, None, None]
    e2 = jnp.arange(4, dtype=jnp.int32)[None, :, None, None]
    ch = jnp.arange(nc, dtype=jnp.int32)[None, None, :, None]
    t = jnp.arange(rows // (nx * ny * nc), dtype=jnp.int32)[None, None, None, :]
    tt = t.shape[-1]

    def row_order(cc):
        xh = jnp.where(cc == 0, (me_x + e2) % nx, (me_x + e1) % nx)
        yh = jnp.where(cc == 0, (me_y + e1) % ny, (me_y + e2) % ny)
        return (((xh * ny + yh) * nc + ch) * tt + t).reshape(rows)

    w_full = w_out[0]
    cols = w_full.shape[1] // 2
    w_keep = lax.dynamic_slice_in_dim(w_full, me_c * cols, cols, 1)
    w_give = lax.dynamic_slice_in_dim(w_full, (1 - me_c) * cols, cols, 1)
    own_rows = jnp.take(attended, row_order(me_c), axis=0, mode="clip")
    oth_rows = jnp.take(attended, row_order(1 - me_c), axis=0, mode="clip")
    keep = jnp.dot(own_rows, w_keep, preferred_element_type=jnp.float32)
    give = jnp.dot(oth_rows, w_give, preferred_element_type=jnp.float32)
    got = _send(give.astype(jnp.bfloat16), core_perm)
    summed = (keep + got.astype(jnp.float32)).reshape(4, 4, nc, rows // (nx * ny * nc), cols)
    r1 = reduce_ring(summed, 0, sizes)
    r2 = reduce_ring(r1, 1, sizes)
    mine = lax.dynamic_index_in_dim(r2, me_c, 0, keepdims=False)
    other = lax.dynamic_index_in_dim(r2, 1 - me_c, 0, keepdims=False)
    got = _send(other.astype(jnp.bfloat16), core_perm).astype(jnp.float32)
    out = jnp.where(
        me_c == 0, jnp.concatenate([mine, got], axis=1), jnp.concatenate([got, mine], axis=1)
    )
    return out.astype(jnp.bfloat16)


def solution(mesh):
    n_ctx, n_head = mesh.devices.shape
    devices = mesh.devices.reshape(n_ctx, 4, 4, n_head // 16)
    grid = Mesh(devices, ("ctx",) + HEAD_AXES)
    in_specs = (
        P("ctx", HEAD_AXES),
        P(None, HEAD_AXES, None),
        P(HEAD_AXES, None, None),
        P(HEAD_AXES, None, None),
        P(HEAD_AXES, "ctx"),
        P("ctx"),
    )
    out_specs = P(("ctx",) + HEAD_AXES, None)
    return jax.shard_map(
        on_device, mesh=grid, in_specs=in_specs, out_specs=out_specs, check_vma=False
    )
```

time: 298 us -> 213 us (0.71)
  waiting for transfers between devices: 204 us -> 48.8 us
  starting transfers between devices: 4.56 us -> 88.5 us
  other arithmetic: 31 us -> 9.54 us
  local copies, waits for them, and re-layouts: 2.87 us -> 11.9 us
    reduce_scatter x1 -> x0, waiting for transfers between devices: 105 us -> none  [on_device(): lax.psum_scatter(jnp.dot(pieces_out, w_proj, preferred_element_type=jnp.f...]
    ppermute x2 -> x21, starting transfers between devices: 4.48 us -> 88.5 us  [the longest x20 86.6 us: _send(): return lax.ppermute(value, HEAD_AXES, perm)]
    all_gather x2 -> x1, waiting for transfers between devices: 97.3 us -> 28.6 us  [on_device(): vals_all = lax.all_gather(values, 'ctx').reshape(n_ctx * rows, head_dim)]
    ppermute x2 -> x21, waiting for transfers between devices: 1.01 us -> 20.2 us  [the longest x20 17.9 us: _send(): return lax.ppermute(value, HEAD_AXES, perm)]
    select_n x32 -> x4, other arithmetic: 16.8 us -> 0.06 us  [the longest x2 0.03 us: project(): jnp.where(me_c == 0, jnp.concatenate([mine, got], axis=1), jnp.concatenat...]
    convert_element_type x17 -> x1, other arithmetic: 11.3 us -> 0.64 us  [reduce_out(): return out.astype(jnp.bfloat16)]
    gather x0 -> x4, local copies, waits for them, and re-layouts: none -> 7.02 us  [the longest x1 2.69 us: project(): w_own = jnp.take(w16, source_rows(me_c), axis=0, mode='clip')]
    dot_general x5 -> x6, matrix products: 10 us -> 14.5 us  [the longest x1 4.79 us: on_device(): lax.dot_general(onehot, vals_all, (((0,), (0,)), ((), ())), preferred_ele...]
  transfers between devices with their start and end apart: 5 -> 22, of which waited for: 4 -> 14; matrix products, arithmetic and copies ran while one was open for 2% -> 8% of each run, Pallas kernels for 0% -> 0%
where the time goes in v1:
time: 213 us
  starting transfers between devices  88.5 us (42%)
  waiting for transfers between devices  48.8 us (23%)
  blocking collectives  22.8 us (11%)
  matrix products  16.4 us (8%)
  between operations  14.7 us (7%)
  local copies, waits for them, and re-layouts  11.9 us (6%)
  other arithmetic  9.54 us (4%)
    ppermute x20, starting transfers between devices, _send(): return lax.ppermute(value, HEAD_AXES, perm)  86.6 us
    all_gather x1, waiting for transfers between devices, on_device(): vals_all = lax.all_gather(values, 'ctx').reshape(n_ctx * rows, head_dim)  28.6 us
    all_gather x1, blocking collectives, on_device(): codes_all = lax.all_gather(code_row, 'ctx').reshape(n_ctx * rows)  22.8 us
    ppermute x20, waiting for transfers between devices, _send(): return lax.ppermute(value, HEAD_AXES, perm)  17.9 us
    dot_general x1, matrix products, on_device(): lax.dot_general(onehot, vals_all, (((0,), (0,)), ((), ())), preferred_ele...  4.79 us
  transfers between devices with their start and end apart: 22, of which 14 were waited for; matrix products, arithmetic and copies ran while one was open for 8% of the time, Pallas kernels for 0%

profile of v1, /device:TPU:1, one launch (start us, length us, event | category | flops | bytes accessed | tf_op | source)
XLA Modules:
  0.0 212.5 jit_solution(14787387796997774650)
XLA Ops:
  6.5 0.9 constant_dynamic-slice_fusion.1
  7.5 8.9 %collective-permute-start = (bf16[128,128]{1,0:T(8,128)(2,1)S(1)}, bf16[128,128]{1,0:T(8,128)(2,1)S(1)}, u32[]{:S(2)}, u32[]{:S(2)}) collective-permute-start(bf16[128,128]{1,0:T(8,128)(2,1)S(1)} %get-tuple-element.24), channel_id=1, source_target_pairs={{0,1},{1,0},{2,3},{3,2},{4,5},{5,4},{6,7},{7,6},{8,9},{9,8},{10,11... | collective-permute-start | bytes 98312 | tf_op jit(solution)/shard_map/ppermute | solution.py:41
  16.4 0.8 collective-permute-done
  17.2 1.9 collective-permute-start.1
  19.2 4.6 %collective-permute-start.3 = (bf16[128,256]{1,0:T(8,128)(2,1)S(1)}, bf16[128,256]{1,0:T(8,128)(2,1)S(1)}, u32[]{:S(2)}, u32[]{:S(2)}) collective-permute-start(bf16[128,256]{1,0:T(8,128)(2,1)S(1)} %maximum_select_fusion.3), channel_id=1, source_target_pairs={{0,6},{1,25},{2,0},{3,27},{4,2},{5,29},{6,4},{7,31},{8,14},{9,1},{... | collective-permute-start | bytes 196616 | tf_op jit(solution)/shard_map/ppermute | solution.py:41
  23.8 1.9 collective-permute-start.2
  25.7 4.6 %collective-permute-start.4 = (bf16[64,256]{1,0:T(8,128)(2,1)S(1)}, bf16[64,256]{1,0:T(8,128)(2,1)S(1)}, u32[]{:S(2)}, u32[]{:S(2)}) collective-permute-start(bf16[64,256]{1,0:T(8,128)(2,1)S(1)} %slice.113), channel_id=1, source_target_pairs={{0,6},{1,25},{2,0},{3,27},{4,2},{5,29},{6,4},{7,31},{8,14},{9,1},{... | collective-permute-start | bytes 98312 | tf_op jit(solution)/shard_map/ppermute | solution.py:41
  30.3 1.0 collective-permute-done.4
  31.3 0.7 fusion.65
  32.1 1.9 collective-permute-start.5
  34.0 4.6 %collective-permute-start.7 = (bf16[4,128,256]{2,1,0:T(8,128)(2,1)}, bf16[4,128,256]{2,1,0:T(8,128)(2,1)}, u32[]{:S(2)}, u32[]{:S(2)}) collective-permute-start(bf16[4,128,256]{2,1,0:T(8,128)(2,1)} %get-tuple-element.20), channel_id=1, source_target_pairs={{0,24},{1,7},{2,26},{3,1},{4,28},{5,3},{6,30},{7,5},{8,0},{9,15},{... | collective-permute-start | bytes 786440 | tf_op jit(solution)/shard_map/ppermute | solution.py:41
  38.6 2.4 %collective-permute-done.5 = bf16[4,128,256]{2,1,0:T(8,128)(2,1)} collective-permute-done((bf16[4,128,256]{2,1,0:T(8,128)(2,1)}, bf16[4,128,256]{2,1,0:T(8,128)(2,1)}, u32[]{:S(2)}, u32[]{:S(2)}) %collective-permute-start.5) | collective-permute-done | bytes 262176 | tf_op jit(solution)/shard_map/ppermute | solution.py:41
  41.0 0.9 slice.114
  41.9 1.9 collective-permute-start.6
  43.8 1.6 slice.115
  45.4 4.6 %collective-permute-start.8 = (bf16[2,128,256]{2,1,0:T(8,128)(2,1)}, bf16[2,128,256]{2,1,0:T(8,128)(2,1)}, u32[]{:S(2)}, u32[]{:S(2)}) collective-permute-start(bf16[2,128,256]{2,1,0:T(8,128)(2,1)} %slice.115), channel_id=1, source_target_pairs={{0,24},{1,7},{2,26},{3,1},{4,28},{5,3},{6,30},{7,5},{8,0},{9,15},{... | collective-permute-start | bytes 393224 | tf_op jit(solution)/shard_map/ppermute | solution.py:41
  50.2 2.0 collective-permute-done.8
  52.2 1.0 maximum_bitcast_fusion
  53.2 2.1 pad_maximum_fusion
  55.3 6.2 %collective-permute-start.9 = (bf16[4,4,128,256]{3,2,1,0:T(8,128)(2,1)}, bf16[4,4,128,256]{3,2,1,0:T(8,128)(2,1)}, u32[]{:S(2)}, u32[]{:S(2)}) collective-permute-start(bf16[4,4,128,256]{3,2,1,0:T(8,128)(2,1)} %pad_maximum_fusion), channel_id=1, source_target_pairs={{0,1},{1,0},{2,3},{3,2},{4,5},{5,4},{6,7},{7,6},{8,9},{9,8},{10,11... | collective-permute-start | bytes 3145736 | tf_op jit(solution)/shard_map/ppermute | solution.py:41
  61.6 2.6 %gather_fusion.1 = bf16[16,256,384]{2,1,0:T(8,128)(2,1)} fusion(bf16[16,256,384]{2,1,0:T(8,128)(2,1)S(1)} %bitcast.101, s32[1024]{0:T(1024)S(1)} %pad_clamp_fusion.2), kind=kCustom, calls=%fused_computation.1 | custom fusion | bytes 6291520 | tf_op jit(solution)/shard_map/jit(_take)/gather | solution.py:174
  64.2 2.7 %gather_fusion = bf16[16,256,384]{2,1,0:T(8,128)(2,1)} fusion(bf16[16,256,384]{2,1,0:T(8,128)(2,1)S(1)} %bitcast.100, s32[1024]{0:T(1024)S(1)} %pad_clamp_fusion.3), kind=kCustom, calls=%fused_computation | custom fusion | bytes 6291520 | tf_op jit(solution)/shard_map/jit(_take)/gather | solution.py:173
  67.0 3.1 %convolution_bitcast_fusion.1 = bf16[128,384]{1,0:T(8,128)(2,1)S(1)} fusion(bf16[16,128,256]{2,1,0:T(8,128)(2,1)} %bitcast.10, bf16[16,256,384]{2,1,0:T(8,128)(2,1)} %gather_fusion), kind=kOutput, calls=%fused_computation.16 | convolution fusion | flops 402653184 | bytes 4292608 | tf_op jit(solution)/shard_map/dot_general | solution.py:176
  70.2 2.0 convolution_bitcast_fusion
  72.2 0.6 slice.120
  73.7 22.8 %all-gather.1 = s32[16,1,256]{2,1,0:T(1,128)S(1)} all-gather(s32[1,1,256]{2,1,0:T(1,128)S(1)} %bitcast.113), channel_id=1, replica_groups=mesh['ctx'=16,'hx'=4,'hy'=4,'hc'=2] {'ctx'}, dimensions={0}, use_global_device_ids=true | all-gather | bytes 17408 | tf_op jit(solution)/shard_map/all_gather | solution.py:110
  96.6 2.8 %convert_reduce_fusion = f32[512]{0:T(512)S(1)} fusion(s32[4096]{0:T(1024)S(1)} %bitcast.109, pred[4096]{0:T(1024)(128)(4,1)S(1)} %iota_compare_fusion.2), kind=kLoop, calls=%fused_computation.4 | loop fusion | flops 10485248 | bytes 22528 | tf_op jit(solution)/shard_map/reduce_sum | solution.py:115
  99.5 1.8 collective-permute-start.10
  101.3 0.3 select_reduce_fusion
  101.6 2.3 %collective-permute-done.10 = bf16[256,256]{1,0:T(8,128)(2,1)S(1)} collective-permute-done((bf16[256,256]{1,0:T(8,128)(2,1)S(1)}, bf16[256,256]{1,0:T(8,128)(2,1)S(1)}, u32[]{:S(2)}, u32[]{:S(2)}) %collective-permute-start.10) | collective-permute-done | bytes 131104 | tf_op jit(solution)/shard_map/ppermute | solution.py:123
  103.9 0.3 select_reduce_fusion.1
  104.3 0.3 copy-done.11
  104.5 0.3 fusion.20
  104.8 0.6 fusion.17
  105.5 28.6 %all-gather.4.cloned.1.call-done = bf16[4096,128]{1,0:T(8,128)(2,1)} async-done(((bf16[256,128]{1,0:T(8,128)(2,1)}), bf16[4096,128]{1,0:T(8,128)(2,1)}) %all-gather.4.cloned.1.call-update) | async-done | bytes 1048592 | tf_op jit(solution)/shard_map/all_gather | solution.py:124
  134.1 4.8 %fusion.1 = f32[512,128]{1,0:T(8,128)S(1)} fusion(bf16[4096,128]{1,0:T(8,128)(2,1)} %all-gather.4.cloned.1.call-done, s32[4096]{0:T(1024)S(1)} %bitcast.110, pred[4096]{0:T(1024)(128)(4,1)S(1)} %iota_compare_fusion.2), kind=kOutput, calls=%fused_computation.7 | convolution fusion | flops 541065216 | bytes 1331200 | tf_op jit(solution)/shard_map/dot_general | solution.py:125
  138.9 0.6 fusion.18
  139.6 0.3 fusion.7
  139.9 0.9 gather_fusion.3
  140.8 2.4 %convolution_convert_fusion = bf16[256,2048]{1,0:T(8,128)(2,1)} fusion(bf16[256,128]{1,0:T(8,128)(2,1)S(1)} %gather_fusion.3, bf16[1,128,4096]{2,1,0:T(8,128)(2,1)} %param.8, s32[]{:T(128)S(6)} %select_n.281), kind=kOutput, calls=%fused_computation.11 | convolution fusion | flops 134742016 | bytes 1638404 | tf_op jit(solution)/shard_map/dot_general | solution.py:213
  143.2 12.2 %collective-permute-start.11 = (bf16[256,2048]{1,0:T(8,128)(2,1)}, bf16[256,2048]{1,0:T(8,128)(2,1)}, u32[]{:S(2)}, u32[]{:S(2)}) collective-permute-start(bf16[256,2048]{1,0:T(8,128)(2,1)} %convolution_convert_fusion), channel_id=1, source_target_pairs={{0,1},{1,0},{2,3},{3,2},{4,5},{5,4},{6,7},{7,6},{8,9},{9,8},{10,11... | collective-permute-start | bytes 3145736 | tf_op jit(solution)/shard_map/ppermute | solution.py:41
  155.6 0.1 reshape.624
  155.7 0.9 gather_fusion.2
  156.5 1.5 collective-permute-done.11
  158.0 1.8 convert_add_fusion
  159.8 0.1 convert.37
  160.0 3.1 %collective-permute-start.12 = (bf16[2,2,8,2048]{3,2,1,0:T(8,128)(2,1)S(1)}, bf16[2,2,8,2048]{3,2,1,0:T(8,128)(2,1)S(1)}, u32[]{:S(2)}, u32[]{:S(2)}) collective-permute-start(bf16[2,2,8,2048]{3,2,1,0:T(8,128)(2,1)S(1)} %get-tuple-element.9), channel_id=1, source_target_pairs={{0,2},{1,9},{2,4},{3,11},{4,6},{5,13},{6,0},{7,15},{8,10},{9,17},{... | collective-permute-start | bytes 393224 | tf_op jit(solution)/shard_map/ppermute | solution.py:41
  163.1 3.4 %collective-permute-start.14 = (bf16[2,2,8,2048]{3,2,1,0:T(8,128)(2,1)S(1)}, bf16[2,2,8,2048]{3,2,1,0:T(8,128)(2,1)S(1)}, u32[]{:S(2)}, u32[]{:S(2)}) collective-permute-start(bf16[2,2,8,2048]{3,2,1,0:T(8,128)(2,1)S(1)} %get-tuple-element.10), channel_id=1, source_target_pairs={{0,6},{1,25},{2,0},{3,27},{4,2},{5,29},{6,4},{7,31},{8,14},{9,1},{... | collective-permute-start | bytes 393224 | tf_op jit(solution)/shard_map/ppermute | solution.py:41
  166.5 0.7 collective-permute-done.12
  167.2 1.9 collective-permute-done.14
  169.2 3.1 %collective-permute-start.13 = (bf16[4,2,8,2048]{3,2,1,0:T(8,128)(2,1)S(1)}, bf16[4,2,8,2048]{3,2,1,0:T(8,128)(2,1)S(1)}, u32[]{:S(2)}, u32[]{:S(2)}) collective-permute-start(bf16[4,2,8,2048]{3,2,1,0:T(8,128)(2,1)S(1)} %pad_maximum_fusion.2), channel_id=1, source_target_pairs={{0,2},{1,9},{2,4},{3,11},{4,6},{5,13},{6,0},{7,15},{8,10},{9,17},{... | collective-permute-start | bytes 786440 | tf_op jit(solution)/shard_map/ppermute | solution.py:41
  172.4 3.4 %collective-permute-start.15 = (bf16[4,2,8,2048]{3,2,1,0:T(8,128)(2,1)S(1)}, bf16[4,2,8,2048]{3,2,1,0:T(8,128)(2,1)S(1)}, u32[]{:S(2)}, u32[]{:S(2)}) collective-permute-start(bf16[4,2,8,2048]{3,2,1,0:T(8,128)(2,1)S(1)} %pad_maximum_fusion.3), channel_id=1, source_target_pairs={{0,6},{1,25},{2,0},{3,27},{4,2},{5,29},{6,4},{7,31},{8,14},{9,1},{... | collective-permute-start | bytes 786440 | tf_op jit(solution)/shard_map/ppermute | solution.py:41
  175.8 2.0 collective-permute-done.13
  177.8 2.0 collective-permute-done.15
  179.9 3.1 %collective-permute-start.16 = (bf16[1,8,2048]{2,1,0:T(8,128)(2,1)S(1)}, bf16[1,8,2048]{2,1,0:T(8,128)(2,1)S(1)}, u32[]{:S(2)}, u32[]{:S(2)}) collective-permute-start(bf16[1,8,2048]{2,1,0:T(8,128)(2,1)S(1)} %get-tuple-element.15), channel_id=1, source_target_pairs={{0,8},{1,3},{2,10},{3,5},{4,12},{5,7},{6,14},{7,1},{8,16},{9,11},{... | collective-permute-start | bytes 98312 | tf_op jit(solution)/shard_map/ppermute | solution.py:41
  183.0 3.4 %collective-permute-start.18 = (bf16[1,8,2048]{2,1,0:T(8,128)(2,1)S(1)}, bf16[1,8,2048]{2,1,0:T(8,128)(2,1)S(1)}, u32[]{:S(2)}, u32[]{:S(2)}) collective-permute-start(bf16[1,8,2048]{2,1,0:T(8,128)(2,1)S(1)} %get-tuple-element.16), channel_id=1, source_target_pairs={{0,24},{1,7},{2,26},{3,1},{4,28},{5,3},{6,30},{7,5},{8,0},{9,15},{... | collective-permute-start | bytes 98312 | tf_op jit(solution)/shard_map/ppermute | solution.py:41
  186.4 1.3 collective-permute-done.18
  187.7 3.1 %collective-permute-start.17 = (bf16[2,8,2048]{2,1,0:T(8,128)(2,1)S(1)}, bf16[2,8,2048]{2,1,0:T(8,128)(2,1)S(1)}, u32[]{:S(2)}, u32[]{:S(2)}) collective-permute-start(bf16[2,8,2048]{2,1,0:T(8,128)(2,1)S(1)} %pad_maximum_fusion.6), channel_id=1, source_target_pairs={{0,8},{1,3},{2,10},{3,5},{4,12},{5,7},{6,14},{7,1},{8,16},{9,11},{... | collective-permute-start | bytes 196616 | tf_op jit(solution)/shard_map/ppermute | solution.py:41
  190.8 3.4 %collective-permute-start.19 = (bf16[2,8,2048]{2,1,0:T(8,128)(2,1)S(1)}, bf16[2,8,2048]{2,1,0:T(8,128)(2,1)S(1)}, u32[]{:S(2)}, u32[]{:S(2)}) collective-permute-start(bf16[2,8,2048]{2,1,0:T(8,128)(2,1)S(1)} %pad_maximum_fusion.7), channel_id=1, source_target_pairs={{0,24},{1,7},{2,26},{3,1},{4,28},{5,3},{6,30},{7,5},{8,0},{9,15},{... | collective-permute-start | bytes 196616 | tf_op jit(solution)/shard_map/ppermute | solution.py:41
  194.3 1.5 collective-permute-done.19
  195.8 0.9 fusion.41
  196.8 7.4 %collective-permute-start.20 = (bf16[8,2048]{1,0:T(8,128)(2,1)S(1)}, bf16[8,2048]{1,0:T(8,128)(2,1)S(1)}, u32[]{:S(2)}, u32[]{:S(2)}) collective-permute-start(bf16[8,2048]{1,0:T(8,128)(2,1)S(1)} %get-tuple-element.22), channel_id=1, source_target_pairs={{0,1},{1,0},{2,3},{3,2},{4,5},{5,4},{6,7},{7,6},{8,9},{9,8},{10,11... | collective-permute-start | bytes 98312 | tf_op jit(solution)/shard_map/ppermute | solution.py:41
  204.2 0.8 collective-permute-done.20
  205.0 0.6 fusion.43
  (75 shorter events, 1.3 us)
Async XLA Ops:
  6.5 55.0 %copy-start = (bf16[4096,1,384]{2,0,1:T(8,128)(2,1)S(1)}, bf16[4096,1,384]{2,0,1:T(8,128)(2,1)}, u32[]{:S(2)}) copy-start(bf16[4096,1,384]{2,0,1:T(8,128)(2,1)} %param.7) | copy-start | bytes 9437188
  6.5 127.5 %all-gather.4.cloned.1.call-start = ((), (), s32[]{:S(2)}) async-start(), calls=%async_computation | async-start | bytes 1114112 | tf_op jit(solution)/shard_map/all_gather | solution.py:124
  7.5 9.8 %collective-permute-start = (bf16[128,128]{1,0:T(8,128)(2,1)S(1)}, bf16[128,128]{1,0:T(8,128)(2,1)S(1)}, u32[]{:S(2)}, u32[]{:S(2)}) collective-permute-start(bf16[128,128]{1,0:T(8,128)(2,1)S(1)} %get-tuple-element.24), channel_id=1, source_target_pairs={{0,1},{1,0},{2,3},{3,2},{4,5},{5,4},{6,7},{7,6},{8,9},{9,8},{10,11... | collective-permute-start | bytes 98312 | tf_op jit(solution)/shard_map/ppermute | solution.py:41
  17.2 6.5 %collective-permute-start.1 = (bf16[128,256]{1,0:T(8,128)(2,1)S(1)}, bf16[128,256]{1,0:T(8,128)(2,1)S(1)}, u32[]{:S(2)}, u32[]{:S(2)}) collective-permute-start(bf16[128,256]{1,0:T(8,128)(2,1)S(1)} %maximum_select_fusion.3), channel_id=1, source_target_pairs={{0,2},{1,9},{2,4},{3,11},{4,6},{5,13},{6,0},{7,15},{8,10},{9,17},{... | collective-permute-start | bytes 196616 | tf_op jit(solution)/shard_map/ppermute | solution.py:41
  19.2 6.5 %collective-permute-start.3 = (bf16[128,256]{1,0:T(8,128)(2,1)S(1)}, bf16[128,256]{1,0:T(8,128)(2,1)S(1)}, u32[]{:S(2)}, u32[]{:S(2)}) collective-permute-start(bf16[128,256]{1,0:T(8,128)(2,1)S(1)} %maximum_select_fusion.3), channel_id=1, source_target_pairs={{0,6},{1,25},{2,0},{3,27},{4,2},{5,29},{6,4},{7,31},{8,14},{9,1},{... | collective-permute-start | bytes 196616 | tf_op jit(solution)/shard_map/ppermute | solution.py:41
  23.8 6.6 %collective-permute-start.2 = (bf16[64,256]{1,0:T(8,128)(2,1)S(1)}, bf16[64,256]{1,0:T(8,128)(2,1)S(1)}, u32[]{:S(2)}, u32[]{:S(2)}) collective-permute-start(bf16[64,256]{1,0:T(8,128)(2,1)S(1)} %slice.112), channel_id=1, source_target_pairs={{0,2},{1,9},{2,4},{3,11},{4,6},{5,13},{6,0},{7,15},{8,10},{9,17},{... | collective-permute-start | bytes 98312 | tf_op jit(solution)/shard_map/ppermute | solution.py:41
  25.7 5.6 %collective-permute-start.4 = (bf16[64,256]{1,0:T(8,128)(2,1)S(1)}, bf16[64,256]{1,0:T(8,128)(2,1)S(1)}, u32[]{:S(2)}, u32[]{:S(2)}) collective-permute-start(bf16[64,256]{1,0:T(8,128)(2,1)S(1)} %slice.113), channel_id=1, source_target_pairs={{0,6},{1,25},{2,0},{3,27},{4,2},{5,29},{6,4},{7,31},{8,14},{9,1},{... | collective-permute-start | bytes 98312 | tf_op jit(solution)/shard_map/ppermute | solution.py:41
  32.1 8.9 %collective-permute-start.5 = (bf16[4,128,256]{2,1,0:T(8,128)(2,1)}, bf16[4,128,256]{2,1,0:T(8,128)(2,1)}, u32[]{:S(2)}, u32[]{:S(2)}) collective-permute-start(bf16[4,128,256]{2,1,0:T(8,128)(2,1)} %get-tuple-element.20), channel_id=1, source_target_pairs={{0,8},{1,3},{2,10},{3,5},{4,12},{5,7},{6,14},{7,1},{8,16},{9,11},{... | collective-permute-start | bytes 786440 | tf_op jit(solution)/shard_map/ppermute | solution.py:41
  34.0 9.9 %collective-permute-start.7 = (bf16[4,128,256]{2,1,0:T(8,128)(2,1)}, bf16[4,128,256]{2,1,0:T(8,128)(2,1)}, u32[]{:S(2)}, u32[]{:S(2)}) collective-permute-start(bf16[4,128,256]{2,1,0:T(8,128)(2,1)} %get-tuple-element.20), channel_id=1, source_target_pairs={{0,24},{1,7},{2,26},{3,1},{4,28},{5,3},{6,30},{7,5},{8,0},{9,15},{... | collective-permute-start | bytes 786440 | tf_op jit(solution)/shard_map/ppermute | solution.py:41
  41.9 8.3 %collective-permute-start.6 = (bf16[2,128,256]{2,1,0:T(8,128)(2,1)S(1)}, bf16[2,128,256]{2,1,0:T(8,128)(2,1)}, u32[]{:S(2)}, u32[]{:S(2)}) collective-permute-start(bf16[2,128,256]{2,1,0:T(8,128)(2,1)S(1)} %slice.114), channel_id=1, source_target_pairs={{0,8},{1,3},{2,10},{3,5},{4,12},{5,7},{6,14},{7,1},{8,16},{9,11},{... | collective-permute-start | bytes 393224 | tf_op jit(solution)/shard_map/ppermute | solution.py:41
  45.4 6.8 %collective-permute-start.8 = (bf16[2,128,256]{2,1,0:T(8,128)(2,1)}, bf16[2,128,256]{2,1,0:T(8,128)(2,1)}, u32[]{:S(2)}, u32[]{:S(2)}) collective-permute-start(bf16[2,128,256]{2,1,0:T(8,128)(2,1)} %slice.115), channel_id=1, source_target_pairs={{0,24},{1,7},{2,26},{3,1},{4,28},{5,3},{6,30},{7,5},{8,0},{9,15},{... | collective-permute-start | bytes 393224 | tf_op jit(solution)/shard_map/ppermute | solution.py:41
  55.3 14.8 %collective-permute-start.9 = (bf16[4,4,128,256]{3,2,1,0:T(8,128)(2,1)}, bf16[4,4,128,256]{3,2,1,0:T(8,128)(2,1)}, u32[]{:S(2)}, u32[]{:S(2)}) collective-permute-start(bf16[4,4,128,256]{3,2,1,0:T(8,128)(2,1)} %pad_maximum_fusion), channel_id=1, source_target_pairs={{0,1},{1,0},{2,3},{3,2},{4,5},{5,4},{6,7},{7,6},{8,9},{9,8},{10,11... | collective-permute-start | bytes 3145736 | tf_op jit(solution)/shard_map/ppermute | solution.py:41
  66.9 3.3 %copy-start.1 = (bf16[16,256,384]{2,1,0:T(8,128)(2,1)S(1)}, bf16[16,256,384]{2,1,0:T(8,128)(2,1)}, u32[]{:S(2)}) copy-start(bf16[16,256,384]{2,1,0:T(8,128)(2,1)} %gather_fusion.1) | copy-start | bytes 9437188
  70.1 3.6 %copy-start.10 = (s32[1,256]{1,0:T(1,128)S(1)}, s32[1,256]{1,0:T(1,128)}, u32[]{:S(2)}) copy-start(s32[1,256]{1,0:T(1,128)} %param.10) | copy-start | bytes 3076
  70.1 31.2 %copy-start.7 = (bf16[1,512,128]{2,1,0:T(8,128)(2,1)S(1)}, bf16[1,512,128]{2,1,0:T(8,128)(2,1)}, u32[]{:S(2)}) copy-start(bf16[1,512,128]{2,1,0:T(8,128)(2,1)} %param.9) | copy-start | bytes 393220
  99.5 4.8 %copy-start.8 = (bf16[256,256]{1,0:T(8,128)(2,1)}, bf16[256,256]{1,0:T(8,128)(2,1)S(1)}, u32[]{:S(2)}) copy-start(bf16[256,256]{1,0:T(8,128)(2,1)S(1)} %slice.117) | copy-start | bytes 393220
  99.5 4.4 %collective-permute-start.10 = (bf16[256,256]{1,0:T(8,128)(2,1)S(1)}, bf16[256,256]{1,0:T(8,128)(2,1)S(1)}, u32[]{:S(2)}, u32[]{:S(2)}) collective-permute-start(bf16[256,256]{1,0:T(8,128)(2,1)S(1)} %slice.117), channel_id=1, source_target_pairs={{0,32},{32,64},{64,96},{96,128},{128,160},{160,192},{192,224},{224... | collective-permute-start | bytes 393224 | tf_op jit(solution)/shard_map/ppermute | solution.py:123
  101.6 3.2 %copy-start.2 = (f32[256,512]{1,0:T(8,128)}, f32[256,512]{1,0:T(8,128)S(1)}, u32[]{:S(2)}) copy-start(f32[256,512]{1,0:T(8,128)S(1)} %get-tuple-element.32) | copy-start | bytes 1572868
  103.9 0.6 copy-start.11
  104.2 1.2 copy-start.5
  105.5 34.0 %copy-start.9 = (bf16[256,256]{1,0:T(8,128)(2,1)S(1)}, bf16[256,256]{1,0:T(8,128)(2,1)}, u32[]{:S(2)}) copy-start(bf16[256,256]{1,0:T(8,128)(2,1)} %copy-done.8) | copy-start | bytes 393220
  134.1 4.8 %copy-start.3 = (f32[256,512]{1,0:T(8,128)S(1)}, f32[256,512]{1,0:T(8,128)}, u32[]{:S(2)}) copy-start(f32[256,512]{1,0:T(8,128)} %copy-done.2) | copy-start | bytes 1572868
  134.1 5.5 %copy-start.6 = (f32[256,512]{1,0:T(8,128)S(1)}, f32[256,512]{1,0:T(8,128)}, u32[]{:S(2)}) copy-start(f32[256,512]{1,0:T(8,128)} %copy-done.5) | copy-start | bytes 1572868
  134.1 5.5 %copy-start.12 = (bf16[256,256]{1,0:T(8,128)(2,1)S(1)}, bf16[256,256]{1,0:T(8,128)(2,1)}, u32[]{:S(2)}) copy-start(bf16[256,256]{1,0:T(8,128)(2,1)} %copy-done.11) | copy-start | bytes 393220
  143.2 14.8 %collective-permute-start.11 = (bf16[256,2048]{1,0:T(8,128)(2,1)}, bf16[256,2048]{1,0:T(8,128)(2,1)}, u32[]{:S(2)}, u32[]{:S(2)}) collective-permute-start(bf16[256,2048]{1,0:T(8,128)(2,1)} %convolution_convert_fusion), channel_id=1, source_target_pairs={{0,1},{1,0},{2,3},{3,2},{4,5},{5,4},{6,7},{7,6},{8,9},{9,8},{10,11... | collective-permute-start | bytes 3145736 | tf_op jit(solution)/shard_map/ppermute | solution.py:41
  160.0 7.2 %collective-permute-start.12 = (bf16[2,2,8,2048]{3,2,1,0:T(8,128)(2,1)S(1)}, bf16[2,2,8,2048]{3,2,1,0:T(8,128)(2,1)S(1)}, u32[]{:S(2)}, u32[]{:S(2)}) collective-permute-start(bf16[2,2,8,2048]{3,2,1,0:T(8,128)(2,1)S(1)} %get-tuple-element.9), channel_id=1, source_target_pairs={{0,2},{1,9},{2,4},{3,11},{4,6},{5,13},{6,0},{7,15},{8,10},{9,17},{... | collective-permute-start | bytes 393224 | tf_op jit(solution)/shard_map/ppermute | solution.py:41
  163.1 6.0 %collective-permute-start.14 = (bf16[2,2,8,2048]{3,2,1,0:T(8,128)(2,1)S(1)}, bf16[2,2,8,2048]{3,2,1,0:T(8,128)(2,1)S(1)}, u32[]{:S(2)}, u32[]{:S(2)}) collective-permute-start(bf16[2,2,8,2048]{3,2,1,0:T(8,128)(2,1)S(1)} %get-tuple-element.10), channel_id=1, source_target_pairs={{0,6},{1,25},{2,0},{3,27},{4,2},{5,29},{6,4},{7,31},{8,14},{9,1},{... | collective-permute-start | bytes 393224 | tf_op jit(solution)/shard_map/ppermute | solution.py:41
  169.2 8.6 %collective-permute-start.13 = (bf16[4,2,8,2048]{3,2,1,0:T(8,128)(2,1)S(1)}, bf16[4,2,8,2048]{3,2,1,0:T(8,128)(2,1)S(1)}, u32[]{:S(2)}, u32[]{:S(2)}) collective-permute-start(bf16[4,2,8,2048]{3,2,1,0:T(8,128)(2,1)S(1)} %pad_maximum_fusion.2), channel_id=1, source_target_pairs={{0,2},{1,9},{2,4},{3,11},{4,6},{5,13},{6,0},{7,15},{8,10},{9,17},{... | collective-permute-start | bytes 786440 | tf_op jit(solution)/shard_map/ppermute | solution.py:41
  172.4 7.4 %collective-permute-start.15 = (bf16[4,2,8,2048]{3,2,1,0:T(8,128)(2,1)S(1)}, bf16[4,2,8,2048]{3,2,1,0:T(8,128)(2,1)S(1)}, u32[]{:S(2)}, u32[]{:S(2)}) collective-permute-start(bf16[4,2,8,2048]{3,2,1,0:T(8,128)(2,1)S(1)} %pad_maximum_fusion.3), channel_id=1, source_target_pairs={{0,6},{1,25},{2,0},{3,27},{4,2},{5,29},{6,4},{7,31},{8,14},{9,1},{... | collective-permute-start | bytes 786440 | tf_op jit(solution)/shard_map/ppermute | solution.py:41
  179.9 7.8 %copy-start.4 = (f32[4,2,8,2048]{3,2,1,0:T(8,128)}, f32[4,2,8,2048]{3,2,1,0:T(8,128)S(1)}, u32[]{:S(2)}) copy-start(f32[4,2,8,2048]{3,2,1,0:T(8,128)S(1)} %get-tuple-element.6) | copy-start | bytes 1572868
  179.9 6.5 %collective-permute-start.16 = (bf16[1,8,2048]{2,1,0:T(8,128)(2,1)S(1)}, bf16[1,8,2048]{2,1,0:T(8,128)(2,1)S(1)}, u32[]{:S(2)}, u32[]{:S(2)}) collective-permute-start(bf16[1,8,2048]{2,1,0:T(8,128)(2,1)S(1)} %get-tuple-element.15), channel_id=1, source_target_pairs={{0,8},{1,3},{2,10},{3,5},{4,12},{5,7},{6,14},{7,1},{8,16},{9,11},{... | collective-permute-start | bytes 98312 | tf_op jit(solution)/shard_map/ppermute | solution.py:41
  183.0 4.7 %collective-permute-start.18 = (bf16[1,8,2048]{2,1,0:T(8,128)(2,1)S(1)}, bf16[1,8,2048]{2,1,0:T(8,128)(2,1)S(1)}, u32[]{:S(2)}, u32[]{:S(2)}) collective-permute-start(bf16[1,8,2048]{2,1,0:T(8,128)(2,1)S(1)} %get-tuple-element.16), channel_id=1, source_target_pairs={{0,24},{1,7},{2,26},{3,1},{4,28},{5,3},{6,30},{7,5},{8,0},{9,15},{... | collective-permute-start | bytes 98312 | tf_op jit(solution)/shard_map/ppermute | solution.py:41
  187.7 6.6 %collective-permute-start.17 = (bf16[2,8,2048]{2,1,0:T(8,128)(2,1)S(1)}, bf16[2,8,2048]{2,1,0:T(8,128)(2,1)S(1)}, u32[]{:S(2)}, u32[]{:S(2)}) collective-permute-start(bf16[2,8,2048]{2,1,0:T(8,128)(2,1)S(1)} %pad_maximum_fusion.6), channel_id=1, source_target_pairs={{0,8},{1,3},{2,10},{3,5},{4,12},{5,7},{6,14},{7,1},{8,16},{9,11},{... | collective-permute-start | bytes 196616 | tf_op jit(solution)/shard_map/ppermute | solution.py:41
  190.8 5.0 %collective-permute-start.19 = (bf16[2,8,2048]{2,1,0:T(8,128)(2,1)S(1)}, bf16[2,8,2048]{2,1,0:T(8,128)(2,1)S(1)}, u32[]{:S(2)}, u32[]{:S(2)}) collective-permute-start(bf16[2,8,2048]{2,1,0:T(8,128)(2,1)S(1)} %pad_maximum_fusion.7), channel_id=1, source_target_pairs={{0,24},{1,7},{2,26},{3,1},{4,28},{5,3},{6,30},{7,5},{8,0},{9,15},{... | collective-permute-start | bytes 196616 | tf_op jit(solution)/shard_map/ppermute | solution.py:41
  196.8 8.3 %collective-permute-start.20 = (bf16[8,2048]{1,0:T(8,128)(2,1)S(1)}, bf16[8,2048]{1,0:T(8,128)(2,1)S(1)}, u32[]{:S(2)}, u32[]{:S(2)}) collective-permute-start(bf16[8,2048]{1,0:T(8,128)(2,1)S(1)} %get-tuple-element.22), channel_id=1, source_target_pairs={{0,1},{1,0},{2,3},{3,2},{4,5},{5,4},{6,7},{7,6},{8,9},{9,8},{10,11... | collective-permute-start | bytes 98312 | tf_op jit(solution)/shard_map/ppermute | solution.py:41
Sparse Core Ops, SparseCore 0:
  73.0 61.0 all-gather.3

commit v2 on v1

--- a/solution.py
+++ b/solution.py
@@ -106,22 +106,29 @@
     scale = 1.0 / math.sqrt(head_dim)
     half = rows // 2
 
-    code_row = codes[0]
-    codes_all = lax.all_gather(code_row, "ctx").reshape(n_ctx * rows)
+    projected = project(tokens_in, w_qkv, sizes)
+    queries = projected[:, :head_dim].astype(jnp.bfloat16)
+    key_vals = projected[:, head_dim:].astype(jnp.bfloat16)
+    values = key_vals[:, head_dim:]
+
+    route = [(i, i + 1) for i in range(n_ctx - 1)]
+    prev_kv = lax.ppermute(key_vals, "ctx", route)
+    code_row = codes[0].reshape(-1, head_dim)
+    hi = (code_row // 16).astype(jnp.bfloat16)
+    lo = (code_row % 16).astype(jnp.bfloat16)
+    pad = jnp.zeros((16 - 2 * code_row.shape[0], head_dim), jnp.bfloat16)
+    blob = jnp.concatenate([values, hi, lo, pad], axis=0)
+    blobs = lax.all_gather(blob, "ctx")
+    vals_all = blobs[:, :rows].reshape(n_ctx * rows, head_dim)
+    nr = code_row.shape[0]
+    hi_all = blobs[:, rows : rows + nr].astype(jnp.int32)
+    lo_all = blobs[:, rows + nr : rows + 2 * nr].astype(jnp.int32)
+    codes_all = (hi_all * 16 + lo_all).reshape(n_ctx * rows)
     limit = g * BLK - reach[0]
     cached = jnp.arange(n_ctx * rows, dtype=jnp.int32) < limit
     code_ids = jnp.arange(num_codes, dtype=jnp.int32)
     onehot = ((codes_all[:, None] == code_ids[None, :]) & cached[:, None]).astype(jnp.bfloat16)
     cache_c = jnp.sum(onehot.astype(jnp.float32), axis=0)
-
-    projected = project(tokens_in, w_qkv, sizes)
-    queries = projected[:, :head_dim].astype(jnp.bfloat16)
-    key_vals = projected[:, head_dim:].astype(jnp.bfloat16)
-    values = key_vals[:, head_dim:]
-
-    route = [(i, i + 1) for i in range(n_ctx - 1)]
-    prev_kv = lax.ppermute(key_vals, "ctx", route)
-    vals_all = lax.all_gather(values, "ctx").reshape(n_ctx * rows, head_dim)
     cache_v = lax.dot_general(
         onehot, vals_all, (((0,), (0,)), ((), ())), preferred_element_type=jnp.float32
     )
@@ -145,40 +152,20 @@
 
 def project(tokens_in, w_qkv, sizes):
     nx, ny, nc = sizes
+    n_head = nx * ny * nc
     core_perm = _core_perm(*sizes)
-    me_x, me_y, me_c = lax.axis_index("hx"), lax.axis_index("hy"), lax.axis_index("hc")
+    me_c = lax.axis_index("hc")
     rows, width = tokens_in.shape
-    half = rows // 2
-    mine = lax.dynamic_slice_in_dim(tokens_in, me_c * half, half, 0)
-    other = lax.dynamic_slice_in_dim(tokens_in, (1 - me_c) * half, half, 0)
-    got = _send(other, core_perm)
-    chip = jnp.where(
-        me_c == 0, jnp.concatenate([mine, got], axis=1), jnp.concatenate([got, mine], axis=1)
-    )
-    g1 = gather_ring(chip, 0, sizes)
-    g2 = gather_ring(g1, 1, sizes)
-    g2p = _send(g2, core_perm)
-
-    w_local = w_qkv[:, 0, :]
-    nw = w_local.shape[1]
-    w16 = w_local.reshape(nx * ny, nc * width, nw)
-    k2 = jnp.arange(4, dtype=jnp.int32)[:, None]
-    k1 = jnp.arange(4, dtype=jnp.int32)[None, :]
-
-    def source_rows(cc):
-        xs = jnp.where(cc == 0, (me_x - k2) % nx, (me_x - k1) % nx)
-        ys = jnp.where(cc == 0, (me_y - k1) % ny, (me_y - k2) % ny)
-        return (xs * ny + ys).reshape(nx * ny)
-
-    w_own = jnp.take(w16, source_rows(me_c), axis=0, mode="clip")
-    w_oth = jnp.take(w16, source_rows(1 - me_c), axis=0, mode="clip")
+    half = rows // nc
+    spread = jnp.broadcast_to(
+        tokens_in.reshape(1, nc, half, width), (n_head // nc, nc, half, width)
+    ).reshape(n_head, half, width)
+    mine = lax.all_to_all(spread, HEAD_AXES, 0, 0, tiled=True)
+    theirs = _send(mine, core_perm)
+    w_local = w_qkv[:, 0, :].reshape(n_head, width, -1)
     dims = (((0, 2), (0, 1)), ((), ()))
-    proj_own = lax.dot_general(
-        g2.reshape(nx * ny, half, nc * width), w_own, dims, preferred_element_type=jnp.float32
-    )
-    proj_oth = lax.dot_general(
-        g2p.reshape(nx * ny, half, nc * width), w_oth, dims, preferred_element_type=jnp.float32
-    )
+    proj_own = lax.dot_general(mine, w_local, dims, preferred_element_type=jnp.float32)
+    proj_oth = lax.dot_general(theirs, w_local, dims, preferred_element_type=jnp.float32)
     projected = jnp.where(
         me_c == 0,
         jnp.concatenate([proj_own, proj_oth], axis=0),
@@ -189,38 +176,21 @@
 
 def reduce_out(attended, w_out, sizes):
     nx, ny, nc = sizes
+    n_head = nx * ny * nc
     core_perm = _core_perm(*sizes)
-    me_x, me_y, me_c = lax.axis_index("hx"), lax.axis_index("hy"), lax.axis_index("hc")
+    me_c = lax.axis_index("hc")
     rows = attended.shape[0]
-    e1 = jnp.arange(4, dtype=jnp.int32)[:, None, None, None]
-    e2 = jnp.arange(4, dtype=jnp.int32)[None, :, None, None]
-    ch = jnp.arange(nc, dtype=jnp.int32)[None, None, :, None]
-    t = jnp.arange(rows // (nx * ny * nc), dtype=jnp.int32)[None, None, None, :]
-    tt = t.shape[-1]
-
-    def row_order(cc):
-        xh = jnp.where(cc == 0, (me_x + e2) % nx, (me_x + e1) % nx)
-        yh = jnp.where(cc == 0, (me_y + e1) % ny, (me_y + e2) % ny)
-        return (((xh * ny + yh) * nc + ch) * tt + t).reshape(rows)
-
     w_full = w_out[0]
-    cols = w_full.shape[1] // 2
-    w_keep = lax.dynamic_slice_in_dim(w_full, me_c * cols, cols, 1)
-    w_give = lax.dynamic_slice_in_dim(w_full, (1 - me_c) * cols, cols, 1)
-    own_rows = jnp.take(attended, row_order(me_c), axis=0, mode="clip")
-    oth_rows = jnp.take(attended, row_order(1 - me_c), axis=0, mode="clip")
-    keep = jnp.dot(own_rows, w_keep, preferred_element_type=jnp.float32)
-    give = jnp.dot(oth_rows, w_give, preferred_element_type=jnp.float32)
+    cols = w_full.shape[1] // nc
+    full = jnp.dot(attended, w_full, preferred_element_type=jnp.float32)
+    keep = lax.dynamic_slice_in_dim(full, me_c * cols, cols, 1)
+    give = lax.dynamic_slice_in_dim(full, (1 - me_c) * cols, cols, 1)
     got = _send(give.astype(jnp.bfloat16), core_perm)
-    summed = (keep + got.astype(jnp.float32)).reshape(4, 4, nc, rows // (nx * ny * nc), cols)
-    r1 = reduce_ring(summed, 0, sizes)
-    r2 = reduce_ring(r1, 1, sizes)
-    mine = lax.dynamic_index_in_dim(r2, me_c, 0, keepdims=False)
-    other = lax.dynamic_index_in_dim(r2, 1 - me_c, 0, keepdims=False)
-    got = _send(other.astype(jnp.bfloat16), core_perm).astype(jnp.float32)
-    out = jnp.where(
-        me_c == 0, jnp.concatenate([mine, got], axis=1), jnp.concatenate([got, mine], axis=1)
-    )
+    summed = (keep + got.astype(jnp.float32)).astype(jnp.bfloat16)
+    chunks = summed.reshape(n_head, rows // n_head, cols)
+    parts = lax.all_to_all(chunks, HEAD_AXES, 0, 0, tiled=True).astype(jnp.float32)
+    parts = parts.reshape(n_head // nc, nc, rows // n_head, cols).sum(axis=0)
+    out = jnp.concatenate([parts[i] for i in range(nc)], axis=1)
     return out.astype(jnp.bfloat16)
 
 

time: 213 us -> 171 us (0.80)
  starting transfers between devices: 88.5 us -> 16.6 us
  blocking collectives: 22.8 us -> 51.3 us
  waiting for transfers between devices: 48.8 us -> 59.2 us
  local copies, waits for them, and re-layouts: 11.9 us -> 5.4 us
    ppermute x20 -> x2, starting transfers between devices: 86.6 us -> 14.2 us  [_send(): return lax.ppermute(value, HEAD_AXES, perm)]
    all_to_all x0 -> x2, blocking collectives: none -> 51.3 us  [the longest x1 27.2 us: project(): mine = lax.all_to_all(spread, HEAD_AXES, 0, 0, tiled=True)]
    all_gather x1, waiting for transfers between devices: 28.6 us -> 53.8 us  [on_device(): blobs = lax.all_gather(blob, 'ctx')]
    all_gather x1 -> x0, blocking collectives: 22.8 us -> none  [on_device(): codes_all = lax.all_gather(code_row, 'ctx').reshape(n_ctx * rows)]
    ppermute x20 -> x2, waiting for transfers between devices: 17.9 us -> 3.38 us  [_send(): return lax.ppermute(value, HEAD_AXES, perm)]
    gather x4 -> x0, local copies, waits for them, and re-layouts: 7.02 us -> none  [the longest x1 2.69 us: project(): w_own = jnp.take(w16, source_rows(me_c), axis=0, mode='clip')]
    another operation x9 -> x1, other arithmetic: 4.21 us -> 0.04 us  [the longest x4 3.87 us: gather_ring(): return jnp.stack([blk, p1, far, m1])]
    convert_element_type x2 -> x1, local copies, waits for them, and re-layouts: 0.05 us -> 2.75 us  [reduce_out(): got = _send(give.astype(jnp.bfloat16), core_perm)]
  transfers between devices with their start and end apart: 22 -> 4, of which waited for: 14 -> 4; matrix products, arithmetic and copies ran while one was open for 8% -> 2% of each run, Pallas kernels for 0% -> 0%
where the time goes in v2:
time: 171 us
  waiting for transfers between devices  59.2 us (35%)
  blocking collectives  51.3 us (30%)
  starting transfers between devices  16.6 us (10%)
  matrix products  15.2 us (9%)
  between operations  14.2 us (8%)
  other arithmetic  9.01 us (5%)
  local copies, waits for them, and re-layouts  5.4 us (3%)
    all_gather x1, waiting for transfers between devices, on_device(): blobs = lax.all_gather(blob, 'ctx')  53.8 us
    all_to_all x1, blocking collectives, project(): mine = lax.all_to_all(spread, HEAD_AXES, 0, 0, tiled=True)  27.2 us
    all_to_all x1, blocking collectives, reduce_out(): lax.all_to_all(chunks, HEAD_AXES, 0, 0, tiled=True).astype(jnp.float32)  24.1 us
    ppermute x2, starting transfers between devices, _send(): return lax.ppermute(value, HEAD_AXES, perm)  14.2 us
    dot_general x1, matrix products, reduce_out(): full = jnp.dot(attended, w_full, preferred_element_type=jnp.float32)  4.32 us
    dot_general x1, matrix products, on_device(): lax.dot_general(onehot, vals_all, (((0,), (0,)), ((), ())), preferred_ele...  3.49 us
  transfers between devices with their start and end apart: 4, of which 4 were waited for; matrix products, arithmetic and copies ran while one was open for 2% of the time, Pallas kernels for 0%

profile of v2, /device:TPU:1, one launch (start us, length us, event | category | flops | bytes accessed | tf_op | source)
XLA Modules:
  0.0 170.9 jit_solution(3024052862455470817)
XLA Ops:
  6.5 0.0 copy-start
  6.5 0.0 copy-start.3
  6.5 0.0 all-gather.3.cloned.1.call-start
  6.5 1.2 broadcast_in_dim.37
  7.8 27.2 %all_to_all.10 = bf16[32,128,128]{2,1,0:T(8,128)(2,1)} all-to-all(bf16[32,128,128]{2,1,0:T(8,128)(2,1)S(1)} %bitcast.41), channel_id=1, replica_groups=mesh['ctx'=16,'hx'=4,'hy'=4,'hc'=2] {'hx','hy','hc'}, dimensions={0} | all-to-all | bytes 2097152 | tf_op jit(solution)/shard_map/all_to_all | solution.py:163
  35.0 2.0 %collective-permute-start = (bf16[32,128,128]{2,1,0:T(8,128)(2,1)}, bf16[32,128,128]{2,1,0:T(8,128)(2,1)}, u32[]{:S(2)}, u32[]{:S(2)}) collective-permute-start(bf16[32,128,128]{2,1,0:T(8,128)(2,1)} %all_to_all.10), channel_id=1, source_target_pairs={{0,1},{1,0},{2,3},{3,2},{4,5},{5,4},{6,7},{7,6},{8,9},{9,8},{10,11... | collective-permute-start | bytes 3145736 | tf_op jit(solution)/shard_map/ppermute | solution.py:41
  37.1 0.1 pad.5.clone
  37.1 0.0 copy-done.3
  37.1 0.0 copy-done
  37.2 1.9 %convolution_bitcast_fusion.1 = bf16[128,384]{1,0:T(8,128)(2,1)S(1)} fusion(bf16[32,128,128]{2,1,0:T(8,128)(2,1)} %all_to_all.10, bf16[32,128,384]{2,1,0:T(8,128)(2,1)S(1)} %bitcast.38), kind=kOutput, calls=%fused_computation.12 | convolution fusion | flops 402653184 | bytes 4292608 | tf_op jit(solution)/shard_map/dot_general | solution.py:167
  39.1 0.8 collective-permute-done
  39.9 1.9 %convolution_bitcast_fusion = bf16[128,384]{1,0:T(8,128)(2,1)S(1)} fusion(bf16[32,128,128]{2,1,0:T(8,128)(2,1)} %collective-permute-done, bf16[32,128,384]{2,1,0:T(8,128)(2,1)S(1)} %bitcast.39), kind=kOutput, calls=%fused_computation.11 | convolution fusion | flops 402653184 | bytes 4292608 | tf_op jit(solution)/shard_map/dot_general | solution.py:168
  41.9 0.7 maximum_maximum_fusion
  42.6 0.0 all-gather.3.cloned.1.call-update
  43.3 2.4 %collective-permute-start.1 = (bf16[256,256]{1,0:T(8,128)(2,1)S(1)}, bf16[256,256]{1,0:T(8,128)(2,1)}, u32[]{:S(2)}, u32[]{:S(2)}) collective-permute-start(bf16[256,256]{1,0:T(8,128)(2,1)S(1)} %slice.46), channel_id=1, source_target_pairs={{0,32},{32,64},{64,96},{96,128},{128,160},{160,192},{192,224},{224... | collective-permute-start | bytes 393224 | tf_op jit(solution)/shard_map/ppermute | solution.py:115
  45.7 2.1 %collective-permute-done.1 = bf16[256,256]{1,0:T(8,128)(2,1)} collective-permute-done((bf16[256,256]{1,0:T(8,128)(2,1)S(1)}, bf16[256,256]{1,0:T(8,128)(2,1)}, u32[]{:S(2)}, u32[]{:S(2)}) %collective-permute-start.1) | collective-permute-done | bytes 131104 | tf_op jit(solution)/shard_map/ppermute | solution.py:115
  47.8 1.9 %select_reduce_fusion.1 = (f32[256]{0:T(256)S(1)}, f32[256,512]{1,0:T(8,128)}) fusion(s32[512]{0:T(512)S(1)} %iota_add_fusion, pred[512]{0:T(512)(128)(4,1)S(1)} %get-tuple-element.13, pred[512]{0:T(512)(128)(4,1)S(1)} %get-tuple-element.14, bf16[256,256]{1,0:T(8,128)(2,1)} %collective-permute-done.1, bf16[256,256]{1,0:T(8,128)(2,1)S(1)} %slice.46, ...), kind=kOutput, calls=%fused_computation.22 | convolution fusion | flops 34602752 | bytes 856064 | tf_op jit(solution)/shard_map/dot_general | solution.py:69
  49.7 53.8 %all-gather.3.cloned.1.call-done = bf16[4352,128]{1,0:T(8,128)(2,1)} async-done(((bf16[272,128]{1,0:T(8,128)(2,1)}), bf16[4352,128]{1,0:T(8,128)(2,1)}) %all-gather.3.cloned.1.call-update) | async-done | bytes 1114128 | tf_op jit(solution)/shard_map/all_gather | solution.py:121
  103.5 0.9 convert_add_fusion
  104.3 1.3 slice.52
  105.6 2.8 %convert_reduce_fusion = f32[512]{0:T(512)S(1)} fusion(s32[4096]{0:T(1024)S(1)} %bitcast.46, pred[4096]{0:T(1024)(128)(4,1)S(1)} %iota_compare_fusion.2), kind=kLoop, calls=%fused_computation | loop fusion | flops 10485248 | bytes 22528 | tf_op jit(solution)/shard_map/reduce_sum | solution.py:131
  108.4 0.0 copy-start.2
  108.5 0.0 copy-start.1
  108.5 3.5 %fusion.1 = f32[512,128]{1,0:T(8,128)S(1)} fusion(bf16[4096,128]{1,0:T(8,128)(2,1)S(1)} %bitcast.42, s32[4096]{0:T(1024)S(1)} %bitcast.47, pred[4096]{0:T(1024)(128)(4,1)S(1)} %iota_compare_fusion.2), kind=kOutput, calls=%fused_computation.3 | convolution fusion | flops 541065216 | bytes 1331200 | tf_op jit(solution)/shard_map/dot_general | solution.py:132
  112.0 0.0 copy-done.2
  112.0 0.3 select_reduce_fusion
  112.3 0.7 fusion.14
  113.0 0.6 fusion.13
  113.6 0.0 copy-done.1
  113.6 0.3 fusion.16
  113.9 4.3 %fusion.8 = f32[256,4096]{1,0:T(8,128)} fusion(f32[256,128]{1,0:T(8,128)S(1)} %fusion.14, bf16[1,128,4096]{2,1,0:T(8,128)(2,1)} %param.8, f32[256,512]{1,0:T(8,128)} %get-tuple-element.10, f32[256]{0:T(256)S(1)} %max.7, s32[512]{0:T(512)S(1)} %iota_add_fusion, pred[512]{0:T(512)(128)(4,1)S(1)} %get-tuple-element.13, ...), kind=kOutput, calls=%fused_computation.16 | convolution fusion | flops 303136768 | bytes 6165504 | tf_op jit(solution)/shard_map/dot_general | solution.py:185
  118.2 2.8 %dynamic-slice_convert_fusion = bf16[256,2048]{1,0:T(8,128)(2,1)} fusion(f32[256,4096]{1,0:T(8,128)} %fusion.8, s32[]{:T(128)S(6)} %select_n.49), kind=kLoop, calls=%fused_computation.8 | loop fusion | bytes 2097156 | tf_op jit(solution)/shard_map/convert_element_type | solution.py:188
  121.0 12.2 %collective-permute-start.2 = (bf16[256,2048]{1,0:T(8,128)(2,1)}, bf16[256,2048]{1,0:T(8,128)(2,1)}, u32[]{:S(2)}, u32[]{:S(2)}) collective-permute-start(bf16[256,2048]{1,0:T(8,128)(2,1)} %dynamic-slice_convert_fusion), channel_id=1, source_target_pairs={{0,1},{1,0},{2,3},{3,2},{4,5},{5,4},{6,7},{7,6},{8,9},{9,8},{10,11... | collective-permute-start | bytes 3145736 | tf_op jit(solution)/shard_map/ppermute | solution.py:41
  133.1 2.6 %collective-permute-done.2 = bf16[256,2048]{1,0:T(8,128)(2,1)} collective-permute-done((bf16[256,2048]{1,0:T(8,128)(2,1)}, bf16[256,2048]{1,0:T(8,128)(2,1)}, u32[]{:S(2)}, u32[]{:S(2)}) %collective-permute-start.2) | collective-permute-done | bytes 1048608 | tf_op jit(solution)/shard_map/ppermute | solution.py:41
  135.7 2.2 %fusion.9 = bf16[32,8,2048]{2,1,0:T(8,128)(2,1)S(1)} fusion(bf16[256,2048]{1,0:T(8,128)(2,1)} %collective-permute-done.2, f32[256,4096]{1,0:T(8,128)} %fusion.8, s32[]{:T(128)S(6)} %select_n.48), kind=kLoop, calls=%fused_computation.17 | loop fusion | flops 1572864 | bytes 4194308 | tf_op jit(solution)/shard_map/reshape | solution.py:190
  137.9 24.1 %all_to_all.11 = bf16[32,8,2048]{2,1,0:T(8,128)(2,1)} all-to-all(bf16[32,8,2048]{2,1,0:T(8,128)(2,1)S(1)} %fusion.9), channel_id=1, replica_groups=mesh['ctx'=16,'hx'=4,'hy'=4,'hc'=2] {'hx','hy','hc'}, dimensions={0} | all-to-all | bytes 2097152 | tf_op jit(solution)/shard_map/all_to_all | solution.py:191
  162.0 1.4 reduce
  163.4 0.6 pad_maximum_fusion.3
  (12 shorter events, 0.1 us)
Async XLA Ops:
  6.5 30.6 %copy-start = (bf16[4096,1,384]{2,0,1:T(8,128)(2,1)S(1)}, bf16[4096,1,384]{2,0,1:T(8,128)(2,1)}, u32[]{:S(2)}) copy-start(bf16[4096,1,384]{2,0,1:T(8,128)(2,1)} %param.7) | copy-start | bytes 9437188
  6.5 30.6 %copy-start.3 = (s32[1,256]{1,0:T(1,128)S(1)}, s32[1,256]{1,0:T(1,128)}, u32[]{:S(2)}) copy-start(s32[1,256]{1,0:T(1,128)} %param.10) | copy-start | bytes 3076
  6.5 96.9 %all-gather.3.cloned.1.call-start = ((), (), s32[]{:S(2)}) async-start(), calls=%async_computation.2 | async-start | bytes 1183744 | tf_op jit(solution)/shard_map/all_gather | solution.py:121
  35.0 4.9 %collective-permute-start = (bf16[32,128,128]{2,1,0:T(8,128)(2,1)}, bf16[32,128,128]{2,1,0:T(8,128)(2,1)}, u32[]{:S(2)}, u32[]{:S(2)}) collective-permute-start(bf16[32,128,128]{2,1,0:T(8,128)(2,1)} %all_to_all.10), channel_id=1, source_target_pairs={{0,1},{1,0},{2,3},{3,2},{4,5},{5,4},{6,7},{7,6},{8,9},{9,8},{10,11... | collective-permute-start | bytes 3145736 | tf_op jit(solution)/shard_map/ppermute | solution.py:41
  43.3 4.5 %collective-permute-start.1 = (bf16[256,256]{1,0:T(8,128)(2,1)S(1)}, bf16[256,256]{1,0:T(8,128)(2,1)}, u32[]{:S(2)}, u32[]{:S(2)}) collective-permute-start(bf16[256,256]{1,0:T(8,128)(2,1)S(1)} %slice.46), channel_id=1, source_target_pairs={{0,32},{32,64},{64,96},{96,128},{128,160},{160,192},{192,224},{224... | collective-permute-start | bytes 393224 | tf_op jit(solution)/shard_map/ppermute | solution.py:115
  108.4 3.5 %copy-start.2 = (bf16[1,512,128]{2,1,0:T(8,128)(2,1)S(1)}, bf16[1,512,128]{2,1,0:T(8,128)(2,1)}, u32[]{:S(2)}) copy-start(bf16[1,512,128]{2,1,0:T(8,128)(2,1)} %param.9) | copy-start | bytes 393220
  108.5 5.1 %copy-start.1 = (f32[256,512]{1,0:T(8,128)S(1)}, f32[256,512]{1,0:T(8,128)}, u32[]{:S(2)}) copy-start(f32[256,512]{1,0:T(8,128)} %get-tuple-element.10) | copy-start | bytes 1572868
  121.0 14.8 %collective-permute-start.2 = (bf16[256,2048]{1,0:T(8,128)(2,1)}, bf16[256,2048]{1,0:T(8,128)(2,1)}, u32[]{:S(2)}, u32[]{:S(2)}) collective-permute-start(bf16[256,2048]{1,0:T(8,128)(2,1)} %dynamic-slice_convert_fusion), channel_id=1, source_target_pairs={{0,1},{1,0},{2,3},{3,2},{4,5},{5,4},{6,7},{7,6},{8,9},{9,8},{10,11... | collective-permute-start | bytes 3145736 | tf_op jit(solution)/shard_map/ppermute | solution.py:41
Sparse Core Ops, SparseCore 0:
  42.8 60.6 all-gather.2

commit v3 on v2

--- a/solution.py
+++ b/solution.py
@@ -111,27 +111,36 @@
     key_vals = projected[:, head_dim:].astype(jnp.bfloat16)
     values = key_vals[:, head_dim:]
 
+    code_row = codes[0]
+    code_ids = jnp.arange(num_codes, dtype=jnp.int32)
+    hi = (code_row // 16).astype(jnp.bfloat16).reshape(1, -1)
+    lo = (code_row % 16).astype(jnp.bfloat16).reshape(1, -1)
+    kvw = key_vals.shape[1]
+    code_rows = jnp.pad(jnp.concatenate([hi, lo], axis=0), ((0, 0), (0, kvw - rows)))
+    kv_blob = jnp.concatenate([key_vals, code_rows, jnp.zeros((14, kvw), jnp.bfloat16)], axis=0)
     route = [(i, i + 1) for i in range(n_ctx - 1)]
-    prev_kv = lax.ppermute(key_vals, "ctx", route)
-    code_row = codes[0].reshape(-1, head_dim)
-    hi = (code_row // 16).astype(jnp.bfloat16)
-    lo = (code_row % 16).astype(jnp.bfloat16)
-    pad = jnp.zeros((16 - 2 * code_row.shape[0], head_dim), jnp.bfloat16)
-    blob = jnp.concatenate([values, hi, lo, pad], axis=0)
-    blobs = lax.all_gather(blob, "ctx")
-    vals_all = blobs[:, :rows].reshape(n_ctx * rows, head_dim)
-    nr = code_row.shape[0]
-    hi_all = blobs[:, rows : rows + nr].astype(jnp.int32)
-    lo_all = blobs[:, rows + nr : rows + 2 * nr].astype(jnp.int32)
-    codes_all = (hi_all * 16 + lo_all).reshape(n_ctx * rows)
-    limit = g * BLK - reach[0]
-    cached = jnp.arange(n_ctx * rows, dtype=jnp.int32) < limit
-    code_ids = jnp.arange(num_codes, dtype=jnp.int32)
-    onehot = ((codes_all[:, None] == code_ids[None, :]) & cached[:, None]).astype(jnp.bfloat16)
-    cache_c = jnp.sum(onehot.astype(jnp.float32), axis=0)
-    cache_v = lax.dot_general(
-        onehot, vals_all, (((0,), (0,)), ((), ())), preferred_element_type=jnp.float32
-    )
+    prev_blob = lax.ppermute(kv_blob, "ctx", route)
+    prev_kv = prev_blob[:rows]
+    prev_codes = (
+        prev_blob[rows, :rows].astype(jnp.int32) * 16 + prev_blob[rows + 1, :rows].astype(jnp.int32)
+    )
+
+    onehot_own = (code_row[:, None] == code_ids[None, :]).astype(jnp.bfloat16)
+    sums = lax.dot_general(
+        onehot_own, values, (((0,), (0,)), ((), ())), preferred_element_type=jnp.float32
+    )
+    counts = jnp.sum(onehot_own.astype(jnp.float32), axis=0)
+    span = num_codes // n_ctx
+    cache_v, cache_c = code_prefix(sums, counts, span, n_ctx, head_dim)
+    prev_ok = (jnp.arange(rows, dtype=jnp.int32) < BLK - reach[0]) & (g > 0)
+    onehot_prev = (
+        (prev_codes[:, None] == code_ids[None, :]) & prev_ok[:, None]
+    ).astype(jnp.bfloat16)
+    cache_v = cache_v + lax.dot_general(
+        onehot_prev, prev_kv[:, head_dim:], (((0,), (0,)), ((), ())),
+        preferred_element_type=jnp.float32,
+    )
+    cache_c = cache_c + jnp.sum(onehot_prev.astype(jnp.float32), axis=0)
 
     ext_kv = jnp.concatenate([prev_kv, key_vals], axis=0)
     attended = attend_block(
@@ -148,6 +157,37 @@
     )
 
     return reduce_out(attended, w_out, sizes)
+
+
+def _pack(sums, counts, span, n, head_dim):
+    hi = jnp.floor(counts / 64.0)
+    lo = counts - hi * 64.0
+    tail = jnp.zeros((n, 8, head_dim), jnp.float32)
+    tail = tail.at[:, 0, :span].set(hi.reshape(n, span)).at[:, 1, :span].set(lo.reshape(n, span))
+    return jnp.concatenate([sums.reshape(n, span, head_dim), tail], axis=1).astype(jnp.bfloat16)
+
+
+def _unpack(blob, span):
+    blob = blob.astype(jnp.float32)
+    sums = blob[:, :span]
+    counts = blob[:, span, :span] * 64.0 + blob[:, span + 1, :span]
+    return sums, counts
+
+
+def code_prefix(sums, counts, span, n, head_dim):
+    got = lax.all_to_all(_pack(sums, counts, span, n, head_dim), "ctx", 0, 0, tiled=True)
+    block_sums, block_counts = _unpack(got, span)
+    b = jnp.arange(n, dtype=jnp.int32)
+    before = (b[None, :] <= b[:, None] - 2).astype(jnp.bfloat16)
+    pre_sums = jnp.einsum(
+        "bc,cxd->bxd", before, block_sums.astype(jnp.bfloat16), preferred_element_type=jnp.float32
+    )
+    pre_counts = jnp.dot(
+        before, block_counts.astype(jnp.bfloat16), preferred_element_type=jnp.float32
+    )
+    back = lax.all_to_all(_pack(pre_sums, pre_counts, span, n, head_dim), "ctx", 0, 0, tiled=True)
+    cache_v, cache_c = _unpack(back, span)
+    return cache_v.reshape(n * span, head_dim), cache_c.reshape(n * span)
 
 
 def project(tokens_in, w_qkv, sizes):

time: 171 us -> 135 us (0.79)
  waiting for transfers between devices: 59.2 us -> 18.5 us
  starting transfers between devices: 16.6 us -> 33 us
  between operations: 14.2 us -> 1.01 us
  blocking collectives: 51.3 us -> 48.3 us
  other arithmetic: 9.01 us -> 11.9 us
    all_gather x1 -> x0, waiting for transfers between devices: 53.8 us -> none  [on_device(): blobs = lax.all_gather(blob, 'ctx')]
    all_to_all x0 -> x2, starting transfers between devices: none -> 20.8 us  [the longest x1 13.2 us: code_prefix(): lax.all_to_all(_pack(sums, counts, span, n, head_dim), 'ctx', 0, 0, tiled...]
    all_to_all x0 -> x2, waiting for transfers between devices: none -> 15.9 us  [the longest x1 8.15 us: code_prefix(): lax.all_to_all(_pack(pre_sums, pre_counts, span, n, head_dim), 'ctx', 0,...]
    ppermute x2, starting transfers between devices: 14.2 us -> 8.31 us  [_send(): return lax.ppermute(value, HEAD_AXES, perm)]
    all_to_all x1, blocking collectives: 24.1 us -> 21.1 us  [reduce_out(): lax.all_to_all(chunks, HEAD_AXES, 0, 0, tiled=True).astype(jnp.float32)]
    ppermute x1, waiting for transfers between devices: 2.06 us -> 0.01 us  [on_device(): prev_blob = lax.ppermute(kv_blob, 'ctx', route)]
    reduce_sum x1 -> x2, other arithmetic: 2.82 us -> 0.87 us  [the longest x1 0.74 us: on_device(): cache_c = cache_c + jnp.sum(onehot_prev.astype(jnp.float32), axis=0)]
    dot_general x1 -> x4, matrix products: 3.49 us -> 2.77 us  [the longest x1 1.29 us: on_device(): lax.dot_general(onehot_prev, prev_kv[:, head_dim:], (((0,), (0,)), ((), (...]
  transfers between devices with their start and end apart: 4 -> 5, of which waited for: 4 -> 3; matrix products, arithmetic and copies ran while one was open for 2% -> 8% of each run, Pallas kernels for 0% -> 0%
where the time goes in v3:
time: 135 us
  blocking collectives  48.3 us (36%)
  starting transfers between devices  33 us (24%)
  waiting for transfers between devices  18.5 us (14%)
  matrix products  15.1 us (11%)
  other arithmetic  11.9 us (9%)
  local copies, waits for them, and re-layouts  6.93 us (5%)
    all_to_all x1, blocking collectives, project(): mine = lax.all_to_all(spread, HEAD_AXES, 0, 0, tiled=True)  27.2 us
    all_to_all x1, blocking collectives, reduce_out(): lax.all_to_all(chunks, HEAD_AXES, 0, 0, tiled=True).astype(jnp.float32)  21.1 us
    all_to_all x1, starting transfers between devices, code_prefix(): lax.all_to_all(_pack(sums, counts, span, n, head_dim), 'ctx', 0, 0, tiled...  13.2 us
    ppermute x2, starting transfers between devices, _send(): return lax.ppermute(value, HEAD_AXES, perm)  8.31 us
    all_to_all x1, waiting for transfers between devices, code_prefix(): lax.all_to_all(_pack(pre_sums, pre_counts, span, n, head_dim), 'ctx', 0,...  8.15 us
    all_to_all x1, waiting for transfers between devices, code_prefix(): lax.all_to_all(_pack(sums, counts, span, n, head_dim), 'ctx', 0, 0, tiled...  7.7 us
    all_to_all x1, starting transfers between devices, code_prefix(): lax.all_to_all(_pack(pre_sums, pre_counts, span, n, head_dim), 'ctx', 0,...  7.64 us
    dot_general x1, matrix products, reduce_out(): full = jnp.dot(attended, w_full, preferred_element_type=jnp.float32)  4.28 us
  transfers between devices with their start and end apart: 5, of which 3 were waited for; matrix products, arithmetic and copies ran while one was open for 8% of the time, Pallas kernels for 0%

profile of v3, /device:TPU:1, one launch (start us, length us, event | category | flops | bytes accessed | tf_op | source)
XLA Modules:
  0.0 134.6 jit_solution(6416464542017364360)
XLA Ops:
  0.0 0.0 copy-start
  0.0 1.2 broadcast_in_dim.41
  1.2 27.2 %all_to_all.20 = bf16[32,128,128]{2,1,0:T(8,128)(2,1)} all-to-all(bf16[32,128,128]{2,1,0:T(8,128)(2,1)S(1)} %bitcast.52), channel_id=1, replica_groups=mesh['ctx'=16,'hx'=4,'hy'=4,'hc'=2] {'hx','hy','hc'}, dimensions={0} | all-to-all | bytes 2097152 | tf_op jit(solution)/shard_map/all_to_all | solution.py:203
  28.4 2.0 %collective-permute-start = (bf16[32,128,128]{2,1,0:T(8,128)(2,1)}, bf16[32,128,128]{2,1,0:T(8,128)(2,1)}, u32[]{:S(2)}, u32[]{:S(2)}) collective-permute-start(bf16[32,128,128]{2,1,0:T(8,128)(2,1)} %all_to_all.20), channel_id=1, source_target_pairs={{0,1},{1,0},{2,3},{3,2},{4,5},{5,4},{6,7},{7,6},{8,9},{9,8},{10,11... | collective-permute-start | bytes 3145736 | tf_op jit(solution)/shard_map/ppermute | solution.py:41
  30.5 0.0 copy-done.5
  30.5 0.1 convert_reduce_fusion.1
  31.3 0.1 reduce_sum.39
  31.4 0.2 scatter.15
  31.6 0.0 copy-start.6
  31.6 0.0 copy-start.10
  31.6 0.0 copy-done
  31.6 1.9 %convolution_bitcast_fusion.1 = bf16[128,384]{1,0:T(8,128)(2,1)S(1)} fusion(bf16[32,128,128]{2,1,0:T(8,128)(2,1)} %all_to_all.20, bf16[32,128,384]{2,1,0:T(8,128)(2,1)S(1)} %bitcast.49), kind=kOutput, calls=%fused_computation.8 | convolution fusion | flops 402653184 | bytes 4292608 | tf_op jit(solution)/shard_map/dot_general | solution.py:207
  33.6 0.0 collective-permute-done
  33.6 1.9 %convolution_bitcast_fusion = bf16[128,384]{1,0:T(8,128)(2,1)S(1)} fusion(bf16[32,128,128]{2,1,0:T(8,128)(2,1)} %collective-permute-done, bf16[32,128,384]{2,1,0:T(8,128)(2,1)S(1)} %bitcast.50), kind=kOutput, calls=%fused_computation.7 | convolution fusion | flops 402653184 | bytes 4292608 | tf_op jit(solution)/shard_map/dot_general | solution.py:208
  35.6 0.0 copy-start.2
  35.6 0.4 convolution_convert_fusion.1
  36.0 0.7 pad_maximum_fusion
  36.7 13.2 %all-to-all-start.1 = ((bf16[16,40,128]{2,1,0:T(8,128)(2,1)}), bf16[16,40,128]{2,1,0:T(8,128)(2,1)}, u32[]{:S(2)}, u32[]{:S(2)}) async-start(bf16[16,40,128]{2,1,0:T(8,128)(2,1)} %pad_maximum_fusion), calls=%async_computation.1 | async-start | bytes 327680 | tf_op jit(solution)/shard_map/all_to_all | solution.py:178
  49.9 0.1 pad.29.clone
  50.0 0.8 maximum_maximum_fusion
  50.8 3.9 %collective-permute-start.1 = (bf16[272,256]{1,0:T(8,128)(2,1)}, bf16[272,256]{1,0:T(8,128)(2,1)}, u32[]{:S(2)}, u32[]{:S(2)}) collective-permute-start(bf16[272,256]{1,0:T(8,128)(2,1)} %maximum_maximum_fusion), channel_id=1, source_target_pairs={{0,32},{32,64},{64,96},{96,128},{128,160},{160,192},{192,224},{224... | collective-permute-start | bytes 417800 | tf_op jit(solution)/shard_map/ppermute | solution.py:122
  54.6 7.7 %all-to-all-done.1 = bf16[16,40,128]{2,1,0:T(8,128)(2,1)} async-done(((bf16[16,40,128]{2,1,0:T(8,128)(2,1)}), bf16[16,40,128]{2,1,0:T(8,128)(2,1)}, u32[]{:S(2)}, u32[]{:S(2)}) %all-to-all-start.1) | async-done | bytes 163872 | tf_op jit(solution)/shard_map/all_to_all | solution.py:178
  62.3 1.0 fusion.72
  63.3 0.9 convolution_convert_fusion
  64.2 0.2 subtract_bitcast_fusion
  64.4 0.2 scatter.19
  64.5 0.9 pad_maximum_fusion.1
  65.5 0.7 copy.21
  66.2 7.6 %all-to-all-start.2 = ((bf16[16,40,128]{2,1,0:T(8,128)(2,1)}), bf16[16,40,128]{2,1,0:T(8,128)(2,1)}, u32[]{:S(2)}, u32[]{:S(2)}) async-start(bf16[16,40,128]{2,1,0:T(8,128)(2,1)} %copy.21), calls=%async_computation.2 | async-start | bytes 327680 | tf_op jit(solution)/shard_map/all_to_all | solution.py:188
  73.8 0.0 copy-start.8
  73.9 0.0 collective-permute-done.1
  73.9 0.9 slice.173
  74.8 0.0 copy-start.3
  74.8 0.8 fusion.61
  75.6 0.0 copy-done.10
  75.6 0.7 convert_reduce_fusion
  76.3 0.0 copy-done.6
  76.3 0.0 copy-done.3
  76.3 1.6 %select_reduce_fusion.1 = (f32[256]{0:T(256)}, f32[256,512]{1,0:T(8,128)}) fusion(s32[512]{0:T(512)S(1)} %iota_add_fusion, pred[512]{0:T(512)(128)(4,1)S(1)} %iota_compare_fusion.6, pred[512]{0:T(512)(128)(4,1)S(1)} %fusion.59, bf16[256,256]{1,0:T(8,128)(2,1)S(1)} %slice.173, bf16[256,256]{1,0:T(8,128)(2,1)S(1)} %slice.172, bf16[256,384]{1,0:T(8,128)(2,1)S(1)} %fusion.13), kind=kOutput, calls=%fused_computation.23 | convolution fusion | flops 34602752 | bytes 856064 | tf_op jit(solution)/shard_map/dot_general | solution.py:69
  77.9 8.2 %all-to-all-done.2 = bf16[16,40,128]{2,1,0:T(8,128)(2,1)} async-done(((bf16[16,40,128]{2,1,0:T(8,128)(2,1)}), bf16[16,40,128]{2,1,0:T(8,128)(2,1)}, u32[]{:S(2)}, u32[]{:S(2)}) %all-to-all-start.2) | async-done | bytes 163872 | tf_op jit(solution)/shard_map/all_to_all | solution.py:188
  86.1 0.9 copy_convert_fusion
  87.0 0.0 copy-done.2
  87.0 0.0 copy-done.8
  87.1 0.7 add.81
  87.7 0.1 copy.23
  87.8 0.0 copy-start.4
  87.8 0.8 broadcast_compare_fusion
  88.6 1.2 select_reduce_fusion
  89.8 0.6 max.7
  90.5 1.3 convolution_add_fusion
  91.8 0.6 fusion.12
  92.4 0.6 fusion.11
  93.0 0.0 copy-done.1
  93.0 0.0 copy-done.7
  93.1 0.3 fusion.14
  93.4 0.0 copy-done.4
  93.4 4.3 %fusion.2 = f32[256,4096]{1,0:T(8,128)} fusion(f32[256,128]{1,0:T(8,128)S(1)} %fusion.12, bf16[1,128,4096]{2,1,0:T(8,128)(2,1)} %param.16, f32[256,512]{1,0:T(8,128)} %get-tuple-element.66, f32[256]{0:T(256)S(1)} %max.7, s32[512]{0:T(512)S(1)} %iota_add_fusion, pred[512]{0:T(512)(128)(4,1)} %copy-done.8, pred[512]{0:T(512)(128)(4,1)} %copy-done.6, ...), kind=kOutput, calls=%fused_computation.12 | convolution fusion | flops 303136768 | bytes 6165504 | tf_op jit(solution)/shard_map/dot_general | solution.py:225
  97.6 2.8 %dynamic-slice_convert_fusion = bf16[256,2048]{1,0:T(8,128)(2,1)} fusion(f32[256,4096]{1,0:T(8,128)} %fusion.2, s32[]{:T(128)S(6)} %select_n.51), kind=kLoop, calls=%fused_computation.1 | loop fusion | bytes 2097156 | tf_op jit(solution)/shard_map/convert_element_type | solution.py:228
  100.4 6.3 %collective-permute-start.2 = (bf16[256,2048]{1,0:T(8,128)(2,1)}, bf16[256,2048]{1,0:T(8,128)(2,1)}, u32[]{:S(2)}, u32[]{:S(2)}) collective-permute-start(bf16[256,2048]{1,0:T(8,128)(2,1)} %dynamic-slice_convert_fusion), channel_id=1, source_target_pairs={{0,1},{1,0},{2,3},{3,2},{4,5},{5,4},{6,7},{7,6},{8,9},{9,8},{10,11... | collective-permute-start | bytes 3145736 | tf_op jit(solution)/shard_map/ppermute | solution.py:41
  106.7 2.6 %collective-permute-done.2 = bf16[256,2048]{1,0:T(8,128)(2,1)} collective-permute-done((bf16[256,2048]{1,0:T(8,128)(2,1)}, bf16[256,2048]{1,0:T(8,128)(2,1)}, u32[]{:S(2)}, u32[]{:S(2)}) %collective-permute-start.2) | collective-permute-done | bytes 1048608 | tf_op jit(solution)/shard_map/ppermute | solution.py:41
  109.3 2.2 %fusion.3 = bf16[32,8,2048]{2,1,0:T(8,128)(2,1)S(1)} fusion(bf16[256,2048]{1,0:T(8,128)(2,1)} %collective-permute-done.2, f32[256,4096]{1,0:T(8,128)} %fusion.2, s32[]{:T(128)S(6)} %select_n.50), kind=kLoop, calls=%fused_computation.13 | loop fusion | flops 1572864 | bytes 4194308 | tf_op jit(solution)/shard_map/reshape | solution.py:230
  111.5 21.1 %all_to_all.21 = bf16[32,8,2048]{2,1,0:T(8,128)(2,1)} all-to-all(bf16[32,8,2048]{2,1,0:T(8,128)(2,1)S(1)} %fusion.3), channel_id=1, replica_groups=mesh['ctx'=16,'hx'=4,'hy'=4,'hc'=2] {'hx','hy','hc'}, dimensions={0} | all-to-all | bytes 2097152 | tf_op jit(solution)/shard_map/all_to_all | solution.py:231
  132.6 1.4 %reduce.8 = bf16[2,8,2048]{2,1,0:T(8,128)(2,1)S(1)} reduce(bf16[16,2,8,2048]{3,2,1,0:T(8,128)(2,1)} %bitcast.51, bf16[]{:T(256)} %constant.162.clone.1), dimensions={0}, to_apply=%region_5.6.clone | reduce | flops 491520 | bytes 1114114 | tf_op jit(solution)/shard_map/reduce_sum | solution.py:232
  134.0 0.6 pad_maximum_fusion.5
  (23 shorter events, 0.2 us)
Async XLA Ops:
  0.0 31.6 %copy-start = (bf16[4096,1,384]{2,0,1:T(8,128)(2,1)S(1)}, bf16[4096,1,384]{2,0,1:T(8,128)(2,1)}, u32[]{:S(2)}) copy-start(bf16[4096,1,384]{2,0,1:T(8,128)(2,1)} %param.15) | copy-start | bytes 9437188
  0.0 30.5 %copy-start.5 = (s32[1,256]{1,0:T(1,128)S(1)}, s32[1,256]{1,0:T(1,128)}, u32[]{:S(2)}) copy-start(s32[1,256]{1,0:T(1,128)} %param.18) | copy-start | bytes 3076
  28.4 5.1 %collective-permute-start = (bf16[32,128,128]{2,1,0:T(8,128)(2,1)}, bf16[32,128,128]{2,1,0:T(8,128)(2,1)}, u32[]{:S(2)}, u32[]{:S(2)}) collective-permute-start(bf16[32,128,128]{2,1,0:T(8,128)(2,1)} %all_to_all.20), channel_id=1, source_target_pairs={{0,1},{1,0},{2,3},{3,2},{4,5},{5,4},{6,7},{7,6},{8,9},{9,8},{10,11... | collective-permute-start | bytes 3145736 | tf_op jit(solution)/shard_map/ppermute | solution.py:41
  31.6 44.7 %copy-start.6 = (pred[512]{0:T(512)(128)(4,1)}, pred[512]{0:T(512)(128)(4,1)S(1)}, u32[]{:S(2)}) copy-start(pred[512]{0:T(512)(128)(4,1)S(1)} %fusion.59) | copy-start | bytes 1540
  31.6 44.0 %copy-start.10 = (pred[256]{0:T(512)(128)(4,1)}, pred[256]{0:T(512)(128)(4,1)S(1)}, u32[]{:S(2)}) copy-start(pred[256]{0:T(512)(128)(4,1)S(1)} %compare_and_fusion) | copy-start | bytes 772
  35.6 51.4 %copy-start.2 = (bf16[256,384]{1,0:T(8,128)(2,1)}, bf16[256,384]{1,0:T(8,128)(2,1)S(1)}, u32[]{:S(2)}) copy-start(bf16[256,384]{1,0:T(8,128)(2,1)S(1)} %fusion.13) | copy-start | bytes 589828
  36.7 25.6 %all-to-all-start.1 = ((bf16[16,40,128]{2,1,0:T(8,128)(2,1)}), bf16[16,40,128]{2,1,0:T(8,128)(2,1)}, u32[]{:S(2)}, u32[]{:S(2)}) async-start(bf16[16,40,128]{2,1,0:T(8,128)(2,1)} %pad_maximum_fusion), calls=%async_computation.1 | async-start | bytes 327680 | tf_op jit(solution)/shard_map/all_to_all | solution.py:178
  50.8 23.1 %collective-permute-start.1 = (bf16[272,256]{1,0:T(8,128)(2,1)}, bf16[272,256]{1,0:T(8,128)(2,1)}, u32[]{:S(2)}, u32[]{:S(2)}) collective-permute-start(bf16[272,256]{1,0:T(8,128)(2,1)} %maximum_maximum_fusion), channel_id=1, source_target_pairs={{0,32},{32,64},{64,96},{96,128},{128,160},{160,192},{192,224},{224... | collective-permute-start | bytes 417800 | tf_op jit(solution)/shard_map/ppermute | solution.py:122
  66.2 19.9 %all-to-all-start.2 = ((bf16[16,40,128]{2,1,0:T(8,128)(2,1)}), bf16[16,40,128]{2,1,0:T(8,128)(2,1)}, u32[]{:S(2)}, u32[]{:S(2)}) async-start(bf16[16,40,128]{2,1,0:T(8,128)(2,1)} %copy.21), calls=%async_computation.2 | async-start | bytes 327680 | tf_op jit(solution)/shard_map/all_to_all | solution.py:188
  73.8 13.2 %copy-start.8 = (pred[512]{0:T(512)(128)(4,1)}, pred[512]{0:T(512)(128)(4,1)S(1)}, u32[]{:S(2)}) copy-start(pred[512]{0:T(512)(128)(4,1)S(1)} %iota_compare_fusion.6) | copy-start | bytes 1540
  74.8 1.5 %copy-start.3 = (bf16[256,256]{1,0:T(8,128)(2,1)}, bf16[256,256]{1,0:T(8,128)(2,1)S(1)}, u32[]{:S(2)}) copy-start(bf16[256,256]{1,0:T(8,128)(2,1)S(1)} %slice.173) | copy-start | bytes 393220
  87.7 5.3 %copy-start.1 = (f32[256,512]{1,0:T(8,128)S(1)}, f32[256,512]{1,0:T(8,128)}, u32[]{:S(2)}) copy-start(f32[256,512]{1,0:T(8,128)} %get-tuple-element.66) | copy-start | bytes 1572868
  87.7 5.3 %copy-start.7 = (pred[512]{0:T(512)(128)(4,1)S(1)}, pred[512]{0:T(512)(128)(4,1)}, u32[]{:S(2)}) copy-start(pred[512]{0:T(512)(128)(4,1)} %copy-done.6) | copy-start | bytes 1540
  87.7 5.3 %copy-start.9 = (pred[512]{0:T(512)(128)(4,1)S(1)}, pred[512]{0:T(512)(128)(4,1)}, u32[]{:S(2)}) copy-start(pred[512]{0:T(512)(128)(4,1)} %copy-done.8) | copy-start | bytes 1540
  87.8 5.5 %copy-start.4 = (bf16[256,256]{1,0:T(8,128)(2,1)S(1)}, bf16[256,256]{1,0:T(8,128)(2,1)}, u32[]{:S(2)}) copy-start(bf16[256,256]{1,0:T(8,128)(2,1)} %copy-done.3) | copy-start | bytes 393220
  100.4 8.9 %collective-permute-start.2 = (bf16[256,2048]{1,0:T(8,128)(2,1)}, bf16[256,2048]{1,0:T(8,128)(2,1)}, u32[]{:S(2)}, u32[]{:S(2)}) collective-permute-start(bf16[256,2048]{1,0:T(8,128)(2,1)} %dynamic-slice_convert_fusion), channel_id=1, source_target_pairs={{0,1},{1,0},{2,3},{3,2},{4,5},{5,4},{6,7},{7,6},{8,9},{9,8},{10,11... | collective-permute-start | bytes 3145736 | tf_op jit(solution)/shard_map/ppermute | solution.py:41

commit v4 on v3

--- a/solution.py
+++ b/solution.py
@@ -62,9 +62,7 @@
     return data[0] + gp.astype(jnp.float32) + gm.astype(jnp.float32)
 
 
-def attend_block(
-    queries, keys_win, vals_win, cache_v, cache_c, book, reach_one, prev_flag, block_len, scale
-):
+def attend_exact(queries, keys_win, vals_win, book, reach_one, prev_flag, block_len, scale):
     exact = (
         lax.dot_general(
             queries, keys_win, (((1,), (1,)), ((), ())), preferred_element_type=jnp.float32
@@ -80,16 +78,20 @@
     prev_ok = (cols < block_len) & (cols >= block_len - reach_one) & prev_flag
     curr_ok = (cols >= block_len) & (cols - block_len <= rows)
     allowed = prev_ok | curr_ok
+    top_e = jnp.max(jnp.where(allowed, exact, -jnp.inf), axis=1)
+    probs = jnp.exp(jnp.where(allowed, exact - top_e[:, None], -jnp.inf))
+    numer = jnp.dot(probs.astype(jnp.bfloat16), vals_win, preferred_element_type=jnp.float32)
+    denom = jnp.sum(probs, axis=1)
+    return top_e, numer, denom, coded
+
+
+def attend_cache(top_e, numer_e, denom_e, coded, cache_v, cache_c):
     valid = cache_c > 0.5
-    top = jnp.maximum(
-        jnp.max(jnp.where(allowed, exact, -jnp.inf), axis=1),
-        jnp.max(jnp.where(valid[None, :], coded, -jnp.inf), axis=1),
-    )
-    probs = jnp.exp(jnp.where(allowed, exact - top[:, None], -jnp.inf))
+    top = jnp.maximum(top_e, jnp.max(jnp.where(valid[None, :], coded, -jnp.inf), axis=1))
+    alpha = jnp.exp(top_e - top)
     weights = jnp.exp(jnp.where(valid[None, :], coded - top[:, None], -jnp.inf))
-    numer = jnp.dot(probs.astype(jnp.bfloat16), vals_win, preferred_element_type=jnp.float32)
-    numer = numer + jnp.dot(weights, cache_v, precision=lax.Precision.HIGHEST)
-    denom = jnp.sum(probs, axis=1) + jnp.dot(weights, cache_c, precision=lax.Precision.HIGHEST)
+    numer = alpha[:, None] * numer_e + jnp.dot(weights, cache_v, precision=lax.Precision.HIGHEST)
+    denom = alpha * denom_e + jnp.dot(weights, cache_c, precision=lax.Precision.HIGHEST)
     return (numer / denom[:, None]).astype(jnp.bfloat16)
 
 
@@ -143,18 +145,17 @@
     cache_c = cache_c + jnp.sum(onehot_prev.astype(jnp.float32), axis=0)
 
     ext_kv = jnp.concatenate([prev_kv, key_vals], axis=0)
-    attended = attend_block(
+    top_e, numer_e, denom_e, coded = attend_exact(
         queries,
         ext_kv[:, :head_dim],
         ext_kv[:, head_dim:],
-        cache_v,
-        cache_c,
         codebook[0],
         reach[0],
         g > 0,
         BLK,
         scale,
     )
+    attended = attend_cache(top_e, numer_e, denom_e, coded, cache_v, cache_c)
 
     return reduce_out(attended, w_out, sizes)
 

time: 135 us -> 135 us (level)
  blocking collectives: 48.3 us -> 20.7 us
  waiting for transfers between devices: 18.5 us -> 35.2 us
  starting transfers between devices: 33 us -> 43 us
  local copies, waits for them, and re-layouts: 6.93 us -> 8.71 us
    all_to_all x1 -> x0, blocking collectives: 27.2 us -> none  [project(): mine = lax.all_to_all(spread, HEAD_AXES, 0, 0, tiled=True)]
    all_to_all x0 -> x1, waiting for transfers between devices: none -> 16.2 us  [project(): mine = lax.all_to_all(spread, HEAD_AXES, 0, 0, tiled=True)]
    all_to_all x0 -> x1, starting transfers between devices: none -> 11.1 us  [project(): mine = lax.all_to_all(spread, HEAD_AXES, 0, 0, tiled=True)]
  transfers between devices with their start and end apart: 5 -> 6, of which waited for: 3 -> 5; matrix products, arithmetic and copies ran while one was open for 8% -> 8% of each run, Pallas kernels for 0% -> 0%
where the time goes in v4:
time: 135 us; the launch traced here: 134 us
  starting transfers between devices  43 us (32%)
  waiting for transfers between devices  35.2 us (26%)
  blocking collectives  20.7 us (15%)
  matrix products  13.8 us (10%)
  other arithmetic  11.8 us (9%)
  local copies, waits for them, and re-layouts  8.71 us (6%)
    all_to_all x1, blocking collectives, reduce_out(): lax.all_to_all(chunks, HEAD_AXES, 0, 0, tiled=True).astype(jnp.float32)  20.7 us
    all_to_all x1, waiting for transfers between devices, project(): mine = lax.all_to_all(spread, HEAD_AXES, 0, 0, tiled=True)  16.2 us
    all_to_all x1, starting transfers between devices, code_prefix(): lax.all_to_all(_pack(sums, counts, span, n, head_dim), 'ctx', 0, 0, tiled...  12.4 us
    all_to_all x1, starting transfers between devices, project(): mine = lax.all_to_all(spread, HEAD_AXES, 0, 0, tiled=True)  11.1 us
    ppermute x2, starting transfers between devices, _send(): return lax.ppermute(value, HEAD_AXES, perm)  8.31 us
    all_to_all x1, waiting for transfers between devices, code_prefix(): lax.all_to_all(_pack(sums, counts, span, n, head_dim), 'ctx', 0, 0, tiled...  8.05 us
    all_to_all x1, waiting for transfers between devices, code_prefix(): lax.all_to_all(_pack(pre_sums, pre_counts, span, n, head_dim), 'ctx', 0,...  7.82 us
    all_to_all x1, starting transfers between devices, code_prefix(): lax.all_to_all(_pack(pre_sums, pre_counts, span, n, head_dim), 'ctx', 0,...  7.3 us
  transfers between devices with their start and end apart: 6, of which 5 were waited for; matrix products, arithmetic and copies ran while one was open for 8% of the time, Pallas kernels for 0%

profile of v4, /device:TPU:1, one launch (start us, length us, event | category | flops | bytes accessed | tf_op | source)
XLA Modules:
  0.0 134.3 jit_solution(12642976262335528385)
XLA Ops:
  0.0 0.0 copy-start
  0.0 0.0 copy-start.6
  0.0 2.3 %broadcast_in_dim.42 = bf16[16,2,128,128]{3,2,1,0:T(8,128)(2,1)} broadcast(bf16[2,128,128]{2,1,0:T(8,128)(2,1)} %bitcast.55), dimensions={1,2,3} | broadcast | bytes 1114112 | tf_op jit(solution)/shard_map/broadcast_in_dim | solution.py:201
  2.3 11.1 %all-to-all-start = ((bf16[32,128,128]{2,1,0:T(8,128)(2,1)}), bf16[32,128,128]{2,1,0:T(8,128)(2,1)}, u32[]{:S(2)}, u32[]{:S(2)}) async-start(bf16[32,128,128]{2,1,0:T(8,128)(2,1)} %bitcast.51), calls=%async_computation | async-start | bytes 2097152 | tf_op jit(solution)/shard_map/all_to_all | solution.py:204
  14.1 0.0 copy-done.6
  14.1 0.1 convert_reduce_fusion.1
  14.2 0.1 reduce_sum.39
  14.3 16.2 %all-to-all-done = bf16[32,128,128]{2,1,0:T(8,128)(2,1)} async-done(((bf16[32,128,128]{2,1,0:T(8,128)(2,1)}), bf16[32,128,128]{2,1,0:T(8,128)(2,1)}, u32[]{:S(2)}, u32[]{:S(2)}) %all-to-all-start) | async-done | bytes 1048608 | tf_op jit(solution)/shard_map/all_to_all | solution.py:204
  30.5 2.0 %collective-permute-start = (bf16[32,128,128]{2,1,0:T(8,128)(2,1)}, bf16[32,128,128]{2,1,0:T(8,128)(2,1)}, u32[]{:S(2)}, u32[]{:S(2)}) collective-permute-start(bf16[32,128,128]{2,1,0:T(8,128)(2,1)} %all-to-all-done), channel_id=1, source_target_pairs={{0,1},{1,0},{2,3},{3,2},{4,5},{5,4},{6,7},{7,6},{8,9},{9,8},{10,11... | collective-permute-start | bytes 3145736 | tf_op jit(solution)/shard_map/ppermute | solution.py:41
  32.5 0.2 scatter.15
  32.7 0.0 copy-start.7
  32.7 0.0 copy-start.9
  32.8 0.0 copy-start.8
  32.8 0.0 copy-done
  32.8 1.9 %convolution_bitcast_fusion.1 = bf16[128,384]{1,0:T(8,128)(2,1)S(1)} fusion(bf16[32,128,128]{2,1,0:T(8,128)(2,1)} %all-to-all-done, bf16[32,128,384]{2,1,0:T(8,128)(2,1)S(1)} %bitcast.49), kind=kOutput, calls=%fused_computation.8 | convolution fusion | flops 402653184 | bytes 4292608 | tf_op jit(solution)/shard_map/dot_general | solution.py:208
  34.8 0.6 collective-permute-done
  35.3 1.9 %convolution_bitcast_fusion = bf16[128,384]{1,0:T(8,128)(2,1)S(1)} fusion(bf16[32,128,128]{2,1,0:T(8,128)(2,1)} %collective-permute-done, bf16[32,128,384]{2,1,0:T(8,128)(2,1)S(1)} %bitcast.50), kind=kOutput, calls=%fused_computation.7 | convolution fusion | flops 402653184 | bytes 4292608 | tf_op jit(solution)/shard_map/dot_general | solution.py:209
  37.3 0.0 copy-start.2
  37.3 0.4 convolution_convert_fusion.1
  37.8 0.7 pad_maximum_fusion
  38.4 12.4 %all-to-all-start.1 = ((bf16[16,40,128]{2,1,0:T(8,128)(2,1)}), bf16[16,40,128]{2,1,0:T(8,128)(2,1)}, u32[]{:S(2)}, u32[]{:S(2)}) async-start(bf16[16,40,128]{2,1,0:T(8,128)(2,1)} %pad_maximum_fusion), calls=%async_computation.1 | async-start | bytes 327680 | tf_op jit(solution)/shard_map/all_to_all | solution.py:179
  50.9 0.1 pad.29.clone
  51.0 0.8 maximum_maximum_fusion
  51.7 3.9 %collective-permute-start.1 = (bf16[272,256]{1,0:T(8,128)(2,1)}, bf16[272,256]{1,0:T(8,128)(2,1)}, u32[]{:S(2)}, u32[]{:S(2)}) collective-permute-start(bf16[272,256]{1,0:T(8,128)(2,1)} %maximum_maximum_fusion), channel_id=1, source_target_pairs={{0,32},{32,64},{64,96},{96,128},{128,160},{160,192},{192,224},{224... | collective-permute-start | bytes 417800 | tf_op jit(solution)/shard_map/ppermute | solution.py:124
  55.6 8.0 %all-to-all-done.1 = bf16[16,40,128]{2,1,0:T(8,128)(2,1)} async-done(((bf16[16,40,128]{2,1,0:T(8,128)(2,1)}), bf16[16,40,128]{2,1,0:T(8,128)(2,1)}, u32[]{:S(2)}, u32[]{:S(2)}) %all-to-all-start.1) | async-done | bytes 163872 | tf_op jit(solution)/shard_map/all_to_all | solution.py:179
  63.6 1.0 fusion.74
  64.6 0.9 convolution_convert_fusion
  65.5 0.2 subtract_bitcast_fusion
  65.7 0.2 scatter.19
  65.9 0.9 pad_maximum_fusion.1
  66.8 0.7 copy.21
  67.5 7.3 %all-to-all-start.2 = ((bf16[16,40,128]{2,1,0:T(8,128)(2,1)}), bf16[16,40,128]{2,1,0:T(8,128)(2,1)}, u32[]{:S(2)}, u32[]{:S(2)}) async-start(bf16[16,40,128]{2,1,0:T(8,128)(2,1)} %copy.21), calls=%async_computation.2 | async-start | bytes 327680 | tf_op jit(solution)/shard_map/all_to_all | solution.py:189
  74.8 0.0 collective-permute-done.1
  74.8 0.8 fusion.63
  75.6 0.9 slice.173
  76.5 0.0 copy-start.3
  76.5 0.0 copy-done.9
  76.5 0.7 convert_reduce_fusion
  77.2 0.0 copy-done.3
  77.2 0.3 select_reduce_fusion.1
  77.6 0.0 copy-done.7
  77.6 0.0 copy-done.8
  77.6 0.8 copy-done.1
  78.4 0.8 fusion.15
  79.2 7.8 %all-to-all-done.2 = bf16[16,40,128]{2,1,0:T(8,128)(2,1)} async-done(((bf16[16,40,128]{2,1,0:T(8,128)(2,1)}), bf16[16,40,128]{2,1,0:T(8,128)(2,1)}, u32[]{:S(2)}, u32[]{:S(2)}) %all-to-all-start.2) | async-done | bytes 163872 | tf_op jit(solution)/shard_map/all_to_all | solution.py:189
  87.1 0.9 copy_convert_fusion
  88.0 0.0 copy-done.2
  88.0 0.0 copy-done.4
  88.1 0.7 add.81
  88.7 0.1 copy.23
  88.8 0.7 broadcast_compare_fusion
  89.5 1.3 select_reduce_fusion
  90.8 1.3 convolution_add_fusion
  92.1 0.6 fusion.13
  92.7 0.6 fusion.12
  93.3 0.0 copy-done.5
  93.4 4.3 %fusion.3 = f32[256,4096]{1,0:T(8,128)} fusion(f32[256,128]{1,0:T(8,128)S(1)} %fusion.13, bf16[1,128,4096]{2,1,0:T(8,128)(2,1)} %param.16, f32[256,512]{1,0:T(8,128)} %copy-done.1, f32[256]{0:T(256)S(1)} %get-tuple-element.67, s32[512]{0:T(512)S(1)} %iota_add_fusion, pred[512]{0:T(512)(128)(4,1)} %copy-done.8, pred[512]{0:T(512)(128)(4,1)} %copy-done.7, ...), kind=kOutput, calls=%fused_computation.13 | convolution fusion | flops 303169536 | bytes 6166528 | tf_op jit(solution)/shard_map/dot_general | solution.py:226
  97.7 2.7 %dynamic-slice_convert_fusion = bf16[256,2048]{1,0:T(8,128)(2,1)} fusion(f32[256,4096]{1,0:T(8,128)} %fusion.3, s32[]{:T(128)S(6)} %select_n.51), kind=kLoop, calls=%fused_computation.1 | loop fusion | bytes 2097156 | tf_op jit(solution)/shard_map/convert_element_type | solution.py:229
  100.4 6.3 %collective-permute-start.2 = (bf16[256,2048]{1,0:T(8,128)(2,1)}, bf16[256,2048]{1,0:T(8,128)(2,1)}, u32[]{:S(2)}, u32[]{:S(2)}) collective-permute-start(bf16[256,2048]{1,0:T(8,128)(2,1)} %dynamic-slice_convert_fusion), channel_id=1, source_target_pairs={{0,1},{1,0},{2,3},{3,2},{4,5},{5,4},{6,7},{7,6},{8,9},{9,8},{10,11... | collective-permute-start | bytes 3145736 | tf_op jit(solution)/shard_map/ppermute | solution.py:41
  106.7 2.6 %collective-permute-done.2 = bf16[256,2048]{1,0:T(8,128)(2,1)} collective-permute-done((bf16[256,2048]{1,0:T(8,128)(2,1)}, bf16[256,2048]{1,0:T(8,128)(2,1)}, u32[]{:S(2)}, u32[]{:S(2)}) %collective-permute-start.2) | collective-permute-done | bytes 1048608 | tf_op jit(solution)/shard_map/ppermute | solution.py:41
  109.3 2.2 %fusion.4 = bf16[32,8,2048]{2,1,0:T(8,128)(2,1)S(1)} fusion(bf16[256,2048]{1,0:T(8,128)(2,1)} %collective-permute-done.2, f32[256,4096]{1,0:T(8,128)} %fusion.3, s32[]{:T(128)S(6)} %select_n.50), kind=kLoop, calls=%fused_computation.14 | loop fusion | flops 1572864 | bytes 4194308 | tf_op jit(solution)/shard_map/reshape | solution.py:231
  111.6 20.7 %all_to_all.20 = bf16[32,8,2048]{2,1,0:T(8,128)(2,1)} all-to-all(bf16[32,8,2048]{2,1,0:T(8,128)(2,1)S(1)} %fusion.4), channel_id=1, replica_groups=mesh['ctx'=16,'hx'=4,'hy'=4,'hc'=2] {'hx','hy','hc'}, dimensions={0} | all-to-all | bytes 2097152 | tf_op jit(solution)/shard_map/all_to_all | solution.py:232
  132.3 1.4 %reduce.8 = bf16[2,8,2048]{2,1,0:T(8,128)(2,1)S(1)} reduce(bf16[16,2,8,2048]{3,2,1,0:T(8,128)(2,1)} %bitcast.52, bf16[]{:T(256)} %constant.162.clone.1), dimensions={0}, to_apply=%region_5.6.clone | reduce | flops 491520 | bytes 1114114 | tf_op jit(solution)/shard_map/reduce_sum | solution.py:233
  133.7 0.6 pad_maximum_fusion.5
  (22 shorter events, 0.2 us)
Async XLA Ops:
  0.0 32.8 %copy-start = (bf16[4096,1,384]{2,0,1:T(8,128)(2,1)S(1)}, bf16[4096,1,384]{2,0,1:T(8,128)(2,1)}, u32[]{:S(2)}) copy-start(bf16[4096,1,384]{2,0,1:T(8,128)(2,1)} %param.15) | copy-start | bytes 9437188
  0.0 14.1 %copy-start.6 = (s32[1,256]{1,0:T(1,128)S(1)}, s32[1,256]{1,0:T(1,128)}, u32[]{:S(2)}) copy-start(s32[1,256]{1,0:T(1,128)} %param.18) | copy-start | bytes 3076
  2.3 28.2 %all-to-all-start = ((bf16[32,128,128]{2,1,0:T(8,128)(2,1)}), bf16[32,128,128]{2,1,0:T(8,128)(2,1)}, u32[]{:S(2)}, u32[]{:S(2)}) async-start(bf16[32,128,128]{2,1,0:T(8,128)(2,1)} %bitcast.51), calls=%async_computation | async-start | bytes 2097152 | tf_op jit(solution)/shard_map/all_to_all | solution.py:204
  30.5 4.9 %collective-permute-start = (bf16[32,128,128]{2,1,0:T(8,128)(2,1)}, bf16[32,128,128]{2,1,0:T(8,128)(2,1)}, u32[]{:S(2)}, u32[]{:S(2)}) collective-permute-start(bf16[32,128,128]{2,1,0:T(8,128)(2,1)} %all-to-all-done), channel_id=1, source_target_pairs={{0,1},{1,0},{2,3},{3,2},{4,5},{5,4},{6,7},{7,6},{8,9},{9,8},{10,11... | collective-permute-start | bytes 3145736 | tf_op jit(solution)/shard_map/ppermute | solution.py:41
  32.7 44.9 %copy-start.7 = (pred[512]{0:T(512)(128)(4,1)}, pred[512]{0:T(512)(128)(4,1)S(1)}, u32[]{:S(2)}) copy-start(pred[512]{0:T(512)(128)(4,1)S(1)} %fusion.61) | copy-start | bytes 1540
  32.7 43.7 %copy-start.9 = (pred[256]{0:T(512)(128)(4,1)}, pred[256]{0:T(512)(128)(4,1)S(1)}, u32[]{:S(2)}) copy-start(pred[256]{0:T(512)(128)(4,1)S(1)} %compare_and_fusion) | copy-start | bytes 772
  32.8 44.8 %copy-start.8 = (pred[512]{0:T(512)(128)(4,1)}, pred[512]{0:T(512)(128)(4,1)S(1)}, u32[]{:S(2)}) copy-start(pred[512]{0:T(512)(128)(4,1)S(1)} %iota_compare_fusion.6) | copy-start | bytes 1540
  37.3 50.7 %copy-start.2 = (bf16[256,384]{1,0:T(8,128)(2,1)}, bf16[256,384]{1,0:T(8,128)(2,1)S(1)}, u32[]{:S(2)}) copy-start(bf16[256,384]{1,0:T(8,128)(2,1)S(1)} %fusion.14) | copy-start | bytes 589828
  38.4 25.2 %all-to-all-start.1 = ((bf16[16,40,128]{2,1,0:T(8,128)(2,1)}), bf16[16,40,128]{2,1,0:T(8,128)(2,1)}, u32[]{:S(2)}, u32[]{:S(2)}) async-start(bf16[16,40,128]{2,1,0:T(8,128)(2,1)} %pad_maximum_fusion), calls=%async_computation.1 | async-start | bytes 327680 | tf_op jit(solution)/shard_map/all_to_all | solution.py:179
  51.7 23.1 %collective-permute-start.1 = (bf16[272,256]{1,0:T(8,128)(2,1)}, bf16[272,256]{1,0:T(8,128)(2,1)}, u32[]{:S(2)}, u32[]{:S(2)}) collective-permute-start(bf16[272,256]{1,0:T(8,128)(2,1)} %maximum_maximum_fusion), channel_id=1, source_target_pairs={{0,32},{32,64},{64,96},{96,128},{128,160},{160,192},{192,224},{224... | collective-permute-start | bytes 417800 | tf_op jit(solution)/shard_map/ppermute | solution.py:124
  67.5 19.6 %all-to-all-start.2 = ((bf16[16,40,128]{2,1,0:T(8,128)(2,1)}), bf16[16,40,128]{2,1,0:T(8,128)(2,1)}, u32[]{:S(2)}, u32[]{:S(2)}) async-start(bf16[16,40,128]{2,1,0:T(8,128)(2,1)} %copy.21), calls=%async_computation.2 | async-start | bytes 327680 | tf_op jit(solution)/shard_map/all_to_all | solution.py:189
  75.6 12.4 %copy-start.4 = (s32[1,256]{1,0:T(1,128)}, s32[1,256]{1,0:T(1,128)S(1)}, u32[]{:S(2)}) copy-start(s32[1,256]{1,0:T(1,128)S(1)} %fusion.63) | copy-start | bytes 3076
  76.5 0.8 copy-start.3
  77.6 0.8 copy-start.1
  88.7 4.6 %copy-start.5 = (f32[256]{0:T(256)S(1)}, f32[256]{0:T(256)}, u32[]{:S(2)}) copy-start(f32[256]{0:T(256)} %fusion.15) | copy-start | bytes 3076
  100.4 8.9 %collective-permute-start.2 = (bf16[256,2048]{1,0:T(8,128)(2,1)}, bf16[256,2048]{1,0:T(8,128)(2,1)}, u32[]{:S(2)}, u32[]{:S(2)}) collective-permute-start(bf16[256,2048]{1,0:T(8,128)(2,1)} %dynamic-slice_convert_fusion), channel_id=1, source_target_pairs={{0,1},{1,0},{2,3},{3,2},{4,5},{5,4},{6,7},{7,6},{8,9},{9,8},{10,11... | collective-permute-start | bytes 3145736 | tf_op jit(solution)/shard_map/ppermute | solution.py:41

commit v5 on v4

--- a/solution.py
+++ b/solution.py
@@ -199,9 +199,11 @@
     rows, width = tokens_in.shape
     half = rows // nc
     spread = jnp.broadcast_to(
-        tokens_in.reshape(1, nc, half, width), (n_head // nc, nc, half, width)
-    ).reshape(n_head, half, width)
-    mine = lax.all_to_all(spread, HEAD_AXES, 0, 0, tiled=True)
+        tokens_in.reshape(1, nc, half, width), (ny, nc, half, width)
+    ).reshape(ny * nc, half, width)
+    row_of_x = lax.all_to_all(spread, ("hy", "hc"), 0, 0, tiled=True)
+    wide = jnp.broadcast_to(row_of_x[None], (nx,) + row_of_x.shape)
+    mine = lax.all_to_all(wide, "hx", 0, 0, tiled=True).reshape(n_head, half, width)
     theirs = _send(mine, core_perm)
     w_local = w_qkv[:, 0, :].reshape(n_head, width, -1)
     dims = (((0, 2), (0, 1)), ((), ()))
@@ -217,20 +219,22 @@
 
 def reduce_out(attended, w_out, sizes):
     nx, ny, nc = sizes
-    n_head = nx * ny * nc
     core_perm = _core_perm(*sizes)
     me_c = lax.axis_index("hc")
     rows = attended.shape[0]
     w_full = w_out[0]
     cols = w_full.shape[1] // nc
-    full = jnp.dot(attended, w_full, preferred_element_type=jnp.float32)
-    keep = lax.dynamic_slice_in_dim(full, me_c * cols, cols, 1)
-    give = lax.dynamic_slice_in_dim(full, (1 - me_c) * cols, cols, 1)
-    got = _send(give.astype(jnp.bfloat16), core_perm)
+    w_keep = lax.dynamic_slice_in_dim(w_full, me_c * cols, cols, 1)
+    w_give = lax.dynamic_slice_in_dim(w_full, (1 - me_c) * cols, cols, 1)
+    keep = jnp.dot(attended, w_keep, preferred_element_type=jnp.float32)
+    give = jnp.dot(attended, w_give, preferred_element_type=jnp.float32).astype(jnp.bfloat16)
+    got = _send(give, core_perm)
     summed = (keep + got.astype(jnp.float32)).astype(jnp.bfloat16)
-    chunks = summed.reshape(n_head, rows // n_head, cols)
-    parts = lax.all_to_all(chunks, HEAD_AXES, 0, 0, tiled=True).astype(jnp.float32)
-    parts = parts.reshape(n_head // nc, nc, rows // n_head, cols).sum(axis=0)
+    by_x = lax.all_to_all(summed.reshape(nx, rows // nx, cols), "hx", 0, 0, tiled=True)
+    part = by_x.astype(jnp.float32).sum(axis=0).astype(jnp.bfloat16)
+    chunks = part.reshape(ny * nc, rows // (nx * ny * nc), cols)
+    parts = lax.all_to_all(chunks, ("hy", "hc"), 0, 0, tiled=True).astype(jnp.float32)
+    parts = parts.reshape(ny, nc, rows // (nx * ny * nc), cols).sum(axis=0)
     out = jnp.concatenate([parts[i] for i in range(nc)], axis=1)
     return out.astype(jnp.bfloat16)
 

time: 135 us -> 142 us (1.052)
  blocking collectives: 20.7 us -> 44.5 us
  starting transfers between devices: 43 us -> 36.8 us
  other arithmetic: 11.8 us -> 7.98 us
  waiting for transfers between devices: 35.2 us -> 31.6 us
  local copies, waits for them, and re-layouts: 8.71 us -> 6.01 us
    all_to_all x1 -> x3, blocking collectives: 20.7 us -> 44.5 us  [the longest x1 18 us: reduce_out(): lax.all_to_all(summed.reshape(nx, rows // nx, cols), 'hx', 0, 0, tiled=True)]
    all_to_all x1, starting transfers between devices: 11.1 us -> 4.24 us  [project(): lax.all_to_all(wide, 'hx', 0, 0, tiled=True).reshape(n_head, half, width)]
    convert_element_type x1 -> x0, local copies, waits for them, and re-layouts: 2.75 us -> none  [reduce_out(): got = _send(give.astype(jnp.bfloat16), core_perm)]
    all_to_all x1, waiting for transfers between devices: 16.2 us -> 13.9 us  [project(): lax.all_to_all(wide, 'hx', 0, 0, tiled=True).reshape(n_head, half, width)]
    reshape x1 -> x0, other arithmetic: 2.2 us -> none  [reduce_out(): chunks = summed.reshape(n_head, rows // n_head, cols)]
    ppermute x2, starting transfers between devices: 8.31 us -> 10.1 us  [_send(): return lax.ppermute(value, HEAD_AXES, perm)]
    dot_general x1 -> x3, matrix products: 4.34 us -> 3.56 us  [the longest x1 1.81 us: reduce_out(): keep = jnp.dot(attended, w_keep, preferred_element_type=jnp.float32)]
  transfers between devices with their start and end apart: 6 -> 6, of which waited for: 5 -> 4; matrix products, arithmetic and copies ran while one was open for 8% -> 6% of each run, Pallas kernels for 0% -> 0%
where the time goes in v5:
time: 142 us; the launch traced here: 141 us
  blocking collectives  44.5 us (31%)
  starting transfers between devices  36.8 us (26%)
  waiting for transfers between devices  31.6 us (22%)
  matrix products  13.3 us (9%)
  other arithmetic  7.98 us (6%)
  local copies, waits for them, and re-layouts  6.01 us (4%)
    all_to_all x1, blocking collectives, reduce_out(): lax.all_to_all(summed.reshape(nx, rows // nx, cols), 'hx', 0, 0, tiled=True)  18 us
    all_to_all x1, blocking collectives, project(): row_of_x = lax.all_to_all(spread, ('hy', 'hc'), 0, 0, tiled=True)  15.8 us
    all_to_all x1, waiting for transfers between devices, project(): lax.all_to_all(wide, 'hx', 0, 0, tiled=True).reshape(n_head, half, width)  13.9 us
    all_to_all x1, starting transfers between devices, code_prefix(): lax.all_to_all(_pack(sums, counts, span, n, head_dim), 'ctx', 0, 0, tiled...  11.4 us
    all_to_all x1, blocking collectives, reduce_out(): lax.all_to_all(chunks, ('hy', 'hc'), 0, 0, tiled=True).astype(jnp.float32)  10.8 us
    ppermute x2, starting transfers between devices, _send(): return lax.ppermute(value, HEAD_AXES, perm)  10.1 us
    all_to_all x1, waiting for transfers between devices, code_prefix(): lax.all_to_all(_pack(sums, counts, span, n, head_dim), 'ctx', 0, 0, tiled...  8.08 us
    all_to_all x1, starting transfers between devices, code_prefix(): lax.all_to_all(_pack(pre_sums, pre_counts, span, n, head_dim), 'ctx', 0,...  7.12 us
  transfers between devices with their start and end apart: 6, of which 4 were waited for; matrix products, arithmetic and copies ran while one was open for 6% of the time, Pallas kernels for 0%

profile of v5, /device:TPU:1, one launch (start us, length us, event | category | flops | bytes accessed | tf_op | source)
XLA Modules:
  0.0 141.3 jit_solution(3323787091602803421)
XLA Ops:
  0.0 0.0 copy-start
  0.0 1.0 broadcast_in_dim.28
  1.0 15.8 %all_to_all.30 = bf16[8,128,128]{2,1,0:T(8,128)(2,1)S(1)} all-to-all(bf16[8,128,128]{2,1,0:T(8,128)(2,1)S(1)} %bitcast.62), channel_id=1, replica_groups=mesh['ctx'=16,'hx'=4,'hy'=4,'hc'=2] {'hy','hc'}, dimensions={0} | all-to-all | bytes 524288 | tf_op jit(solution)/shard_map/all_to_all | solution.py:204
  16.8 1.2 broadcast_in_dim.29
  18.1 4.2 %all-to-all-start.1 = ((bf16[4,8,128,128]{3,2,1,0:T(8,128)(2,1)}), bf16[4,8,128,128]{3,2,1,0:T(8,128)(2,1)}, u32[]{:S(2)}, u32[]{:S(2)}) async-start(bf16[4,8,128,128]{3,2,1,0:T(8,128)(2,1)} %broadcast_in_dim.29), calls=%async_computation.1 | async-start | bytes 2097152 | tf_op jit(solution)/shard_map/all_to_all | solution.py:206
  22.3 0.0 copy-done.12
  22.3 0.1 convert_reduce_fusion.1
  22.5 0.1 reduce_sum.51
  22.5 13.9 %all-to-all-done.1 = bf16[4,8,128,128]{3,2,1,0:T(8,128)(2,1)} async-done(((bf16[4,8,128,128]{3,2,1,0:T(8,128)(2,1)}), bf16[4,8,128,128]{3,2,1,0:T(8,128)(2,1)}, u32[]{:S(2)}, u32[]{:S(2)}) %all-to-all-start.1) | async-done | bytes 1048608 | tf_op jit(solution)/shard_map/all_to_all | solution.py:206
  36.5 3.9 %collective-permute-start = (bf16[32,128,128]{2,1,0:T(8,128)(2,1)}, bf16[32,128,128]{2,1,0:T(8,128)(2,1)}, u32[]{:S(2)}, u32[]{:S(2)}) collective-permute-start(bf16[32,128,128]{2,1,0:T(8,128)(2,1)} %bitcast.3), channel_id=1, source_target_pairs={{0,1},{1,0},{2,3},{3,2},{4,5},{5,4},{6,7},{7,6},{8,9},{9,8},{10,11... | collective-permute-start | bytes 3145736 | tf_op jit(solution)/shard_map/ppermute | solution.py:41
  40.4 0.2 scatter.15
  41.2 0.0 copy-start.13
  41.2 0.0 copy-start.14
  41.3 0.0 copy-done
  41.3 1.9 %convolution_bitcast_fusion.1 = bf16[128,384]{1,0:T(8,128)(2,1)S(1)} fusion(bf16[32,128,128]{2,1,0:T(8,128)(2,1)} %bitcast.3, bf16[32,128,384]{2,1,0:T(8,128)(2,1)S(1)} %bitcast.57), kind=kOutput, calls=%fused_computation.8 | convolution fusion | flops 402653184 | bytes 4292608 | tf_op jit(solution)/shard_map/dot_general | solution.py:210
  43.2 0.0 collective-permute-done
  43.2 1.9 %convolution_bitcast_fusion = bf16[128,384]{1,0:T(8,128)(2,1)S(1)} fusion(bf16[32,128,128]{2,1,0:T(8,128)(2,1)} %collective-permute-done, bf16[32,128,384]{2,1,0:T(8,128)(2,1)S(1)} %bitcast.58), kind=kOutput, calls=%fused_computation.7 | convolution fusion | flops 402653184 | bytes 4292608 | tf_op jit(solution)/shard_map/dot_general | solution.py:211
  45.2 0.0 copy-start.2
  45.2 0.4 convolution_convert_fusion.2
  45.7 0.7 pad_maximum_fusion
  46.3 11.4 %all-to-all-start.2 = ((bf16[16,40,128]{2,1,0:T(8,128)(2,1)}), bf16[16,40,128]{2,1,0:T(8,128)(2,1)S(1)}, u32[]{:S(2)}, u32[]{:S(2)}) async-start(bf16[16,40,128]{2,1,0:T(8,128)(2,1)} %pad_maximum_fusion), calls=%async_computation.2 | async-start | bytes 327680 | tf_op jit(solution)/shard_map/all_to_all | solution.py:179
  57.8 0.0 copy-start.16
  57.8 0.1 pad.29.clone
  57.9 0.0 copy-start.5
  57.9 0.8 maximum_maximum_fusion
  58.7 3.9 %collective-permute-start.1 = (bf16[272,256]{1,0:T(8,128)(2,1)}, bf16[272,256]{1,0:T(8,128)(2,1)}, u32[]{:S(2)}, u32[]{:S(2)}) collective-permute-start(bf16[272,256]{1,0:T(8,128)(2,1)} %maximum_maximum_fusion), channel_id=1, source_target_pairs={{0,32},{32,64},{64,96},{96,128},{128,160},{160,192},{192,224},{224... | collective-permute-start | bytes 417800 | tf_op jit(solution)/shard_map/ppermute | solution.py:124
  62.6 8.1 %all-to-all-done.2 = bf16[16,40,128]{2,1,0:T(8,128)(2,1)S(1)} async-done(((bf16[16,40,128]{2,1,0:T(8,128)(2,1)}), bf16[16,40,128]{2,1,0:T(8,128)(2,1)S(1)}, u32[]{:S(2)}, u32[]{:S(2)}) %all-to-all-start.2) | async-done | bytes 163872 | tf_op jit(solution)/shard_map/all_to_all | solution.py:179
  70.7 0.2 convolution_convert_fusion.1
  71.0 0.2 subtract_bitcast_fusion
  71.2 0.2 scatter.19
  71.3 0.7 copy.21
  72.1 7.1 %all-to-all-start.3 = ((bf16[16,40,128]{2,1,0:T(8,128)(2,1)}), bf16[16,40,128]{2,1,0:T(8,128)(2,1)S(1)}, u32[]{:S(2)}, u32[]{:S(2)}) async-start(bf16[16,40,128]{2,1,0:T(8,128)(2,1)} %copy.21), calls=%async_computation.3 | async-start | bytes 327680 | tf_op jit(solution)/shard_map/all_to_all | solution.py:189
  79.2 0.0 collective-permute-done.1
  79.2 0.8 fusion.58
  80.0 0.9 slice.173
  80.9 0.7 convert_reduce_fusion
  81.6 1.2 select_reduce_fusion.1
  82.8 0.8 copy-done.3
  83.6 0.9 fusion.19
  84.5 6.9 %all-to-all-done.3 = bf16[16,40,128]{2,1,0:T(8,128)(2,1)S(1)} async-done(((bf16[16,40,128]{2,1,0:T(8,128)(2,1)}), bf16[16,40,128]{2,1,0:T(8,128)(2,1)S(1)}, u32[]{:S(2)}, u32[]{:S(2)}) %all-to-all-start.3) | async-done | bytes 163872 | tf_op jit(solution)/shard_map/all_to_all | solution.py:189
  91.4 0.0 copy-done.16
  91.4 0.0 copy-done.2
  91.5 0.0 copy-start.6
  91.5 0.7 add.81
  92.2 0.0 copy-start.15
  92.2 0.0 copy-start.17
  92.2 0.0 copy-start.1
  92.2 0.8 broadcast_compare_fusion
  93.0 1.3 select_reduce_fusion
  94.3 0.1 copy.23
  94.4 0.6 fusion.16
  95.0 1.3 convolution_add_fusion
  96.3 0.6 fusion.17
  97.0 0.3 fusion.2
  97.4 0.0 copy-done.1
  97.4 1.4 convolution_convert_fusion
  98.8 6.2 %collective-permute-start.2 = (bf16[256,2048]{1,0:T(8,128)(2,1)}, bf16[256,2048]{1,0:T(8,128)(2,1)}, u32[]{:S(2)}, u32[]{:S(2)}) collective-permute-start(bf16[256,2048]{1,0:T(8,128)(2,1)} %convolution_convert_fusion), channel_id=1, source_target_pairs={{0,1},{1,0},{2,3},{3,2},{4,5},{5,4},{6,7},{7,6},{8,9},{9,8},{10,11... | collective-permute-start | bytes 3145736 | tf_op jit(solution)/shard_map/ppermute | solution.py:41
  105.1 2.6 %collective-permute-done.2 = bf16[256,2048]{1,0:T(8,128)(2,1)} collective-permute-done((bf16[256,2048]{1,0:T(8,128)(2,1)}, bf16[256,2048]{1,0:T(8,128)(2,1)}, u32[]{:S(2)}, u32[]{:S(2)}) %collective-permute-start.2) | collective-permute-done | bytes 1048608 | tf_op jit(solution)/shard_map/ppermute | solution.py:41
  107.7 1.8 %add_convert_fusion = bf16[256,2048]{1,0:T(8,128)(2,1)S(1)} fusion(bf16[256,2048]{1,0:T(8,128)(2,1)} %collective-permute-done.2, bf16[256,128]{1,0:T(8,128)(2,1)S(1)} %fusion.2, bf16[1,128,4096]{2,1,0:T(8,128)(2,1)} %param.16, s32[]{:T(128)S(6)} %select_n.50), kind=kOutput, calls=%fused_computation.1 | convolution fusion | flops 135790592 | bytes 2686980 | tf_op jit(solution)/shard_map/dot_general | solution.py:229
  109.5 18.0 %all_to_all.31 = bf16[4,64,2048]{2,1,0:T(8,128)(2,1)} all-to-all(bf16[4,64,2048]{2,1,0:T(8,128)(2,1)S(1)} %bitcast.59), channel_id=1, replica_groups=mesh['ctx'=16,'hx'=4,'hy'=4,'hc'=2] {'hx'}, dimensions={0} | all-to-all | bytes 2097152 | tf_op jit(solution)/shard_map/all_to_all | solution.py:233
  127.5 1.4 reduce_sum.54
  128.9 10.8 %all_to_all.32 = bf16[8,8,2048]{2,1,0:T(8,128)(2,1)} all-to-all(bf16[8,8,2048]{2,1,0:T(8,128)(2,1)S(1)} %bitcast.60), channel_id=1, replica_groups=mesh['ctx'=16,'hx'=4,'hy'=4,'hc'=2] {'hy','hc'}, dimensions={0} | all-to-all | bytes 524288 | tf_op jit(solution)/shard_map/all_to_all | solution.py:236
  139.6 1.0 reduce.9
  140.7 0.6 pad_maximum_fusion.4
  (42 shorter events, 0.3 us)
Async XLA Ops:
  0.0 41.3 %copy-start = (bf16[4096,1,384]{2,0,1:T(8,128)(2,1)S(1)}, bf16[4096,1,384]{2,0,1:T(8,128)(2,1)}, u32[]{:S(2)}) copy-start(bf16[4096,1,384]{2,0,1:T(8,128)(2,1)} %param.15) | copy-start | bytes 9437188
  0.0 22.3 %copy-start.12 = (s32[1,256]{1,0:T(1,128)S(1)}, s32[1,256]{1,0:T(1,128)}, u32[]{:S(2)}) copy-start(s32[1,256]{1,0:T(1,128)} %param.18) | copy-start | bytes 3076
  18.1 18.4 %all-to-all-start.1 = ((bf16[4,8,128,128]{3,2,1,0:T(8,128)(2,1)}), bf16[4,8,128,128]{3,2,1,0:T(8,128)(2,1)}, u32[]{:S(2)}, u32[]{:S(2)}) async-start(bf16[4,8,128,128]{3,2,1,0:T(8,128)(2,1)} %broadcast_in_dim.29), calls=%async_computation.1 | async-start | bytes 2097152 | tf_op jit(solution)/shard_map/all_to_all | solution.py:206
  36.5 6.8 %collective-permute-start = (bf16[32,128,128]{2,1,0:T(8,128)(2,1)}, bf16[32,128,128]{2,1,0:T(8,128)(2,1)}, u32[]{:S(2)}, u32[]{:S(2)}) collective-permute-start(bf16[32,128,128]{2,1,0:T(8,128)(2,1)} %bitcast.3), channel_id=1, source_target_pairs={{0,1},{1,0},{2,3},{3,2},{4,5},{5,4},{6,7},{7,6},{8,9},{9,8},{10,11... | collective-permute-start | bytes 3145736 | tf_op jit(solution)/shard_map/ppermute | solution.py:41
  41.2 39.7 %copy-start.13 = (pred[256]{0:T(512)(128)(4,1)}, pred[256]{0:T(512)(128)(4,1)S(1)}, u32[]{:S(2)}) copy-start(pred[256]{0:T(512)(128)(4,1)S(1)} %compare_and_fusion) | copy-start | bytes 772
  41.2 41.6 %copy-start.14 = (pred[512]{0:T(512)(128)(4,1)}, pred[512]{0:T(512)(128)(4,1)S(1)}, u32[]{:S(2)}) copy-start(pred[512]{0:T(512)(128)(4,1)S(1)} %fusion.56) | copy-start | bytes 1540
  45.2 46.2 %copy-start.2 = (bf16[256,384]{1,0:T(8,128)(2,1)}, bf16[256,384]{1,0:T(8,128)(2,1)S(1)}, u32[]{:S(2)}) copy-start(bf16[256,384]{1,0:T(8,128)(2,1)S(1)} %fusion.18) | copy-start | bytes 589828
  46.3 24.3 %all-to-all-start.2 = ((bf16[16,40,128]{2,1,0:T(8,128)(2,1)}), bf16[16,40,128]{2,1,0:T(8,128)(2,1)S(1)}, u32[]{:S(2)}, u32[]{:S(2)}) async-start(bf16[16,40,128]{2,1,0:T(8,128)(2,1)} %pad_maximum_fusion), calls=%async_computation.2 | async-start | bytes 327680 | tf_op jit(solution)/shard_map/all_to_all | solution.py:179
  57.8 33.6 %copy-start.16 = (pred[512]{0:T(512)(128)(4,1)}, pred[512]{0:T(512)(128)(4,1)S(1)}, u32[]{:S(2)}) copy-start(pred[512]{0:T(512)(128)(4,1)S(1)} %iota_compare_fusion.6) | copy-start | bytes 1540
  57.9 33.5 %copy-start.9 = (s32[512]{0:T(512)}, s32[512]{0:T(512)S(1)}, u32[]{:S(2)}) copy-start(s32[512]{0:T(512)S(1)} %iota_add_fusion) | copy-start | bytes 6148
  57.9 0.8 copy-start.5
  58.7 20.5 %collective-permute-start.1 = (bf16[272,256]{1,0:T(8,128)(2,1)}, bf16[272,256]{1,0:T(8,128)(2,1)}, u32[]{:S(2)}, u32[]{:S(2)}) collective-permute-start(bf16[272,256]{1,0:T(8,128)(2,1)} %maximum_maximum_fusion), channel_id=1, source_target_pairs={{0,32},{32,64},{64,96},{96,128},{128,160},{160,192},{192,224},{224... | collective-permute-start | bytes 417800 | tf_op jit(solution)/shard_map/ppermute | solution.py:124
  72.1 19.3 %all-to-all-start.3 = ((bf16[16,40,128]{2,1,0:T(8,128)(2,1)}), bf16[16,40,128]{2,1,0:T(8,128)(2,1)S(1)}, u32[]{:S(2)}, u32[]{:S(2)}) async-start(bf16[16,40,128]{2,1,0:T(8,128)(2,1)} %copy.21), calls=%async_computation.3 | async-start | bytes 327680 | tf_op jit(solution)/shard_map/all_to_all | solution.py:189
  80.9 0.8 copy-start.7
  82.8 0.8 copy-start.3
  91.5 5.5 %copy-start.6 = (bf16[256,256]{1,0:T(8,128)(2,1)S(1)}, bf16[256,256]{1,0:T(8,128)(2,1)}, u32[]{:S(2)}) copy-start(bf16[256,256]{1,0:T(8,128)(2,1)} %copy-done.5) | copy-start | bytes 393220
  92.2 4.8 %copy-start.11 = (f32[256]{0:T(256)S(1)}, f32[256]{0:T(256)}, u32[]{:S(2)}) copy-start(f32[256]{0:T(256)} %fusion.19) | copy-start | bytes 3076
  92.2 4.8 %copy-start.4 = (f32[256,512]{1,0:T(8,128)S(1)}, f32[256,512]{1,0:T(8,128)}, u32[]{:S(2)}) copy-start(f32[256,512]{1,0:T(8,128)} %copy-done.3) | copy-start | bytes 1572868
  92.2 4.9 %copy-start.8 = (bf16[256,256]{1,0:T(8,128)(2,1)S(1)}, bf16[256,256]{1,0:T(8,128)(2,1)}, u32[]{:S(2)}) copy-start(bf16[256,256]{1,0:T(8,128)(2,1)} %copy-done.7) | copy-start | bytes 393220
  92.2 4.9 %copy-start.10 = (s32[512]{0:T(512)S(1)}, s32[512]{0:T(512)}, u32[]{:S(2)}) copy-start(s32[512]{0:T(512)} %copy-done.9) | copy-start | bytes 6148
  92.2 4.9 %copy-start.15 = (pred[512]{0:T(512)(128)(4,1)S(1)}, pred[512]{0:T(512)(128)(4,1)}, u32[]{:S(2)}) copy-start(pred[512]{0:T(512)(128)(4,1)} %copy-done.14) | copy-start | bytes 1540
  92.2 4.9 %copy-start.17 = (pred[512]{0:T(512)(128)(4,1)S(1)}, pred[512]{0:T(512)(128)(4,1)}, u32[]{:S(2)}) copy-start(pred[512]{0:T(512)(128)(4,1)} %copy-done.16) | copy-start | bytes 1540
  92.2 5.2 %copy-start.1 = (bf16[1,128,4096]{2,1,0:T(8,128)(2,1)S(1)}, bf16[1,128,4096]{2,1,0:T(8,128)(2,1)}, u32[]{:S(2)}) copy-start(bf16[1,128,4096]{2,1,0:T(8,128)(2,1)} %param.16) | copy-start | bytes 3145732
  98.8 8.9 %collective-permute-start.2 = (bf16[256,2048]{1,0:T(8,128)(2,1)}, bf16[256,2048]{1,0:T(8,128)(2,1)}, u32[]{:S(2)}, u32[]{:S(2)}) collective-permute-start(bf16[256,2048]{1,0:T(8,128)(2,1)} %convolution_convert_fusion), channel_id=1, source_target_pairs={{0,1},{1,0},{2,3},{3,2},{4,5},{5,4},{6,7},{7,6},{8,9},{9,8},{10,11... | collective-permute-start | bytes 3145736 | tf_op jit(solution)/shard_map/ppermute | solution.py:41

commit v6 on v4

--- a/solution.py
+++ b/solution.py
@@ -217,17 +217,18 @@
 
 def reduce_out(attended, w_out, sizes):
     nx, ny, nc = sizes
-    n_head = nx * ny * nc
     core_perm = _core_perm(*sizes)
     me_c = lax.axis_index("hc")
     rows = attended.shape[0]
     w_full = w_out[0]
     cols = w_full.shape[1] // nc
-    full = jnp.dot(attended, w_full, preferred_element_type=jnp.float32)
-    keep = lax.dynamic_slice_in_dim(full, me_c * cols, cols, 1)
-    give = lax.dynamic_slice_in_dim(full, (1 - me_c) * cols, cols, 1)
-    got = _send(give.astype(jnp.bfloat16), core_perm)
+    w_keep = lax.dynamic_slice_in_dim(w_full, me_c * cols, cols, 1)
+    w_give = lax.dynamic_slice_in_dim(w_full, (1 - me_c) * cols, cols, 1)
+    keep = jnp.dot(attended, w_keep, preferred_element_type=jnp.float32)
+    give = jnp.dot(attended, w_give, preferred_element_type=jnp.float32).astype(jnp.bfloat16)
+    got = _send(give, core_perm)
     summed = (keep + got.astype(jnp.float32)).astype(jnp.bfloat16)
+    n_head = nx * ny * nc
     chunks = summed.reshape(n_head, rows // n_head, cols)
     parts = lax.all_to_all(chunks, HEAD_AXES, 0, 0, tiled=True).astype(jnp.float32)
     parts = parts.reshape(n_head // nc, nc, rows // n_head, cols).sum(axis=0)

time: 135 us -> 126 us (0.933)
  other arithmetic: 11.8 us -> 6.98 us
  local copies, waits for them, and re-layouts: 8.71 us -> 5.99 us
    convert_element_type x1 -> x0, local copies, waits for them, and re-layouts: 2.75 us -> none  [reduce_out(): got = _send(give.astype(jnp.bfloat16), core_perm)]
    reshape x1 -> x0, other arithmetic: 2.2 us -> none  [reduce_out(): chunks = summed.reshape(n_head, rows // n_head, cols)]
    dot_general x1 -> x3, matrix products: 4.34 us -> 3.56 us  [the longest x1 1.81 us: reduce_out(): keep = jnp.dot(attended, w_keep, preferred_element_type=jnp.float32)]
  transfers between devices with their start and end apart: 6 -> 6, of which waited for: 5 -> 4; matrix products, arithmetic and copies ran while one was open for 8% -> 7% of each run, Pallas kernels for 0% -> 0%
where the time goes in v6:
time: 126 us
  starting transfers between devices  43.3 us (34%)
  waiting for transfers between devices  33.9 us (27%)
  blocking collectives  21.1 us (17%)
  matrix products  13.3 us (11%)
  other arithmetic  6.98 us (6%)
  local copies, waits for them, and re-layouts  5.99 us (5%)
    all_to_all x1, blocking collectives, reduce_out(): lax.all_to_all(chunks, HEAD_AXES, 0, 0, tiled=True).astype(jnp.float32)  21.1 us
    all_to_all x1, waiting for transfers between devices, project(): mine = lax.all_to_all(spread, HEAD_AXES, 0, 0, tiled=True)  16.8 us
    all_to_all x1, starting transfers between devices, code_prefix(): lax.all_to_all(_pack(sums, counts, span, n, head_dim), 'ctx', 0, 0, tiled...  12.3 us
    all_to_all x1, starting transfers between devices, project(): mine = lax.all_to_all(spread, HEAD_AXES, 0, 0, tiled=True)  11.1 us
    ppermute x2, starting transfers between devices, _send(): return lax.ppermute(value, HEAD_AXES, perm)  8.31 us
    all_to_all x1, starting transfers between devices, code_prefix(): lax.all_to_all(_pack(pre_sums, pre_counts, span, n, head_dim), 'ctx', 0,...  7.59 us
    all_to_all x1, waiting for transfers between devices, code_prefix(): lax.all_to_all(_pack(sums, counts, span, n, head_dim), 'ctx', 0, 0, tiled...  7.55 us
    all_to_all x1, waiting for transfers between devices, code_prefix(): lax.all_to_all(_pack(pre_sums, pre_counts, span, n, head_dim), 'ctx', 0,...  6.88 us
  transfers between devices with their start and end apart: 6, of which 4 were waited for; matrix products, arithmetic and copies ran while one was open for 7% of the time, Pallas kernels for 0%

profile of v6, /device:TPU:1, one launch (start us, length us, event | category | flops | bytes accessed | tf_op | source)
XLA Modules:
  0.0 125.6 jit_solution(16954939605081237981)
XLA Ops:
  0.0 0.0 copy-start
  0.0 2.2 %broadcast_in_dim.42 = bf16[16,2,128,128]{3,2,1,0:T(8,128)(2,1)} broadcast(bf16[2,128,128]{2,1,0:T(8,128)(2,1)} %bitcast.62), dimensions={1,2,3} | broadcast | bytes 1114112 | tf_op jit(solution)/shard_map/broadcast_in_dim | solution.py:201
  2.2 11.1 %all-to-all-start = ((bf16[32,128,128]{2,1,0:T(8,128)(2,1)}), bf16[32,128,128]{2,1,0:T(8,128)(2,1)}, u32[]{:S(2)}, u32[]{:S(2)}) async-start(bf16[32,128,128]{2,1,0:T(8,128)(2,1)} %bitcast.58), calls=%async_computation | async-start | bytes 2097152 | tf_op jit(solution)/shard_map/all_to_all | solution.py:204
  13.4 0.0 copy-done.12
  13.4 0.1 convert_reduce_fusion.1
  13.5 0.1 reduce_sum.39
  13.6 16.8 %all-to-all-done = bf16[32,128,128]{2,1,0:T(8,128)(2,1)} async-done(((bf16[32,128,128]{2,1,0:T(8,128)(2,1)}), bf16[32,128,128]{2,1,0:T(8,128)(2,1)}, u32[]{:S(2)}, u32[]{:S(2)}) %all-to-all-start) | async-done | bytes 1048608 | tf_op jit(solution)/shard_map/all_to_all | solution.py:204
  30.4 2.0 %collective-permute-start = (bf16[32,128,128]{2,1,0:T(8,128)(2,1)}, bf16[32,128,128]{2,1,0:T(8,128)(2,1)}, u32[]{:S(2)}, u32[]{:S(2)}) collective-permute-start(bf16[32,128,128]{2,1,0:T(8,128)(2,1)} %all-to-all-done), channel_id=1, source_target_pairs={{0,1},{1,0},{2,3},{3,2},{4,5},{5,4},{6,7},{7,6},{8,9},{9,8},{10,11... | collective-permute-start | bytes 3145736 | tf_op jit(solution)/shard_map/ppermute | solution.py:41
  32.5 0.2 scatter.15
  33.4 0.0 copy-start.13
  33.4 0.0 copy-start.14
  33.4 0.0 copy-done
  33.4 1.9 %convolution_bitcast_fusion.1 = bf16[128,384]{1,0:T(8,128)(2,1)S(1)} fusion(bf16[32,128,128]{2,1,0:T(8,128)(2,1)} %all-to-all-done, bf16[32,128,384]{2,1,0:T(8,128)(2,1)S(1)} %bitcast.56), kind=kOutput, calls=%fused_computation.8 | convolution fusion | flops 402653184 | bytes 4292608 | tf_op jit(solution)/shard_map/dot_general | solution.py:208
  35.4 0.0 collective-permute-done
  35.4 1.9 %convolution_bitcast_fusion = bf16[128,384]{1,0:T(8,128)(2,1)S(1)} fusion(bf16[32,128,128]{2,1,0:T(8,128)(2,1)} %collective-permute-done, bf16[32,128,384]{2,1,0:T(8,128)(2,1)S(1)} %bitcast.57), kind=kOutput, calls=%fused_computation.7 | convolution fusion | flops 402653184 | bytes 4292608 | tf_op jit(solution)/shard_map/dot_general | solution.py:209
  37.4 0.0 copy-start.2
  37.4 0.4 convolution_convert_fusion.2
  37.8 0.7 pad_maximum_fusion
  38.5 12.3 %all-to-all-start.1 = ((bf16[16,40,128]{2,1,0:T(8,128)(2,1)}), bf16[16,40,128]{2,1,0:T(8,128)(2,1)S(1)}, u32[]{:S(2)}, u32[]{:S(2)}) async-start(bf16[16,40,128]{2,1,0:T(8,128)(2,1)} %pad_maximum_fusion), calls=%async_computation.1 | async-start | bytes 327680 | tf_op jit(solution)/shard_map/all_to_all | solution.py:179
  50.9 0.0 copy-start.16
  50.9 0.1 pad.29.clone
  51.0 0.0 copy-start.5
  51.0 0.8 maximum_maximum_fusion
  51.8 0.0 copy-done.5
  51.8 3.9 %collective-permute-start.1 = (bf16[272,256]{1,0:T(8,128)(2,1)}, bf16[272,256]{1,0:T(8,128)(2,1)}, u32[]{:S(2)}, u32[]{:S(2)}) collective-permute-start(bf16[272,256]{1,0:T(8,128)(2,1)} %maximum_maximum_fusion), channel_id=1, source_target_pairs={{0,32},{32,64},{64,96},{96,128},{128,160},{160,192},{192,224},{224... | collective-permute-start | bytes 417800 | tf_op jit(solution)/shard_map/ppermute | solution.py:124
  55.7 7.5 %all-to-all-done.1 = bf16[16,40,128]{2,1,0:T(8,128)(2,1)S(1)} async-done(((bf16[16,40,128]{2,1,0:T(8,128)(2,1)}), bf16[16,40,128]{2,1,0:T(8,128)(2,1)S(1)}, u32[]{:S(2)}, u32[]{:S(2)}) %all-to-all-start.1) | async-done | bytes 163872 | tf_op jit(solution)/shard_map/all_to_all | solution.py:179
  63.3 0.2 convolution_convert_fusion.1
  63.5 0.2 subtract_bitcast_fusion
  63.7 0.2 scatter.19
  63.9 0.7 copy.21
  64.6 7.6 %all-to-all-start.2 = ((bf16[16,40,128]{2,1,0:T(8,128)(2,1)}), bf16[16,40,128]{2,1,0:T(8,128)(2,1)S(1)}, u32[]{:S(2)}, u32[]{:S(2)}) async-start(bf16[16,40,128]{2,1,0:T(8,128)(2,1)} %copy.21), calls=%async_computation.2 | async-start | bytes 327680 | tf_op jit(solution)/shard_map/all_to_all | solution.py:189
  72.2 0.0 collective-permute-done.1
  72.2 0.8 fusion.59
  73.0 0.9 slice.173
  73.9 0.0 copy-start.7
  73.9 0.0 copy-done.13
  73.9 0.7 convert_reduce_fusion
  74.7 0.0 copy-done.7
  74.7 1.2 select_reduce_fusion.1
  75.9 0.0 copy-done.14
  75.9 0.8 copy-done.3
  76.7 0.9 fusion.20
  77.5 6.9 %all-to-all-done.2 = bf16[16,40,128]{2,1,0:T(8,128)(2,1)S(1)} async-done(((bf16[16,40,128]{2,1,0:T(8,128)(2,1)}), bf16[16,40,128]{2,1,0:T(8,128)(2,1)S(1)}, u32[]{:S(2)}, u32[]{:S(2)}) %all-to-all-start.2) | async-done | bytes 163872 | tf_op jit(solution)/shard_map/all_to_all | solution.py:189
  84.4 0.0 copy-done.16
  84.4 0.0 copy-done.2
  84.4 0.0 copy-start.6
  84.5 0.7 add.81
  85.2 0.0 copy-start.15
  85.2 0.0 copy-start.17
  85.2 0.0 copy-start.1
  85.2 0.8 broadcast_compare_fusion
  86.0 1.3 select_reduce_fusion
  87.3 0.1 copy.23
  87.4 0.6 fusion.17
  88.0 1.3 %convolution_add_fusion = f32[512,128]{1,0:T(8,128)S(1)} fusion(f32[512,128]{1,0:T(8,128)S(1)} %bitcast.60, s32[256]{0:T(256)S(1)} %bitcast.64, pred[256]{0:T(512)(128)(4,1)} %copy-done.13, bf16[272,256]{1,0:T(8,128)(2,1)} %collective-permute-done.1), kind=kOutput, calls=%fused_computation.4 | convolution fusion | flops 33882112 | bytes 591360 | tf_op jit(solution)/shard_map/dot_general | solution.py:141
  89.3 0.6 fusion.18
  90.0 0.3 fusion.2
  90.4 1.4 %convolution_convert_fusion = bf16[256,2048]{1,0:T(8,128)(2,1)} fusion(bf16[256,128]{1,0:T(8,128)(2,1)S(1)} %fusion.2, bf16[1,128,4096]{2,1,0:T(8,128)(2,1)S(1)} %copy-done.1, s32[]{:T(128)S(6)} %select_n.51), kind=kOutput, calls=%fused_computation | convolution fusion | flops 134742016 | bytes 1638404 | tf_op jit(solution)/shard_map/dot_general | solution.py:228
  91.8 6.3 %collective-permute-start.2 = (bf16[256,2048]{1,0:T(8,128)(2,1)}, bf16[256,2048]{1,0:T(8,128)(2,1)}, u32[]{:S(2)}, u32[]{:S(2)}) collective-permute-start(bf16[256,2048]{1,0:T(8,128)(2,1)} %convolution_convert_fusion), channel_id=1, source_target_pairs={{0,1},{1,0},{2,3},{3,2},{4,5},{5,4},{6,7},{7,6},{8,9},{9,8},{10,11... | collective-permute-start | bytes 3145736 | tf_op jit(solution)/shard_map/ppermute | solution.py:41
  98.1 2.6 %collective-permute-done.2 = bf16[256,2048]{1,0:T(8,128)(2,1)} collective-permute-done((bf16[256,2048]{1,0:T(8,128)(2,1)}, bf16[256,2048]{1,0:T(8,128)(2,1)}, u32[]{:S(2)}, u32[]{:S(2)}) %collective-permute-start.2) | collective-permute-done | bytes 1048608 | tf_op jit(solution)/shard_map/ppermute | solution.py:41
  100.7 1.8 %fusion.3 = bf16[32,8,2048]{2,1,0:T(8,128)(2,1)S(1)} fusion(bf16[256,2048]{1,0:T(8,128)(2,1)} %collective-permute-done.2, bf16[256,128]{1,0:T(8,128)(2,1)S(1)} %fusion.2, bf16[1,128,4096]{2,1,0:T(8,128)(2,1)} %param.16, s32[]{:T(128)S(6)} %select_n.50), kind=kOutput, calls=%fused_computation.13 | convolution fusion | flops 135790592 | bytes 2686980 | tf_op jit(solution)/shard_map/dot_general | solution.py:227
  102.5 21.1 %all_to_all.20 = bf16[32,8,2048]{2,1,0:T(8,128)(2,1)} all-to-all(bf16[32,8,2048]{2,1,0:T(8,128)(2,1)S(1)} %fusion.3), channel_id=1, replica_groups=mesh['ctx'=16,'hx'=4,'hy'=4,'hc'=2] {'hx','hy','hc'}, dimensions={0} | all-to-all | bytes 2097152 | tf_op jit(solution)/shard_map/all_to_all | solution.py:233
  123.6 1.4 %reduce.8 = bf16[2,8,2048]{2,1,0:T(8,128)(2,1)S(1)} reduce(bf16[16,2,8,2048]{3,2,1,0:T(8,128)(2,1)} %bitcast.59, bf16[]{:T(256)} %constant.164.clone.1), dimensions={0}, to_apply=%region_5.6.clone | reduce | flops 491520 | bytes 1114114 | tf_op jit(solution)/shard_map/reduce_sum | solution.py:234
  125.0 0.6 pad_maximum_fusion.4
  (38 shorter events, 0.3 us)
Async XLA Ops:
  0.0 33.4 %copy-start = (bf16[4096,1,384]{2,0,1:T(8,128)(2,1)S(1)}, bf16[4096,1,384]{2,0,1:T(8,128)(2,1)}, u32[]{:S(2)}) copy-start(bf16[4096,1,384]{2,0,1:T(8,128)(2,1)} %param.15) | copy-start | bytes 9437188
  0.0 13.4 %copy-start.12 = (s32[1,256]{1,0:T(1,128)S(1)}, s32[1,256]{1,0:T(1,128)}, u32[]{:S(2)}) copy-start(s32[1,256]{1,0:T(1,128)} %param.18) | copy-start | bytes 3076
  2.2 28.2 %all-to-all-start = ((bf16[32,128,128]{2,1,0:T(8,128)(2,1)}), bf16[32,128,128]{2,1,0:T(8,128)(2,1)}, u32[]{:S(2)}, u32[]{:S(2)}) async-start(bf16[32,128,128]{2,1,0:T(8,128)(2,1)} %bitcast.58), calls=%async_computation | async-start | bytes 2097152 | tf_op jit(solution)/shard_map/all_to_all | solution.py:204
  30.4 4.9 %collective-permute-start = (bf16[32,128,128]{2,1,0:T(8,128)(2,1)}, bf16[32,128,128]{2,1,0:T(8,128)(2,1)}, u32[]{:S(2)}, u32[]{:S(2)}) collective-permute-start(bf16[32,128,128]{2,1,0:T(8,128)(2,1)} %all-to-all-done), channel_id=1, source_target_pairs={{0,1},{1,0},{2,3},{3,2},{4,5},{5,4},{6,7},{7,6},{8,9},{9,8},{10,11... | collective-permute-start | bytes 3145736 | tf_op jit(solution)/shard_map/ppermute | solution.py:41
  33.4 40.6 %copy-start.13 = (pred[256]{0:T(512)(128)(4,1)}, pred[256]{0:T(512)(128)(4,1)S(1)}, u32[]{:S(2)}) copy-start(pred[256]{0:T(512)(128)(4,1)S(1)} %compare_and_fusion) | copy-start | bytes 772
  33.4 42.5 %copy-start.14 = (pred[512]{0:T(512)(128)(4,1)}, pred[512]{0:T(512)(128)(4,1)S(1)}, u32[]{:S(2)}) copy-start(pred[512]{0:T(512)(128)(4,1)S(1)} %fusion.57) | copy-start | bytes 1540
  37.4 47.1 %copy-start.2 = (bf16[256,384]{1,0:T(8,128)(2,1)}, bf16[256,384]{1,0:T(8,128)(2,1)S(1)}, u32[]{:S(2)}) copy-start(bf16[256,384]{1,0:T(8,128)(2,1)S(1)} %fusion.19) | copy-start | bytes 589828
  38.5 24.8 %all-to-all-start.1 = ((bf16[16,40,128]{2,1,0:T(8,128)(2,1)}), bf16[16,40,128]{2,1,0:T(8,128)(2,1)S(1)}, u32[]{:S(2)}, u32[]{:S(2)}) async-start(bf16[16,40,128]{2,1,0:T(8,128)(2,1)} %pad_maximum_fusion), calls=%async_computation.1 | async-start | bytes 327680 | tf_op jit(solution)/shard_map/all_to_all | solution.py:179
  50.9 33.5 %copy-start.16 = (pred[512]{0:T(512)(128)(4,1)}, pred[512]{0:T(512)(128)(4,1)S(1)}, u32[]{:S(2)}) copy-start(pred[512]{0:T(512)(128)(4,1)S(1)} %iota_compare_fusion.6) | copy-start | bytes 1540
  51.0 33.4 %copy-start.9 = (s32[512]{0:T(512)}, s32[512]{0:T(512)S(1)}, u32[]{:S(2)}) copy-start(s32[512]{0:T(512)S(1)} %iota_add_fusion) | copy-start | bytes 6148
  51.0 0.8 copy-start.5
  51.8 20.5 %collective-permute-start.1 = (bf16[272,256]{1,0:T(8,128)(2,1)}, bf16[272,256]{1,0:T(8,128)(2,1)}, u32[]{:S(2)}, u32[]{:S(2)}) collective-permute-start(bf16[272,256]{1,0:T(8,128)(2,1)} %maximum_maximum_fusion), channel_id=1, source_target_pairs={{0,32},{32,64},{64,96},{96,128},{128,160},{160,192},{192,224},{224... | collective-permute-start | bytes 417800 | tf_op jit(solution)/shard_map/ppermute | solution.py:124
  64.6 19.8 %all-to-all-start.2 = ((bf16[16,40,128]{2,1,0:T(8,128)(2,1)}), bf16[16,40,128]{2,1,0:T(8,128)(2,1)S(1)}, u32[]{:S(2)}, u32[]{:S(2)}) async-start(bf16[16,40,128]{2,1,0:T(8,128)(2,1)} %copy.21), calls=%async_computation.2 | async-start | bytes 327680 | tf_op jit(solution)/shard_map/all_to_all | solution.py:189
  73.9 0.8 copy-start.7
  75.9 0.8 copy-start.3
  84.4 5.5 %copy-start.6 = (bf16[256,256]{1,0:T(8,128)(2,1)S(1)}, bf16[256,256]{1,0:T(8,128)(2,1)}, u32[]{:S(2)}) copy-start(bf16[256,256]{1,0:T(8,128)(2,1)} %copy-done.5) | copy-start | bytes 393220
  85.1 4.8 %copy-start.11 = (f32[256]{0:T(256)S(1)}, f32[256]{0:T(256)}, u32[]{:S(2)}) copy-start(f32[256]{0:T(256)} %fusion.20) | copy-start | bytes 3076
  85.1 4.8 %copy-start.4 = (f32[256,512]{1,0:T(8,128)S(1)}, f32[256,512]{1,0:T(8,128)}, u32[]{:S(2)}) copy-start(f32[256,512]{1,0:T(8,128)} %copy-done.3) | copy-start | bytes 1572868
  85.2 4.9 %copy-start.8 = (bf16[256,256]{1,0:T(8,128)(2,1)S(1)}, bf16[256,256]{1,0:T(8,128)(2,1)}, u32[]{:S(2)}) copy-start(bf16[256,256]{1,0:T(8,128)(2,1)} %copy-done.7) | copy-start | bytes 393220
  85.2 4.9 %copy-start.10 = (s32[512]{0:T(512)S(1)}, s32[512]{0:T(512)}, u32[]{:S(2)}) copy-start(s32[512]{0:T(512)} %copy-done.9) | copy-start | bytes 6148
  85.2 4.9 %copy-start.15 = (pred[512]{0:T(512)(128)(4,1)S(1)}, pred[512]{0:T(512)(128)(4,1)}, u32[]{:S(2)}) copy-start(pred[512]{0:T(512)(128)(4,1)} %copy-done.14) | copy-start | bytes 1540
  85.2 4.9 %copy-start.17 = (pred[512]{0:T(512)(128)(4,1)S(1)}, pred[512]{0:T(512)(128)(4,1)}, u32[]{:S(2)}) copy-start(pred[512]{0:T(512)(128)(4,1)} %copy-done.16) | copy-start | bytes 1540
  85.2 5.2 %copy-start.1 = (bf16[1,128,4096]{2,1,0:T(8,128)(2,1)S(1)}, bf16[1,128,4096]{2,1,0:T(8,128)(2,1)}, u32[]{:S(2)}) copy-start(bf16[1,128,4096]{2,1,0:T(8,128)(2,1)} %param.16) | copy-start | bytes 3145732
  91.8 8.9 %collective-permute-start.2 = (bf16[256,2048]{1,0:T(8,128)(2,1)}, bf16[256,2048]{1,0:T(8,128)(2,1)}, u32[]{:S(2)}, u32[]{:S(2)}) collective-permute-start(bf16[256,2048]{1,0:T(8,128)(2,1)} %convolution_convert_fusion), channel_id=1, source_target_pairs={{0,1},{1,0},{2,3},{3,2},{4,5},{5,4},{6,7},{7,6},{8,9},{9,8},{10,11... | collective-permute-start | bytes 3145736 | tf_op jit(solution)/shard_map/ppermute | solution.py:41

commit v7 on v6

--- a/solution.py
+++ b/solution.py
@@ -8,6 +8,7 @@
 
 BLK = 256
 HEAD_AXES = ("hx", "hy", "hc")
+CTX_AXES = ("ca", "cb")
 
 
 def _flat(x, y, c, ny, nc):
@@ -100,8 +101,9 @@
     sizes = (nx, ny, nc)
     core_perm = _core_perm(*sizes)
     me_x, me_y, me_c = lax.axis_index("hx"), lax.axis_index("hy"), lax.axis_index("hc")
-    n_ctx = lax.axis_size("ctx")
-    g = lax.axis_index("ctx")
+    na, nb = lax.axis_size("ca"), lax.axis_size("cb")
+    n_ctx = na * nb
+    g = lax.axis_index("ca") * nb + lax.axis_index("cb")
     rows, width = tokens_in.shape
     head_dim = codebook.shape[2]
     num_codes = codebook.shape[1]
@@ -121,7 +123,7 @@
     code_rows = jnp.pad(jnp.concatenate([hi, lo], axis=0), ((0, 0), (0, kvw - rows)))
     kv_blob = jnp.concatenate([key_vals, code_rows, jnp.zeros((14, kvw), jnp.bfloat16)], axis=0)
     route = [(i, i + 1) for i in range(n_ctx - 1)]
-    prev_blob = lax.ppermute(kv_blob, "ctx", route)
+    prev_blob = lax.ppermute(kv_blob, CTX_AXES, route)
     prev_kv = prev_blob[:rows]
     prev_codes = (
         prev_blob[rows, :rows].astype(jnp.int32) * 16 + prev_blob[rows + 1, :rows].astype(jnp.int32)
@@ -133,7 +135,7 @@
     )
     counts = jnp.sum(onehot_own.astype(jnp.float32), axis=0)
     span = num_codes // n_ctx
-    cache_v, cache_c = code_prefix(sums, counts, span, n_ctx, head_dim)
+    cache_v, cache_c = code_prefix(sums, counts, span, na, nb, head_dim)
     prev_ok = (jnp.arange(rows, dtype=jnp.int32) < BLK - reach[0]) & (g > 0)
     onehot_prev = (
         (prev_codes[:, None] == code_ids[None, :]) & prev_ok[:, None]
@@ -175,8 +177,12 @@
     return sums, counts
 
 
-def code_prefix(sums, counts, span, n, head_dim):
-    got = lax.all_to_all(_pack(sums, counts, span, n, head_dim), "ctx", 0, 0, tiled=True)
+def code_prefix(sums, counts, span, na, nb, head_dim):
+    n = na * nb
+    blob = _pack(sums, counts, span, n, head_dim)
+    blob = blob.reshape(na, nb, -1, head_dim).transpose(1, 0, 2, 3)
+    step = lax.all_to_all(blob, "cb", 0, 0, tiled=True).transpose(1, 0, 2, 3)
+    got = lax.all_to_all(step, "ca", 0, 0, tiled=True).reshape(n, -1, head_dim)
     block_sums, block_counts = _unpack(got, span)
     b = jnp.arange(n, dtype=jnp.int32)
     before = (b[None, :] <= b[:, None] - 2).astype(jnp.bfloat16)
@@ -186,10 +192,11 @@
     pre_counts = jnp.dot(
         before, block_counts.astype(jnp.bfloat16), preferred_element_type=jnp.float32
     )
-    back = lax.all_to_all(_pack(pre_sums, pre_counts, span, n, head_dim), "ctx", 0, 0, tiled=True)
-    cache_v, cache_c = _unpack(back, span)
+    back = _pack(pre_sums, pre_counts, span, n, head_dim).reshape(na, nb, -1, head_dim)
+    step = lax.all_to_all(back, "ca", 0, 0, tiled=True).transpose(1, 0, 2, 3)
+    back = lax.all_to_all(step, "cb", 0, 0, tiled=True).transpose(1, 0, 2, 3)
+    cache_v, cache_c = _unpack(back.reshape(n, -1, head_dim), span)
     return cache_v.reshape(n * span, head_dim), cache_c.reshape(n * span)
-
 
 def project(tokens_in, w_qkv, sizes):
     nx, ny, nc = sizes
@@ -238,17 +245,17 @@
 
 def solution(mesh):
     n_ctx, n_head = mesh.devices.shape
-    devices = mesh.devices.reshape(n_ctx, 4, 4, n_head // 16)
-    grid = Mesh(devices, ("ctx",) + HEAD_AXES)
+    devices = mesh.devices.reshape(4, n_ctx // 4, 4, 4, n_head // 16)
+    grid = Mesh(devices, CTX_AXES + HEAD_AXES)
     in_specs = (
-        P("ctx", HEAD_AXES),
+        P(CTX_AXES, HEAD_AXES),
         P(None, HEAD_AXES, None),
         P(HEAD_AXES, None, None),
         P(HEAD_AXES, None, None),
-        P(HEAD_AXES, "ctx"),
-        P("ctx"),
-    )
-    out_specs = P(("ctx",) + HEAD_AXES, None)
+        P(HEAD_AXES, CTX_AXES),
+        P(CTX_AXES),
+    )
+    out_specs = P(CTX_AXES + HEAD_AXES, None)
     return jax.shard_map(
         on_device, mesh=grid, in_specs=in_specs, out_specs=out_specs, check_vma=False
     )

time: 126 us -> 144 us (1.14)
  blocking collectives: 21.1 us -> 47.9 us
  starting transfers between devices: 43.3 us -> 37.8 us
  waiting for transfers between devices: 33.9 us -> 28.9 us
    all_to_all x0 -> x1, blocking collectives: none -> 27.2 us  [project(): mine = lax.all_to_all(spread, HEAD_AXES, 0, 0, tiled=True)]
    all_to_all x3 -> x4, waiting for transfers between devices: 31.2 us -> 21.5 us  [the longest x1 12.7 us: code_prefix(): got = lax.all_to_all(step, 'ca', 0, 0, tiled=True).reshape(n, -1, head_dim)]
    all_to_all x3 -> x4, starting transfers between devices: 31.1 us -> 24.4 us  [the longest x1 13.2 us: code_prefix(): got = lax.all_to_all(step, 'ca', 0, 0, tiled=True).reshape(n, -1, head_dim)]
    ppermute x1, waiting for transfers between devices: 0.01 us -> 4.27 us  [on_device(): prev_blob = lax.ppermute(kv_blob, CTX_AXES, route)]
    ppermute x2, starting transfers between devices: 8.31 us -> 11.4 us  [_send(): return lax.ppermute(value, HEAD_AXES, perm)]
    ppermute x1, starting transfers between devices: 3.92 us -> 2.01 us  [on_device(): prev_blob = lax.ppermute(kv_blob, CTX_AXES, route)]
  transfers between devices with their start and end apart: 6 -> 7, of which waited for: 4 -> 7; matrix products, arithmetic and copies ran while one was open for 7% -> 6% of each run, Pallas kernels for 0% -> 0%
where the time goes in v7:
time: 144 us; the launch traced here: 143 us
  blocking collectives  47.9 us (33%)
  starting transfers between devices  37.8 us (26%)
  waiting for transfers between devices  28.9 us (20%)
  matrix products  14.3 us (10%)
  local copies, waits for them, and re-layouts  7.34 us (5%)
  other arithmetic  5.95 us (4%)
    all_to_all x1, blocking collectives, project(): mine = lax.all_to_all(spread, HEAD_AXES, 0, 0, tiled=True)  27.2 us
    all_to_all x1, blocking collectives, reduce_out(): lax.all_to_all(chunks, HEAD_AXES, 0, 0, tiled=True).astype(jnp.float32)  20.7 us
    all_to_all x1, starting transfers between devices, code_prefix(): got = lax.all_to_all(step, 'ca', 0, 0, tiled=True).reshape(n, -1, head_dim)  13.2 us
    all_to_all x1, waiting for transfers between devices, code_prefix(): got = lax.all_to_all(step, 'ca', 0, 0, tiled=True).reshape(n, -1, head_dim)  12.7 us
    ppermute x2, starting transfers between devices, _send(): return lax.ppermute(value, HEAD_AXES, perm)  11.4 us
    all_to_all x1, waiting for transfers between devices, code_prefix(): step = lax.all_to_all(blob, 'cb', 0, 0, tiled=True).transpose(1, 0, 2, 3)  4.3 us
    ppermute x1, waiting for transfers between devices, on_device(): prev_blob = lax.ppermute(kv_blob, CTX_AXES, route)  4.27 us
    all_to_all x1, starting transfers between devices, code_prefix(): step = lax.all_to_all(blob, 'cb', 0, 0, tiled=True).transpose(1, 0, 2, 3)  3.82 us
  transfers between devices with their start and end apart: 7, of which 7 were waited for; matrix products, arithmetic and copies ran while one was open for 6% of the time, Pallas kernels for 0%

profile of v7, /device:TPU:1, one launch (start us, length us, event | category | flops | bytes accessed | tf_op | source)
XLA Modules:
  0.0 143.1 jit_solution(16376654199502548785)
XLA Ops:
  0.0 0.0 copy-start
  0.0 0.0 copy-start.5
  0.0 1.2 broadcast_in_dim.42
  1.2 27.2 %all_to_all.30 = bf16[32,128,128]{2,1,0:T(8,128)(2,1)} all-to-all(bf16[32,128,128]{2,1,0:T(8,128)(2,1)S(1)} %bitcast.70), channel_id=1, replica_groups=mesh['ca'=4,'cb'=4,'hx'=4,'hy'=4,'hc'=2] {'hx','hy','hc'}, dimensions={0} | all-to-all | bytes 2097152 | tf_op jit(solution)/shard_map/all_to_all | solution.py:211
  28.4 2.0 %collective-permute-start = (bf16[32,128,128]{2,1,0:T(8,128)(2,1)}, bf16[32,128,128]{2,1,0:T(8,128)(2,1)}, u32[]{:S(2)}, u32[]{:S(2)}) collective-permute-start(bf16[32,128,128]{2,1,0:T(8,128)(2,1)} %all_to_all.30), channel_id=1, source_target_pairs={{0,1},{1,0},{2,3},{3,2},{4,5},{5,4},{6,7},{7,6},{8,9},{9,8},{10,11... | collective-permute-start | bytes 3145736 | tf_op jit(solution)/shard_map/ppermute | solution.py:42
  30.5 0.0 copy-done.5
  30.5 0.1 convert_reduce_fusion.1
  30.6 0.1 reduce_sum.39
  30.7 0.2 scatter.15
  30.9 0.0 copy-done
  30.9 1.9 %convolution_bitcast_fusion.1 = bf16[128,384]{1,0:T(8,128)(2,1)S(1)} fusion(bf16[32,128,128]{2,1,0:T(8,128)(2,1)} %all_to_all.30, bf16[32,128,384]{2,1,0:T(8,128)(2,1)S(1)} %bitcast.67), kind=kOutput, calls=%fused_computation.8 | convolution fusion | flops 402653184 | bytes 4292608 | tf_op jit(solution)/shard_map/dot_general | solution.py:215
  32.9 0.5 collective-permute-done
  33.3 1.9 %convolution_bitcast_fusion = bf16[128,384]{1,0:T(8,128)(2,1)S(1)} fusion(bf16[32,128,128]{2,1,0:T(8,128)(2,1)} %collective-permute-done, bf16[32,128,384]{2,1,0:T(8,128)(2,1)S(1)} %bitcast.68), kind=kOutput, calls=%fused_computation.7 | convolution fusion | flops 402653184 | bytes 4292608 | tf_op jit(solution)/shard_map/dot_general | solution.py:216
  35.3 0.0 copy-start.2
  35.3 0.4 convolution_convert_fusion.2
  35.8 0.7 maximum_bitcast_fusion
  36.4 3.8 %all-to-all-start.1 = ((bf16[4,4,40,128]{3,2,1,0:T(8,128)(2,1)}), bf16[4,4,40,128]{3,2,1,0:T(8,128)(2,1)S(1)}, u32[]{:S(2)}, u32[]{:S(2)}) async-start(bf16[4,4,40,128]{3,2,1,0:T(8,128)(2,1)} %maximum_bitcast_fusion), calls=%async_computation.1 | async-start | bytes 327680 | tf_op jit(solution)/shard_map/all_to_all | solution.py:184
  40.9 4.3 %all-to-all-done.1 = bf16[4,4,40,128]{3,2,1,0:T(8,128)(2,1)S(1)} async-done(((bf16[4,4,40,128]{3,2,1,0:T(8,128)(2,1)}), bf16[4,4,40,128]{3,2,1,0:T(8,128)(2,1)S(1)}, u32[]{:S(2)}, u32[]{:S(2)}) %all-to-all-start.1) | async-done | bytes 163872 | tf_op jit(solution)/shard_map/all_to_all | solution.py:184
  45.2 0.7 copy.31
  45.9 13.2 %all-to-all-start.2 = ((bf16[4,4,40,128]{3,2,1,0:T(8,128)(2,1)}), bf16[4,4,40,128]{3,2,1,0:T(8,128)(2,1)S(1)}, u32[]{:S(2)}, u32[]{:S(2)}) async-start(bf16[4,4,40,128]{3,2,1,0:T(8,128)(2,1)} %copy.31), calls=%async_computation.2 | async-start | bytes 327680 | tf_op jit(solution)/shard_map/all_to_all | solution.py:185
  59.0 0.1 pad.29.clone
  59.1 0.7 slice.172
  59.8 12.7 %all-to-all-done.2 = bf16[4,4,40,128]{3,2,1,0:T(8,128)(2,1)S(1)} async-done(((bf16[4,4,40,128]{3,2,1,0:T(8,128)(2,1)}), bf16[4,4,40,128]{3,2,1,0:T(8,128)(2,1)S(1)}, u32[]{:S(2)}, u32[]{:S(2)}) %all-to-all-start.2) | async-done | bytes 163872 | tf_op jit(solution)/shard_map/all_to_all | solution.py:185
  72.5 0.1 copy.32
  72.6 0.2 convolution_convert_fusion.1
  72.9 0.2 subtract_bitcast_fusion
  73.1 0.2 scatter.19
  73.2 0.1 pad_maximum_fusion
  73.4 0.7 copy.38
  74.1 3.8 %all-to-all-start.3 = ((bf16[4,4,40,128]{3,1,2,0:T(4,128)(2,1)}), bf16[4,4,40,128]{3,1,2,0:T(4,128)(2,1)S(1)}, u32[]{:S(2)}, u32[]{:S(2)}) async-start(bf16[4,4,40,128]{3,1,2,0:T(4,128)(2,1)} %copy.38), calls=%async_computation.3 | async-start | bytes 327680 | tf_op jit(solution)/shard_map/all_to_all | solution.py:196
  77.8 1.7 %maximum_maximum_fusion = bf16[272,256]{1,0:T(8,128)(2,1)} fusion(bf16[1,256]{1,0:T(2,128)(2,1)S(1)} %fusion.58, bf16[1,256]{1,0:T(2,128)(2,1)S(1)} %get-tuple-element.57, bf16[256,256]{1,0:T(8,128)(2,1)} %slice.172, bf16[272]{0:T(512)(128)(2,1)S(1)} %pad.29.clone), kind=kLoop, calls=%fused_computation.58 | loop fusion | flops 557056 | bytes 271904 | tf_op jit(solution)/shard_map/concatenate | solution.py:124
  79.5 2.0 %collective-permute-start.1 = (bf16[272,256]{1,0:T(8,128)(2,1)}, bf16[272,256]{1,0:T(8,128)(2,1)}, u32[]{:S(2)}, u32[]{:S(2)}) collective-permute-start(bf16[272,256]{1,0:T(8,128)(2,1)} %maximum_maximum_fusion), channel_id=1, source_target_pairs={{0,32},{32,64},{64,96},{96,128},{128,160},{160,192},{192,224},{224... | collective-permute-start | bytes 417800 | tf_op jit(solution)/shard_map/ppermute | solution.py:126
  81.5 4.3 %collective-permute-done.1 = bf16[272,256]{1,0:T(8,128)(2,1)} collective-permute-done((bf16[272,256]{1,0:T(8,128)(2,1)}, bf16[272,256]{1,0:T(8,128)(2,1)}, u32[]{:S(2)}, u32[]{:S(2)}) %collective-permute-start.1) | collective-permute-done | bytes 139296 | tf_op jit(solution)/shard_map/ppermute | solution.py:126
  85.8 1.6 %slice.173 = bf16[256,256]{1,0:T(8,128)(2,1)} slice(bf16[272,256]{1,0:T(8,128)(2,1)} %collective-permute-done.1), slice={[0:256], [0:256]} | slice | bytes 262144 | tf_op jit(solution)/shard_map/slice | solution.py:127
  87.3 0.8 fusion.59
  88.1 2.1 %all-to-all-done.3 = bf16[4,4,40,128]{3,1,2,0:T(4,128)(2,1)S(1)} async-done(((bf16[4,4,40,128]{3,1,2,0:T(4,128)(2,1)}), bf16[4,4,40,128]{3,1,2,0:T(4,128)(2,1)S(1)}, u32[]{:S(2)}, u32[]{:S(2)}) %all-to-all-start.3) | async-done | bytes 163872 | tf_op jit(solution)/shard_map/all_to_all | solution.py:196
  90.2 0.8 copy.35
  90.9 3.6 %all-to-all-start.4 = ((bf16[4,4,40,128]{3,1,2,0:T(4,128)(2,1)}), bf16[4,4,40,128]{3,1,2,0:T(4,128)(2,1)S(1)}, u32[]{:S(2)}, u32[]{:S(2)}) async-start(bf16[4,4,40,128]{3,1,2,0:T(4,128)(2,1)} %copy.35), calls=%async_computation.4 | async-start | bytes 327680 | tf_op jit(solution)/shard_map/all_to_all | solution.py:197
  94.6 0.2 convert_reduce_fusion
  94.8 1.2 select_reduce_fusion.1
  96.0 0.0 copy-done.2
  96.0 0.0 copy-start.3
  96.0 0.8 copy-done.3
  96.8 0.3 fusion.20
  97.0 2.4 %all-to-all-done.4 = bf16[4,4,40,128]{3,1,2,0:T(4,128)(2,1)S(1)} async-done(((bf16[4,4,40,128]{3,1,2,0:T(4,128)(2,1)}), bf16[4,4,40,128]{3,1,2,0:T(4,128)(2,1)S(1)}, u32[]{:S(2)}, u32[]{:S(2)}) %all-to-all-start.4) | async-done | bytes 163872 | tf_op jit(solution)/shard_map/all_to_all | solution.py:197
  99.5 0.2 copy.36
  99.7 0.1 add.85
  99.8 0.0 copy-start.4
  99.8 0.0 copy-start.1
  99.8 1.4 select_reduce_fusion
  101.2 0.1 copy.37
  101.3 0.6 fusion.17
  101.9 1.3 convolution_add_fusion
  103.2 0.6 fusion.18
  103.9 0.0 copy-done.4
  103.9 1.2 fusion.2
  105.1 0.0 copy-done.1
  105.1 1.4 convolution_convert_fusion
  106.5 9.4 %collective-permute-start.2 = (bf16[256,2048]{1,0:T(8,128)(2,1)}, bf16[256,2048]{1,0:T(8,128)(2,1)}, u32[]{:S(2)}, u32[]{:S(2)}) collective-permute-start(bf16[256,2048]{1,0:T(8,128)(2,1)} %convolution_convert_fusion), channel_id=1, source_target_pairs={{0,1},{1,0},{2,3},{3,2},{4,5},{5,4},{6,7},{7,6},{8,9},{9,8},{10,11... | collective-permute-start | bytes 3145736 | tf_op jit(solution)/shard_map/ppermute | solution.py:42
  116.0 2.6 %collective-permute-done.2 = bf16[256,2048]{1,0:T(8,128)(2,1)} collective-permute-done((bf16[256,2048]{1,0:T(8,128)(2,1)}, bf16[256,2048]{1,0:T(8,128)(2,1)}, u32[]{:S(2)}, u32[]{:S(2)}) %collective-permute-start.2) | collective-permute-done | bytes 1048608 | tf_op jit(solution)/shard_map/ppermute | solution.py:42
  118.6 1.8 %fusion.3 = bf16[32,8,2048]{2,1,0:T(8,128)(2,1)S(1)} fusion(bf16[256,2048]{1,0:T(8,128)(2,1)} %collective-permute-done.2, bf16[256,128]{1,0:T(8,128)(2,1)S(1)} %fusion.2, bf16[1,128,4096]{2,1,0:T(8,128)(2,1)} %param.16, s32[]{:T(128)S(6)} %select_n.50), kind=kOutput, calls=%fused_computation.13 | convolution fusion | flops 135790592 | bytes 2686980 | tf_op jit(solution)/shard_map/dot_general | solution.py:234
  120.4 20.7 %all_to_all.31 = bf16[32,8,2048]{2,1,0:T(8,128)(2,1)} all-to-all(bf16[32,8,2048]{2,1,0:T(8,128)(2,1)S(1)} %fusion.3), channel_id=1, replica_groups=mesh['ca'=4,'cb'=4,'hx'=4,'hy'=4,'hc'=2] {'hx','hy','hc'}, dimensions={0} | all-to-all | bytes 2097152 | tf_op jit(solution)/shard_map/all_to_all | solution.py:240
  141.1 1.4 reduce.8
  142.5 0.6 pad_maximum_fusion.3
  (20 shorter events, 0.2 us)
Async XLA Ops:
  0.0 30.9 %copy-start = (bf16[4096,1,384]{2,0,1:T(8,128)(2,1)S(1)}, bf16[4096,1,384]{2,0,1:T(8,128)(2,1)}, u32[]{:S(2)}) copy-start(bf16[4096,1,384]{2,0,1:T(8,128)(2,1)} %param.15) | copy-start | bytes 9437188
  0.0 30.5 %copy-start.5 = (s32[1,256]{1,0:T(1,128)S(1)}, s32[1,256]{1,0:T(1,128)}, u32[]{:S(2)}) copy-start(s32[1,256]{1,0:T(1,128)} %param.18) | copy-start | bytes 3076
  28.4 4.9 %collective-permute-start = (bf16[32,128,128]{2,1,0:T(8,128)(2,1)}, bf16[32,128,128]{2,1,0:T(8,128)(2,1)}, u32[]{:S(2)}, u32[]{:S(2)}) collective-permute-start(bf16[32,128,128]{2,1,0:T(8,128)(2,1)} %all_to_all.30), channel_id=1, source_target_pairs={{0,1},{1,0},{2,3},{3,2},{4,5},{5,4},{6,7},{7,6},{8,9},{9,8},{10,11... | collective-permute-start | bytes 3145736 | tf_op jit(solution)/shard_map/ppermute | solution.py:42
  35.3 60.6 %copy-start.2 = (bf16[256,384]{1,0:T(8,128)(2,1)}, bf16[256,384]{1,0:T(8,128)(2,1)S(1)}, u32[]{:S(2)}) copy-start(bf16[256,384]{1,0:T(8,128)(2,1)S(1)} %fusion.19) | copy-start | bytes 589828
  36.4 8.8 %all-to-all-start.1 = ((bf16[4,4,40,128]{3,2,1,0:T(8,128)(2,1)}), bf16[4,4,40,128]{3,2,1,0:T(8,128)(2,1)S(1)}, u32[]{:S(2)}, u32[]{:S(2)}) async-start(bf16[4,4,40,128]{3,2,1,0:T(8,128)(2,1)} %maximum_bitcast_fusion), calls=%async_computation.1 | async-start | bytes 327680 | tf_op jit(solution)/shard_map/all_to_all | solution.py:184
  45.9 26.7 %all-to-all-start.2 = ((bf16[4,4,40,128]{3,2,1,0:T(8,128)(2,1)}), bf16[4,4,40,128]{3,2,1,0:T(8,128)(2,1)S(1)}, u32[]{:S(2)}, u32[]{:S(2)}) async-start(bf16[4,4,40,128]{3,2,1,0:T(8,128)(2,1)} %copy.31), calls=%async_computation.2 | async-start | bytes 327680 | tf_op jit(solution)/shard_map/all_to_all | solution.py:185
  74.1 16.1 %all-to-all-start.3 = ((bf16[4,4,40,128]{3,1,2,0:T(4,128)(2,1)}), bf16[4,4,40,128]{3,1,2,0:T(4,128)(2,1)S(1)}, u32[]{:S(2)}, u32[]{:S(2)}) async-start(bf16[4,4,40,128]{3,1,2,0:T(4,128)(2,1)} %copy.38), calls=%async_computation.3 | async-start | bytes 327680 | tf_op jit(solution)/shard_map/all_to_all | solution.py:196
  79.5 6.3 %collective-permute-start.1 = (bf16[272,256]{1,0:T(8,128)(2,1)}, bf16[272,256]{1,0:T(8,128)(2,1)}, u32[]{:S(2)}, u32[]{:S(2)}) collective-permute-start(bf16[272,256]{1,0:T(8,128)(2,1)} %maximum_maximum_fusion), channel_id=1, source_target_pairs={{0,32},{32,64},{64,96},{96,128},{128,160},{160,192},{192,224},{224... | collective-permute-start | bytes 417800 | tf_op jit(solution)/shard_map/ppermute | solution.py:126
  90.9 8.5 %all-to-all-start.4 = ((bf16[4,4,40,128]{3,1,2,0:T(4,128)(2,1)}), bf16[4,4,40,128]{3,1,2,0:T(4,128)(2,1)S(1)}, u32[]{:S(2)}, u32[]{:S(2)}) async-start(bf16[4,4,40,128]{3,1,2,0:T(4,128)(2,1)} %copy.35), calls=%async_computation.4 | async-start | bytes 327680 | tf_op jit(solution)/shard_map/all_to_all | solution.py:197
  96.0 0.8 copy-start.3
  99.8 4.1 %copy-start.4 = (f32[256,512]{1,0:T(8,128)S(1)}, f32[256,512]{1,0:T(8,128)}, u32[]{:S(2)}) copy-start(f32[256,512]{1,0:T(8,128)} %copy-done.3) | copy-start | bytes 1572868
  99.8 5.3 %copy-start.1 = (bf16[1,128,4096]{2,1,0:T(8,128)(2,1)S(1)}, bf16[1,128,4096]{2,1,0:T(8,128)(2,1)}, u32[]{:S(2)}) copy-start(bf16[1,128,4096]{2,1,0:T(8,128)(2,1)} %param.16) | copy-start | bytes 3145732
  106.5 12.0 %collective-permute-start.2 = (bf16[256,2048]{1,0:T(8,128)(2,1)}, bf16[256,2048]{1,0:T(8,128)(2,1)}, u32[]{:S(2)}, u32[]{:S(2)}) collective-permute-start(bf16[256,2048]{1,0:T(8,128)(2,1)} %convolution_convert_fusion), channel_id=1, source_target_pairs={{0,1},{1,0},{2,3},{3,2},{4,5},{5,4},{6,7},{7,6},{8,9},{9,8},{10,11... | collective-permute-start | bytes 3145736 | tf_op jit(solution)/shard_map/ppermute | solution.py:42

commit v8 on v6

--- a/solution.py
+++ b/solution.py
@@ -108,32 +108,35 @@
     scale = 1.0 / math.sqrt(head_dim)
     half = rows // 2
 
+    code_row = codes[0]
+    code_ids = jnp.arange(num_codes, dtype=jnp.int32)
+    codes_all = lax.all_to_all(
+        jnp.broadcast_to(code_row[None], (n_ctx, rows)), "ctx", 0, 0, tiled=True
+    )
+    limit = g * BLK - reach[0]
+    cached = jnp.arange(n_ctx * rows, dtype=jnp.int32).reshape(n_ctx, rows) < limit
+    cache_c = jnp.sum(
+        ((codes_all[:, :, None] == code_ids[None, None, :]) & cached[:, :, None]).astype(
+            jnp.float32
+        ),
+        axis=(0, 1),
+    )
+
     projected = project(tokens_in, w_qkv, sizes)
     queries = projected[:, :head_dim].astype(jnp.bfloat16)
     key_vals = projected[:, head_dim:].astype(jnp.bfloat16)
     values = key_vals[:, head_dim:]
 
-    code_row = codes[0]
-    code_ids = jnp.arange(num_codes, dtype=jnp.int32)
-    hi = (code_row // 16).astype(jnp.bfloat16).reshape(1, -1)
-    lo = (code_row % 16).astype(jnp.bfloat16).reshape(1, -1)
-    kvw = key_vals.shape[1]
-    code_rows = jnp.pad(jnp.concatenate([hi, lo], axis=0), ((0, 0), (0, kvw - rows)))
-    kv_blob = jnp.concatenate([key_vals, code_rows, jnp.zeros((14, kvw), jnp.bfloat16)], axis=0)
     route = [(i, i + 1) for i in range(n_ctx - 1)]
-    prev_blob = lax.ppermute(kv_blob, "ctx", route)
-    prev_kv = prev_blob[:rows]
-    prev_codes = (
-        prev_blob[rows, :rows].astype(jnp.int32) * 16 + prev_blob[rows + 1, :rows].astype(jnp.int32)
-    )
+    prev_kv = lax.ppermute(key_vals, "ctx", route)
+    prev_codes = lax.dynamic_index_in_dim(codes_all, jnp.maximum(g - 1, 0), 0, keepdims=False)
 
     onehot_own = (code_row[:, None] == code_ids[None, :]).astype(jnp.bfloat16)
     sums = lax.dot_general(
         onehot_own, values, (((0,), (0,)), ((), ())), preferred_element_type=jnp.float32
     )
-    counts = jnp.sum(onehot_own.astype(jnp.float32), axis=0)
     span = num_codes // n_ctx
-    cache_v, cache_c = code_prefix(sums, counts, span, n_ctx, head_dim)
+    cache_v = code_prefix(sums, span, n_ctx, head_dim)
     prev_ok = (jnp.arange(rows, dtype=jnp.int32) < BLK - reach[0]) & (g > 0)
     onehot_prev = (
         (prev_codes[:, None] == code_ids[None, :]) & prev_ok[:, None]
@@ -142,7 +145,6 @@
         onehot_prev, prev_kv[:, head_dim:], (((0,), (0,)), ((), ())),
         preferred_element_type=jnp.float32,
     )
-    cache_c = cache_c + jnp.sum(onehot_prev.astype(jnp.float32), axis=0)
 
     ext_kv = jnp.concatenate([prev_kv, key_vals], axis=0)
     top_e, numer_e, denom_e, coded = attend_exact(
@@ -160,36 +162,14 @@
     return reduce_out(attended, w_out, sizes)
 
 
-def _pack(sums, counts, span, n, head_dim):
-    hi = jnp.floor(counts / 64.0)
-    lo = counts - hi * 64.0
-    tail = jnp.zeros((n, 8, head_dim), jnp.float32)
-    tail = tail.at[:, 0, :span].set(hi.reshape(n, span)).at[:, 1, :span].set(lo.reshape(n, span))
-    return jnp.concatenate([sums.reshape(n, span, head_dim), tail], axis=1).astype(jnp.bfloat16)
-
-
-def _unpack(blob, span):
-    blob = blob.astype(jnp.float32)
-    sums = blob[:, :span]
-    counts = blob[:, span, :span] * 64.0 + blob[:, span + 1, :span]
-    return sums, counts
-
-
-def code_prefix(sums, counts, span, n, head_dim):
-    got = lax.all_to_all(_pack(sums, counts, span, n, head_dim), "ctx", 0, 0, tiled=True)
-    block_sums, block_counts = _unpack(got, span)
+def code_prefix(sums, span, n, head_dim):
+    blob = sums.reshape(n, span, head_dim).astype(jnp.bfloat16)
+    got = lax.all_to_all(blob, "ctx", 0, 0, tiled=True)
     b = jnp.arange(n, dtype=jnp.int32)
     before = (b[None, :] <= b[:, None] - 2).astype(jnp.bfloat16)
-    pre_sums = jnp.einsum(
-        "bc,cxd->bxd", before, block_sums.astype(jnp.bfloat16), preferred_element_type=jnp.float32
-    )
-    pre_counts = jnp.dot(
-        before, block_counts.astype(jnp.bfloat16), preferred_element_type=jnp.float32
-    )
-    back = lax.all_to_all(_pack(pre_sums, pre_counts, span, n, head_dim), "ctx", 0, 0, tiled=True)
-    cache_v, cache_c = _unpack(back, span)
-    return cache_v.reshape(n * span, head_dim), cache_c.reshape(n * span)
-
+    pre_sums = jnp.einsum("bc,cxd->bxd", before, got, preferred_element_type=jnp.float32)
+    back = lax.all_to_all(pre_sums.astype(jnp.bfloat16), "ctx", 0, 0, tiled=True)
+    return back.astype(jnp.float32).reshape(n * span, head_dim)
 
 def project(tokens_in, w_qkv, sizes):
     nx, ny, nc = sizes

time: 126 us -> 140 us (1.11)
  waiting for transfers between devices: 33.9 us -> 42.1 us
  starting transfers between devices: 43.3 us -> 48.6 us
  matrix products: 13.3 us -> 17.5 us
  other arithmetic: 6.98 us -> 5.12 us
  local copies, waits for them, and re-layouts: 5.99 us -> 4.26 us
    all_to_all x2 -> x3, starting transfers between devices: 19.9 us -> 26.5 us  [the longest x1 12.4 us: on_device(): lax.all_to_all(jnp.broadcast_to(code_row[None], (n_ctx, rows)), 'ctx', 0,...]
    all_to_all x2 -> x3, waiting for transfers between devices: 14.4 us -> 20.2 us  [the longest x1 9.06 us: on_device(): lax.all_to_all(jnp.broadcast_to(code_row[None], (n_ctx, rows)), 'ctx', 0,...]
    ppermute x1, waiting for transfers between devices: 0.01 us -> 2.91 us  [on_device(): prev_kv = lax.ppermute(key_vals, 'ctx', route)]
    concatenate x3 -> x0, other arithmetic: 1.48 us -> none  [the longest x1 0.77 us: on_device(): jnp.concatenate([key_vals, code_rows, jnp.zeros((14, kvw), jnp.bfloat16)]...]
  transfers between devices with their start and end apart: 6 -> 7, of which waited for: 4 -> 6; matrix products, arithmetic and copies ran while one was open for 7% -> 7% of each run, Pallas kernels for 0% -> 0%
where the time goes in v8:
time: 140 us; the launch traced here: 139 us
  starting transfers between devices  48.6 us (35%)
  waiting for transfers between devices  42.1 us (30%)
  blocking collectives  20.7 us (15%)
  matrix products  17.5 us (12%)
  other arithmetic  5.12 us (4%)
  local copies, waits for them, and re-layouts  4.26 us (3%)
    all_to_all x1, blocking collectives, reduce_out(): lax.all_to_all(chunks, HEAD_AXES, 0, 0, tiled=True).astype(jnp.float32)  20.7 us
    all_to_all x1, waiting for transfers between devices, project(): mine = lax.all_to_all(spread, HEAD_AXES, 0, 0, tiled=True)  16.4 us
    all_to_all x1, starting transfers between devices, on_device(): lax.all_to_all(jnp.broadcast_to(code_row[None], (n_ctx, rows)), 'ctx', 0,...  12.4 us
    all_to_all x1, starting transfers between devices, project(): mine = lax.all_to_all(spread, HEAD_AXES, 0, 0, tiled=True)  11.1 us
    all_to_all x1, starting transfers between devices, code_prefix(): lax.all_to_all(pre_sums.astype(jnp.bfloat16), 'ctx', 0, 0, tiled=True)  10.7 us
    all_to_all x1, waiting for transfers between devices, on_device(): lax.all_to_all(jnp.broadcast_to(code_row[None], (n_ctx, rows)), 'ctx', 0,...  9.06 us
    all_to_all x1, waiting for transfers between devices, code_prefix(): lax.all_to_all(pre_sums.astype(jnp.bfloat16), 'ctx', 0, 0, tiled=True)  8.96 us
    ppermute x2, starting transfers between devices, _send(): return lax.ppermute(value, HEAD_AXES, perm)  7.77 us
  transfers between devices with their start and end apart: 7, of which 6 were waited for; matrix products, arithmetic and copies ran while one was open for 7% of the time, Pallas kernels for 0%

profile of v8, /device:TPU:1, one launch (start us, length us, event | category | flops | bytes accessed | tf_op | source)
XLA Modules:
  0.0 139.2 jit_solution(10603116775251472532)
XLA Ops:
  0.0 0.0 copy-start
  0.0 0.0 copy-start.4
  0.0 2.3 %broadcast_in_dim.22 = bf16[16,2,128,128]{3,2,1,0:T(8,128)(2,1)} broadcast(bf16[2,128,128]{2,1,0:T(8,128)(2,1)} %bitcast.57), dimensions={1,2,3} | broadcast | bytes 1114112 | tf_op jit(solution)/shard_map/broadcast_in_dim | solution.py:181
  2.3 11.1 %all-to-all-start = ((bf16[32,128,128]{2,1,0:T(8,128)(2,1)}), bf16[32,128,128]{2,1,0:T(8,128)(2,1)}, u32[]{:S(2)}, u32[]{:S(2)}) async-start(bf16[32,128,128]{2,1,0:T(8,128)(2,1)} %bitcast.53), calls=%async_computation | async-start | bytes 2097152 | tf_op jit(solution)/shard_map/all_to_all | solution.py:184
  14.1 16.4 %all-to-all-done = bf16[32,128,128]{2,1,0:T(8,128)(2,1)} async-done(((bf16[32,128,128]{2,1,0:T(8,128)(2,1)}), bf16[32,128,128]{2,1,0:T(8,128)(2,1)}, u32[]{:S(2)}, u32[]{:S(2)}) %all-to-all-start) | async-done | bytes 1048608 | tf_op jit(solution)/shard_map/all_to_all | solution.py:184
  30.4 0.0 copy-done.4
  30.4 0.6 broadcast_in_dim.28
  31.1 12.4 %all-to-all-start.1 = ((s32[16,1,256]{2,1,0:T(1,128)}), s32[16,1,256]{2,1,0:T(1,128)S(1)}, u32[]{:S(2)}, u32[]{:S(2)}) async-start(s32[16,1,256]{2,1,0:T(1,128)} %broadcast_in_dim.28), calls=%async_computation.1 | async-start | bytes 32768 | tf_op jit(solution)/shard_map/all_to_all | solution.py:113
  43.4 2.3 %collective-permute-start = (bf16[32,128,128]{2,1,0:T(8,128)(2,1)}, bf16[32,128,128]{2,1,0:T(8,128)(2,1)}, u32[]{:S(2)}, u32[]{:S(2)}) collective-permute-start(bf16[32,128,128]{2,1,0:T(8,128)(2,1)} %all-to-all-done), channel_id=1, source_target_pairs={{0,1},{1,0},{2,3},{3,2},{4,5},{5,4},{6,7},{7,6},{8,9},{9,8},{10,11... | collective-permute-start | bytes 3145736 | tf_op jit(solution)/shard_map/ppermute | solution.py:41
  45.8 9.1 %all-to-all-done.1 = s32[16,1,256]{2,1,0:T(1,128)S(1)} async-done(((s32[16,1,256]{2,1,0:T(1,128)}), s32[16,1,256]{2,1,0:T(1,128)S(1)}, u32[]{:S(2)}, u32[]{:S(2)}) %all-to-all-start.1) | async-done | bytes 16416 | tf_op jit(solution)/shard_map/all_to_all | solution.py:113
  54.9 1.7 %convert_reduce_fusion = f32[512]{0:T(512)S(1)} fusion(s32[16,256]{1,0:T(8,128)S(1)} %bitcast.58, pred[16,256]{1,0:T(8,128)(4,1)S(1)} %add_compare_fusion), kind=kLoop, calls=%fused_computation | loop fusion | flops 8388096 | bytes 22528 | tf_op jit(solution)/shard_map/reduce_sum | solution.py:118
  56.6 0.0 copy-done
  56.6 1.9 %convolution_bitcast_fusion.1 = bf16[128,384]{1,0:T(8,128)(2,1)S(1)} fusion(bf16[32,128,128]{2,1,0:T(8,128)(2,1)} %all-to-all-done, bf16[32,128,384]{2,1,0:T(8,128)(2,1)S(1)} %bitcast.51), kind=kOutput, calls=%fused_computation.11 | convolution fusion | flops 402653184 | bytes 4292608 | tf_op jit(solution)/shard_map/dot_general | solution.py:188
  58.6 0.0 collective-permute-done
  58.6 1.9 %convolution_bitcast_fusion = bf16[128,384]{1,0:T(8,128)(2,1)S(1)} fusion(bf16[32,128,128]{2,1,0:T(8,128)(2,1)} %collective-permute-done, bf16[32,128,384]{2,1,0:T(8,128)(2,1)S(1)} %bitcast.52), kind=kOutput, calls=%fused_computation.10 | convolution fusion | flops 402653184 | bytes 4292608 | tf_op jit(solution)/shard_map/dot_general | solution.py:189
  60.6 1.1 convolution_convert_fusion.2
  61.6 3.5 %all-to-all-start.2 = ((bf16[16,32,128]{2,1,0:T(8,128)(2,1)}), bf16[16,32,128]{2,1,0:T(8,128)(2,1)S(1)}, u32[]{:S(2)}, u32[]{:S(2)}) async-start(bf16[16,32,128]{2,1,0:T(8,128)(2,1)} %bitcast.55), calls=%async_computation.2 | async-start | bytes 262144 | tf_op jit(solution)/shard_map/all_to_all | solution.py:167
  65.2 0.0 copy-start.2
  65.2 3.1 %collective-permute-start.1 = (bf16[256,256]{1,0:T(8,128)(2,1)S(1)}, bf16[256,256]{1,0:T(8,128)(2,1)S(1)}, u32[]{:S(2)}, u32[]{:S(2)}) collective-permute-start(bf16[256,256]{1,0:T(8,128)(2,1)S(1)} %slice.38), channel_id=1, source_target_pairs={{0,32},{32,64},{64,96},{96,128},{128,160},{160,192},{192,224},{224... | collective-permute-start | bytes 393224 | tf_op jit(solution)/shard_map/ppermute | solution.py:131
  68.4 1.9 %select_reduce_fusion = (f32[256]{0:T(256)S(1)}, f32[256,512]{1,0:T(8,128)}) fusion(pred[512]{0:T(512)(128)(4,1)S(1)} %broadcast_compare_fusion, bf16[1,512,128]{2,1,0:T(8,128)(2,1)} %param.9, bf16[256,384]{1,0:T(8,128)(2,1)S(1)} %fusion.18), kind=kOutput, calls=%fused_computation.26 | convolution fusion | flops 33947392 | bytes 722432 | tf_op jit(solution)/shard_map/dot_general | solution.py:73
  70.3 2.9 %collective-permute-done.1 = bf16[256,256]{1,0:T(8,128)(2,1)S(1)} collective-permute-done((bf16[256,256]{1,0:T(8,128)(2,1)S(1)}, bf16[256,256]{1,0:T(8,128)(2,1)S(1)}, u32[]{:S(2)}, u32[]{:S(2)}) %collective-permute-start.1) | collective-permute-done | bytes 131104 | tf_op jit(solution)/shard_map/ppermute | solution.py:131
  73.2 0.0 copy-start.5
  73.2 0.0 copy-done.2
  73.2 0.6 copy-done.5
  73.8 1.0 select_reduce_fusion.1
  74.9 0.0 copy-start.3
  74.9 2.2 %all-to-all-done.2 = bf16[16,32,128]{2,1,0:T(8,128)(2,1)S(1)} async-done(((bf16[16,32,128]{2,1,0:T(8,128)(2,1)}), bf16[16,32,128]{2,1,0:T(8,128)(2,1)S(1)}, u32[]{:S(2)}, u32[]{:S(2)}) %all-to-all-start.2) | async-done | bytes 131104 | tf_op jit(solution)/shard_map/all_to_all | solution.py:167
  77.1 0.2 convolution_convert_fusion.1
  77.3 0.7 copy.15
  78.0 10.7 %all-to-all-start.3 = ((bf16[16,32,128]{2,1,0:T(8,128)(2,1)}), bf16[16,32,128]{2,1,0:T(8,128)(2,1)S(1)}, u32[]{:S(2)}, u32[]{:S(2)}) async-start(bf16[16,32,128]{2,1,0:T(8,128)(2,1)} %copy.15), calls=%async_computation.3 | async-start | bytes 262144 | tf_op jit(solution)/shard_map/all_to_all | solution.py:171
  88.7 1.3 fusion.19
  90.0 1.7 %fusion.16 = f32[1,256]{1,0:T(1,128)S(1)} fusion(f32[512,1]{0,1:T(1,128)S(1)} %bitcast.59, f32[256,512]{1,0:T(8,128)} %get-tuple-element.12, f32[256]{0:T(256)S(1)} %max.13, pred[512]{0:T(512)(128)(4,1)S(1)} %broadcast_compare_fusion), kind=kOutput, calls=%fused_computation.32 | convolution fusion | flops 1835008 | bytes 528896 | tf_op jit(solution)/shard_map/dot_general | solution.py:94
  91.7 9.0 %all-to-all-done.3 = bf16[16,32,128]{2,1,0:T(8,128)(2,1)S(1)} async-done(((bf16[16,32,128]{2,1,0:T(8,128)(2,1)}), bf16[16,32,128]{2,1,0:T(8,128)(2,1)S(1)}, u32[]{:S(2)}, u32[]{:S(2)}) %all-to-all-start.3) | async-done | bytes 131104 | tf_op jit(solution)/shard_map/all_to_all | solution.py:171
  100.7 0.0 copy-start.1
  100.7 1.4 convolution_add_fusion
  102.0 1.7 %fusion.17 = f32[256,128]{1,0:T(8,128)S(1)} fusion(f32[512,128]{1,0:T(8,128)S(1)} %convolution_add_fusion, f32[256,512]{1,0:T(8,128)} %get-tuple-element.12, f32[256]{0:T(256)S(1)} %max.13, pred[512]{0:T(512)(128)(4,1)S(1)} %broadcast_compare_fusion), kind=kOutput, calls=%fused_computation.33 | convolution fusion | flops 201588736 | bytes 919040 | tf_op jit(solution)/shard_map/dot_general | solution.py:93
  103.7 0.0 copy-done.3
  103.8 1.4 fusion.3
  105.1 0.0 copy-done.1
  105.1 1.4 %convolution_convert_fusion = bf16[256,2048]{1,0:T(8,128)(2,1)} fusion(bf16[256,128]{1,0:T(8,128)(2,1)S(1)} %fusion.3, bf16[1,128,4096]{2,1,0:T(8,128)(2,1)S(1)} %copy-done.1, s32[]{:T(128)S(6)} %select_n.37), kind=kOutput, calls=%fused_computation.3 | convolution fusion | flops 134742016 | bytes 1638404 | tf_op jit(solution)/shard_map/dot_general | solution.py:208
  106.5 5.4 %collective-permute-start.2 = (bf16[256,2048]{1,0:T(8,128)(2,1)}, bf16[256,2048]{1,0:T(8,128)(2,1)}, u32[]{:S(2)}, u32[]{:S(2)}) collective-permute-start(bf16[256,2048]{1,0:T(8,128)(2,1)} %convolution_convert_fusion), channel_id=1, source_target_pairs={{0,1},{1,0},{2,3},{3,2},{4,5},{5,4},{6,7},{7,6},{8,9},{9,8},{10,11... | collective-permute-start | bytes 3145736 | tf_op jit(solution)/shard_map/ppermute | solution.py:41
  112.0 2.6 %collective-permute-done.2 = bf16[256,2048]{1,0:T(8,128)(2,1)} collective-permute-done((bf16[256,2048]{1,0:T(8,128)(2,1)}, bf16[256,2048]{1,0:T(8,128)(2,1)}, u32[]{:S(2)}, u32[]{:S(2)}) %collective-permute-start.2) | collective-permute-done | bytes 1048608 | tf_op jit(solution)/shard_map/ppermute | solution.py:41
  114.6 1.8 %fusion.4 = bf16[32,8,2048]{2,1,0:T(8,128)(2,1)S(1)} fusion(bf16[256,2048]{1,0:T(8,128)(2,1)} %collective-permute-done.2, bf16[256,128]{1,0:T(8,128)(2,1)S(1)} %fusion.3, bf16[1,128,4096]{2,1,0:T(8,128)(2,1)} %param.8, s32[]{:T(128)S(6)} %select_n.36), kind=kOutput, calls=%fused_computation.16 | convolution fusion | flops 135790592 | bytes 2686980 | tf_op jit(solution)/shard_map/dot_general | solution.py:207
  116.4 20.7 %all_to_all.26 = bf16[32,8,2048]{2,1,0:T(8,128)(2,1)} all-to-all(bf16[32,8,2048]{2,1,0:T(8,128)(2,1)S(1)} %fusion.4), channel_id=1, replica_groups=mesh['ctx'=16,'hx'=4,'hy'=4,'hc'=2] {'hx','hy','hc'}, dimensions={0} | all-to-all | bytes 2097152 | tf_op jit(solution)/shard_map/all_to_all | solution.py:213
  137.1 1.4 reduce
  138.5 0.6 pad_maximum_fusion.2
  (13 shorter events, 0.1 us)
Async XLA Ops:
  0.0 56.6 %copy-start = (bf16[4096,1,384]{2,0,1:T(8,128)(2,1)S(1)}, bf16[4096,1,384]{2,0,1:T(8,128)(2,1)}, u32[]{:S(2)}) copy-start(bf16[4096,1,384]{2,0,1:T(8,128)(2,1)} %param.7) | copy-start | bytes 9437188
  0.0 30.4 %copy-start.4 = (s32[1,256]{1,0:T(1,128)S(1)}, s32[1,256]{1,0:T(1,128)}, u32[]{:S(2)}) copy-start(s32[1,256]{1,0:T(1,128)} %param.10) | copy-start | bytes 3076
  2.3 28.2 %all-to-all-start = ((bf16[32,128,128]{2,1,0:T(8,128)(2,1)}), bf16[32,128,128]{2,1,0:T(8,128)(2,1)}, u32[]{:S(2)}, u32[]{:S(2)}) async-start(bf16[32,128,128]{2,1,0:T(8,128)(2,1)} %bitcast.53), calls=%async_computation | async-start | bytes 2097152 | tf_op jit(solution)/shard_map/all_to_all | solution.py:184
  31.1 23.8 %all-to-all-start.1 = ((s32[16,1,256]{2,1,0:T(1,128)}), s32[16,1,256]{2,1,0:T(1,128)S(1)}, u32[]{:S(2)}, u32[]{:S(2)}) async-start(s32[16,1,256]{2,1,0:T(1,128)} %broadcast_in_dim.28), calls=%async_computation.1 | async-start | bytes 32768 | tf_op jit(solution)/shard_map/all_to_all | solution.py:113
  43.4 15.1 %collective-permute-start = (bf16[32,128,128]{2,1,0:T(8,128)(2,1)}, bf16[32,128,128]{2,1,0:T(8,128)(2,1)}, u32[]{:S(2)}, u32[]{:S(2)}) collective-permute-start(bf16[32,128,128]{2,1,0:T(8,128)(2,1)} %all-to-all-done), channel_id=1, source_target_pairs={{0,1},{1,0},{2,3},{3,2},{4,5},{5,4},{6,7},{7,6},{8,9},{9,8},{10,11... | collective-permute-start | bytes 3145736 | tf_op jit(solution)/shard_map/ppermute | solution.py:41
  61.6 15.5 %all-to-all-start.2 = ((bf16[16,32,128]{2,1,0:T(8,128)(2,1)}), bf16[16,32,128]{2,1,0:T(8,128)(2,1)S(1)}, u32[]{:S(2)}, u32[]{:S(2)}) async-start(bf16[16,32,128]{2,1,0:T(8,128)(2,1)} %bitcast.55), calls=%async_computation.2 | async-start | bytes 262144 | tf_op jit(solution)/shard_map/all_to_all | solution.py:167
  65.2 8.0 %copy-start.2 = (bf16[256,256]{1,0:T(8,128)(2,1)}, bf16[256,256]{1,0:T(8,128)(2,1)S(1)}, u32[]{:S(2)}) copy-start(bf16[256,256]{1,0:T(8,128)(2,1)S(1)} %slice.38) | copy-start | bytes 393220
  65.2 8.0 %collective-permute-start.1 = (bf16[256,256]{1,0:T(8,128)(2,1)S(1)}, bf16[256,256]{1,0:T(8,128)(2,1)S(1)}, u32[]{:S(2)}, u32[]{:S(2)}) collective-permute-start(bf16[256,256]{1,0:T(8,128)(2,1)S(1)} %slice.38), channel_id=1, source_target_pairs={{0,32},{32,64},{64,96},{96,128},{128,160},{160,192},{192,224},{224... | collective-permute-start | bytes 393224 | tf_op jit(solution)/shard_map/ppermute | solution.py:131
  73.2 0.6 copy-start.5
  74.9 28.9 %copy-start.3 = (bf16[256,256]{1,0:T(8,128)(2,1)S(1)}, bf16[256,256]{1,0:T(8,128)(2,1)}, u32[]{:S(2)}) copy-start(bf16[256,256]{1,0:T(8,128)(2,1)} %copy-done.2) | copy-start | bytes 393220
  78.0 22.6 %all-to-all-start.3 = ((bf16[16,32,128]{2,1,0:T(8,128)(2,1)}), bf16[16,32,128]{2,1,0:T(8,128)(2,1)S(1)}, u32[]{:S(2)}, u32[]{:S(2)}) async-start(bf16[16,32,128]{2,1,0:T(8,128)(2,1)} %copy.15), calls=%async_computation.3 | async-start | bytes 262144 | tf_op jit(solution)/shard_map/all_to_all | solution.py:171
  100.7 4.5 %copy-start.1 = (bf16[1,128,4096]{2,1,0:T(8,128)(2,1)S(1)}, bf16[1,128,4096]{2,1,0:T(8,128)(2,1)}, u32[]{:S(2)}) copy-start(bf16[1,128,4096]{2,1,0:T(8,128)(2,1)} %param.8) | copy-start | bytes 3145732
  106.5 8.0 %collective-permute-start.2 = (bf16[256,2048]{1,0:T(8,128)(2,1)}, bf16[256,2048]{1,0:T(8,128)(2,1)}, u32[]{:S(2)}, u32[]{:S(2)}) collective-permute-start(bf16[256,2048]{1,0:T(8,128)(2,1)} %convolution_convert_fusion), channel_id=1, source_target_pairs={{0,1},{1,0},{2,3},{3,2},{4,5},{5,4},{6,7},{7,6},{8,9},{9,8},{10,11... | collective-permute-start | bytes 3145736 | tf_op jit(solution)/shard_map/ppermute | solution.py:41

commit v9 on v6

--- a/solution.py
+++ b/solution.py
@@ -177,19 +177,17 @@
 
 def code_prefix(sums, counts, span, n, head_dim):
     got = lax.all_to_all(_pack(sums, counts, span, n, head_dim), "ctx", 0, 0, tiled=True)
-    block_sums, block_counts = _unpack(got, span)
     b = jnp.arange(n, dtype=jnp.int32)
     before = (b[None, :] <= b[:, None] - 2).astype(jnp.bfloat16)
-    pre_sums = jnp.einsum(
-        "bc,cxd->bxd", before, block_sums.astype(jnp.bfloat16), preferred_element_type=jnp.float32
-    )
-    pre_counts = jnp.dot(
-        before, block_counts.astype(jnp.bfloat16), preferred_element_type=jnp.float32
-    )
-    back = lax.all_to_all(_pack(pre_sums, pre_counts, span, n, head_dim), "ctx", 0, 0, tiled=True)
+    pre = jnp.einsum("bc,cxd->bxd", before, got, preferred_element_type=jnp.float32)
+    total = pre[:, span] * 64.0 + pre[:, span + 1]
+    hi = jnp.floor(total / 64.0)
+    lo = total - hi * 64.0
+    rows = lax.broadcasted_iota(jnp.int32, pre.shape, 1)
+    pre = jnp.where(rows == span, hi[:, None, :], jnp.where(rows == span + 1, lo[:, None, :], pre))
+    back = lax.all_to_all(pre.astype(jnp.bfloat16), "ctx", 0, 0, tiled=True)
     cache_v, cache_c = _unpack(back, span)
     return cache_v.reshape(n * span, head_dim), cache_c.reshape(n * span)
-
 
 def project(tokens_in, w_qkv, sizes):
     nx, ny, nc = sizes
@@ -199,14 +197,14 @@
     rows, width = tokens_in.shape
     half = rows // nc
     spread = jnp.broadcast_to(
-        tokens_in.reshape(1, nc, half, width), (n_head // nc, nc, half, width)
-    ).reshape(n_head, half, width)
-    mine = lax.all_to_all(spread, HEAD_AXES, 0, 0, tiled=True)
+        tokens_in.reshape(nc, half, width).transpose(1, 0, 2)[:, None],
+        (half, n_head // nc, nc, width),
+    ).reshape(half, n_head, width)
+    mine = lax.all_to_all(spread, HEAD_AXES, 1, 1, tiled=True).reshape(half, n_head * width)
     theirs = _send(mine, core_perm)
-    w_local = w_qkv[:, 0, :].reshape(n_head, width, -1)
-    dims = (((0, 2), (0, 1)), ((), ()))
-    proj_own = lax.dot_general(mine, w_local, dims, preferred_element_type=jnp.float32)
-    proj_oth = lax.dot_general(theirs, w_local, dims, preferred_element_type=jnp.float32)
+    w_local = w_qkv[:, 0, :]
+    proj_own = jnp.dot(mine, w_local, preferred_element_type=jnp.float32)
+    proj_oth = jnp.dot(theirs, w_local, preferred_element_type=jnp.float32)
     projected = jnp.where(
         me_c == 0,
         jnp.concatenate([proj_own, proj_oth], axis=0),

time: 126 us -> 127 us (level)
  local copies, waits for them, and re-layouts: 5.99 us -> 8.14 us
  other arithmetic: 6.98 us -> 5.15 us
    all_to_all x0 -> x1, local copies, waits for them, and re-layouts: none -> 2.29 us  [project(): lax.all_to_all(spread, HEAD_AXES, 1, 1, tiled=True)]
    dot_general x4 -> x3, matrix products: 4.3 us -> 4.18 us  [the longest x1 1.97 us: project(): proj_oth = jnp.dot(theirs, w_local, preferred_element_type=jnp.float32)]
  transfers between devices with their start and end apart: 6 -> 6, of which waited for: 4 -> 4; matrix products, arithmetic and copies ran while one was open for 7% -> 6% of each run, Pallas kernels for 0% -> 0%
where the time goes in v9:
time: 127 us; the launch traced here: 126 us
  starting transfers between devices  43.3 us (34%)
  waiting for transfers between devices  34.6 us (27%)
  blocking collectives  21.1 us (17%)
  matrix products  13.2 us (10%)
  local copies, waits for them, and re-layouts  8.14 us (6%)
  other arithmetic  5.15 us (4%)
    all_to_all x1, blocking collectives, reduce_out(): lax.all_to_all(chunks, HEAD_AXES, 0, 0, tiled=True).astype(jnp.float32)  21.1 us
    all_to_all x1, waiting for transfers between devices, project(): lax.all_to_all(spread, HEAD_AXES, 1, 1, tiled=True)  16.8 us
    all_to_all x1, starting transfers between devices, code_prefix(): lax.all_to_all(_pack(sums, counts, span, n, head_dim), 'ctx', 0, 0, tiled...  12.3 us
    all_to_all x1, starting transfers between devices, project(): lax.all_to_all(spread, HEAD_AXES, 1, 1, tiled=True)  11.1 us
    ppermute x2, starting transfers between devices, _send(): return lax.ppermute(value, HEAD_AXES, perm)  8.3 us
    all_to_all x1, waiting for transfers between devices, code_prefix(): back = lax.all_to_all(pre.astype(jnp.bfloat16), 'ctx', 0, 0, tiled=True)  7.6 us
    all_to_all x1, starting transfers between devices, code_prefix(): back = lax.all_to_all(pre.astype(jnp.bfloat16), 'ctx', 0, 0, tiled=True)  7.6 us
    all_to_all x1, waiting for transfers between devices, code_prefix(): lax.all_to_all(_pack(sums, counts, span, n, head_dim), 'ctx', 0, 0, tiled...  7.56 us
  transfers between devices with their start and end apart: 6, of which 4 were waited for; matrix products, arithmetic and copies ran while one was open for 6% of the time, Pallas kernels for 0%

profile of v9, /device:TPU:1, one launch (start us, length us, event | category | flops | bytes accessed | tf_op | source)
XLA Modules:
  0.0 126.5 jit_solution(7735579804155001758)
XLA Ops:
  0.0 0.0 copy-start
  0.0 0.0 copy-start.8
  0.0 2.3 %broadcast_in_dim.60 = bf16[128,16,2,128]{3,0,2,1:T(8,128)(2,1)} broadcast(bf16[128,2,128]{2,0,1:T(8,128)(2,1)} %bitcast.56), dimensions={0,2,3} | broadcast | bytes 1114112 | tf_op jit(solution)/shard_map/broadcast_in_dim | solution.py:199
  2.3 11.1 %all-to-all-start = ((bf16[128,32,128]{2,0,1:T(8,128)(2,1)}), bf16[128,32,128]{2,0,1:T(8,128)(2,1)}, u32[]{:S(2)}, u32[]{:S(2)}) async-start(bf16[128,32,128]{2,0,1:T(8,128)(2,1)} %bitcast.50), calls=%async_computation | async-start | bytes 2097152 | tf_op jit(solution)/shard_map/all_to_all | solution.py:203
  13.4 0.0 copy-done.8
  13.4 0.1 convert_reduce_fusion.1
  13.6 0.1 reduce_sum.39
  13.6 16.8 %all-to-all-done = bf16[128,32,128]{2,0,1:T(8,128)(2,1)} async-done(((bf16[128,32,128]{2,0,1:T(8,128)(2,1)}), bf16[128,32,128]{2,0,1:T(8,128)(2,1)}, u32[]{:S(2)}, u32[]{:S(2)}) %all-to-all-start) | async-done | bytes 1048608 | tf_op jit(solution)/shard_map/all_to_all | solution.py:203
  30.5 2.3 %copy.17 = bf16[128,32,128]{0,2,1:T(8,128)(2,1)} copy(bf16[128,32,128]{2,0,1:T(8,128)(2,1)} %all-to-all-done) | data formatting | bytes 2097152 | tf_op jit(solution)/shard_map/all_to_all | solution.py:203
  32.8 2.0 %collective-permute-start = (bf16[128,4096]{0,1:T(8,128)(2,1)}, bf16[128,4096]{0,1:T(8,128)(2,1)}, u32[]{:S(2)}, u32[]{:S(2)}) collective-permute-start(bf16[128,4096]{0,1:T(8,128)(2,1)} %bitcast.52), channel_id=1, source_target_pairs={{0,1},{1,0},{2,3},{3,2},{4,5},{5,4},{6,7},{7,6},{8,9},{9,8},{10,11... | collective-permute-start | bytes 3145736 | tf_op jit(solution)/shard_map/ppermute | solution.py:41
  35.5 0.4 scatter.9
  35.9 0.0 copy-done
  35.9 2.0 %fusion.2 = bf16[128,384]{1,0:T(8,128)(2,1)S(1)} fusion(bf16[128,4096]{0,1:T(8,128)(2,1)} %bitcast.53, bf16[4096,1,384]{2,0,1:T(8,128)(2,1)S(1)} %copy-done), kind=kOutput, calls=%fused_computation.2 | convolution fusion | flops 402653184 | bytes 4292608 | tf_op jit(solution)/shard_map/dot_general | solution.py:206
  37.9 0.0 collective-permute-done
  37.9 2.0 %fusion = bf16[128,384]{1,0:T(8,128)(2,1)S(1)} fusion(bf16[128,4096]{0,1:T(8,128)(2,1)} %collective-permute-done, bf16[4096,1,384]{2,0,1:T(8,128)(2,1)S(1)} %copy-done), kind=kOutput, calls=%fused_computation | convolution fusion | flops 402653184 | bytes 4292608 | tf_op jit(solution)/shard_map/dot_general | solution.py:207
  40.0 0.4 convolution_convert_fusion.1
  40.4 0.7 pad_maximum_fusion
  41.1 12.3 %all-to-all-start.1 = ((bf16[16,40,128]{2,1,0:T(8,128)(2,1)}), bf16[16,40,128]{2,1,0:T(8,128)(2,1)S(1)}, u32[]{:S(2)}, u32[]{:S(2)}) async-start(bf16[16,40,128]{2,1,0:T(8,128)(2,1)} %pad_maximum_fusion), calls=%async_computation.1 | async-start | bytes 327680 | tf_op jit(solution)/shard_map/all_to_all | solution.py:179
  53.4 0.1 pad.18.clone
  53.6 0.0 copy-start.4
  53.6 0.8 maximum_maximum_fusion
  54.3 0.0 copy-done.4
  54.3 3.9 %collective-permute-start.1 = (bf16[272,256]{1,0:T(8,128)(2,1)}, bf16[272,256]{1,0:T(8,128)(2,1)}, u32[]{:S(2)}, u32[]{:S(2)}) collective-permute-start(bf16[272,256]{1,0:T(8,128)(2,1)} %maximum_maximum_fusion), channel_id=1, source_target_pairs={{0,32},{32,64},{64,96},{96,128},{128,160},{160,192},{192,224},{224... | collective-permute-start | bytes 417800 | tf_op jit(solution)/shard_map/ppermute | solution.py:124
  58.3 7.6 %all-to-all-done.1 = bf16[16,40,128]{2,1,0:T(8,128)(2,1)S(1)} async-done(((bf16[16,40,128]{2,1,0:T(8,128)(2,1)}), bf16[16,40,128]{2,1,0:T(8,128)(2,1)S(1)}, u32[]{:S(2)}, u32[]{:S(2)}) %all-to-all-start.1) | async-done | bytes 163872 | tf_op jit(solution)/shard_map/all_to_all | solution.py:179
  65.8 0.2 fusion.41
  66.1 0.2 select_convert_fusion
  66.2 0.7 copy.19
  66.9 7.6 %all-to-all-start.2 = ((bf16[16,40,128]{2,1,0:T(8,128)(2,1)}), bf16[16,40,128]{2,1,0:T(8,128)(2,1)S(1)}, u32[]{:S(2)}, u32[]{:S(2)}) async-start(bf16[16,40,128]{2,1,0:T(8,128)(2,1)} %copy.19), calls=%async_computation.2 | async-start | bytes 327680 | tf_op jit(solution)/shard_map/all_to_all | solution.py:188
  74.5 0.0 collective-permute-done.1
  74.6 0.8 fusion.59
  75.3 0.9 slice.121
  76.2 0.0 copy-start.6
  76.2 0.2 convert_reduce_fusion
  76.4 0.5 copy-done.6
  76.9 1.2 select_reduce_fusion.1
  78.0 0.0 copy-start.2
  78.1 0.8 copy-done.2
  78.8 0.3 fusion.24
  79.1 7.6 %all-to-all-done.2 = bf16[16,40,128]{2,1,0:T(8,128)(2,1)S(1)} async-done(((bf16[16,40,128]{2,1,0:T(8,128)(2,1)}), bf16[16,40,128]{2,1,0:T(8,128)(2,1)S(1)}, u32[]{:S(2)}, u32[]{:S(2)}) %all-to-all-start.2) | async-done | bytes 163872 | tf_op jit(solution)/shard_map/all_to_all | solution.py:188
  86.8 0.1 add.76
  86.9 0.0 copy-start.3
  86.9 0.0 copy-start.5
  86.9 0.0 copy-start.7
  86.9 0.0 copy-start.1
  86.9 1.3 %select_reduce_fusion = (f32[256]{0:T(256)S(1)}, f32[256,512]{1,0:T(8,128)S(1)}) fusion(pred[512]{0:T(512)(128)(4,1)S(1)} %get-tuple-element.31, bf16[1,512,128]{2,1,0:T(8,128)(2,1)} %param.13, bf16[256,384]{1,0:T(8,128)(2,1)S(1)} %fusion.23), kind=kOutput, calls=%fused_computation.22 | convolution fusion | flops 33947392 | bytes 722432 | tf_op jit(solution)/shard_map/dot_general | solution.py:73
  88.3 0.6 fusion.21
  88.9 1.3 %convolution_add_fusion = f32[512,128]{1,0:T(8,128)S(1)} fusion(f32[512,128]{1,0:T(8,128)S(1)} %bitcast.54, s32[256]{0:T(256)S(1)} %bitcast.58, pred[256]{0:T(512)(128)(4,1)S(1)} %compare_and_fusion, bf16[272,256]{1,0:T(8,128)(2,1)} %collective-permute-done.1), kind=kOutput, calls=%fused_computation.8 | convolution fusion | flops 33882112 | bytes 591104 | tf_op jit(solution)/shard_map/dot_general | solution.py:141
  90.2 0.6 fusion.22
  90.9 0.0 copy-done.3
  90.9 0.0 copy-done.5
  90.9 0.0 copy-done.7
  90.9 0.3 fusion.6
  91.3 0.0 copy-done.1
  91.3 1.4 %convolution_convert_fusion = bf16[256,2048]{1,0:T(8,128)(2,1)} fusion(bf16[256,128]{1,0:T(8,128)(2,1)S(1)} %fusion.6, bf16[1,128,4096]{2,1,0:T(8,128)(2,1)S(1)} %copy-done.1, s32[]{:T(128)S(6)} %select_n.60), kind=kOutput, calls=%fused_computation.4 | convolution fusion | flops 134742016 | bytes 1638404 | tf_op jit(solution)/shard_map/dot_general | solution.py:226
  92.7 6.3 %collective-permute-start.2 = (bf16[256,2048]{1,0:T(8,128)(2,1)}, bf16[256,2048]{1,0:T(8,128)(2,1)}, u32[]{:S(2)}, u32[]{:S(2)}) collective-permute-start(bf16[256,2048]{1,0:T(8,128)(2,1)} %convolution_convert_fusion), channel_id=1, source_target_pairs={{0,1},{1,0},{2,3},{3,2},{4,5},{5,4},{6,7},{7,6},{8,9},{9,8},{10,11... | collective-permute-start | bytes 3145736 | tf_op jit(solution)/shard_map/ppermute | solution.py:41
  99.0 2.6 %collective-permute-done.2 = bf16[256,2048]{1,0:T(8,128)(2,1)} collective-permute-done((bf16[256,2048]{1,0:T(8,128)(2,1)}, bf16[256,2048]{1,0:T(8,128)(2,1)}, u32[]{:S(2)}, u32[]{:S(2)}) %collective-permute-start.2) | collective-permute-done | bytes 1048608 | tf_op jit(solution)/shard_map/ppermute | solution.py:41
  101.6 1.8 %fusion.7 = bf16[32,8,2048]{2,1,0:T(8,128)(2,1)S(1)} fusion(bf16[256,2048]{1,0:T(8,128)(2,1)} %collective-permute-done.2, bf16[256,128]{1,0:T(8,128)(2,1)S(1)} %fusion.6, bf16[1,128,4096]{2,1,0:T(8,128)(2,1)} %param.12, s32[]{:T(128)S(6)} %select_n.59), kind=kOutput, calls=%fused_computation.14 | convolution fusion | flops 135790592 | bytes 2686980 | tf_op jit(solution)/shard_map/dot_general | solution.py:225
  103.4 21.1 %all_to_all.20 = bf16[32,8,2048]{2,1,0:T(8,128)(2,1)} all-to-all(bf16[32,8,2048]{2,1,0:T(8,128)(2,1)S(1)} %fusion.7), channel_id=1, replica_groups=mesh['ctx'=16,'hx'=4,'hy'=4,'hc'=2] {'hx','hy','hc'}, dimensions={0} | all-to-all | bytes 2097152 | tf_op jit(solution)/shard_map/all_to_all | solution.py:231
  124.5 1.4 %reduce.4 = bf16[2,8,2048]{2,1,0:T(8,128)(2,1)S(1)} reduce(bf16[16,2,8,2048]{3,2,1,0:T(8,128)(2,1)} %bitcast.51, bf16[]{:T(256)} %constant.126.clone.1), dimensions={0}, to_apply=%region_5.6.clone | reduce | flops 491520 | bytes 1114114 | tf_op jit(solution)/shard_map/reduce_sum | solution.py:232
  125.9 0.6 pad_maximum_fusion.3
  (21 shorter events, 0.3 us)
Async XLA Ops:
  0.0 35.9 %copy-start = (bf16[4096,1,384]{2,0,1:T(8,128)(2,1)S(1)}, bf16[4096,1,384]{2,0,1:T(8,128)(2,1)}, u32[]{:S(2)}) copy-start(bf16[4096,1,384]{2,0,1:T(8,128)(2,1)} %param.11) | copy-start | bytes 9437188
  0.0 13.4 %copy-start.8 = (s32[1,256]{1,0:T(1,128)S(1)}, s32[1,256]{1,0:T(1,128)}, u32[]{:S(2)}) copy-start(s32[1,256]{1,0:T(1,128)} %param.14) | copy-start | bytes 3076
  2.3 28.2 %all-to-all-start = ((bf16[128,32,128]{2,0,1:T(8,128)(2,1)}), bf16[128,32,128]{2,0,1:T(8,128)(2,1)}, u32[]{:S(2)}, u32[]{:S(2)}) async-start(bf16[128,32,128]{2,0,1:T(8,128)(2,1)} %bitcast.50), calls=%async_computation | async-start | bytes 2097152 | tf_op jit(solution)/shard_map/all_to_all | solution.py:203
  32.8 5.2 %collective-permute-start = (bf16[128,4096]{0,1:T(8,128)(2,1)}, bf16[128,4096]{0,1:T(8,128)(2,1)}, u32[]{:S(2)}, u32[]{:S(2)}) collective-permute-start(bf16[128,4096]{0,1:T(8,128)(2,1)} %bitcast.52), channel_id=1, source_target_pairs={{0,1},{1,0},{2,3},{3,2},{4,5},{5,4},{6,7},{7,6},{8,9},{9,8},{10,11... | collective-permute-start | bytes 3145736 | tf_op jit(solution)/shard_map/ppermute | solution.py:41
  41.1 24.7 %all-to-all-start.1 = ((bf16[16,40,128]{2,1,0:T(8,128)(2,1)}), bf16[16,40,128]{2,1,0:T(8,128)(2,1)S(1)}, u32[]{:S(2)}, u32[]{:S(2)}) async-start(bf16[16,40,128]{2,1,0:T(8,128)(2,1)} %pad_maximum_fusion), calls=%async_computation.1 | async-start | bytes 327680 | tf_op jit(solution)/shard_map/all_to_all | solution.py:179
  53.6 0.8 copy-start.4
  54.3 20.2 %collective-permute-start.1 = (bf16[272,256]{1,0:T(8,128)(2,1)}, bf16[272,256]{1,0:T(8,128)(2,1)}, u32[]{:S(2)}, u32[]{:S(2)}) collective-permute-start(bf16[272,256]{1,0:T(8,128)(2,1)} %maximum_maximum_fusion), channel_id=1, source_target_pairs={{0,32},{32,64},{64,96},{96,128},{128,160},{160,192},{192,224},{224... | collective-permute-start | bytes 417800 | tf_op jit(solution)/shard_map/ppermute | solution.py:124
  66.9 19.8 %all-to-all-start.2 = ((bf16[16,40,128]{2,1,0:T(8,128)(2,1)}), bf16[16,40,128]{2,1,0:T(8,128)(2,1)S(1)}, u32[]{:S(2)}, u32[]{:S(2)}) async-start(bf16[16,40,128]{2,1,0:T(8,128)(2,1)} %copy.19), calls=%async_computation.2 | async-start | bytes 327680 | tf_op jit(solution)/shard_map/all_to_all | solution.py:188
  76.2 0.6 copy-start.6
  78.0 0.8 copy-start.2
  86.9 4.0 %copy-start.3 = (f32[256,512]{1,0:T(8,128)S(1)}, f32[256,512]{1,0:T(8,128)}, u32[]{:S(2)}) copy-start(f32[256,512]{1,0:T(8,128)} %copy-done.2) | copy-start | bytes 1572868
  86.9 4.0 %copy-start.5 = (bf16[256,256]{1,0:T(8,128)(2,1)S(1)}, bf16[256,256]{1,0:T(8,128)(2,1)}, u32[]{:S(2)}) copy-start(bf16[256,256]{1,0:T(8,128)(2,1)} %copy-done.4) | copy-start | bytes 393220
  86.9 4.0 %copy-start.7 = (bf16[256,256]{1,0:T(8,128)(2,1)S(1)}, bf16[256,256]{1,0:T(8,128)(2,1)}, u32[]{:S(2)}) copy-start(bf16[256,256]{1,0:T(8,128)(2,1)} %copy-done.6) | copy-start | bytes 393220
  86.9 4.4 %copy-start.1 = (bf16[1,128,4096]{2,1,0:T(8,128)(2,1)S(1)}, bf16[1,128,4096]{2,1,0:T(8,128)(2,1)}, u32[]{:S(2)}) copy-start(bf16[1,128,4096]{2,1,0:T(8,128)(2,1)} %param.12) | copy-start | bytes 3145732
  92.7 8.9 %collective-permute-start.2 = (bf16[256,2048]{1,0:T(8,128)(2,1)}, bf16[256,2048]{1,0:T(8,128)(2,1)}, u32[]{:S(2)}, u32[]{:S(2)}) collective-permute-start(bf16[256,2048]{1,0:T(8,128)(2,1)} %convolution_convert_fusion), channel_id=1, source_target_pairs={{0,1},{1,0},{2,3},{3,2},{4,5},{5,4},{6,7},{7,6},{8,9},{9,8},{10,11... | collective-permute-start | bytes 3145736 | tf_op jit(solution)/shard_map/ppermute | solution.py:41

commit v10 on v9

--- a/solution.py
+++ b/solution.py
@@ -197,14 +197,14 @@
     rows, width = tokens_in.shape
     half = rows // nc
     spread = jnp.broadcast_to(
-        tokens_in.reshape(nc, half, width).transpose(1, 0, 2)[:, None],
-        (half, n_head // nc, nc, width),
-    ).reshape(half, n_head, width)
-    mine = lax.all_to_all(spread, HEAD_AXES, 1, 1, tiled=True).reshape(half, n_head * width)
+        tokens_in.reshape(1, nc, half, width), (n_head // nc, nc, half, width)
+    ).reshape(n_head, half, width)
+    mine = lax.all_to_all(spread, HEAD_AXES, 0, 0, tiled=True)
     theirs = _send(mine, core_perm)
-    w_local = w_qkv[:, 0, :]
-    proj_own = jnp.dot(mine, w_local, preferred_element_type=jnp.float32)
-    proj_oth = jnp.dot(theirs, w_local, preferred_element_type=jnp.float32)
+    w_local = w_qkv[:, 0, :].reshape(n_head, width, -1)
+    dims = (((0, 2), (0, 1)), ((), ()))
+    proj_own = lax.dot_general(mine, w_local, dims, preferred_element_type=jnp.float32)
+    proj_oth = lax.dot_general(theirs, w_local, dims, preferred_element_type=jnp.float32)
     projected = jnp.where(
         me_c == 0,
         jnp.concatenate([proj_own, proj_oth], axis=0),
@@ -222,10 +222,12 @@
     cols = w_full.shape[1] // nc
     w_keep = lax.dynamic_slice_in_dim(w_full, me_c * cols, cols, 1)
     w_give = lax.dynamic_slice_in_dim(w_full, (1 - me_c) * cols, cols, 1)
-    keep = jnp.dot(attended, w_keep, preferred_element_type=jnp.float32)
-    give = jnp.dot(attended, w_give, preferred_element_type=jnp.float32).astype(jnp.bfloat16)
-    got = _send(give, core_perm)
-    summed = (keep + got.astype(jnp.float32)).astype(jnp.bfloat16)
+    w_theirs = _send(w_give, core_perm)
+    att_theirs = _send(attended, core_perm)
+    summed = (
+        jnp.dot(attended, w_keep, preferred_element_type=jnp.float32)
+        + jnp.dot(att_theirs, w_theirs, preferred_element_type=jnp.float32)
+    ).astype(jnp.bfloat16)
     n_head = nx * ny * nc
     chunks = summed.reshape(n_head, rows // n_head, cols)
     parts = lax.all_to_all(chunks, HEAD_AXES, 0, 0, tiled=True).astype(jnp.float32)

time: 127 us -> 121 us (0.953)
  waiting for transfers between devices: 34.6 us -> 28.2 us
  starting transfers between devices: 43.3 us -> 45.6 us
  matrix products: 13.2 us -> 11.8 us
    all_to_all x1, waiting for transfers between devices: 16.8 us -> 12.6 us  [project(): mine = lax.all_to_all(spread, HEAD_AXES, 0, 0, tiled=True)]
    ppermute x2 -> x3, starting transfers between devices: 8.3 us -> 10.6 us  [_send(): return lax.ppermute(value, HEAD_AXES, perm)]
    all_to_all x1 -> x0, local copies, waits for them, and re-layouts: 2.29 us -> none  [project(): lax.all_to_all(spread, HEAD_AXES, 1, 1, tiled=True)]
    ppermute x2 -> x3, waiting for transfers between devices: 2.61 us -> 0.43 us  [_send(): return lax.ppermute(value, HEAD_AXES, perm)]
    dynamic_slice x0 -> x1, local copies, waits for them, and re-layouts: none -> 1.89 us  [reduce_out(): w_give = lax.dynamic_slice_in_dim(w_full, (1 - me_c) * cols, cols, 1)]
    dot_general x4, matrix products: 7.15 us -> 5.77 us  [the longest x1 1.94 us: project(): lax.dot_general(mine, w_local, dims, preferred_element_type=jnp.float32)]
  transfers between devices with their start and end apart: 6 -> 7, of which waited for: 4 -> 4; matrix products, arithmetic and copies ran while one was open for 6% -> 15% of each run, Pallas kernels for 0% -> 0%
where the time goes in v10:
time: 121 us
  starting transfers between devices  45.6 us (38%)
  waiting for transfers between devices  28.2 us (23%)
  blocking collectives  21.1 us (17%)
  matrix products  11.8 us (10%)
  local copies, waits for them, and re-layouts  7.71 us (6%)
  other arithmetic  5.17 us (4%)
    all_to_all x1, blocking collectives, reduce_out(): lax.all_to_all(chunks, HEAD_AXES, 0, 0, tiled=True).astype(jnp.float32)  21.1 us
    all_to_all x1, waiting for transfers between devices, project(): mine = lax.all_to_all(spread, HEAD_AXES, 0, 0, tiled=True)  12.6 us
    all_to_all x1, starting transfers between devices, code_prefix(): lax.all_to_all(_pack(sums, counts, span, n, head_dim), 'ctx', 0, 0, tiled...  12.4 us
    all_to_all x1, starting transfers between devices, project(): mine = lax.all_to_all(spread, HEAD_AXES, 0, 0, tiled=True)  11.1 us
    ppermute x3, starting transfers between devices, _send(): return lax.ppermute(value, HEAD_AXES, perm)  10.6 us
    all_to_all x1, waiting for transfers between devices, code_prefix(): back = lax.all_to_all(pre.astype(jnp.bfloat16), 'ctx', 0, 0, tiled=True)  7.6 us
    all_to_all x1, starting transfers between devices, code_prefix(): back = lax.all_to_all(pre.astype(jnp.bfloat16), 'ctx', 0, 0, tiled=True)  7.6 us
    all_to_all x1, waiting for transfers between devices, code_prefix(): lax.all_to_all(_pack(sums, counts, span, n, head_dim), 'ctx', 0, 0, tiled...  7.57 us
  transfers between devices with their start and end apart: 7, of which 4 were waited for; matrix products, arithmetic and copies ran while one was open for 15% of the time, Pallas kernels for 0%

profile of v10, /device:TPU:1, one launch (start us, length us, event | category | flops | bytes accessed | tf_op | source)
XLA Modules:
  0.0 120.6 jit_solution(10203792408940575555)
XLA Ops:
  0.0 0.0 copy-start
  0.0 0.0 copy-start.8
  0.0 2.3 %broadcast_in_dim.62 = bf16[16,2,128,128]{3,2,1,0:T(8,128)(2,1)} broadcast(bf16[2,128,128]{2,1,0:T(8,128)(2,1)} %bitcast.53), dimensions={1,2,3} | broadcast | bytes 1114112 | tf_op jit(solution)/shard_map/broadcast_in_dim | solution.py:199
  2.3 11.1 %all-to-all-start = ((bf16[32,128,128]{2,1,0:T(8,128)(2,1)}), bf16[32,128,128]{2,1,0:T(8,128)(2,1)}, u32[]{:S(2)}, u32[]{:S(2)}) async-start(bf16[32,128,128]{2,1,0:T(8,128)(2,1)} %bitcast.49), calls=%async_computation | async-start | bytes 2097152 | tf_op jit(solution)/shard_map/all_to_all | solution.py:202
  13.4 1.9 %dynamic-slice_bitcast_fusion = bf16[128,2048]{1,0:T(8,128)(2,1)} fusion(bf16[1,128,4096]{2,1,0:T(8,128)(2,1)} %param.12, s32[]{:T(128)S(6)} %select_n.60), kind=kLoop, calls=%fused_computation.15 | loop fusion | bytes 1048580 | tf_op jit(solution)/shard_map/dynamic_slice | solution.py:224
  15.3 2.3 %collective-permute-start.3 = (bf16[128,2048]{1,0:T(8,128)(2,1)}, bf16[128,2048]{1,0:T(8,128)(2,1)}, u32[]{:S(2)}, u32[]{:S(2)}) collective-permute-start(bf16[128,2048]{1,0:T(8,128)(2,1)} %dynamic-slice_bitcast_fusion), channel_id=1, source_target_pairs={{0,1},{1,0},{2,3},{3,2},{4,5},{5,4},{6,7},{7,6},{8,9},{9,8},{10,11... | collective-permute-start | bytes 1572872 | tf_op jit(solution)/shard_map/ppermute | solution.py:41
  17.6 0.0 copy-done.8
  17.6 0.1 convert_reduce_fusion.1
  17.8 0.1 reduce_sum.39
  17.9 12.6 %all-to-all-done = bf16[32,128,128]{2,1,0:T(8,128)(2,1)} async-done(((bf16[32,128,128]{2,1,0:T(8,128)(2,1)}), bf16[32,128,128]{2,1,0:T(8,128)(2,1)}, u32[]{:S(2)}, u32[]{:S(2)}) %all-to-all-start) | async-done | bytes 1048608 | tf_op jit(solution)/shard_map/all_to_all | solution.py:202
  30.4 2.0 %collective-permute-start = (bf16[32,128,128]{2,1,0:T(8,128)(2,1)}, bf16[32,128,128]{2,1,0:T(8,128)(2,1)}, u32[]{:S(2)}, u32[]{:S(2)}) collective-permute-start(bf16[32,128,128]{2,1,0:T(8,128)(2,1)} %all-to-all-done), channel_id=1, source_target_pairs={{0,1},{1,0},{2,3},{3,2},{4,5},{5,4},{6,7},{7,6},{8,9},{9,8},{10,11... | collective-permute-start | bytes 3145736 | tf_op jit(solution)/shard_map/ppermute | solution.py:41
  33.2 0.4 scatter.9
  33.6 0.0 copy-done
  33.6 1.9 %convolution_bitcast_fusion.1 = bf16[128,384]{1,0:T(8,128)(2,1)S(1)} fusion(bf16[32,128,128]{2,1,0:T(8,128)(2,1)} %all-to-all-done, bf16[32,128,384]{2,1,0:T(8,128)(2,1)S(1)} %bitcast.47), kind=kOutput, calls=%fused_computation.8 | convolution fusion | flops 402653184 | bytes 4292608 | tf_op jit(solution)/shard_map/dot_general | solution.py:206
  35.6 0.0 collective-permute-done
  35.6 1.9 %convolution_bitcast_fusion = bf16[128,384]{1,0:T(8,128)(2,1)S(1)} fusion(bf16[32,128,128]{2,1,0:T(8,128)(2,1)} %collective-permute-done, bf16[32,128,384]{2,1,0:T(8,128)(2,1)S(1)} %bitcast.48), kind=kOutput, calls=%fused_computation.7 | convolution fusion | flops 402653184 | bytes 4292608 | tf_op jit(solution)/shard_map/dot_general | solution.py:207
  37.6 0.4 convolution_convert_fusion
  38.0 0.7 pad_maximum_fusion
  38.7 12.4 %all-to-all-start.1 = ((bf16[16,40,128]{2,1,0:T(8,128)(2,1)}), bf16[16,40,128]{2,1,0:T(8,128)(2,1)S(1)}, u32[]{:S(2)}, u32[]{:S(2)}) async-start(bf16[16,40,128]{2,1,0:T(8,128)(2,1)} %pad_maximum_fusion), calls=%async_computation.1 | async-start | bytes 327680 | tf_op jit(solution)/shard_map/all_to_all | solution.py:179
  51.1 0.1 pad.18.clone
  51.2 0.0 copy-start.4
  51.2 0.8 maximum_maximum_fusion
  52.0 0.0 copy-done.4
  52.0 3.9 %collective-permute-start.1 = (bf16[272,256]{1,0:T(8,128)(2,1)}, bf16[272,256]{1,0:T(8,128)(2,1)}, u32[]{:S(2)}, u32[]{:S(2)}) collective-permute-start(bf16[272,256]{1,0:T(8,128)(2,1)} %maximum_maximum_fusion), channel_id=1, source_target_pairs={{0,32},{32,64},{64,96},{96,128},{128,160},{160,192},{192,224},{224... | collective-permute-start | bytes 417800 | tf_op jit(solution)/shard_map/ppermute | solution.py:124
  55.9 7.6 %all-to-all-done.1 = bf16[16,40,128]{2,1,0:T(8,128)(2,1)S(1)} async-done(((bf16[16,40,128]{2,1,0:T(8,128)(2,1)}), bf16[16,40,128]{2,1,0:T(8,128)(2,1)S(1)}, u32[]{:S(2)}, u32[]{:S(2)}) %all-to-all-start.1) | async-done | bytes 163872 | tf_op jit(solution)/shard_map/all_to_all | solution.py:179
  63.5 0.2 fusion.34
  63.7 0.2 select_convert_fusion
  63.9 0.7 copy.13
  64.6 7.6 %all-to-all-start.2 = ((bf16[16,40,128]{2,1,0:T(8,128)(2,1)}), bf16[16,40,128]{2,1,0:T(8,128)(2,1)S(1)}, u32[]{:S(2)}, u32[]{:S(2)}) async-start(bf16[16,40,128]{2,1,0:T(8,128)(2,1)} %copy.13), calls=%async_computation.2 | async-start | bytes 327680 | tf_op jit(solution)/shard_map/all_to_all | solution.py:188
  72.2 0.0 collective-permute-done.1
  72.2 0.8 fusion.52
  72.9 0.9 slice.121
  73.9 0.0 copy-start.6
  73.9 0.2 convert_reduce_fusion
  74.0 0.5 copy-done.6
  74.5 1.2 select_reduce_fusion.1
  75.7 0.0 copy-start.2
  75.7 0.8 copy-done.2
  76.5 0.3 fusion.17
  76.7 7.6 %all-to-all-done.2 = bf16[16,40,128]{2,1,0:T(8,128)(2,1)S(1)} async-done(((bf16[16,40,128]{2,1,0:T(8,128)(2,1)}), bf16[16,40,128]{2,1,0:T(8,128)(2,1)S(1)}, u32[]{:S(2)}, u32[]{:S(2)}) %all-to-all-start.2) | async-done | bytes 163872 | tf_op jit(solution)/shard_map/all_to_all | solution.py:188
  84.4 0.1 add.76
  84.5 0.0 copy-start.3
  84.5 0.0 copy-start.5
  84.5 0.0 copy-start.7
  84.5 0.0 copy-start.1
  84.5 1.3 %select_reduce_fusion = (f32[256]{0:T(256)S(1)}, f32[256,512]{1,0:T(8,128)S(1)}) fusion(pred[512]{0:T(512)(128)(4,1)S(1)} %get-tuple-element.31, bf16[1,512,128]{2,1,0:T(8,128)(2,1)} %param.13, bf16[256,384]{1,0:T(8,128)(2,1)S(1)} %fusion.16), kind=kOutput, calls=%fused_computation.19 | convolution fusion | flops 33947392 | bytes 722432 | tf_op jit(solution)/shard_map/dot_general | solution.py:73
  85.9 1.3 %convolution_add_fusion.1 = f32[512,128]{1,0:T(8,128)S(1)} fusion(f32[512,128]{1,0:T(8,128)S(1)} %bitcast.51, s32[256]{0:T(256)S(1)} %bitcast.55, pred[256]{0:T(512)(128)(4,1)S(1)} %compare_and_fusion, bf16[272,256]{1,0:T(8,128)(2,1)} %collective-permute-done.1), kind=kOutput, calls=%fused_computation.5 | convolution fusion | flops 33882112 | bytes 591104 | tf_op jit(solution)/shard_map/dot_general | solution.py:141
  87.2 0.6 fusion.15
  87.8 0.6 fusion.14
  88.5 0.0 copy-done.3
  88.5 0.0 copy-done.5
  88.5 0.0 copy-done.7
  88.5 0.3 fusion.4
  88.9 6.3 %collective-permute-start.2 = (bf16[256,128]{1,0:T(8,128)(2,1)S(1)}, bf16[256,128]{1,0:T(8,128)(2,1)S(1)}, u32[]{:S(2)}, u32[]{:S(2)}) collective-permute-start(bf16[256,128]{1,0:T(8,128)(2,1)S(1)} %fusion.4), channel_id=1, source_target_pairs={{0,1},{1,0},{2,3},{3,2},{4,5},{5,4},{6,7},{7,6},{8,9},{9,8},{10,11... | collective-permute-start | bytes 196616 | tf_op jit(solution)/shard_map/ppermute | solution.py:41
  95.2 0.0 copy-done.1
  95.2 0.4 fusion.5
  95.6 0.0 collective-permute-done.3
  95.6 0.4 collective-permute-done.2
  96.0 1.5 %fusion.1 = bf16[32,8,2048]{2,1,0:T(8,128)(2,1)S(1)} fusion(f32[256,2048]{1,0:T(8,128)S(1)} %fusion.5, bf16[256,128]{1,0:T(8,128)(2,1)S(1)} %collective-permute-done.2, bf16[128,2048]{1,0:T(8,128)(2,1)} %collective-permute-done.3), kind=kOutput, calls=%fused_computation.2 | convolution fusion | flops 135266304 | bytes 3735552 | tf_op jit(solution)/shard_map/dot_general | solution.py:229
  97.5 21.1 %all_to_all.20 = bf16[32,8,2048]{2,1,0:T(8,128)(2,1)} all-to-all(bf16[32,8,2048]{2,1,0:T(8,128)(2,1)S(1)} %fusion.1), channel_id=1, replica_groups=mesh['ctx'=16,'hx'=4,'hy'=4,'hc'=2] {'hx','hy','hc'}, dimensions={0} | all-to-all | bytes 2097152 | tf_op jit(solution)/shard_map/all_to_all | solution.py:233
  118.6 1.4 %reduce.4 = bf16[2,8,2048]{2,1,0:T(8,128)(2,1)S(1)} reduce(bf16[16,2,8,2048]{3,2,1,0:T(8,128)(2,1)} %bitcast.50, bf16[]{:T(256)} %constant.126.clone.1), dimensions={0}, to_apply=%region_5.6.clone | reduce | flops 491520 | bytes 1114114 | tf_op jit(solution)/shard_map/reduce_sum | solution.py:234
  120.0 0.6 pad_maximum_fusion.3
  (21 shorter events, 0.3 us)
Async XLA Ops:
  0.0 33.6 %copy-start = (bf16[4096,1,384]{2,0,1:T(8,128)(2,1)S(1)}, bf16[4096,1,384]{2,0,1:T(8,128)(2,1)}, u32[]{:S(2)}) copy-start(bf16[4096,1,384]{2,0,1:T(8,128)(2,1)} %param.11) | copy-start | bytes 9437188
  0.0 17.6 %copy-start.8 = (s32[1,256]{1,0:T(1,128)S(1)}, s32[1,256]{1,0:T(1,128)}, u32[]{:S(2)}) copy-start(s32[1,256]{1,0:T(1,128)} %param.14) | copy-start | bytes 3076
  2.3 28.2 %all-to-all-start = ((bf16[32,128,128]{2,1,0:T(8,128)(2,1)}), bf16[32,128,128]{2,1,0:T(8,128)(2,1)}, u32[]{:S(2)}, u32[]{:S(2)}) async-start(bf16[32,128,128]{2,1,0:T(8,128)(2,1)} %bitcast.49), calls=%async_computation | async-start | bytes 2097152 | tf_op jit(solution)/shard_map/all_to_all | solution.py:202
  15.3 80.3 %collective-permute-start.3 = (bf16[128,2048]{1,0:T(8,128)(2,1)}, bf16[128,2048]{1,0:T(8,128)(2,1)}, u32[]{:S(2)}, u32[]{:S(2)}) collective-permute-start(bf16[128,2048]{1,0:T(8,128)(2,1)} %dynamic-slice_bitcast_fusion), channel_id=1, source_target_pairs={{0,1},{1,0},{2,3},{3,2},{4,5},{5,4},{6,7},{7,6},{8,9},{9,8},{10,11... | collective-permute-start | bytes 1572872 | tf_op jit(solution)/shard_map/ppermute | solution.py:41
  30.4 5.1 %collective-permute-start = (bf16[32,128,128]{2,1,0:T(8,128)(2,1)}, bf16[32,128,128]{2,1,0:T(8,128)(2,1)}, u32[]{:S(2)}, u32[]{:S(2)}) collective-permute-start(bf16[32,128,128]{2,1,0:T(8,128)(2,1)} %all-to-all-done), channel_id=1, source_target_pairs={{0,1},{1,0},{2,3},{3,2},{4,5},{5,4},{6,7},{7,6},{8,9},{9,8},{10,11... | collective-permute-start | bytes 3145736 | tf_op jit(solution)/shard_map/ppermute | solution.py:41
  38.7 24.8 %all-to-all-start.1 = ((bf16[16,40,128]{2,1,0:T(8,128)(2,1)}), bf16[16,40,128]{2,1,0:T(8,128)(2,1)S(1)}, u32[]{:S(2)}, u32[]{:S(2)}) async-start(bf16[16,40,128]{2,1,0:T(8,128)(2,1)} %pad_maximum_fusion), calls=%async_computation.1 | async-start | bytes 327680 | tf_op jit(solution)/shard_map/all_to_all | solution.py:179
  51.2 0.8 copy-start.4
  52.0 20.2 %collective-permute-start.1 = (bf16[272,256]{1,0:T(8,128)(2,1)}, bf16[272,256]{1,0:T(8,128)(2,1)}, u32[]{:S(2)}, u32[]{:S(2)}) collective-permute-start(bf16[272,256]{1,0:T(8,128)(2,1)} %maximum_maximum_fusion), channel_id=1, source_target_pairs={{0,32},{32,64},{64,96},{96,128},{128,160},{160,192},{192,224},{224... | collective-permute-start | bytes 417800 | tf_op jit(solution)/shard_map/ppermute | solution.py:124
  64.6 19.8 %all-to-all-start.2 = ((bf16[16,40,128]{2,1,0:T(8,128)(2,1)}), bf16[16,40,128]{2,1,0:T(8,128)(2,1)S(1)}, u32[]{:S(2)}, u32[]{:S(2)}) async-start(bf16[16,40,128]{2,1,0:T(8,128)(2,1)} %copy.13), calls=%async_computation.2 | async-start | bytes 327680 | tf_op jit(solution)/shard_map/all_to_all | solution.py:188
  73.9 0.7 copy-start.6
  75.7 0.8 copy-start.2
  84.5 4.0 %copy-start.3 = (f32[256,512]{1,0:T(8,128)S(1)}, f32[256,512]{1,0:T(8,128)}, u32[]{:S(2)}) copy-start(f32[256,512]{1,0:T(8,128)} %copy-done.2) | copy-start | bytes 1572868
  84.5 4.0 %copy-start.5 = (bf16[256,256]{1,0:T(8,128)(2,1)S(1)}, bf16[256,256]{1,0:T(8,128)(2,1)}, u32[]{:S(2)}) copy-start(bf16[256,256]{1,0:T(8,128)(2,1)} %copy-done.4) | copy-start | bytes 393220
  84.5 4.0 %copy-start.7 = (bf16[256,256]{1,0:T(8,128)(2,1)S(1)}, bf16[256,256]{1,0:T(8,128)(2,1)}, u32[]{:S(2)}) copy-start(bf16[256,256]{1,0:T(8,128)(2,1)} %copy-done.6) | copy-start | bytes 393220
  84.5 10.7 %copy-start.1 = (bf16[1,128,4096]{2,1,0:T(8,128)(2,1)S(1)}, bf16[1,128,4096]{2,1,0:T(8,128)(2,1)}, u32[]{:S(2)}) copy-start(bf16[1,128,4096]{2,1,0:T(8,128)(2,1)} %param.12) | copy-start | bytes 3145732
  88.9 7.2 %collective-permute-start.2 = (bf16[256,128]{1,0:T(8,128)(2,1)S(1)}, bf16[256,128]{1,0:T(8,128)(2,1)S(1)}, u32[]{:S(2)}, u32[]{:S(2)}) collective-permute-start(bf16[256,128]{1,0:T(8,128)(2,1)S(1)} %fusion.4), channel_id=1, source_target_pairs={{0,1},{1,0},{2,3},{3,2},{4,5},{5,4},{6,7},{7,6},{8,9},{9,8},{10,11... | collective-permute-start | bytes 196616 | tf_op jit(solution)/shard_map/ppermute | solution.py:41

commit v11 on v10

--- a/solution.py
+++ b/solution.py
@@ -108,24 +108,17 @@
     scale = 1.0 / math.sqrt(head_dim)
     half = rows // 2
 
+    code_row = codes[0]
+    code_ids = jnp.arange(num_codes, dtype=jnp.int32)
+    route = [(i, i + 1) for i in range(n_ctx - 1)]
+    prev_codes = lax.ppermute(code_row, "ctx", route)
+    prev_codes, tokens_in = lax.optimization_barrier((prev_codes, tokens_in))
+
     projected = project(tokens_in, w_qkv, sizes)
     queries = projected[:, :head_dim].astype(jnp.bfloat16)
     key_vals = projected[:, head_dim:].astype(jnp.bfloat16)
     values = key_vals[:, head_dim:]
-
-    code_row = codes[0]
-    code_ids = jnp.arange(num_codes, dtype=jnp.int32)
-    hi = (code_row // 16).astype(jnp.bfloat16).reshape(1, -1)
-    lo = (code_row % 16).astype(jnp.bfloat16).reshape(1, -1)
-    kvw = key_vals.shape[1]
-    code_rows = jnp.pad(jnp.concatenate([hi, lo], axis=0), ((0, 0), (0, kvw - rows)))
-    kv_blob = jnp.concatenate([key_vals, code_rows, jnp.zeros((14, kvw), jnp.bfloat16)], axis=0)
-    route = [(i, i + 1) for i in range(n_ctx - 1)]
-    prev_blob = lax.ppermute(kv_blob, "ctx", route)
-    prev_kv = prev_blob[:rows]
-    prev_codes = (
-        prev_blob[rows, :rows].astype(jnp.int32) * 16 + prev_blob[rows + 1, :rows].astype(jnp.int32)
-    )
+    prev_kv = lax.ppermute(key_vals, "ctx", route)
 
     onehot_own = (code_row[:, None] == code_ids[None, :]).astype(jnp.bfloat16)
     sums = lax.dot_general(

time: 121 us -> 127 us (1.050)
  blocking collectives: 21.1 us -> 46.2 us
  waiting for transfers between devices: 28.2 us -> 14.3 us
  starting transfers between devices: 45.6 us -> 43.1 us
  local copies, waits for them, and re-layouts: 7.71 us -> 5.69 us
  other arithmetic: 5.17 us -> 3.62 us
    all_to_all x0 -> x1, blocking collectives: none -> 25.4 us  [project(): mine = lax.all_to_all(spread, HEAD_AXES, 0, 0, tiled=True)]
    all_to_all x1 -> x0, waiting for transfers between devices: 12.6 us -> none  [project(): mine = lax.all_to_all(spread, HEAD_AXES, 0, 0, tiled=True)]
    all_to_all x1 -> x0, starting transfers between devices: 11.1 us -> none  [project(): mine = lax.all_to_all(spread, HEAD_AXES, 0, 0, tiled=True)]
    ppermute x1 -> x2, starting transfers between devices: 3.91 us -> 8.81 us  [the longest x1 4.62 us: on_device(): prev_codes = lax.ppermute(code_row, 'ctx', route)]
    all_to_all x1, waiting for transfers between devices: 7.57 us -> 2.96 us  [code_prefix(): lax.all_to_all(_pack(sums, counts, span, n, head_dim), 'ctx', 0, 0, tiled...]
    all_to_all x1, starting transfers between devices: 12.4 us -> 16.5 us  [code_prefix(): lax.all_to_all(_pack(sums, counts, span, n, head_dim), 'ctx', 0, 0, tiled...]
    all_to_all x1, waiting for transfers between devices: 7.6 us -> 9.76 us  [code_prefix(): back = lax.all_to_all(pre.astype(jnp.bfloat16), 'ctx', 0, 0, tiled=True)]
  transfers between devices with their start and end apart: 7 -> 7, of which waited for: 4 -> 5; matrix products, arithmetic and copies ran while one was open for 15% -> 11% of each run, Pallas kernels for 0% -> 0%
where the time goes in v11:
time: 127 us
  blocking collectives  46.2 us (36%)
  starting transfers between devices  43.1 us (34%)
  waiting for transfers between devices  14.3 us (11%)
  matrix products  12.7 us (10%)
  local copies, waits for them, and re-layouts  5.69 us (4%)
  other arithmetic  3.62 us (3%)
    all_to_all x1, blocking collectives, project(): mine = lax.all_to_all(spread, HEAD_AXES, 0, 0, tiled=True)  25.4 us
    all_to_all x1, blocking collectives, reduce_out(): lax.all_to_all(chunks, HEAD_AXES, 0, 0, tiled=True).astype(jnp.float32)  20.8 us
    all_to_all x1, starting transfers between devices, code_prefix(): lax.all_to_all(_pack(sums, counts, span, n, head_dim), 'ctx', 0, 0, tiled...  16.5 us
    ppermute x3, starting transfers between devices, _send(): return lax.ppermute(value, HEAD_AXES, perm)  10.6 us
    all_to_all x1, waiting for transfers between devices, code_prefix(): back = lax.all_to_all(pre.astype(jnp.bfloat16), 'ctx', 0, 0, tiled=True)  9.76 us
    all_to_all x1, starting transfers between devices, code_prefix(): back = lax.all_to_all(pre.astype(jnp.bfloat16), 'ctx', 0, 0, tiled=True)  7.25 us
    ppermute x1, starting transfers between devices, on_device(): prev_codes = lax.ppermute(code_row, 'ctx', route)  4.62 us
    ppermute x1, starting transfers between devices, on_device(): prev_kv = lax.ppermute(key_vals, 'ctx', route)  4.19 us
  transfers between devices with their start and end apart: 7, of which 5 were waited for; matrix products, arithmetic and copies ran while one was open for 11% of the time, Pallas kernels for 0%

profile of v11, /device:TPU:1, one launch (start us, length us, event | category | flops | bytes accessed | tf_op | source)
XLA Modules:
  0.0 126.6 jit_solution(7188443735875184433)
XLA Ops:
  0.0 0.0 copy-start
  0.0 0.0 copy-start.4
  0.0 4.6 %collective-permute-start = (s32[256]{0:T(256)}, s32[256]{0:T(256)S(1)}, u32[]{:S(2)}, u32[]{:S(2)}) collective-permute-start(s32[256]{0:T(256)} %bitcast.55), channel_id=1, source_target_pairs={{0,32},{32,64},{64,96},{96,128},{128,160},{160,192},{192,224},{224... | collective-permute-start | bytes 3080 | tf_op jit(solution)/shard_map/ppermute | solution.py:114
  4.6 0.9 collective-permute-done
  5.6 1.1 broadcast_in_dim.59
  6.6 25.4 %all_to_all.20 = bf16[32,128,128]{2,1,0:T(8,128)(2,1)} all-to-all(bf16[32,128,128]{2,1,0:T(8,128)(2,1)S(1)} %bitcast.49), channel_id=1, replica_groups=mesh['ctx'=16,'hx'=4,'hy'=4,'hc'=2] {'hx','hy','hc'}, dimensions={0} | all-to-all | bytes 2097152 | tf_op jit(solution)/shard_map/all_to_all | solution.py:195
  32.1 2.0 %collective-permute-start.1 = (bf16[32,128,128]{2,1,0:T(8,128)(2,1)}, bf16[32,128,128]{2,1,0:T(8,128)(2,1)}, u32[]{:S(2)}, u32[]{:S(2)}) collective-permute-start(bf16[32,128,128]{2,1,0:T(8,128)(2,1)} %all_to_all.20), channel_id=1, source_target_pairs={{0,1},{1,0},{2,3},{3,2},{4,5},{5,4},{6,7},{7,6},{8,9},{9,8},{10,11... | collective-permute-start | bytes 3145736 | tf_op jit(solution)/shard_map/ppermute | solution.py:41
  34.1 0.0 copy-done.4
  34.1 0.1 convert_reduce_fusion.1
  34.2 0.1 reduce_sum.39
  34.4 0.4 scatter.9
  34.7 0.0 copy-done
  34.8 1.9 %convolution_bitcast_fusion.1 = bf16[128,384]{1,0:T(8,128)(2,1)S(1)} fusion(bf16[32,128,128]{2,1,0:T(8,128)(2,1)} %all_to_all.20, bf16[32,128,384]{2,1,0:T(8,128)(2,1)S(1)} %bitcast.46), kind=kOutput, calls=%fused_computation.8 | convolution fusion | flops 402653184 | bytes 4292608 | tf_op jit(solution)/shard_map/dot_general | solution.py:199
  36.7 0.2 collective-permute-done.1
  36.9 1.9 %convolution_bitcast_fusion = bf16[128,384]{1,0:T(8,128)(2,1)S(1)} fusion(bf16[32,128,128]{2,1,0:T(8,128)(2,1)} %collective-permute-done.1, bf16[32,128,384]{2,1,0:T(8,128)(2,1)S(1)} %bitcast.47), kind=kOutput, calls=%fused_computation.7 | convolution fusion | flops 402653184 | bytes 4292608 | tf_op jit(solution)/shard_map/dot_general | solution.py:200
  38.9 0.4 convolution_convert_fusion
  39.4 0.7 pad_maximum_fusion
  40.0 16.5 %all-to-all-start.1 = ((bf16[16,40,128]{2,1,0:T(8,128)(2,1)}), bf16[16,40,128]{2,1,0:T(8,128)(2,1)S(1)}, u32[]{:S(2)}, u32[]{:S(2)}) async-start(bf16[16,40,128]{2,1,0:T(8,128)(2,1)} %pad_maximum_fusion), calls=%async_computation.1 | async-start | bytes 327680 | tf_op jit(solution)/shard_map/all_to_all | solution.py:172
  56.5 1.9 %dynamic-slice_bitcast_fusion = bf16[128,2048]{1,0:T(8,128)(2,1)} fusion(bf16[1,128,4096]{2,1,0:T(8,128)(2,1)} %param.12, s32[]{:T(128)S(6)} %select_n.44), kind=kLoop, calls=%fused_computation.15 | loop fusion | bytes 1048580 | tf_op jit(solution)/shard_map/dynamic_slice | solution.py:217
  58.4 2.3 %collective-permute-start.4 = (bf16[128,2048]{1,0:T(8,128)(2,1)}, bf16[128,2048]{1,0:T(8,128)(2,1)}, u32[]{:S(2)}, u32[]{:S(2)}) collective-permute-start(bf16[128,2048]{1,0:T(8,128)(2,1)} %dynamic-slice_bitcast_fusion), channel_id=1, source_target_pairs={{0,1},{1,0},{2,3},{3,2},{4,5},{5,4},{6,7},{7,6},{8,9},{9,8},{10,11... | collective-permute-start | bytes 1572872 | tf_op jit(solution)/shard_map/ppermute | solution.py:41
  61.5 0.7 slice.107
  62.1 4.2 %collective-permute-start.2 = (bf16[256,256]{1,0:T(8,128)(2,1)}, bf16[256,256]{1,0:T(8,128)(2,1)}, u32[]{:S(2)}, u32[]{:S(2)}) collective-permute-start(bf16[256,256]{1,0:T(8,128)(2,1)} %slice.107), channel_id=1, source_target_pairs={{0,32},{32,64},{64,96},{96,128},{128,160},{160,192},{192,224},{224... | collective-permute-start | bytes 393224 | tf_op jit(solution)/shard_map/ppermute | solution.py:121
  66.3 3.0 %all-to-all-done.1 = bf16[16,40,128]{2,1,0:T(8,128)(2,1)S(1)} async-done(((bf16[16,40,128]{2,1,0:T(8,128)(2,1)}), bf16[16,40,128]{2,1,0:T(8,128)(2,1)S(1)}, u32[]{:S(2)}, u32[]{:S(2)}) %all-to-all-start.1) | async-done | bytes 163872 | tf_op jit(solution)/shard_map/all_to_all | solution.py:172
  69.3 0.2 fusion.34
  69.5 0.2 select_convert_fusion
  69.7 0.7 copy.13
  70.4 7.3 %all-to-all-start.2 = ((bf16[16,40,128]{2,1,0:T(8,128)(2,1)}), bf16[16,40,128]{2,1,0:T(8,128)(2,1)S(1)}, u32[]{:S(2)}, u32[]{:S(2)}) async-start(bf16[16,40,128]{2,1,0:T(8,128)(2,1)} %copy.13), calls=%async_computation.2 | async-start | bytes 327680 | tf_op jit(solution)/shard_map/all_to_all | solution.py:181
  77.7 0.2 convert_reduce_fusion
  77.8 0.0 collective-permute-done.2
  77.8 1.2 select_reduce_fusion.1
  79.0 0.0 copy-start.2
  79.0 0.8 copy-done.2
  79.9 0.3 fusion.17
  80.1 9.8 %all-to-all-done.2 = bf16[16,40,128]{2,1,0:T(8,128)(2,1)S(1)} async-done(((bf16[16,40,128]{2,1,0:T(8,128)(2,1)}), bf16[16,40,128]{2,1,0:T(8,128)(2,1)S(1)}, u32[]{:S(2)}, u32[]{:S(2)}) %all-to-all-start.2) | async-done | bytes 163872 | tf_op jit(solution)/shard_map/all_to_all | solution.py:181
  90.0 0.1 add.56
  90.0 0.0 copy-start.3
  90.0 0.0 copy-start.1
  90.0 1.3 %select_reduce_fusion = (f32[256]{0:T(256)S(1)}, f32[256,512]{1,0:T(8,128)S(1)}) fusion(pred[512]{0:T(512)(128)(4,1)S(1)} %get-tuple-element.35, bf16[1,512,128]{2,1,0:T(8,128)(2,1)} %param.13, bf16[256,384]{1,0:T(8,128)(2,1)S(1)} %fusion.16), kind=kOutput, calls=%fused_computation.19 | convolution fusion | flops 33947392 | bytes 722432 | tf_op jit(solution)/shard_map/dot_general | solution.py:73
  91.4 1.3 %convolution_add_fusion.1 = f32[512,128]{1,0:T(8,128)S(1)} fusion(f32[512,128]{1,0:T(8,128)S(1)} %bitcast.50, s32[256]{0:T(256)S(1)} %collective-permute-done, pred[256]{0:T(512)(128)(4,1)S(1)} %compare_and_fusion, bf16[256,256]{1,0:T(8,128)(2,1)} %collective-permute-done.2), kind=kOutput, calls=%fused_computation.5 | convolution fusion | flops 33882112 | bytes 591104 | tf_op jit(solution)/shard_map/dot_general | solution.py:134
  92.7 0.6 fusion.15
  93.4 0.6 fusion.14
  94.0 0.0 copy-done.3
  94.0 1.2 fusion.4
  95.2 6.2 %collective-permute-start.3 = (bf16[256,128]{1,0:T(8,128)(2,1)S(1)}, bf16[256,128]{1,0:T(8,128)(2,1)S(1)}, u32[]{:S(2)}, u32[]{:S(2)}) collective-permute-start(bf16[256,128]{1,0:T(8,128)(2,1)S(1)} %fusion.4), channel_id=1, source_target_pairs={{0,1},{1,0},{2,3},{3,2},{4,5},{5,4},{6,7},{7,6},{8,9},{9,8},{10,11... | collective-permute-start | bytes 196616 | tf_op jit(solution)/shard_map/ppermute | solution.py:41
  101.5 0.0 copy-done.1
  101.5 0.4 fusion.5
  101.9 0.0 collective-permute-done.4
  101.9 0.4 collective-permute-done.3
  102.3 1.5 %fusion.1 = bf16[32,8,2048]{2,1,0:T(8,128)(2,1)S(1)} fusion(f32[256,2048]{1,0:T(8,128)S(1)} %fusion.5, bf16[256,128]{1,0:T(8,128)(2,1)S(1)} %collective-permute-done.3, bf16[128,2048]{1,0:T(8,128)(2,1)} %collective-permute-done.4), kind=kOutput, calls=%fused_computation.2 | convolution fusion | flops 135266304 | bytes 3735552 | tf_op jit(solution)/shard_map/dot_general | solution.py:222
  103.8 20.8 %all_to_all.21 = bf16[32,8,2048]{2,1,0:T(8,128)(2,1)} all-to-all(bf16[32,8,2048]{2,1,0:T(8,128)(2,1)S(1)} %fusion.1), channel_id=1, replica_groups=mesh['ctx'=16,'hx'=4,'hy'=4,'hc'=2] {'hx','hy','hc'}, dimensions={0} | all-to-all | bytes 2097152 | tf_op jit(solution)/shard_map/all_to_all | solution.py:226
  124.6 1.4 %reduce.4 = bf16[2,8,2048]{2,1,0:T(8,128)(2,1)S(1)} reduce(bf16[16,2,8,2048]{3,2,1,0:T(8,128)(2,1)} %bitcast.48, bf16[]{:T(256)} %constant.116), dimensions={0}, to_apply=%region_5.6.clone | reduce | flops 491520 | bytes 1114114 | tf_op jit(solution)/shard_map/reduce_sum | solution.py:227
  126.0 0.6 pad_maximum_fusion.3
  (17 shorter events, 0.2 us)
Async XLA Ops:
  0.0 34.7 %copy-start = (bf16[4096,1,384]{2,0,1:T(8,128)(2,1)S(1)}, bf16[4096,1,384]{2,0,1:T(8,128)(2,1)}, u32[]{:S(2)}) copy-start(bf16[4096,1,384]{2,0,1:T(8,128)(2,1)} %param.11) | copy-start | bytes 9437188
  0.0 34.1 %copy-start.4 = (s32[1,256]{1,0:T(1,128)S(1)}, s32[1,256]{1,0:T(1,128)}, u32[]{:S(2)}) copy-start(s32[1,256]{1,0:T(1,128)} %param.14) | copy-start | bytes 3076
  0.0 5.5 %collective-permute-start = (s32[256]{0:T(256)}, s32[256]{0:T(256)S(1)}, u32[]{:S(2)}, u32[]{:S(2)}) collective-permute-start(s32[256]{0:T(256)} %bitcast.55), channel_id=1, source_target_pairs={{0,32},{32,64},{64,96},{96,128},{128,160},{160,192},{192,224},{224... | collective-permute-start | bytes 3080 | tf_op jit(solution)/shard_map/ppermute | solution.py:114
  32.1 4.9 %collective-permute-start.1 = (bf16[32,128,128]{2,1,0:T(8,128)(2,1)}, bf16[32,128,128]{2,1,0:T(8,128)(2,1)}, u32[]{:S(2)}, u32[]{:S(2)}) collective-permute-start(bf16[32,128,128]{2,1,0:T(8,128)(2,1)} %all_to_all.20), channel_id=1, source_target_pairs={{0,1},{1,0},{2,3},{3,2},{4,5},{5,4},{6,7},{7,6},{8,9},{9,8},{10,11... | collective-permute-start | bytes 3145736 | tf_op jit(solution)/shard_map/ppermute | solution.py:41
  40.0 29.2 %all-to-all-start.1 = ((bf16[16,40,128]{2,1,0:T(8,128)(2,1)}), bf16[16,40,128]{2,1,0:T(8,128)(2,1)S(1)}, u32[]{:S(2)}, u32[]{:S(2)}) async-start(bf16[16,40,128]{2,1,0:T(8,128)(2,1)} %pad_maximum_fusion), calls=%async_computation.1 | async-start | bytes 327680 | tf_op jit(solution)/shard_map/all_to_all | solution.py:172
  58.4 43.5 %collective-permute-start.4 = (bf16[128,2048]{1,0:T(8,128)(2,1)}, bf16[128,2048]{1,0:T(8,128)(2,1)}, u32[]{:S(2)}, u32[]{:S(2)}) collective-permute-start(bf16[128,2048]{1,0:T(8,128)(2,1)} %dynamic-slice_bitcast_fusion), channel_id=1, source_target_pairs={{0,1},{1,0},{2,3},{3,2},{4,5},{5,4},{6,7},{7,6},{8,9},{9,8},{10,11... | collective-permute-start | bytes 1572872 | tf_op jit(solution)/shard_map/ppermute | solution.py:41
  62.1 15.7 %collective-permute-start.2 = (bf16[256,256]{1,0:T(8,128)(2,1)}, bf16[256,256]{1,0:T(8,128)(2,1)}, u32[]{:S(2)}, u32[]{:S(2)}) collective-permute-start(bf16[256,256]{1,0:T(8,128)(2,1)} %slice.107), channel_id=1, source_target_pairs={{0,32},{32,64},{64,96},{96,128},{128,160},{160,192},{192,224},{224... | collective-permute-start | bytes 393224 | tf_op jit(solution)/shard_map/ppermute | solution.py:121
  70.4 19.5 %all-to-all-start.2 = ((bf16[16,40,128]{2,1,0:T(8,128)(2,1)}), bf16[16,40,128]{2,1,0:T(8,128)(2,1)S(1)}, u32[]{:S(2)}, u32[]{:S(2)}) async-start(bf16[16,40,128]{2,1,0:T(8,128)(2,1)} %copy.13), calls=%async_computation.2 | async-start | bytes 327680 | tf_op jit(solution)/shard_map/all_to_all | solution.py:181
  79.0 0.8 copy-start.2
  90.0 4.0 %copy-start.3 = (f32[256,512]{1,0:T(8,128)S(1)}, f32[256,512]{1,0:T(8,128)}, u32[]{:S(2)}) copy-start(f32[256,512]{1,0:T(8,128)} %copy-done.2) | copy-start | bytes 1572868
  90.0 11.4 %copy-start.1 = (bf16[1,128,4096]{2,1,0:T(8,128)(2,1)S(1)}, bf16[1,128,4096]{2,1,0:T(8,128)(2,1)}, u32[]{:S(2)}) copy-start(bf16[1,128,4096]{2,1,0:T(8,128)(2,1)} %param.12) | copy-start | bytes 3145732
  95.2 7.1 %collective-permute-start.3 = (bf16[256,128]{1,0:T(8,128)(2,1)S(1)}, bf16[256,128]{1,0:T(8,128)(2,1)S(1)}, u32[]{:S(2)}, u32[]{:S(2)}) collective-permute-start(bf16[256,128]{1,0:T(8,128)(2,1)S(1)} %fusion.4), channel_id=1, source_target_pairs={{0,1},{1,0},{2,3},{3,2},{4,5},{5,4},{6,7},{7,6},{8,9},{9,8},{10,11... | collective-permute-start | bytes 196616 | tf_op jit(solution)/shard_map/ppermute | solution.py:41

commit v12 on v10

--- a/solution.py
+++ b/solution.py
@@ -228,11 +228,17 @@
         jnp.dot(attended, w_keep, preferred_element_type=jnp.float32)
         + jnp.dot(att_theirs, w_theirs, preferred_element_type=jnp.float32)
     ).astype(jnp.bfloat16)
-    n_head = nx * ny * nc
-    chunks = summed.reshape(n_head, rows // n_head, cols)
-    parts = lax.all_to_all(chunks, HEAD_AXES, 0, 0, tiled=True).astype(jnp.float32)
-    parts = parts.reshape(n_head // nc, nc, rows // n_head, cols).sum(axis=0)
-    out = jnp.concatenate([parts[i] for i in range(nc)], axis=1)
+    n_chip = nx * ny
+    per_chip = rows // n_chip
+    chunks = summed.reshape(n_chip, per_chip, cols)
+    parts = lax.all_to_all(chunks, ("hx", "hy"), 0, 0, tiled=True).astype(jnp.float32)
+    parts = parts.sum(axis=0).reshape(nc, per_chip // nc, cols)
+    mine = lax.dynamic_index_in_dim(parts, me_c, 0, keepdims=False)
+    other = lax.dynamic_index_in_dim(parts, 1 - me_c, 0, keepdims=False).astype(jnp.bfloat16)
+    got = _send(other, core_perm).astype(jnp.float32)
+    out = jnp.where(
+        me_c == 0, jnp.concatenate([mine, got], axis=1), jnp.concatenate([got, mine], axis=1)
+    )
     return out.astype(jnp.bfloat16)
 
 

time: 121 us -> 127 us (1.050)
  blocking collectives: 21.1 us -> 0 us
  waiting for transfers between devices: 28.2 us -> 45.7 us
  starting transfers between devices: 45.6 us -> 54 us
    all_to_all x1 -> x0, blocking collectives: 21.1 us -> none  [reduce_out(): lax.all_to_all(chunks, HEAD_AXES, 0, 0, tiled=True).astype(jnp.float32)]
    all_to_all x0 -> x1, waiting for transfers between devices: none -> 16.7 us  [reduce_out(): lax.all_to_all(chunks, ('hx', 'hy'), 0, 0, tiled=True).astype(jnp.float32)]
    all_to_all x0 -> x1, starting transfers between devices: none -> 4.35 us  [reduce_out(): lax.all_to_all(chunks, ('hx', 'hy'), 0, 0, tiled=True).astype(jnp.float32)]
    ppermute x3 -> x4, starting transfers between devices: 10.6 us -> 14.6 us  [_send(): return lax.ppermute(value, HEAD_AXES, perm)]
  transfers between devices with their start and end apart: 7 -> 9, of which waited for: 4 -> 6; matrix products, arithmetic and copies ran while one was open for 15% -> 14% of each run, Pallas kernels for 0% -> 0%
where the time goes in v12:
time: 127 us; the launch traced here: 126 us
  starting transfers between devices  54 us (43%)
  waiting for transfers between devices  45.7 us (36%)
  matrix products  12.8 us (10%)
  local copies, waits for them, and re-layouts  7.71 us (6%)
  other arithmetic  5.15 us (4%)
    all_to_all x1, waiting for transfers between devices, reduce_out(): lax.all_to_all(chunks, ('hx', 'hy'), 0, 0, tiled=True).astype(jnp.float32)  16.7 us
    ppermute x4, starting transfers between devices, _send(): return lax.ppermute(value, HEAD_AXES, perm)  14.6 us
    all_to_all x1, waiting for transfers between devices, project(): mine = lax.all_to_all(spread, HEAD_AXES, 0, 0, tiled=True)  12.6 us
    all_to_all x1, starting transfers between devices, code_prefix(): lax.all_to_all(_pack(sums, counts, span, n, head_dim), 'ctx', 0, 0, tiled...  12.3 us
    all_to_all x1, starting transfers between devices, project(): mine = lax.all_to_all(spread, HEAD_AXES, 0, 0, tiled=True)  11.1 us
    all_to_all x1, waiting for transfers between devices, code_prefix(): back = lax.all_to_all(pre.astype(jnp.bfloat16), 'ctx', 0, 0, tiled=True)  7.6 us
    all_to_all x1, starting transfers between devices, code_prefix(): back = lax.all_to_all(pre.astype(jnp.bfloat16), 'ctx', 0, 0, tiled=True)  7.6 us
    all_to_all x1, waiting for transfers between devices, code_prefix(): lax.all_to_all(_pack(sums, counts, span, n, head_dim), 'ctx', 0, 0, tiled...  7.59 us
  transfers between devices with their start and end apart: 9, of which 6 were waited for; matrix products, arithmetic and copies ran while one was open for 14% of the time, Pallas kernels for 0%

profile of v12, /device:TPU:1, one launch (start us, length us, event | category | flops | bytes accessed | tf_op | source)
XLA Modules:
  0.0 126.4 jit_solution(2780757570547254756)
XLA Ops:
  0.0 0.0 copy-start
  0.0 0.0 copy-start.8
  0.0 2.3 %broadcast_in_dim.62 = bf16[16,2,128,128]{3,2,1,0:T(8,128)(2,1)} broadcast(bf16[2,128,128]{2,1,0:T(8,128)(2,1)} %bitcast.53), dimensions={1,2,3} | broadcast | bytes 1114112 | tf_op jit(solution)/shard_map/broadcast_in_dim | solution.py:199
  2.3 11.1 %all-to-all-start = ((bf16[32,128,128]{2,1,0:T(8,128)(2,1)}), bf16[32,128,128]{2,1,0:T(8,128)(2,1)}, u32[]{:S(2)}, u32[]{:S(2)}) async-start(bf16[32,128,128]{2,1,0:T(8,128)(2,1)} %bitcast.49), calls=%async_computation | async-start | bytes 2097152 | tf_op jit(solution)/shard_map/all_to_all | solution.py:202
  13.4 1.9 %dynamic-slice_bitcast_fusion = bf16[128,2048]{1,0:T(8,128)(2,1)} fusion(bf16[1,128,4096]{2,1,0:T(8,128)(2,1)} %param.12, s32[]{:T(128)S(6)} %select_n.76), kind=kLoop, calls=%fused_computation.15 | loop fusion | bytes 1048580 | tf_op jit(solution)/shard_map/dynamic_slice | solution.py:224
  15.3 2.3 %collective-permute-start.3 = (bf16[128,2048]{1,0:T(8,128)(2,1)}, bf16[128,2048]{1,0:T(8,128)(2,1)}, u32[]{:S(2)}, u32[]{:S(2)}) collective-permute-start(bf16[128,2048]{1,0:T(8,128)(2,1)} %dynamic-slice_bitcast_fusion), channel_id=1, source_target_pairs={{0,1},{1,0},{2,3},{3,2},{4,5},{5,4},{6,7},{7,6},{8,9},{9,8},{10,11... | collective-permute-start | bytes 1572872 | tf_op jit(solution)/shard_map/ppermute | solution.py:41
  17.6 0.0 copy-done.8
  17.6 0.1 convert_reduce_fusion.2
  17.8 0.1 reduce_sum.39
  17.9 12.6 %all-to-all-done = bf16[32,128,128]{2,1,0:T(8,128)(2,1)} async-done(((bf16[32,128,128]{2,1,0:T(8,128)(2,1)}), bf16[32,128,128]{2,1,0:T(8,128)(2,1)}, u32[]{:S(2)}, u32[]{:S(2)}) %all-to-all-start) | async-done | bytes 1048608 | tf_op jit(solution)/shard_map/all_to_all | solution.py:202
  30.5 2.0 %collective-permute-start = (bf16[32,128,128]{2,1,0:T(8,128)(2,1)}, bf16[32,128,128]{2,1,0:T(8,128)(2,1)}, u32[]{:S(2)}, u32[]{:S(2)}) collective-permute-start(bf16[32,128,128]{2,1,0:T(8,128)(2,1)} %all-to-all-done), channel_id=1, source_target_pairs={{0,1},{1,0},{2,3},{3,2},{4,5},{5,4},{6,7},{7,6},{8,9},{9,8},{10,11... | collective-permute-start | bytes 3145736 | tf_op jit(solution)/shard_map/ppermute | solution.py:41
  33.2 0.4 scatter.9
  33.6 0.0 copy-done
  33.7 1.9 %convolution_bitcast_fusion.1 = bf16[128,384]{1,0:T(8,128)(2,1)S(1)} fusion(bf16[32,128,128]{2,1,0:T(8,128)(2,1)} %all-to-all-done, bf16[32,128,384]{2,1,0:T(8,128)(2,1)S(1)} %bitcast.46), kind=kOutput, calls=%fused_computation.8 | convolution fusion | flops 402653184 | bytes 4292608 | tf_op jit(solution)/shard_map/dot_general | solution.py:206
  35.6 0.0 collective-permute-done
  35.6 1.9 %convolution_bitcast_fusion = bf16[128,384]{1,0:T(8,128)(2,1)S(1)} fusion(bf16[32,128,128]{2,1,0:T(8,128)(2,1)} %collective-permute-done, bf16[32,128,384]{2,1,0:T(8,128)(2,1)S(1)} %bitcast.47), kind=kOutput, calls=%fused_computation.7 | convolution fusion | flops 402653184 | bytes 4292608 | tf_op jit(solution)/shard_map/dot_general | solution.py:207
  37.6 0.4 convolution_convert_fusion
  38.0 0.7 pad_maximum_fusion
  38.7 12.3 %all-to-all-start.1 = ((bf16[16,40,128]{2,1,0:T(8,128)(2,1)}), bf16[16,40,128]{2,1,0:T(8,128)(2,1)S(1)}, u32[]{:S(2)}, u32[]{:S(2)}) async-start(bf16[16,40,128]{2,1,0:T(8,128)(2,1)} %pad_maximum_fusion), calls=%async_computation.1 | async-start | bytes 327680 | tf_op jit(solution)/shard_map/all_to_all | solution.py:179
  51.1 0.1 pad.20.clone
  51.2 0.0 copy-start.4
  51.2 0.8 maximum_maximum_fusion
  51.9 0.0 copy-done.4
  51.9 3.9 %collective-permute-start.1 = (bf16[272,256]{1,0:T(8,128)(2,1)}, bf16[272,256]{1,0:T(8,128)(2,1)}, u32[]{:S(2)}, u32[]{:S(2)}) collective-permute-start(bf16[272,256]{1,0:T(8,128)(2,1)} %maximum_maximum_fusion), channel_id=1, source_target_pairs={{0,32},{32,64},{64,96},{96,128},{128,160},{160,192},{192,224},{224... | collective-permute-start | bytes 417800 | tf_op jit(solution)/shard_map/ppermute | solution.py:124
  55.8 7.6 %all-to-all-done.1 = bf16[16,40,128]{2,1,0:T(8,128)(2,1)S(1)} async-done(((bf16[16,40,128]{2,1,0:T(8,128)(2,1)}), bf16[16,40,128]{2,1,0:T(8,128)(2,1)S(1)}, u32[]{:S(2)}, u32[]{:S(2)}) %all-to-all-start.1) | async-done | bytes 163872 | tf_op jit(solution)/shard_map/all_to_all | solution.py:179
  63.4 0.2 fusion.33
  63.7 0.2 select_convert_fusion
  63.9 0.7 copy.13
  64.6 7.6 %all-to-all-start.2 = ((bf16[16,40,128]{2,1,0:T(8,128)(2,1)}), bf16[16,40,128]{2,1,0:T(8,128)(2,1)S(1)}, u32[]{:S(2)}, u32[]{:S(2)}) async-start(bf16[16,40,128]{2,1,0:T(8,128)(2,1)} %copy.13), calls=%async_computation.2 | async-start | bytes 327680 | tf_op jit(solution)/shard_map/all_to_all | solution.py:188
  72.2 0.0 collective-permute-done.1
  72.2 0.8 fusion.53
  72.9 0.9 slice.111
  73.9 0.0 copy-start.6
  73.9 0.2 convert_reduce_fusion.1
  74.0 0.5 copy-done.6
  74.5 1.2 select_reduce_fusion.1
  75.7 0.8 copy-done.2
  76.5 0.3 fusion.16
  76.7 7.6 %all-to-all-done.2 = bf16[16,40,128]{2,1,0:T(8,128)(2,1)S(1)} async-done(((bf16[16,40,128]{2,1,0:T(8,128)(2,1)}), bf16[16,40,128]{2,1,0:T(8,128)(2,1)S(1)}, u32[]{:S(2)}, u32[]{:S(2)}) %all-to-all-start.2) | async-done | bytes 163872 | tf_op jit(solution)/shard_map/all_to_all | solution.py:188
  84.4 0.1 add.84
  84.5 0.0 copy-start.3
  84.5 0.0 copy-start.5
  84.5 0.0 copy-start.7
  84.5 0.0 copy-start.1
  84.5 1.3 %select_reduce_fusion = (f32[256]{0:T(256)S(1)}, f32[256,512]{1,0:T(8,128)S(1)}) fusion(pred[512]{0:T(512)(128)(4,1)S(1)} %get-tuple-element.31, bf16[1,512,128]{2,1,0:T(8,128)(2,1)} %param.13, bf16[256,384]{1,0:T(8,128)(2,1)S(1)} %fusion.15), kind=kOutput, calls=%fused_computation.19 | convolution fusion | flops 33947392 | bytes 722432 | tf_op jit(solution)/shard_map/dot_general | solution.py:73
  85.9 1.3 %convolution_add_fusion.1 = f32[512,128]{1,0:T(8,128)S(1)} fusion(f32[512,128]{1,0:T(8,128)S(1)} %bitcast.50, s32[256]{0:T(256)S(1)} %bitcast.55, pred[256]{0:T(512)(128)(4,1)S(1)} %compare_and_fusion, bf16[272,256]{1,0:T(8,128)(2,1)} %collective-permute-done.1), kind=kOutput, calls=%fused_computation.5 | convolution fusion | flops 33882112 | bytes 591104 | tf_op jit(solution)/shard_map/dot_general | solution.py:141
  87.2 0.6 fusion.14
  87.8 0.6 fusion.13
  88.5 0.0 copy-done.3
  88.5 0.0 copy-done.5
  88.5 0.0 copy-done.7
  88.5 0.3 fusion.3
  88.9 6.3 %collective-permute-start.2 = (bf16[256,128]{1,0:T(8,128)(2,1)S(1)}, bf16[256,128]{1,0:T(8,128)(2,1)S(1)}, u32[]{:S(2)}, u32[]{:S(2)}) collective-permute-start(bf16[256,128]{1,0:T(8,128)(2,1)S(1)} %fusion.3), channel_id=1, source_target_pairs={{0,1},{1,0},{2,3},{3,2},{4,5},{5,4},{6,7},{7,6},{8,9},{9,8},{10,11... | collective-permute-start | bytes 196616 | tf_op jit(solution)/shard_map/ppermute | solution.py:41
  95.2 0.0 copy-done.1
  95.2 0.4 fusion.4
  95.6 0.0 collective-permute-done.3
  95.6 0.4 collective-permute-done.2
  96.0 2.4 %fusion = bf16[256,2048]{1,0:T(8,128)(2,1)} fusion(f32[256,2048]{1,0:T(8,128)S(1)} %fusion.4, bf16[256,128]{1,0:T(8,128)(2,1)S(1)} %collective-permute-done.2, bf16[128,2048]{1,0:T(8,128)(2,1)} %collective-permute-done.3), kind=kOutput, calls=%fused_computation.1 | convolution fusion | flops 135266304 | bytes 3735552 | tf_op jit(solution)/shard_map/dot_general | solution.py:229
  98.5 4.4 %all-to-all-start.3 = ((bf16[16,16,2048]{2,1,0:T(8,128)(2,1)}), bf16[16,16,2048]{2,1,0:T(8,128)(2,1)}, u32[]{:S(2)}, u32[]{:S(2)}) async-start(bf16[16,16,2048]{2,1,0:T(8,128)(2,1)} %bitcast.48), calls=%async_computation.3 | async-start | bytes 2097152 | tf_op jit(solution)/shard_map/all_to_all | solution.py:234
  102.8 16.7 %all-to-all-done.3 = bf16[16,16,2048]{2,1,0:T(8,128)(2,1)} async-done(((bf16[16,16,2048]{2,1,0:T(8,128)(2,1)}), bf16[16,16,2048]{2,1,0:T(8,128)(2,1)}, u32[]{:S(2)}, u32[]{:S(2)}) %all-to-all-start.3) | async-done | bytes 1048608 | tf_op jit(solution)/shard_map/all_to_all | solution.py:234
  119.5 1.4 %convert_reduce_fusion = bf16[16,2048]{1,0:T(8,128)(2,1)S(1)} fusion(bf16[16,16,2048]{2,1,0:T(8,128)(2,1)} %all-to-all-done.3), kind=kLoop, calls=%fused_computation.2 | loop fusion | flops 1015808 | bytes 1114112 | tf_op jit(solution)/shard_map/reduce_sum | solution.py:235
  120.9 4.0 %collective-permute-start.4 = (bf16[8,2048]{1,0:T(8,128)(2,1)S(1)}, bf16[8,2048]{1,0:T(8,128)(2,1)S(1)}, u32[]{:S(2)}, u32[]{:S(2)}) collective-permute-start(bf16[8,2048]{1,0:T(8,128)(2,1)S(1)} %get-tuple-element.38), channel_id=1, source_target_pairs={{0,1},{1,0},{2,3},{3,2},{4,5},{5,4},{6,7},{7,6},{8,9},{9,8},{10,11... | collective-permute-start | bytes 98312 | tf_op jit(solution)/shard_map/ppermute | solution.py:41
  124.9 0.8 collective-permute-done.4
  125.7 0.6 fusion.38
  (22 shorter events, 0.3 us)
Async XLA Ops:
  0.0 33.6 %copy-start = (bf16[4096,1,384]{2,0,1:T(8,128)(2,1)S(1)}, bf16[4096,1,384]{2,0,1:T(8,128)(2,1)}, u32[]{:S(2)}) copy-start(bf16[4096,1,384]{2,0,1:T(8,128)(2,1)} %param.11) | copy-start | bytes 9437188
  0.0 17.6 %copy-start.8 = (s32[1,256]{1,0:T(1,128)S(1)}, s32[1,256]{1,0:T(1,128)}, u32[]{:S(2)}) copy-start(s32[1,256]{1,0:T(1,128)} %param.14) | copy-start | bytes 3076
  2.3 28.2 %all-to-all-start = ((bf16[32,128,128]{2,1,0:T(8,128)(2,1)}), bf16[32,128,128]{2,1,0:T(8,128)(2,1)}, u32[]{:S(2)}, u32[]{:S(2)}) async-start(bf16[32,128,128]{2,1,0:T(8,128)(2,1)} %bitcast.49), calls=%async_computation | async-start | bytes 2097152 | tf_op jit(solution)/shard_map/all_to_all | solution.py:202
  15.3 80.3 %collective-permute-start.3 = (bf16[128,2048]{1,0:T(8,128)(2,1)}, bf16[128,2048]{1,0:T(8,128)(2,1)}, u32[]{:S(2)}, u32[]{:S(2)}) collective-permute-start(bf16[128,2048]{1,0:T(8,128)(2,1)} %dynamic-slice_bitcast_fusion), channel_id=1, source_target_pairs={{0,1},{1,0},{2,3},{3,2},{4,5},{5,4},{6,7},{7,6},{8,9},{9,8},{10,11... | collective-permute-start | bytes 1572872 | tf_op jit(solution)/shard_map/ppermute | solution.py:41
  30.5 5.1 %collective-permute-start = (bf16[32,128,128]{2,1,0:T(8,128)(2,1)}, bf16[32,128,128]{2,1,0:T(8,128)(2,1)}, u32[]{:S(2)}, u32[]{:S(2)}) collective-permute-start(bf16[32,128,128]{2,1,0:T(8,128)(2,1)} %all-to-all-done), channel_id=1, source_target_pairs={{0,1},{1,0},{2,3},{3,2},{4,5},{5,4},{6,7},{7,6},{8,9},{9,8},{10,11... | collective-permute-start | bytes 3145736 | tf_op jit(solution)/shard_map/ppermute | solution.py:41
  38.7 24.7 %all-to-all-start.1 = ((bf16[16,40,128]{2,1,0:T(8,128)(2,1)}), bf16[16,40,128]{2,1,0:T(8,128)(2,1)S(1)}, u32[]{:S(2)}, u32[]{:S(2)}) async-start(bf16[16,40,128]{2,1,0:T(8,128)(2,1)} %pad_maximum_fusion), calls=%async_computation.1 | async-start | bytes 327680 | tf_op jit(solution)/shard_map/all_to_all | solution.py:179
  51.2 0.8 copy-start.4
  51.9 20.2 %collective-permute-start.1 = (bf16[272,256]{1,0:T(8,128)(2,1)}, bf16[272,256]{1,0:T(8,128)(2,1)}, u32[]{:S(2)}, u32[]{:S(2)}) collective-permute-start(bf16[272,256]{1,0:T(8,128)(2,1)} %maximum_maximum_fusion), channel_id=1, source_target_pairs={{0,32},{32,64},{64,96},{96,128},{128,160},{160,192},{192,224},{224... | collective-permute-start | bytes 417800 | tf_op jit(solution)/shard_map/ppermute | solution.py:124
  64.6 19.8 %all-to-all-start.2 = ((bf16[16,40,128]{2,1,0:T(8,128)(2,1)}), bf16[16,40,128]{2,1,0:T(8,128)(2,1)S(1)}, u32[]{:S(2)}, u32[]{:S(2)}) async-start(bf16[16,40,128]{2,1,0:T(8,128)(2,1)} %copy.13), calls=%async_computation.2 | async-start | bytes 327680 | tf_op jit(solution)/shard_map/all_to_all | solution.py:188
  73.9 0.6 copy-start.6
  75.7 0.8 copy-start.2
  84.5 4.0 %copy-start.3 = (f32[256,512]{1,0:T(8,128)S(1)}, f32[256,512]{1,0:T(8,128)}, u32[]{:S(2)}) copy-start(f32[256,512]{1,0:T(8,128)} %copy-done.2) | copy-start | bytes 1572868
  84.5 4.0 %copy-start.5 = (bf16[256,256]{1,0:T(8,128)(2,1)S(1)}, bf16[256,256]{1,0:T(8,128)(2,1)}, u32[]{:S(2)}) copy-start(bf16[256,256]{1,0:T(8,128)(2,1)} %copy-done.4) | copy-start | bytes 393220
  84.5 4.0 %copy-start.7 = (bf16[256,256]{1,0:T(8,128)(2,1)S(1)}, bf16[256,256]{1,0:T(8,128)(2,1)}, u32[]{:S(2)}) copy-start(bf16[256,256]{1,0:T(8,128)(2,1)} %copy-done.6) | copy-start | bytes 393220
  84.5 10.7 %copy-start.1 = (bf16[1,128,4096]{2,1,0:T(8,128)(2,1)S(1)}, bf16[1,128,4096]{2,1,0:T(8,128)(2,1)}, u32[]{:S(2)}) copy-start(bf16[1,128,4096]{2,1,0:T(8,128)(2,1)} %param.12) | copy-start | bytes 3145732
  88.9 7.2 %collective-permute-start.2 = (bf16[256,128]{1,0:T(8,128)(2,1)S(1)}, bf16[256,128]{1,0:T(8,128)(2,1)S(1)}, u32[]{:S(2)}, u32[]{:S(2)}) collective-permute-start(bf16[256,128]{1,0:T(8,128)(2,1)S(1)} %fusion.3), channel_id=1, source_target_pairs={{0,1},{1,0},{2,3},{3,2},{4,5},{5,4},{6,7},{7,6},{8,9},{9,8},{10,11... | collective-permute-start | bytes 196616 | tf_op jit(solution)/shard_map/ppermute | solution.py:41
  98.5 21.0 %all-to-all-start.3 = ((bf16[16,16,2048]{2,1,0:T(8,128)(2,1)}), bf16[16,16,2048]{2,1,0:T(8,128)(2,1)}, u32[]{:S(2)}, u32[]{:S(2)}) async-start(bf16[16,16,2048]{2,1,0:T(8,128)(2,1)} %bitcast.48), calls=%async_computation.3 | async-start | bytes 2097152 | tf_op jit(solution)/shard_map/all_to_all | solution.py:234
  120.9 4.8 %collective-permute-start.4 = (bf16[8,2048]{1,0:T(8,128)(2,1)S(1)}, bf16[8,2048]{1,0:T(8,128)(2,1)S(1)}, u32[]{:S(2)}, u32[]{:S(2)}) collective-permute-start(bf16[8,2048]{1,0:T(8,128)(2,1)S(1)} %get-tuple-element.38), channel_id=1, source_target_pairs={{0,1},{1,0},{2,3},{3,2},{4,5},{5,4},{6,7},{7,6},{8,9},{9,8},{10,11... | collective-permute-start | bytes 98312 | tf_op jit(solution)/shard_map/ppermute | solution.py:41

commit v13 on v10

--- a/solution.py
+++ b/solution.py
@@ -202,14 +202,11 @@
     mine = lax.all_to_all(spread, HEAD_AXES, 0, 0, tiled=True)
     theirs = _send(mine, core_perm)
     w_local = w_qkv[:, 0, :].reshape(n_head, width, -1)
+    both = jnp.where(
+        me_c == 0, jnp.concatenate([mine, theirs], axis=1), jnp.concatenate([theirs, mine], axis=1)
+    )
     dims = (((0, 2), (0, 1)), ((), ()))
-    proj_own = lax.dot_general(mine, w_local, dims, preferred_element_type=jnp.float32)
-    proj_oth = lax.dot_general(theirs, w_local, dims, preferred_element_type=jnp.float32)
-    projected = jnp.where(
-        me_c == 0,
-        jnp.concatenate([proj_own, proj_oth], axis=0),
-        jnp.concatenate([proj_oth, proj_own], axis=0),
-    )
+    projected = lax.dot_general(both, w_local, dims, preferred_element_type=jnp.float32)
     return projected
 
 

time: 121 us -> 126 us (1.041)
  waiting for transfers between devices: 28.2 us -> 32.1 us
  local copies, waits for them, and re-layouts: 7.71 us -> 9.29 us
    all_to_all x1, waiting for transfers between devices: 12.6 us -> 17 us  [project(): mine = lax.all_to_all(spread, HEAD_AXES, 0, 0, tiled=True)]
    dot_general x2 -> x1, matrix products: 3.88 us -> 3.58 us  [project(): lax.dot_general(both, w_local, dims, preferred_element_type=jnp.float32)]
where the time goes in v13:
time: 126 us; the launch traced here: 125 us
  starting transfers between devices  45.2 us (36%)
  waiting for transfers between devices  32.1 us (25%)
  blocking collectives  20.7 us (16%)
  matrix products  11.6 us (9%)
  local copies, waits for them, and re-layouts  9.29 us (7%)
  other arithmetic  5.13 us (4%)
    all_to_all x1, blocking collectives, reduce_out(): lax.all_to_all(chunks, HEAD_AXES, 0, 0, tiled=True).astype(jnp.float32)  20.7 us
    all_to_all x1, waiting for transfers between devices, project(): mine = lax.all_to_all(spread, HEAD_AXES, 0, 0, tiled=True)  17 us
    all_to_all x1, starting transfers between devices, code_prefix(): lax.all_to_all(_pack(sums, counts, span, n, head_dim), 'ctx', 0, 0, tiled...  12.3 us
    all_to_all x1, starting transfers between devices, project(): mine = lax.all_to_all(spread, HEAD_AXES, 0, 0, tiled=True)  11.1 us
    ppermute x3, starting transfers between devices, _send(): return lax.ppermute(value, HEAD_AXES, perm)  10.6 us
    all_to_all x1, waiting for transfers between devices, code_prefix(): back = lax.all_to_all(pre.astype(jnp.bfloat16), 'ctx', 0, 0, tiled=True)  7.63 us
    all_to_all x1, starting transfers between devices, code_prefix(): back = lax.all_to_all(pre.astype(jnp.bfloat16), 'ctx', 0, 0, tiled=True)  7.26 us
    all_to_all x1, waiting for transfers between devices, code_prefix(): lax.all_to_all(_pack(sums, counts, span, n, head_dim), 'ctx', 0, 0, tiled...  7.02 us
  transfers between devices with their start and end apart: 7, of which 4 were waited for; matrix products, arithmetic and copies ran while one was open for 15% of the time, Pallas kernels for 0%

profile of v13, /device:TPU:1, one launch (start us, length us, event | category | flops | bytes accessed | tf_op | source)
XLA Modules:
  0.0 125.1 jit_solution(618177260754850629)
XLA Ops:
  0.0 0.0 copy-start
  0.0 0.0 copy-start.7
  0.0 2.3 %broadcast_in_dim.62 = bf16[16,2,128,128]{3,2,1,0:T(8,128)(2,1)} broadcast(bf16[2,128,128]{2,1,0:T(8,128)(2,1)} %bitcast.49), dimensions={1,2,3} | broadcast | bytes 1114112 | tf_op jit(solution)/shard_map/broadcast_in_dim | solution.py:199
  2.3 11.1 %all-to-all-start = ((bf16[32,128,128]{2,1,0:T(8,128)(2,1)}), bf16[32,128,128]{2,1,0:T(8,128)(2,1)}, u32[]{:S(2)}, u32[]{:S(2)}) async-start(bf16[32,128,128]{2,1,0:T(8,128)(2,1)} %bitcast.45), calls=%async_computation | async-start | bytes 2097152 | tf_op jit(solution)/shard_map/all_to_all | solution.py:202
  13.4 17.0 %all-to-all-done = bf16[32,128,128]{2,1,0:T(8,128)(2,1)} async-done(((bf16[32,128,128]{2,1,0:T(8,128)(2,1)}), bf16[32,128,128]{2,1,0:T(8,128)(2,1)}, u32[]{:S(2)}, u32[]{:S(2)}) %all-to-all-start) | async-done | bytes 1048608 | tf_op jit(solution)/shard_map/all_to_all | solution.py:202
  30.5 2.0 %collective-permute-start = (bf16[32,128,128]{2,1,0:T(8,128)(2,1)}, bf16[32,128,128]{2,1,0:T(8,128)(2,1)}, u32[]{:S(2)}, u32[]{:S(2)}) collective-permute-start(bf16[32,128,128]{2,1,0:T(8,128)(2,1)} %all-to-all-done), channel_id=1, source_target_pairs={{0,1},{1,0},{2,3},{3,2},{4,5},{5,4},{6,7},{7,6},{8,9},{9,8},{10,11... | collective-permute-start | bytes 3145736 | tf_op jit(solution)/shard_map/ppermute | solution.py:41
  32.5 1.9 %dynamic-slice_bitcast_fusion = bf16[128,2048]{1,0:T(8,128)(2,1)} fusion(bf16[1,128,4096]{2,1,0:T(8,128)(2,1)} %param.12, s32[]{:T(128)S(6)} %select_n.60), kind=kLoop, calls=%fused_computation.23 | loop fusion | bytes 1048580 | tf_op jit(solution)/shard_map/dynamic_slice | solution.py:221
  34.4 2.3 %collective-permute-start.3 = (bf16[128,2048]{1,0:T(8,128)(2,1)}, bf16[128,2048]{1,0:T(8,128)(2,1)}, u32[]{:S(2)}, u32[]{:S(2)}) collective-permute-start(bf16[128,2048]{1,0:T(8,128)(2,1)} %dynamic-slice_bitcast_fusion), channel_id=1, source_target_pairs={{0,1},{1,0},{2,3},{3,2},{4,5},{5,4},{6,7},{7,6},{8,9},{9,8},{10,11... | collective-permute-start | bytes 1572872 | tf_op jit(solution)/shard_map/ppermute | solution.py:41
  37.3 0.0 copy-done.7
  37.4 0.1 convert_reduce_fusion.1
  37.5 0.1 reduce_sum.39
  37.6 0.4 scatter.9
  38.1 0.0 collective-permute-done
  38.1 0.0 copy-done
  38.1 3.6 %fusion.10 = bf16[256,384]{1,0:T(8,128)(2,1)S(1)} fusion(bf16[32,128,384]{2,1,0:T(8,128)(2,1)S(1)} %bitcast.44, bf16[32,128,128]{2,1,0:T(8,128)(2,1)} %collective-permute-done, bf16[32,128,128]{2,1,0:T(8,128)(2,1)} %all-to-all-done, pred[]{:T(512)S(6)} %eq.47), kind=kOutput, calls=%fused_computation.14 | convolution fusion | flops 814841856 | bytes 5439489 | tf_op jit(solution)/shard_map/dot_general | solution.py:209
  41.7 0.0 copy-start.4
  41.7 0.7 copy-done.4
  42.3 0.4 convolution_convert_fusion
  42.7 0.7 pad_maximum_fusion
  43.4 12.3 %all-to-all-start.1 = ((bf16[16,40,128]{2,1,0:T(8,128)(2,1)}), bf16[16,40,128]{2,1,0:T(8,128)(2,1)S(1)}, u32[]{:S(2)}, u32[]{:S(2)}) async-start(bf16[16,40,128]{2,1,0:T(8,128)(2,1)} %pad_maximum_fusion), calls=%async_computation.1 | async-start | bytes 327680 | tf_op jit(solution)/shard_map/all_to_all | solution.py:179
  55.8 0.1 pad.18.clone
  55.9 0.9 slice.120
  56.8 0.8 maximum_maximum_fusion
  57.6 3.9 %collective-permute-start.1 = (bf16[272,256]{1,0:T(8,128)(2,1)}, bf16[272,256]{1,0:T(8,128)(2,1)}, u32[]{:S(2)}, u32[]{:S(2)}) collective-permute-start(bf16[272,256]{1,0:T(8,128)(2,1)} %maximum_maximum_fusion), channel_id=1, source_target_pairs={{0,32},{32,64},{64,96},{96,128},{128,160},{160,192},{192,224},{224... | collective-permute-start | bytes 417800 | tf_op jit(solution)/shard_map/ppermute | solution.py:124
  61.5 7.0 %all-to-all-done.1 = bf16[16,40,128]{2,1,0:T(8,128)(2,1)S(1)} async-done(((bf16[16,40,128]{2,1,0:T(8,128)(2,1)}), bf16[16,40,128]{2,1,0:T(8,128)(2,1)S(1)}, u32[]{:S(2)}, u32[]{:S(2)}) %all-to-all-start.1) | async-done | bytes 163872 | tf_op jit(solution)/shard_map/all_to_all | solution.py:179
  68.5 0.2 fusion.42
  68.8 0.2 select_convert_fusion
  68.9 0.7 copy.13
  69.7 7.3 %all-to-all-start.2 = ((bf16[16,40,128]{2,1,0:T(8,128)(2,1)}), bf16[16,40,128]{2,1,0:T(8,128)(2,1)S(1)}, u32[]{:S(2)}, u32[]{:S(2)}) async-start(bf16[16,40,128]{2,1,0:T(8,128)(2,1)} %copy.13), calls=%async_computation.2 | async-start | bytes 327680 | tf_op jit(solution)/shard_map/all_to_all | solution.py:188
  76.9 0.0 collective-permute-done.1
  76.9 0.8 fusion.60
  77.7 0.9 slice.121
  78.6 0.0 copy-start.5
  78.6 0.2 convert_reduce_fusion
  78.8 0.5 copy-done.5
  79.3 1.2 select_reduce_fusion.1
  80.4 0.0 copy-start.2
  80.4 0.8 copy-done.2
  81.2 0.3 fusion.25
  81.5 7.6 %all-to-all-done.2 = bf16[16,40,128]{2,1,0:T(8,128)(2,1)S(1)} async-done(((bf16[16,40,128]{2,1,0:T(8,128)(2,1)}), bf16[16,40,128]{2,1,0:T(8,128)(2,1)S(1)}, u32[]{:S(2)}, u32[]{:S(2)}) %all-to-all-start.2) | async-done | bytes 163872 | tf_op jit(solution)/shard_map/all_to_all | solution.py:188
  89.2 0.1 add.76
  89.3 0.0 copy-start.3
  89.3 0.0 copy-start.6
  89.3 1.3 %select_reduce_fusion = (f32[256]{0:T(256)S(1)}, f32[256,512]{1,0:T(8,128)S(1)}) fusion(pred[512]{0:T(512)(128)(4,1)S(1)} %get-tuple-element.31, bf16[1,512,128]{2,1,0:T(8,128)(2,1)} %param.13, bf16[256,384]{1,0:T(8,128)(2,1)} %copy-done.4), kind=kOutput, calls=%fused_computation.27 | convolution fusion | flops 33947392 | bytes 722432 | tf_op jit(solution)/shard_map/dot_general | solution.py:73
  90.6 0.0 copy-start.1
  90.6 1.4 %convolution_add_fusion.1 = f32[512,128]{1,0:T(8,128)S(1)} fusion(f32[512,128]{1,0:T(8,128)S(1)} %bitcast.47, s32[256]{0:T(256)S(1)} %bitcast.51, pred[256]{0:T(512)(128)(4,1)S(1)} %compare_and_fusion, bf16[272,256]{1,0:T(8,128)(2,1)} %collective-permute-done.1), kind=kOutput, calls=%fused_computation.15 | convolution fusion | flops 33882112 | bytes 591104 | tf_op jit(solution)/shard_map/dot_general | solution.py:141
  92.0 0.6 fusion.24
  92.7 0.6 fusion.23
  93.3 0.0 copy-done.3
  93.3 0.0 copy-done.6
  93.3 0.3 fusion.13
  93.7 6.3 %collective-permute-start.2 = (bf16[256,128]{1,0:T(8,128)(2,1)S(1)}, bf16[256,128]{1,0:T(8,128)(2,1)S(1)}, u32[]{:S(2)}, u32[]{:S(2)}) collective-permute-start(bf16[256,128]{1,0:T(8,128)(2,1)S(1)} %fusion.13), channel_id=1, source_target_pairs={{0,1},{1,0},{2,3},{3,2},{4,5},{5,4},{6,7},{7,6},{8,9},{9,8},{10,11... | collective-permute-start | bytes 196616 | tf_op jit(solution)/shard_map/ppermute | solution.py:41
  100.0 0.0 copy-done.1
  100.0 0.4 fusion.14
  100.4 0.0 collective-permute-done.3
  100.4 0.4 collective-permute-done.2
  100.9 1.5 %fusion.1 = bf16[32,8,2048]{2,1,0:T(8,128)(2,1)S(1)} fusion(f32[256,2048]{1,0:T(8,128)S(1)} %fusion.14, bf16[256,128]{1,0:T(8,128)(2,1)S(1)} %collective-permute-done.2, bf16[128,2048]{1,0:T(8,128)(2,1)} %collective-permute-done.3), kind=kOutput, calls=%fused_computation.2 | convolution fusion | flops 135266304 | bytes 3735552 | tf_op jit(solution)/shard_map/dot_general | solution.py:226
  102.3 20.7 %all_to_all.20 = bf16[32,8,2048]{2,1,0:T(8,128)(2,1)} all-to-all(bf16[32,8,2048]{2,1,0:T(8,128)(2,1)S(1)} %fusion.1), channel_id=1, replica_groups=mesh['ctx'=16,'hx'=4,'hy'=4,'hc'=2] {'hx','hy','hc'}, dimensions={0} | all-to-all | bytes 2097152 | tf_op jit(solution)/shard_map/all_to_all | solution.py:230
  123.0 1.4 %reduce.4 = bf16[2,8,2048]{2,1,0:T(8,128)(2,1)S(1)} reduce(bf16[16,2,8,2048]{3,2,1,0:T(8,128)(2,1)} %bitcast.46, bf16[]{:T(256)} %constant.126.clone.1), dimensions={0}, to_apply=%region_5.6.clone | reduce | flops 491520 | bytes 1114114 | tf_op jit(solution)/shard_map/reduce_sum | solution.py:231
  124.4 0.6 pad_maximum_fusion.3
  (19 shorter events, 0.2 us)
Async XLA Ops:
  0.0 38.1 %copy-start = (bf16[4096,1,384]{2,0,1:T(8,128)(2,1)S(1)}, bf16[4096,1,384]{2,0,1:T(8,128)(2,1)}, u32[]{:S(2)}) copy-start(bf16[4096,1,384]{2,0,1:T(8,128)(2,1)} %param.11) | copy-start | bytes 9437188
  0.0 37.3 %copy-start.7 = (s32[1,256]{1,0:T(1,128)S(1)}, s32[1,256]{1,0:T(1,128)}, u32[]{:S(2)}) copy-start(s32[1,256]{1,0:T(1,128)} %param.14) | copy-start | bytes 3076
  2.3 28.2 %all-to-all-start = ((bf16[32,128,128]{2,1,0:T(8,128)(2,1)}), bf16[32,128,128]{2,1,0:T(8,128)(2,1)}, u32[]{:S(2)}, u32[]{:S(2)}) async-start(bf16[32,128,128]{2,1,0:T(8,128)(2,1)} %bitcast.45), calls=%async_computation | async-start | bytes 2097152 | tf_op jit(solution)/shard_map/all_to_all | solution.py:202
  30.5 7.6 %collective-permute-start = (bf16[32,128,128]{2,1,0:T(8,128)(2,1)}, bf16[32,128,128]{2,1,0:T(8,128)(2,1)}, u32[]{:S(2)}, u32[]{:S(2)}) collective-permute-start(bf16[32,128,128]{2,1,0:T(8,128)(2,1)} %all-to-all-done), channel_id=1, source_target_pairs={{0,1},{1,0},{2,3},{3,2},{4,5},{5,4},{6,7},{7,6},{8,9},{9,8},{10,11... | collective-permute-start | bytes 3145736 | tf_op jit(solution)/shard_map/ppermute | solution.py:41
  34.4 66.0 %collective-permute-start.3 = (bf16[128,2048]{1,0:T(8,128)(2,1)}, bf16[128,2048]{1,0:T(8,128)(2,1)}, u32[]{:S(2)}, u32[]{:S(2)}) collective-permute-start(bf16[128,2048]{1,0:T(8,128)(2,1)} %dynamic-slice_bitcast_fusion), channel_id=1, source_target_pairs={{0,1},{1,0},{2,3},{3,2},{4,5},{5,4},{6,7},{7,6},{8,9},{9,8},{10,11... | collective-permute-start | bytes 1572872 | tf_op jit(solution)/shard_map/ppermute | solution.py:41
  41.7 0.7 copy-start.4
  43.4 25.1 %all-to-all-start.1 = ((bf16[16,40,128]{2,1,0:T(8,128)(2,1)}), bf16[16,40,128]{2,1,0:T(8,128)(2,1)S(1)}, u32[]{:S(2)}, u32[]{:S(2)}) async-start(bf16[16,40,128]{2,1,0:T(8,128)(2,1)} %pad_maximum_fusion), calls=%async_computation.1 | async-start | bytes 327680 | tf_op jit(solution)/shard_map/all_to_all | solution.py:179
  57.6 19.3 %collective-permute-start.1 = (bf16[272,256]{1,0:T(8,128)(2,1)}, bf16[272,256]{1,0:T(8,128)(2,1)}, u32[]{:S(2)}, u32[]{:S(2)}) collective-permute-start(bf16[272,256]{1,0:T(8,128)(2,1)} %maximum_maximum_fusion), channel_id=1, source_target_pairs={{0,32},{32,64},{64,96},{96,128},{128,160},{160,192},{192,224},{224... | collective-permute-start | bytes 417800 | tf_op jit(solution)/shard_map/ppermute | solution.py:124
  69.7 19.5 %all-to-all-start.2 = ((bf16[16,40,128]{2,1,0:T(8,128)(2,1)}), bf16[16,40,128]{2,1,0:T(8,128)(2,1)S(1)}, u32[]{:S(2)}, u32[]{:S(2)}) async-start(bf16[16,40,128]{2,1,0:T(8,128)(2,1)} %copy.13), calls=%async_computation.2 | async-start | bytes 327680 | tf_op jit(solution)/shard_map/all_to_all | solution.py:188
  78.6 0.6 copy-start.5
  80.4 0.8 copy-start.2
  89.3 4.1 %copy-start.3 = (f32[256,512]{1,0:T(8,128)S(1)}, f32[256,512]{1,0:T(8,128)}, u32[]{:S(2)}) copy-start(f32[256,512]{1,0:T(8,128)} %copy-done.2) | copy-start | bytes 1572868
  89.3 4.1 %copy-start.6 = (bf16[256,256]{1,0:T(8,128)(2,1)S(1)}, bf16[256,256]{1,0:T(8,128)(2,1)}, u32[]{:S(2)}) copy-start(bf16[256,256]{1,0:T(8,128)(2,1)} %copy-done.5) | copy-start | bytes 393220
  90.6 9.4 %copy-start.1 = (bf16[1,128,4096]{2,1,0:T(8,128)(2,1)S(1)}, bf16[1,128,4096]{2,1,0:T(8,128)(2,1)}, u32[]{:S(2)}) copy-start(bf16[1,128,4096]{2,1,0:T(8,128)(2,1)} %param.12) | copy-start | bytes 3145732
  93.7 7.2 %collective-permute-start.2 = (bf16[256,128]{1,0:T(8,128)(2,1)S(1)}, bf16[256,128]{1,0:T(8,128)(2,1)S(1)}, u32[]{:S(2)}, u32[]{:S(2)}) collective-permute-start(bf16[256,128]{1,0:T(8,128)(2,1)S(1)} %fusion.13), channel_id=1, source_target_pairs={{0,1},{1,0},{2,3},{3,2},{4,5},{5,4},{6,7},{7,6},{8,9},{9,8},{10,11... | collective-permute-start | bytes 196616 | tf_op jit(solution)/shard_map/ppermute | solution.py:41

commit v14 on v10

--- a/solution.py
+++ b/solution.py
@@ -224,15 +224,15 @@
     w_give = lax.dynamic_slice_in_dim(w_full, (1 - me_c) * cols, cols, 1)
     w_theirs = _send(w_give, core_perm)
     att_theirs = _send(attended, core_perm)
-    summed = (
-        jnp.dot(attended, w_keep, preferred_element_type=jnp.float32)
-        + jnp.dot(att_theirs, w_theirs, preferred_element_type=jnp.float32)
-    ).astype(jnp.bfloat16)
+    own = lax.optimization_barrier(jnp.dot(attended, w_keep, preferred_element_type=jnp.float32))
+    summed = (own + jnp.dot(att_theirs, w_theirs, preferred_element_type=jnp.float32)).astype(
+        jnp.bfloat16
+    )
     n_head = nx * ny * nc
     chunks = summed.reshape(n_head, rows // n_head, cols)
     parts = lax.all_to_all(chunks, HEAD_AXES, 0, 0, tiled=True).astype(jnp.float32)
     parts = parts.reshape(n_head // nc, nc, rows // n_head, cols).sum(axis=0)
-    out = jnp.concatenate([parts[i] for i in range(nc)], axis=1)
+    out = parts.transpose(1, 0, 2).reshape(rows // n_head, nc * cols)
     return out.astype(jnp.bfloat16)
 
 

time: 121 us -> 122 us (level)
  no operation moved by 1% of the time
where the time goes in v14:
time: 122 us; the launch traced here: 121 us
  starting transfers between devices  45.6 us (37%)
  waiting for transfers between devices  28.2 us (23%)
  blocking collectives  21.1 us (17%)
  matrix products  11.8 us (10%)
  local copies, waits for them, and re-layouts  7.73 us (6%)
  other arithmetic  5.17 us (4%)
    all_to_all x1, blocking collectives, reduce_out(): lax.all_to_all(chunks, HEAD_AXES, 0, 0, tiled=True).astype(jnp.float32)  21.1 us
    all_to_all x1, waiting for transfers between devices, project(): mine = lax.all_to_all(spread, HEAD_AXES, 0, 0, tiled=True)  12.6 us
    all_to_all x1, starting transfers between devices, code_prefix(): lax.all_to_all(_pack(sums, counts, span, n, head_dim), 'ctx', 0, 0, tiled...  12.3 us
    all_to_all x1, starting transfers between devices, project(): mine = lax.all_to_all(spread, HEAD_AXES, 0, 0, tiled=True)  11.1 us
    ppermute x3, starting transfers between devices, _send(): return lax.ppermute(value, HEAD_AXES, perm)  10.6 us
    all_to_all x1, waiting for transfers between devices, code_prefix(): back = lax.all_to_all(pre.astype(jnp.bfloat16), 'ctx', 0, 0, tiled=True)  7.6 us
    all_to_all x1, starting transfers between devices, code_prefix(): back = lax.all_to_all(pre.astype(jnp.bfloat16), 'ctx', 0, 0, tiled=True)  7.6 us
    all_to_all x1, waiting for transfers between devices, code_prefix(): lax.all_to_all(_pack(sums, counts, span, n, head_dim), 'ctx', 0, 0, tiled...  7.57 us
  transfers between devices with their start and end apart: 7, of which 4 were waited for; matrix products, arithmetic and copies ran while one was open for 15% of the time, Pallas kernels for 0%

profile of v14, /device:TPU:1, one launch (start us, length us, event | category | flops | bytes accessed | tf_op | source)
XLA Modules:
  0.0 120.6 jit_solution(5134390794313150004)
XLA Ops:
  0.0 0.0 copy-start
  0.0 0.0 copy-start.8
  0.0 2.3 %broadcast_in_dim.62 = bf16[16,2,128,128]{3,2,1,0:T(8,128)(2,1)} broadcast(bf16[2,128,128]{2,1,0:T(8,128)(2,1)} %bitcast.52), dimensions={1,2,3} | broadcast | bytes 1114112 | tf_op jit(solution)/shard_map/broadcast_in_dim | solution.py:199
  2.3 11.1 %all-to-all-start = ((bf16[32,128,128]{2,1,0:T(8,128)(2,1)}), bf16[32,128,128]{2,1,0:T(8,128)(2,1)}, u32[]{:S(2)}, u32[]{:S(2)}) async-start(bf16[32,128,128]{2,1,0:T(8,128)(2,1)} %bitcast.48), calls=%async_computation | async-start | bytes 2097152 | tf_op jit(solution)/shard_map/all_to_all | solution.py:202
  13.4 1.9 %dynamic-slice_bitcast_fusion = bf16[128,2048]{1,0:T(8,128)(2,1)} fusion(bf16[1,128,4096]{2,1,0:T(8,128)(2,1)} %param.12, s32[]{:T(128)S(6)} %select_n.60), kind=kLoop, calls=%fused_computation.15 | loop fusion | bytes 1048580 | tf_op jit(solution)/shard_map/dynamic_slice | solution.py:224
  15.3 2.3 %collective-permute-start.3 = (bf16[128,2048]{1,0:T(8,128)(2,1)}, bf16[128,2048]{1,0:T(8,128)(2,1)}, u32[]{:S(2)}, u32[]{:S(2)}) collective-permute-start(bf16[128,2048]{1,0:T(8,128)(2,1)} %dynamic-slice_bitcast_fusion), channel_id=1, source_target_pairs={{0,1},{1,0},{2,3},{3,2},{4,5},{5,4},{6,7},{7,6},{8,9},{9,8},{10,11... | collective-permute-start | bytes 1572872 | tf_op jit(solution)/shard_map/ppermute | solution.py:41
  17.6 0.0 copy-done.8
  17.7 0.1 convert_reduce_fusion.1
  17.8 0.1 reduce_sum.39
  17.9 12.6 %all-to-all-done = bf16[32,128,128]{2,1,0:T(8,128)(2,1)} async-done(((bf16[32,128,128]{2,1,0:T(8,128)(2,1)}), bf16[32,128,128]{2,1,0:T(8,128)(2,1)}, u32[]{:S(2)}, u32[]{:S(2)}) %all-to-all-start) | async-done | bytes 1048608 | tf_op jit(solution)/shard_map/all_to_all | solution.py:202
  30.5 2.0 %collective-permute-start = (bf16[32,128,128]{2,1,0:T(8,128)(2,1)}, bf16[32,128,128]{2,1,0:T(8,128)(2,1)}, u32[]{:S(2)}, u32[]{:S(2)}) collective-permute-start(bf16[32,128,128]{2,1,0:T(8,128)(2,1)} %all-to-all-done), channel_id=1, source_target_pairs={{0,1},{1,0},{2,3},{3,2},{4,5},{5,4},{6,7},{7,6},{8,9},{9,8},{10,11... | collective-permute-start | bytes 3145736 | tf_op jit(solution)/shard_map/ppermute | solution.py:41
  33.2 0.4 scatter.9
  33.7 0.0 copy-done
  33.7 1.9 %convolution_bitcast_fusion.1 = bf16[128,384]{1,0:T(8,128)(2,1)S(1)} fusion(bf16[32,128,128]{2,1,0:T(8,128)(2,1)} %all-to-all-done, bf16[32,128,384]{2,1,0:T(8,128)(2,1)S(1)} %bitcast.46), kind=kOutput, calls=%fused_computation.8 | convolution fusion | flops 402653184 | bytes 4292608 | tf_op jit(solution)/shard_map/dot_general | solution.py:206
  35.6 0.0 collective-permute-done
  35.6 1.9 %convolution_bitcast_fusion = bf16[128,384]{1,0:T(8,128)(2,1)S(1)} fusion(bf16[32,128,128]{2,1,0:T(8,128)(2,1)} %collective-permute-done, bf16[32,128,384]{2,1,0:T(8,128)(2,1)S(1)} %bitcast.47), kind=kOutput, calls=%fused_computation.7 | convolution fusion | flops 402653184 | bytes 4292608 | tf_op jit(solution)/shard_map/dot_general | solution.py:207
  37.6 0.4 convolution_convert_fusion
  38.0 0.7 pad_maximum_fusion
  38.7 12.3 %all-to-all-start.1 = ((bf16[16,40,128]{2,1,0:T(8,128)(2,1)}), bf16[16,40,128]{2,1,0:T(8,128)(2,1)S(1)}, u32[]{:S(2)}, u32[]{:S(2)}) async-start(bf16[16,40,128]{2,1,0:T(8,128)(2,1)} %pad_maximum_fusion), calls=%async_computation.1 | async-start | bytes 327680 | tf_op jit(solution)/shard_map/all_to_all | solution.py:179
  51.1 0.1 pad.16.clone
  51.2 0.0 copy-start.4
  51.2 0.8 maximum_maximum_fusion
  52.0 0.0 copy-done.4
  52.0 3.9 %collective-permute-start.1 = (bf16[272,256]{1,0:T(8,128)(2,1)}, bf16[272,256]{1,0:T(8,128)(2,1)}, u32[]{:S(2)}, u32[]{:S(2)}) collective-permute-start(bf16[272,256]{1,0:T(8,128)(2,1)} %maximum_maximum_fusion), channel_id=1, source_target_pairs={{0,32},{32,64},{64,96},{96,128},{128,160},{160,192},{192,224},{224... | collective-permute-start | bytes 417800 | tf_op jit(solution)/shard_map/ppermute | solution.py:124
  55.9 7.6 %all-to-all-done.1 = bf16[16,40,128]{2,1,0:T(8,128)(2,1)S(1)} async-done(((bf16[16,40,128]{2,1,0:T(8,128)(2,1)}), bf16[16,40,128]{2,1,0:T(8,128)(2,1)S(1)}, u32[]{:S(2)}, u32[]{:S(2)}) %all-to-all-start.1) | async-done | bytes 163872 | tf_op jit(solution)/shard_map/all_to_all | solution.py:179
  63.5 0.2 fusion.34
  63.7 0.2 select_convert_fusion
  63.9 0.7 copy.13
  64.6 7.6 %all-to-all-start.2 = ((bf16[16,40,128]{2,1,0:T(8,128)(2,1)}), bf16[16,40,128]{2,1,0:T(8,128)(2,1)S(1)}, u32[]{:S(2)}, u32[]{:S(2)}) async-start(bf16[16,40,128]{2,1,0:T(8,128)(2,1)} %copy.13), calls=%async_computation.2 | async-start | bytes 327680 | tf_op jit(solution)/shard_map/all_to_all | solution.py:188
  72.2 0.0 collective-permute-done.1
  72.2 0.8 fusion.52
  73.0 0.9 slice.111
  73.9 0.0 copy-start.6
  73.9 0.2 convert_reduce_fusion
  74.1 0.5 copy-done.6
  74.5 1.2 select_reduce_fusion.1
  75.7 0.0 copy-start.2
  75.7 0.8 copy-done.2
  76.5 0.3 fusion.17
  76.8 7.6 %all-to-all-done.2 = bf16[16,40,128]{2,1,0:T(8,128)(2,1)S(1)} async-done(((bf16[16,40,128]{2,1,0:T(8,128)(2,1)}), bf16[16,40,128]{2,1,0:T(8,128)(2,1)S(1)}, u32[]{:S(2)}, u32[]{:S(2)}) %all-to-all-start.2) | async-done | bytes 163872 | tf_op jit(solution)/shard_map/all_to_all | solution.py:188
  84.4 0.1 add.76
  84.5 0.0 copy-start.3
  84.5 0.0 copy-start.5
  84.5 0.0 copy-start.7
  84.5 0.0 copy-start.1
  84.5 1.3 %select_reduce_fusion = (f32[256]{0:T(256)S(1)}, f32[256,512]{1,0:T(8,128)S(1)}) fusion(pred[512]{0:T(512)(128)(4,1)S(1)} %get-tuple-element.31, bf16[1,512,128]{2,1,0:T(8,128)(2,1)} %param.13, bf16[256,384]{1,0:T(8,128)(2,1)S(1)} %fusion.16), kind=kOutput, calls=%fused_computation.19 | convolution fusion | flops 33947392 | bytes 722432 | tf_op jit(solution)/shard_map/dot_general | solution.py:73
  85.9 1.3 %convolution_add_fusion.1 = f32[512,128]{1,0:T(8,128)S(1)} fusion(f32[512,128]{1,0:T(8,128)S(1)} %bitcast.50, s32[256]{0:T(256)S(1)} %bitcast.54, pred[256]{0:T(512)(128)(4,1)S(1)} %compare_and_fusion, bf16[272,256]{1,0:T(8,128)(2,1)} %collective-permute-done.1), kind=kOutput, calls=%fused_computation.5 | convolution fusion | flops 33882112 | bytes 591104 | tf_op jit(solution)/shard_map/dot_general | solution.py:141
  87.2 0.6 fusion.15
  87.9 0.6 fusion.14
  88.5 0.0 copy-done.3
  88.5 0.0 copy-done.5
  88.5 0.0 copy-done.7
  88.6 0.3 fusion.4
  88.9 6.3 %collective-permute-start.2 = (bf16[256,128]{1,0:T(8,128)(2,1)S(1)}, bf16[256,128]{1,0:T(8,128)(2,1)S(1)}, u32[]{:S(2)}, u32[]{:S(2)}) collective-permute-start(bf16[256,128]{1,0:T(8,128)(2,1)S(1)} %fusion.4), channel_id=1, source_target_pairs={{0,1},{1,0},{2,3},{3,2},{4,5},{5,4},{6,7},{7,6},{8,9},{9,8},{10,11... | collective-permute-start | bytes 196616 | tf_op jit(solution)/shard_map/ppermute | solution.py:41
  95.2 0.0 copy-done.1
  95.2 0.4 fusion.5
  95.6 0.0 collective-permute-done.3
  95.7 0.4 collective-permute-done.2
  96.1 1.5 %fusion.1 = bf16[32,8,2048]{2,1,0:T(8,128)(2,1)S(1)} fusion(f32[256,2048]{1,0:T(8,128)S(1)} %fusion.5, bf16[256,128]{1,0:T(8,128)(2,1)S(1)} %collective-permute-done.2, bf16[128,2048]{1,0:T(8,128)(2,1)} %collective-permute-done.3), kind=kOutput, calls=%fused_computation.2 | convolution fusion | flops 135266304 | bytes 3735552 | tf_op jit(solution)/shard_map/dot_general | solution.py:228
  97.5 21.1 %all_to_all.20 = bf16[32,8,2048]{2,1,0:T(8,128)(2,1)} all-to-all(bf16[32,8,2048]{2,1,0:T(8,128)(2,1)S(1)} %fusion.1), channel_id=1, replica_groups=mesh['ctx'=16,'hx'=4,'hy'=4,'hc'=2] {'hx','hy','hc'}, dimensions={0} | all-to-all | bytes 2097152 | tf_op jit(solution)/shard_map/all_to_all | solution.py:233
  118.6 2.0 %reduce.4 = bf16[2,8,2048]{2,1,0:T(8,128)(2,1)} reduce(bf16[16,2,8,2048]{3,2,1,0:T(8,128)(2,1)} %bitcast.49, bf16[]{:T(256)} %constant.126.clone.1), dimensions={0}, to_apply=%region_5.6.clone | reduce | flops 491520 | bytes 1114114 | tf_op jit(solution)/shard_map/reduce_sum | solution.py:234
  (20 shorter events, 0.3 us)
Async XLA Ops:
  0.0 33.7 %copy-start = (bf16[4096,1,384]{2,0,1:T(8,128)(2,1)S(1)}, bf16[4096,1,384]{2,0,1:T(8,128)(2,1)}, u32[]{:S(2)}) copy-start(bf16[4096,1,384]{2,0,1:T(8,128)(2,1)} %param.11) | copy-start | bytes 9437188
  0.0 17.6 %copy-start.8 = (s32[1,256]{1,0:T(1,128)S(1)}, s32[1,256]{1,0:T(1,128)}, u32[]{:S(2)}) copy-start(s32[1,256]{1,0:T(1,128)} %param.14) | copy-start | bytes 3076
  2.3 28.2 %all-to-all-start = ((bf16[32,128,128]{2,1,0:T(8,128)(2,1)}), bf16[32,128,128]{2,1,0:T(8,128)(2,1)}, u32[]{:S(2)}, u32[]{:S(2)}) async-start(bf16[32,128,128]{2,1,0:T(8,128)(2,1)} %bitcast.48), calls=%async_computation | async-start | bytes 2097152 | tf_op jit(solution)/shard_map/all_to_all | solution.py:202
  15.3 80.3 %collective-permute-start.3 = (bf16[128,2048]{1,0:T(8,128)(2,1)}, bf16[128,2048]{1,0:T(8,128)(2,1)}, u32[]{:S(2)}, u32[]{:S(2)}) collective-permute-start(bf16[128,2048]{1,0:T(8,128)(2,1)} %dynamic-slice_bitcast_fusion), channel_id=1, source_target_pairs={{0,1},{1,0},{2,3},{3,2},{4,5},{5,4},{6,7},{7,6},{8,9},{9,8},{10,11... | collective-permute-start | bytes 1572872 | tf_op jit(solution)/shard_map/ppermute | solution.py:41
  30.5 5.1 %collective-permute-start = (bf16[32,128,128]{2,1,0:T(8,128)(2,1)}, bf16[32,128,128]{2,1,0:T(8,128)(2,1)}, u32[]{:S(2)}, u32[]{:S(2)}) collective-permute-start(bf16[32,128,128]{2,1,0:T(8,128)(2,1)} %all-to-all-done), channel_id=1, source_target_pairs={{0,1},{1,0},{2,3},{3,2},{4,5},{5,4},{6,7},{7,6},{8,9},{9,8},{10,11... | collective-permute-start | bytes 3145736 | tf_op jit(solution)/shard_map/ppermute | solution.py:41
  38.7 24.7 %all-to-all-start.1 = ((bf16[16,40,128]{2,1,0:T(8,128)(2,1)}), bf16[16,40,128]{2,1,0:T(8,128)(2,1)S(1)}, u32[]{:S(2)}, u32[]{:S(2)}) async-start(bf16[16,40,128]{2,1,0:T(8,128)(2,1)} %pad_maximum_fusion), calls=%async_computation.1 | async-start | bytes 327680 | tf_op jit(solution)/shard_map/all_to_all | solution.py:179
  51.2 0.8 copy-start.4
  52.0 20.2 %collective-permute-start.1 = (bf16[272,256]{1,0:T(8,128)(2,1)}, bf16[272,256]{1,0:T(8,128)(2,1)}, u32[]{:S(2)}, u32[]{:S(2)}) collective-permute-start(bf16[272,256]{1,0:T(8,128)(2,1)} %maximum_maximum_fusion), channel_id=1, source_target_pairs={{0,32},{32,64},{64,96},{96,128},{128,160},{160,192},{192,224},{224... | collective-permute-start | bytes 417800 | tf_op jit(solution)/shard_map/ppermute | solution.py:124
  64.6 19.8 %all-to-all-start.2 = ((bf16[16,40,128]{2,1,0:T(8,128)(2,1)}), bf16[16,40,128]{2,1,0:T(8,128)(2,1)S(1)}, u32[]{:S(2)}, u32[]{:S(2)}) async-start(bf16[16,40,128]{2,1,0:T(8,128)(2,1)} %copy.13), calls=%async_computation.2 | async-start | bytes 327680 | tf_op jit(solution)/shard_map/all_to_all | solution.py:188
  73.9 0.6 copy-start.6
  75.7 0.8 copy-start.2
  84.5 4.0 %copy-start.3 = (f32[256,512]{1,0:T(8,128)S(1)}, f32[256,512]{1,0:T(8,128)}, u32[]{:S(2)}) copy-start(f32[256,512]{1,0:T(8,128)} %copy-done.2) | copy-start | bytes 1572868
  84.5 4.0 %copy-start.5 = (bf16[256,256]{1,0:T(8,128)(2,1)S(1)}, bf16[256,256]{1,0:T(8,128)(2,1)}, u32[]{:S(2)}) copy-start(bf16[256,256]{1,0:T(8,128)(2,1)} %copy-done.4) | copy-start | bytes 393220
  84.5 4.0 %copy-start.7 = (bf16[256,256]{1,0:T(8,128)(2,1)S(1)}, bf16[256,256]{1,0:T(8,128)(2,1)}, u32[]{:S(2)}) copy-start(bf16[256,256]{1,0:T(8,128)(2,1)} %copy-done.6) | copy-start | bytes 393220
  84.5 10.7 %copy-start.1 = (bf16[1,128,4096]{2,1,0:T(8,128)(2,1)S(1)}, bf16[1,128,4096]{2,1,0:T(8,128)(2,1)}, u32[]{:S(2)}) copy-start(bf16[1,128,4096]{2,1,0:T(8,128)(2,1)} %param.12) | copy-start | bytes 3145732
  88.9 7.2 %collective-permute-start.2 = (bf16[256,128]{1,0:T(8,128)(2,1)S(1)}, bf16[256,128]{1,0:T(8,128)(2,1)S(1)}, u32[]{:S(2)}, u32[]{:S(2)}) collective-permute-start(bf16[256,128]{1,0:T(8,128)(2,1)S(1)} %fusion.4), channel_id=1, source_target_pairs={{0,1},{1,0},{2,3},{3,2},{4,5},{5,4},{6,7},{7,6},{8,9},{9,8},{10,11... | collective-permute-start | bytes 196616 | tf_op jit(solution)/shard_map/ppermute | solution.py:41

commit v15 on v14

--- a/solution.py
+++ b/solution.py
@@ -161,10 +161,15 @@
 
 
 def _pack(sums, counts, span, n, head_dim):
-    hi = jnp.floor(counts / 64.0)
-    lo = counts - hi * 64.0
-    tail = jnp.zeros((n, 8, head_dim), jnp.float32)
-    tail = tail.at[:, 0, :span].set(hi.reshape(n, span)).at[:, 1, :span].set(lo.reshape(n, span))
+    hi = jnp.floor(counts / 64.0).reshape(n, 1, span)
+    lo = counts.reshape(n, 1, span) - hi * 64.0
+    lanes = lax.broadcasted_iota(jnp.int32, (n, 8, head_dim), 2)
+    rows = lax.broadcasted_iota(jnp.int32, (n, 8, head_dim), 1)
+    wide_hi = jnp.pad(hi, ((0, 0), (0, 0), (0, head_dim - span)))
+    wide_lo = jnp.pad(lo, ((0, 0), (0, 0), (0, head_dim - span)))
+    tail = jnp.where(
+        (rows == 0) & (lanes < span), wide_hi, jnp.where((rows == 1) & (lanes < span), wide_lo, 0.0)
+    )
     return jnp.concatenate([sums.reshape(n, span, head_dim), tail], axis=1).astype(jnp.bfloat16)
 
 

time: 122 us -> 121 us (level)
  transfers between devices with their start and end apart: 7 -> 7, of which waited for: 4 -> 5; matrix products, arithmetic and copies ran while one was open for 15% -> 15% of each run, Pallas kernels for 0% -> 0%
where the time goes in v15:
time: 121 us; the launch traced here: 120 us
  starting transfers between devices  45.3 us (37%)
  waiting for transfers between devices  28.6 us (24%)
  blocking collectives  20.7 us (17%)
  matrix products  11.8 us (10%)
  local copies, waits for them, and re-layouts  7.36 us (6%)
  other arithmetic  5.26 us (4%)
    all_to_all x1, blocking collectives, reduce_out(): lax.all_to_all(chunks, HEAD_AXES, 0, 0, tiled=True).astype(jnp.float32)  20.7 us
    all_to_all x1, starting transfers between devices, code_prefix(): lax.all_to_all(_pack(sums, counts, span, n, head_dim), 'ctx', 0, 0, tiled...  12.4 us
    all_to_all x1, waiting for transfers between devices, project(): mine = lax.all_to_all(spread, HEAD_AXES, 0, 0, tiled=True)  11.9 us
    all_to_all x1, starting transfers between devices, project(): mine = lax.all_to_all(spread, HEAD_AXES, 0, 0, tiled=True)  11.1 us
    ppermute x3, starting transfers between devices, _send(): return lax.ppermute(value, HEAD_AXES, perm)  10.6 us
    all_to_all x1, waiting for transfers between devices, code_prefix(): lax.all_to_all(_pack(sums, counts, span, n, head_dim), 'ctx', 0, 0, tiled...  7.91 us
    all_to_all x1, waiting for transfers between devices, code_prefix(): back = lax.all_to_all(pre.astype(jnp.bfloat16), 'ctx', 0, 0, tiled=True)  7.64 us
    all_to_all x1, starting transfers between devices, code_prefix(): back = lax.all_to_all(pre.astype(jnp.bfloat16), 'ctx', 0, 0, tiled=True)  7.25 us
  transfers between devices with their start and end apart: 7, of which 5 were waited for; matrix products, arithmetic and copies ran while one was open for 15% of the time, Pallas kernels for 0%

profile of v15, /device:TPU:1, one launch (start us, length us, event | category | flops | bytes accessed | tf_op | source)
XLA Modules:
  0.0 120.0 jit_solution(524652883145437325)
XLA Ops:
  0.0 0.0 copy-start
  0.0 0.0 copy-start.8
  0.0 2.3 %broadcast_in_dim.85 = bf16[16,2,128,128]{3,2,1,0:T(8,128)(2,1)} broadcast(bf16[2,128,128]{2,1,0:T(8,128)(2,1)} %bitcast.54), dimensions={1,2,3} | broadcast | bytes 1114112 | tf_op jit(solution)/shard_map/broadcast_in_dim | solution.py:204
  2.3 11.1 %all-to-all-start = ((bf16[32,128,128]{2,1,0:T(8,128)(2,1)}), bf16[32,128,128]{2,1,0:T(8,128)(2,1)}, u32[]{:S(2)}, u32[]{:S(2)}) async-start(bf16[32,128,128]{2,1,0:T(8,128)(2,1)} %bitcast.50), calls=%async_computation | async-start | bytes 2097152 | tf_op jit(solution)/shard_map/all_to_all | solution.py:207
  13.4 1.9 %dynamic-slice_bitcast_fusion = bf16[128,2048]{1,0:T(8,128)(2,1)} fusion(bf16[1,128,4096]{2,1,0:T(8,128)(2,1)} %param.8, s32[]{:T(128)S(6)} %select_n.70), kind=kLoop, calls=%fused_computation.15 | loop fusion | bytes 1048580 | tf_op jit(solution)/shard_map/dynamic_slice | solution.py:229
  15.3 2.3 %collective-permute-start.3 = (bf16[128,2048]{1,0:T(8,128)(2,1)}, bf16[128,2048]{1,0:T(8,128)(2,1)}, u32[]{:S(2)}, u32[]{:S(2)}) collective-permute-start(bf16[128,2048]{1,0:T(8,128)(2,1)} %dynamic-slice_bitcast_fusion), channel_id=1, source_target_pairs={{0,1},{1,0},{2,3},{3,2},{4,5},{5,4},{6,7},{7,6},{8,9},{9,8},{10,11... | collective-permute-start | bytes 1572872 | tf_op jit(solution)/shard_map/ppermute | solution.py:41
  18.3 0.0 copy-done.8
  18.3 0.1 convert_reduce_fusion.1
  18.4 0.1 reduce_sum.39
  18.6 11.9 %all-to-all-done = bf16[32,128,128]{2,1,0:T(8,128)(2,1)} async-done(((bf16[32,128,128]{2,1,0:T(8,128)(2,1)}), bf16[32,128,128]{2,1,0:T(8,128)(2,1)}, u32[]{:S(2)}, u32[]{:S(2)}) %all-to-all-start) | async-done | bytes 1048608 | tf_op jit(solution)/shard_map/all_to_all | solution.py:207
  30.4 2.0 %collective-permute-start = (bf16[32,128,128]{2,1,0:T(8,128)(2,1)}, bf16[32,128,128]{2,1,0:T(8,128)(2,1)}, u32[]{:S(2)}, u32[]{:S(2)}) collective-permute-start(bf16[32,128,128]{2,1,0:T(8,128)(2,1)} %all-to-all-done), channel_id=1, source_target_pairs={{0,1},{1,0},{2,3},{3,2},{4,5},{5,4},{6,7},{7,6},{8,9},{9,8},{10,11... | collective-permute-start | bytes 3145736 | tf_op jit(solution)/shard_map/ppermute | solution.py:41
  32.6 0.1 select_convert_fusion.1
  32.7 0.0 copy-done
  32.7 1.9 %convolution_bitcast_fusion.1 = bf16[128,384]{1,0:T(8,128)(2,1)S(1)} fusion(bf16[32,128,128]{2,1,0:T(8,128)(2,1)} %all-to-all-done, bf16[32,128,384]{2,1,0:T(8,128)(2,1)S(1)} %bitcast.48), kind=kOutput, calls=%fused_computation.8 | convolution fusion | flops 402653184 | bytes 4292608 | tf_op jit(solution)/shard_map/dot_general | solution.py:211
  34.6 0.7 collective-permute-done
  35.3 1.9 %convolution_bitcast_fusion = bf16[128,384]{1,0:T(8,128)(2,1)S(1)} fusion(bf16[32,128,128]{2,1,0:T(8,128)(2,1)} %collective-permute-done, bf16[32,128,384]{2,1,0:T(8,128)(2,1)S(1)} %bitcast.49), kind=kOutput, calls=%fused_computation.7 | convolution fusion | flops 402653184 | bytes 4292608 | tf_op jit(solution)/shard_map/dot_general | solution.py:212
  37.3 0.4 convolution_convert_fusion
  37.7 0.7 pad_maximum_fusion
  38.4 12.4 %all-to-all-start.1 = ((bf16[16,40,128]{2,1,0:T(8,128)(2,1)}), bf16[16,40,128]{2,1,0:T(8,128)(2,1)S(1)}, u32[]{:S(2)}, u32[]{:S(2)}) async-start(bf16[16,40,128]{2,1,0:T(8,128)(2,1)} %pad_maximum_fusion), calls=%async_computation.1 | async-start | bytes 327680 | tf_op jit(solution)/shard_map/all_to_all | solution.py:184
  50.8 0.1 pad.16.clone
  50.9 0.0 copy-start.4
  50.9 0.8 maximum_maximum_fusion
  51.7 0.0 copy-done.4
  51.7 3.9 %collective-permute-start.1 = (bf16[272,256]{1,0:T(8,128)(2,1)}, bf16[272,256]{1,0:T(8,128)(2,1)}, u32[]{:S(2)}, u32[]{:S(2)}) collective-permute-start(bf16[272,256]{1,0:T(8,128)(2,1)} %maximum_maximum_fusion), channel_id=1, source_target_pairs={{0,32},{32,64},{64,96},{96,128},{128,160},{160,192},{192,224},{224... | collective-permute-start | bytes 417800 | tf_op jit(solution)/shard_map/ppermute | solution.py:124
  55.6 7.9 %all-to-all-done.1 = bf16[16,40,128]{2,1,0:T(8,128)(2,1)S(1)} async-done(((bf16[16,40,128]{2,1,0:T(8,128)(2,1)}), bf16[16,40,128]{2,1,0:T(8,128)(2,1)S(1)}, u32[]{:S(2)}, u32[]{:S(2)}) %all-to-all-start.1) | async-done | bytes 163872 | tf_op jit(solution)/shard_map/all_to_all | solution.py:184
  63.5 0.2 fusion.34
  63.8 0.2 select_convert_fusion
  64.0 0.7 copy.13
  64.6 7.3 %all-to-all-start.2 = ((bf16[16,40,128]{2,1,0:T(8,128)(2,1)}), bf16[16,40,128]{2,1,0:T(8,128)(2,1)S(1)}, u32[]{:S(2)}, u32[]{:S(2)}) async-start(bf16[16,40,128]{2,1,0:T(8,128)(2,1)} %copy.13), calls=%async_computation.2 | async-start | bytes 327680 | tf_op jit(solution)/shard_map/all_to_all | solution.py:193
  71.9 0.0 collective-permute-done.1
  71.9 0.8 fusion.52
  72.7 0.9 slice.62
  73.6 0.0 copy-start.6
  73.6 0.2 convert_reduce_fusion
  73.8 0.5 copy-done.6
  74.2 1.2 select_reduce_fusion.1
  75.4 0.0 copy-start.2
  75.4 0.8 copy-done.2
  76.2 0.3 fusion.17
  76.5 7.6 %all-to-all-done.2 = bf16[16,40,128]{2,1,0:T(8,128)(2,1)S(1)} async-done(((bf16[16,40,128]{2,1,0:T(8,128)(2,1)}), bf16[16,40,128]{2,1,0:T(8,128)(2,1)S(1)}, u32[]{:S(2)}, u32[]{:S(2)}) %all-to-all-start.2) | async-done | bytes 163872 | tf_op jit(solution)/shard_map/all_to_all | solution.py:193
  84.2 0.1 add.74
  84.3 0.0 copy-start.3
  84.3 0.0 copy-start.5
  84.3 0.0 copy-start.7
  84.3 0.0 copy-start.1
  84.3 1.3 %select_reduce_fusion = (f32[256]{0:T(256)S(1)}, f32[256,512]{1,0:T(8,128)S(1)}) fusion(pred[512]{0:T(512)(128)(4,1)S(1)} %get-tuple-element.7, bf16[1,512,128]{2,1,0:T(8,128)(2,1)} %param.9, bf16[256,384]{1,0:T(8,128)(2,1)S(1)} %fusion.16), kind=kOutput, calls=%fused_computation.19 | convolution fusion | flops 33947392 | bytes 722432 | tf_op jit(solution)/shard_map/dot_general | solution.py:73
  85.7 1.3 %convolution_add_fusion.1 = f32[512,128]{1,0:T(8,128)S(1)} fusion(f32[512,128]{1,0:T(8,128)S(1)} %bitcast.52, s32[256]{0:T(256)S(1)} %bitcast.58, pred[256]{0:T(512)(128)(4,1)S(1)} %compare_and_fusion, bf16[272,256]{1,0:T(8,128)(2,1)} %collective-permute-done.1), kind=kOutput, calls=%fused_computation.5 | convolution fusion | flops 33882112 | bytes 591104 | tf_op jit(solution)/shard_map/dot_general | solution.py:141
  87.0 0.6 fusion.15
  87.6 0.6 fusion.14
  88.3 0.0 copy-done.3
  88.3 0.0 copy-done.5
  88.3 0.0 copy-done.7
  88.3 0.3 fusion.4
  88.6 6.3 %collective-permute-start.2 = (bf16[256,128]{1,0:T(8,128)(2,1)S(1)}, bf16[256,128]{1,0:T(8,128)(2,1)S(1)}, u32[]{:S(2)}, u32[]{:S(2)}) collective-permute-start(bf16[256,128]{1,0:T(8,128)(2,1)S(1)} %fusion.4), channel_id=1, source_target_pairs={{0,1},{1,0},{2,3},{3,2},{4,5},{5,4},{6,7},{7,6},{8,9},{9,8},{10,11... | collective-permute-start | bytes 196616 | tf_op jit(solution)/shard_map/ppermute | solution.py:41
  94.9 0.0 copy-done.1
  95.0 0.4 fusion.5
  95.4 0.0 collective-permute-done.3
  95.4 0.4 collective-permute-done.2
  95.8 1.5 %fusion.1 = bf16[32,8,2048]{2,1,0:T(8,128)(2,1)S(1)} fusion(f32[256,2048]{1,0:T(8,128)S(1)} %fusion.5, bf16[256,128]{1,0:T(8,128)(2,1)S(1)} %collective-permute-done.2, bf16[128,2048]{1,0:T(8,128)(2,1)} %collective-permute-done.3), kind=kOutput, calls=%fused_computation.2 | convolution fusion | flops 135266304 | bytes 3735552 | tf_op jit(solution)/shard_map/dot_general | solution.py:233
  97.3 20.7 %all_to_all.20 = bf16[32,8,2048]{2,1,0:T(8,128)(2,1)} all-to-all(bf16[32,8,2048]{2,1,0:T(8,128)(2,1)S(1)} %fusion.1), channel_id=1, replica_groups=mesh['ctx'=16,'hx'=4,'hy'=4,'hc'=2] {'hx','hy','hc'}, dimensions={0} | all-to-all | bytes 2097152 | tf_op jit(solution)/shard_map/all_to_all | solution.py:238
  118.0 2.0 %reduce = bf16[2,8,2048]{2,1,0:T(8,128)(2,1)} reduce(bf16[16,2,8,2048]{3,2,1,0:T(8,128)(2,1)} %bitcast.51, bf16[]{:T(256)} %constant.71.clone.1), dimensions={0}, to_apply=%region_5.6.clone | reduce | flops 491520 | bytes 1114114 | tf_op jit(solution)/shard_map/reduce_sum | solution.py:239
  (23 shorter events, 0.3 us)
Async XLA Ops:
  0.0 32.7 %copy-start = (bf16[4096,1,384]{2,0,1:T(8,128)(2,1)S(1)}, bf16[4096,1,384]{2,0,1:T(8,128)(2,1)}, u32[]{:S(2)}) copy-start(bf16[4096,1,384]{2,0,1:T(8,128)(2,1)} %param.7) | copy-start | bytes 9437188
  0.0 18.3 %copy-start.8 = (s32[1,256]{1,0:T(1,128)S(1)}, s32[1,256]{1,0:T(1,128)}, u32[]{:S(2)}) copy-start(s32[1,256]{1,0:T(1,128)} %param.10) | copy-start | bytes 3076
  2.3 28.2 %all-to-all-start = ((bf16[32,128,128]{2,1,0:T(8,128)(2,1)}), bf16[32,128,128]{2,1,0:T(8,128)(2,1)}, u32[]{:S(2)}, u32[]{:S(2)}) async-start(bf16[32,128,128]{2,1,0:T(8,128)(2,1)} %bitcast.50), calls=%async_computation | async-start | bytes 2097152 | tf_op jit(solution)/shard_map/all_to_all | solution.py:207
  15.3 80.1 %collective-permute-start.3 = (bf16[128,2048]{1,0:T(8,128)(2,1)}, bf16[128,2048]{1,0:T(8,128)(2,1)}, u32[]{:S(2)}, u32[]{:S(2)}) collective-permute-start(bf16[128,2048]{1,0:T(8,128)(2,1)} %dynamic-slice_bitcast_fusion), channel_id=1, source_target_pairs={{0,1},{1,0},{2,3},{3,2},{4,5},{5,4},{6,7},{7,6},{8,9},{9,8},{10,11... | collective-permute-start | bytes 1572872 | tf_op jit(solution)/shard_map/ppermute | solution.py:41
  30.4 4.9 %collective-permute-start = (bf16[32,128,128]{2,1,0:T(8,128)(2,1)}, bf16[32,128,128]{2,1,0:T(8,128)(2,1)}, u32[]{:S(2)}, u32[]{:S(2)}) collective-permute-start(bf16[32,128,128]{2,1,0:T(8,128)(2,1)} %all-to-all-done), channel_id=1, source_target_pairs={{0,1},{1,0},{2,3},{3,2},{4,5},{5,4},{6,7},{7,6},{8,9},{9,8},{10,11... | collective-permute-start | bytes 3145736 | tf_op jit(solution)/shard_map/ppermute | solution.py:41
  38.4 25.1 %all-to-all-start.1 = ((bf16[16,40,128]{2,1,0:T(8,128)(2,1)}), bf16[16,40,128]{2,1,0:T(8,128)(2,1)S(1)}, u32[]{:S(2)}, u32[]{:S(2)}) async-start(bf16[16,40,128]{2,1,0:T(8,128)(2,1)} %pad_maximum_fusion), calls=%async_computation.1 | async-start | bytes 327680 | tf_op jit(solution)/shard_map/all_to_all | solution.py:184
  50.9 0.8 copy-start.4
  51.7 20.2 %collective-permute-start.1 = (bf16[272,256]{1,0:T(8,128)(2,1)}, bf16[272,256]{1,0:T(8,128)(2,1)}, u32[]{:S(2)}, u32[]{:S(2)}) collective-permute-start(bf16[272,256]{1,0:T(8,128)(2,1)} %maximum_maximum_fusion), channel_id=1, source_target_pairs={{0,32},{32,64},{64,96},{96,128},{128,160},{160,192},{192,224},{224... | collective-permute-start | bytes 417800 | tf_op jit(solution)/shard_map/ppermute | solution.py:124
  64.6 19.5 %all-to-all-start.2 = ((bf16[16,40,128]{2,1,0:T(8,128)(2,1)}), bf16[16,40,128]{2,1,0:T(8,128)(2,1)S(1)}, u32[]{:S(2)}, u32[]{:S(2)}) async-start(bf16[16,40,128]{2,1,0:T(8,128)(2,1)} %copy.13), calls=%async_computation.2 | async-start | bytes 327680 | tf_op jit(solution)/shard_map/all_to_all | solution.py:193
  73.6 0.7 copy-start.6
  75.4 0.8 copy-start.2
  84.3 4.0 %copy-start.3 = (f32[256,512]{1,0:T(8,128)S(1)}, f32[256,512]{1,0:T(8,128)}, u32[]{:S(2)}) copy-start(f32[256,512]{1,0:T(8,128)} %copy-done.2) | copy-start | bytes 1572868
  84.3 4.0 %copy-start.5 = (bf16[256,256]{1,0:T(8,128)(2,1)S(1)}, bf16[256,256]{1,0:T(8,128)(2,1)}, u32[]{:S(2)}) copy-start(bf16[256,256]{1,0:T(8,128)(2,1)} %copy-done.4) | copy-start | bytes 393220
  84.3 4.0 %copy-start.7 = (bf16[256,256]{1,0:T(8,128)(2,1)S(1)}, bf16[256,256]{1,0:T(8,128)(2,1)}, u32[]{:S(2)}) copy-start(bf16[256,256]{1,0:T(8,128)(2,1)} %copy-done.6) | copy-start | bytes 393220
  84.3 10.7 %copy-start.1 = (bf16[1,128,4096]{2,1,0:T(8,128)(2,1)S(1)}, bf16[1,128,4096]{2,1,0:T(8,128)(2,1)}, u32[]{:S(2)}) copy-start(bf16[1,128,4096]{2,1,0:T(8,128)(2,1)} %param.8) | copy-start | bytes 3145732
  88.6 7.2 %collective-permute-start.2 = (bf16[256,128]{1,0:T(8,128)(2,1)S(1)}, bf16[256,128]{1,0:T(8,128)(2,1)S(1)}, u32[]{:S(2)}, u32[]{:S(2)}) collective-permute-start(bf16[256,128]{1,0:T(8,128)(2,1)S(1)} %fusion.4), channel_id=1, source_target_pairs={{0,1},{1,0},{2,3},{3,2},{4,5},{5,4},{6,7},{7,6},{8,9},{9,8},{10,11... | collective-permute-start | bytes 196616 | tf_op jit(solution)/shard_map/ppermute | solution.py:41

commit v16 on v15

--- a/solution.py
+++ b/solution.py
@@ -201,9 +201,7 @@
     me_c = lax.axis_index("hc")
     rows, width = tokens_in.shape
     half = rows // nc
-    spread = jnp.broadcast_to(
-        tokens_in.reshape(1, nc, half, width), (n_head // nc, nc, half, width)
-    ).reshape(n_head, half, width)
+    spread = jnp.tile(tokens_in, (n_head // nc, 1)).reshape(n_head, half, width)
     mine = lax.all_to_all(spread, HEAD_AXES, 0, 0, tiled=True)
     theirs = _send(mine, core_perm)
     w_local = w_qkv[:, 0, :].reshape(n_head, width, -1)

time: 121 us -> 121 us (level)
    broadcast_in_dim x1 -> x0, local copies, waits for them, and re-layouts: 2.27 us -> none  [project(): jnp.broadcast_to(tokens_in.reshape(1, nc, half, width), (n_head // nc, nc...]
    another operation x0 -> x1, local copies, waits for them, and re-layouts: none -> 2.24 us  [project(): spread = jnp.tile(tokens_in, (n_head // nc, 1)).reshape(n_head, half, width)]
where the time goes in v16:
time: 121 us; the launch traced here: 120 us
  starting transfers between devices  45.3 us (37%)
  waiting for transfers between devices  28.6 us (24%)
  blocking collectives  20.7 us (17%)
  matrix products  11.8 us (10%)
  local copies, waits for them, and re-layouts  7.33 us (6%)
  other arithmetic  5.26 us (4%)
    all_to_all x1, blocking collectives, reduce_out(): lax.all_to_all(chunks, HEAD_AXES, 0, 0, tiled=True).astype(jnp.float32)  20.7 us
    all_to_all x1, starting transfers between devices, code_prefix(): lax.all_to_all(_pack(sums, counts, span, n, head_dim), 'ctx', 0, 0, tiled...  12.4 us
    all_to_all x1, waiting for transfers between devices, project(): mine = lax.all_to_all(spread, HEAD_AXES, 0, 0, tiled=True)  11.9 us
    all_to_all x1, starting transfers between devices, project(): mine = lax.all_to_all(spread, HEAD_AXES, 0, 0, tiled=True)  11.1 us
    ppermute x3, starting transfers between devices, _send(): return lax.ppermute(value, HEAD_AXES, perm)  10.6 us
    all_to_all x1, waiting for transfers between devices, code_prefix(): lax.all_to_all(_pack(sums, counts, span, n, head_dim), 'ctx', 0, 0, tiled...  7.91 us
    all_to_all x1, waiting for transfers between devices, code_prefix(): back = lax.all_to_all(pre.astype(jnp.bfloat16), 'ctx', 0, 0, tiled=True)  7.64 us
    all_to_all x1, starting transfers between devices, code_prefix(): back = lax.all_to_all(pre.astype(jnp.bfloat16), 'ctx', 0, 0, tiled=True)  7.25 us
  transfers between devices with their start and end apart: 7, of which 5 were waited for; matrix products, arithmetic and copies ran while one was open for 15% of the time, Pallas kernels for 0%

profile of v16, /device:TPU:1, one launch (start us, length us, event | category | flops | bytes accessed | tf_op | source)
XLA Modules:
  0.0 120.0 jit_solution(12385018781396623470)
XLA Ops:
  0.0 0.0 copy-start
  0.0 0.0 copy-start.8
  0.0 2.2 %tile.8 = bf16[16,256,128]{2,1,0:T(8,128)(2,1)} broadcast(bf16[256,128]{1,0:T(8,128)(2,1)} %param.6), dimensions={1,2} | broadcast | bytes 1114112 | tf_op jit(solution)/shard_map/tile | solution.py:204
  2.2 11.1 %all-to-all-start = ((bf16[32,128,128]{2,1,0:T(8,128)(2,1)}), bf16[32,128,128]{2,1,0:T(8,128)(2,1)}, u32[]{:S(2)}, u32[]{:S(2)}) async-start(bf16[32,128,128]{2,1,0:T(8,128)(2,1)} %bitcast.49), calls=%async_computation | async-start | bytes 2097152 | tf_op jit(solution)/shard_map/all_to_all | solution.py:205
  13.4 1.9 %dynamic-slice_bitcast_fusion = bf16[128,2048]{1,0:T(8,128)(2,1)} fusion(bf16[1,128,4096]{2,1,0:T(8,128)(2,1)} %param.8, s32[]{:T(128)S(6)} %select_n.70), kind=kLoop, calls=%fused_computation.15 | loop fusion | bytes 1048580 | tf_op jit(solution)/shard_map/dynamic_slice | solution.py:227
  15.3 2.3 %collective-permute-start.3 = (bf16[128,2048]{1,0:T(8,128)(2,1)}, bf16[128,2048]{1,0:T(8,128)(2,1)}, u32[]{:S(2)}, u32[]{:S(2)}) collective-permute-start(bf16[128,2048]{1,0:T(8,128)(2,1)} %dynamic-slice_bitcast_fusion), channel_id=1, source_target_pairs={{0,1},{1,0},{2,3},{3,2},{4,5},{5,4},{6,7},{7,6},{8,9},{9,8},{10,11... | collective-permute-start | bytes 1572872 | tf_op jit(solution)/shard_map/ppermute | solution.py:41
  18.2 0.0 copy-done.8
  18.3 0.1 convert_reduce_fusion.1
  18.4 0.1 reduce_sum.39
  18.5 11.9 %all-to-all-done = bf16[32,128,128]{2,1,0:T(8,128)(2,1)} async-done(((bf16[32,128,128]{2,1,0:T(8,128)(2,1)}), bf16[32,128,128]{2,1,0:T(8,128)(2,1)}, u32[]{:S(2)}, u32[]{:S(2)}) %all-to-all-start) | async-done | bytes 1048608 | tf_op jit(solution)/shard_map/all_to_all | solution.py:205
  30.4 2.0 %collective-permute-start = (bf16[32,128,128]{2,1,0:T(8,128)(2,1)}, bf16[32,128,128]{2,1,0:T(8,128)(2,1)}, u32[]{:S(2)}, u32[]{:S(2)}) collective-permute-start(bf16[32,128,128]{2,1,0:T(8,128)(2,1)} %all-to-all-done), channel_id=1, source_target_pairs={{0,1},{1,0},{2,3},{3,2},{4,5},{5,4},{6,7},{7,6},{8,9},{9,8},{10,11... | collective-permute-start | bytes 3145736 | tf_op jit(solution)/shard_map/ppermute | solution.py:41
  32.6 0.1 select_convert_fusion.1
  32.6 0.0 copy-done
  32.7 1.9 %convolution_bitcast_fusion.1 = bf16[128,384]{1,0:T(8,128)(2,1)S(1)} fusion(bf16[32,128,128]{2,1,0:T(8,128)(2,1)} %all-to-all-done, bf16[32,128,384]{2,1,0:T(8,128)(2,1)S(1)} %bitcast.47), kind=kOutput, calls=%fused_computation.8 | convolution fusion | flops 402653184 | bytes 4292608 | tf_op jit(solution)/shard_map/dot_general | solution.py:209
  34.6 0.7 collective-permute-done
  35.3 1.9 %convolution_bitcast_fusion = bf16[128,384]{1,0:T(8,128)(2,1)S(1)} fusion(bf16[32,128,128]{2,1,0:T(8,128)(2,1)} %collective-permute-done, bf16[32,128,384]{2,1,0:T(8,128)(2,1)S(1)} %bitcast.48), kind=kOutput, calls=%fused_computation.7 | convolution fusion | flops 402653184 | bytes 4292608 | tf_op jit(solution)/shard_map/dot_general | solution.py:210
  37.3 0.4 convolution_convert_fusion
  37.7 0.7 pad_maximum_fusion
  38.4 12.4 %all-to-all-start.1 = ((bf16[16,40,128]{2,1,0:T(8,128)(2,1)}), bf16[16,40,128]{2,1,0:T(8,128)(2,1)S(1)}, u32[]{:S(2)}, u32[]{:S(2)}) async-start(bf16[16,40,128]{2,1,0:T(8,128)(2,1)} %pad_maximum_fusion), calls=%async_computation.1 | async-start | bytes 327680 | tf_op jit(solution)/shard_map/all_to_all | solution.py:184
  50.8 0.1 pad.16.clone
  50.9 0.0 copy-start.4
  50.9 0.8 maximum_maximum_fusion
  51.7 0.0 copy-done.4
  51.7 3.9 %collective-permute-start.1 = (bf16[272,256]{1,0:T(8,128)(2,1)}, bf16[272,256]{1,0:T(8,128)(2,1)}, u32[]{:S(2)}, u32[]{:S(2)}) collective-permute-start(bf16[272,256]{1,0:T(8,128)(2,1)} %maximum_maximum_fusion), channel_id=1, source_target_pairs={{0,32},{32,64},{64,96},{96,128},{128,160},{160,192},{192,224},{224... | collective-permute-start | bytes 417800 | tf_op jit(solution)/shard_map/ppermute | solution.py:124
  55.6 7.9 %all-to-all-done.1 = bf16[16,40,128]{2,1,0:T(8,128)(2,1)S(1)} async-done(((bf16[16,40,128]{2,1,0:T(8,128)(2,1)}), bf16[16,40,128]{2,1,0:T(8,128)(2,1)S(1)}, u32[]{:S(2)}, u32[]{:S(2)}) %all-to-all-start.1) | async-done | bytes 163872 | tf_op jit(solution)/shard_map/all_to_all | solution.py:184
  63.5 0.2 fusion.34
  63.8 0.2 select_convert_fusion
  63.9 0.7 copy.13
  64.6 7.3 %all-to-all-start.2 = ((bf16[16,40,128]{2,1,0:T(8,128)(2,1)}), bf16[16,40,128]{2,1,0:T(8,128)(2,1)S(1)}, u32[]{:S(2)}, u32[]{:S(2)}) async-start(bf16[16,40,128]{2,1,0:T(8,128)(2,1)} %copy.13), calls=%async_computation.2 | async-start | bytes 327680 | tf_op jit(solution)/shard_map/all_to_all | solution.py:193
  71.9 0.0 collective-permute-done.1
  71.9 0.8 fusion.52
  72.6 0.9 slice.62
  73.6 0.0 copy-start.6
  73.6 0.2 convert_reduce_fusion
  73.7 0.5 copy-done.6
  74.2 1.2 select_reduce_fusion.1
  75.4 0.0 copy-start.2
  75.4 0.8 copy-done.2
  76.2 0.3 fusion.17
  76.4 7.6 %all-to-all-done.2 = bf16[16,40,128]{2,1,0:T(8,128)(2,1)S(1)} async-done(((bf16[16,40,128]{2,1,0:T(8,128)(2,1)}), bf16[16,40,128]{2,1,0:T(8,128)(2,1)S(1)}, u32[]{:S(2)}, u32[]{:S(2)}) %all-to-all-start.2) | async-done | bytes 163872 | tf_op jit(solution)/shard_map/all_to_all | solution.py:193
  84.1 0.1 add.74
  84.2 0.0 copy-start.3
  84.2 0.0 copy-start.5
  84.2 0.0 copy-start.7
  84.2 0.0 copy-start.1
  84.3 1.3 %select_reduce_fusion = (f32[256]{0:T(256)S(1)}, f32[256,512]{1,0:T(8,128)S(1)}) fusion(pred[512]{0:T(512)(128)(4,1)S(1)} %get-tuple-element.7, bf16[1,512,128]{2,1,0:T(8,128)(2,1)} %param.9, bf16[256,384]{1,0:T(8,128)(2,1)S(1)} %fusion.16), kind=kOutput, calls=%fused_computation.19 | convolution fusion | flops 33947392 | bytes 722432 | tf_op jit(solution)/shard_map/dot_general | solution.py:73
  85.6 1.3 %convolution_add_fusion.1 = f32[512,128]{1,0:T(8,128)S(1)} fusion(f32[512,128]{1,0:T(8,128)S(1)} %bitcast.51, s32[256]{0:T(256)S(1)} %bitcast.56, pred[256]{0:T(512)(128)(4,1)S(1)} %compare_and_fusion, bf16[272,256]{1,0:T(8,128)(2,1)} %collective-permute-done.1), kind=kOutput, calls=%fused_computation.5 | convolution fusion | flops 33882112 | bytes 591104 | tf_op jit(solution)/shard_map/dot_general | solution.py:141
  86.9 0.6 fusion.15
  87.6 0.6 fusion.14
  88.2 0.0 copy-done.3
  88.2 0.0 copy-done.5
  88.3 0.0 copy-done.7
  88.3 0.3 fusion.4
  88.6 6.3 %collective-permute-start.2 = (bf16[256,128]{1,0:T(8,128)(2,1)S(1)}, bf16[256,128]{1,0:T(8,128)(2,1)S(1)}, u32[]{:S(2)}, u32[]{:S(2)}) collective-permute-start(bf16[256,128]{1,0:T(8,128)(2,1)S(1)} %fusion.4), channel_id=1, source_target_pairs={{0,1},{1,0},{2,3},{3,2},{4,5},{5,4},{6,7},{7,6},{8,9},{9,8},{10,11... | collective-permute-start | bytes 196616 | tf_op jit(solution)/shard_map/ppermute | solution.py:41
  94.9 0.0 copy-done.1
  94.9 0.4 fusion.5
  95.3 0.0 collective-permute-done.3
  95.4 0.4 collective-permute-done.2
  95.8 1.5 %fusion.1 = bf16[32,8,2048]{2,1,0:T(8,128)(2,1)S(1)} fusion(f32[256,2048]{1,0:T(8,128)S(1)} %fusion.5, bf16[256,128]{1,0:T(8,128)(2,1)S(1)} %collective-permute-done.2, bf16[128,2048]{1,0:T(8,128)(2,1)} %collective-permute-done.3), kind=kOutput, calls=%fused_computation.2 | convolution fusion | flops 135266304 | bytes 3735552 | tf_op jit(solution)/shard_map/dot_general | solution.py:231
  97.3 20.7 %all_to_all.20 = bf16[32,8,2048]{2,1,0:T(8,128)(2,1)} all-to-all(bf16[32,8,2048]{2,1,0:T(8,128)(2,1)S(1)} %fusion.1), channel_id=1, replica_groups=mesh['ctx'=16,'hx'=4,'hy'=4,'hc'=2] {'hx','hy','hc'}, dimensions={0} | all-to-all | bytes 2097152 | tf_op jit(solution)/shard_map/all_to_all | solution.py:236
  118.0 2.0 %reduce = bf16[2,8,2048]{2,1,0:T(8,128)(2,1)} reduce(bf16[16,2,8,2048]{3,2,1,0:T(8,128)(2,1)} %bitcast.50, bf16[]{:T(256)} %constant.71.clone.1), dimensions={0}, to_apply=%region_5.6.clone | reduce | flops 491520 | bytes 1114114 | tf_op jit(solution)/shard_map/reduce_sum | solution.py:237
  (23 shorter events, 0.3 us)
Async XLA Ops:
  0.0 32.6 %copy-start = (bf16[4096,1,384]{2,0,1:T(8,128)(2,1)S(1)}, bf16[4096,1,384]{2,0,1:T(8,128)(2,1)}, u32[]{:S(2)}) copy-start(bf16[4096,1,384]{2,0,1:T(8,128)(2,1)} %param.7) | copy-start | bytes 9437188
  0.0 18.2 %copy-start.8 = (s32[1,256]{1,0:T(1,128)S(1)}, s32[1,256]{1,0:T(1,128)}, u32[]{:S(2)}) copy-start(s32[1,256]{1,0:T(1,128)} %param.10) | copy-start | bytes 3076
  2.2 28.2 %all-to-all-start = ((bf16[32,128,128]{2,1,0:T(8,128)(2,1)}), bf16[32,128,128]{2,1,0:T(8,128)(2,1)}, u32[]{:S(2)}, u32[]{:S(2)}) async-start(bf16[32,128,128]{2,1,0:T(8,128)(2,1)} %bitcast.49), calls=%async_computation | async-start | bytes 2097152 | tf_op jit(solution)/shard_map/all_to_all | solution.py:205
  15.3 80.1 %collective-permute-start.3 = (bf16[128,2048]{1,0:T(8,128)(2,1)}, bf16[128,2048]{1,0:T(8,128)(2,1)}, u32[]{:S(2)}, u32[]{:S(2)}) collective-permute-start(bf16[128,2048]{1,0:T(8,128)(2,1)} %dynamic-slice_bitcast_fusion), channel_id=1, source_target_pairs={{0,1},{1,0},{2,3},{3,2},{4,5},{5,4},{6,7},{7,6},{8,9},{9,8},{10,11... | collective-permute-start | bytes 1572872 | tf_op jit(solution)/shard_map/ppermute | solution.py:41
  30.4 4.9 %collective-permute-start = (bf16[32,128,128]{2,1,0:T(8,128)(2,1)}, bf16[32,128,128]{2,1,0:T(8,128)(2,1)}, u32[]{:S(2)}, u32[]{:S(2)}) collective-permute-start(bf16[32,128,128]{2,1,0:T(8,128)(2,1)} %all-to-all-done), channel_id=1, source_target_pairs={{0,1},{1,0},{2,3},{3,2},{4,5},{5,4},{6,7},{7,6},{8,9},{9,8},{10,11... | collective-permute-start | bytes 3145736 | tf_op jit(solution)/shard_map/ppermute | solution.py:41
  38.4 25.1 %all-to-all-start.1 = ((bf16[16,40,128]{2,1,0:T(8,128)(2,1)}), bf16[16,40,128]{2,1,0:T(8,128)(2,1)S(1)}, u32[]{:S(2)}, u32[]{:S(2)}) async-start(bf16[16,40,128]{2,1,0:T(8,128)(2,1)} %pad_maximum_fusion), calls=%async_computation.1 | async-start | bytes 327680 | tf_op jit(solution)/shard_map/all_to_all | solution.py:184
  50.9 0.8 copy-start.4
  51.7 20.2 %collective-permute-start.1 = (bf16[272,256]{1,0:T(8,128)(2,1)}, bf16[272,256]{1,0:T(8,128)(2,1)}, u32[]{:S(2)}, u32[]{:S(2)}) collective-permute-start(bf16[272,256]{1,0:T(8,128)(2,1)} %maximum_maximum_fusion), channel_id=1, source_target_pairs={{0,32},{32,64},{64,96},{96,128},{128,160},{160,192},{192,224},{224... | collective-permute-start | bytes 417800 | tf_op jit(solution)/shard_map/ppermute | solution.py:124
  64.6 19.5 %all-to-all-start.2 = ((bf16[16,40,128]{2,1,0:T(8,128)(2,1)}), bf16[16,40,128]{2,1,0:T(8,128)(2,1)S(1)}, u32[]{:S(2)}, u32[]{:S(2)}) async-start(bf16[16,40,128]{2,1,0:T(8,128)(2,1)} %copy.13), calls=%async_computation.2 | async-start | bytes 327680 | tf_op jit(solution)/shard_map/all_to_all | solution.py:193
  73.6 0.7 copy-start.6
  75.4 0.8 copy-start.2
  84.2 4.0 %copy-start.3 = (f32[256,512]{1,0:T(8,128)S(1)}, f32[256,512]{1,0:T(8,128)}, u32[]{:S(2)}) copy-start(f32[256,512]{1,0:T(8,128)} %copy-done.2) | copy-start | bytes 1572868
  84.2 4.0 %copy-start.5 = (bf16[256,256]{1,0:T(8,128)(2,1)S(1)}, bf16[256,256]{1,0:T(8,128)(2,1)}, u32[]{:S(2)}) copy-start(bf16[256,256]{1,0:T(8,128)(2,1)} %copy-done.4) | copy-start | bytes 393220
  84.2 4.0 %copy-start.7 = (bf16[256,256]{1,0:T(8,128)(2,1)S(1)}, bf16[256,256]{1,0:T(8,128)(2,1)}, u32[]{:S(2)}) copy-start(bf16[256,256]{1,0:T(8,128)(2,1)} %copy-done.6) | copy-start | bytes 393220
  84.2 10.7 %copy-start.1 = (bf16[1,128,4096]{2,1,0:T(8,128)(2,1)S(1)}, bf16[1,128,4096]{2,1,0:T(8,128)(2,1)}, u32[]{:S(2)}) copy-start(bf16[1,128,4096]{2,1,0:T(8,128)(2,1)} %param.8) | copy-start | bytes 3145732
  88.6 7.2 %collective-permute-start.2 = (bf16[256,128]{1,0:T(8,128)(2,1)S(1)}, bf16[256,128]{1,0:T(8,128)(2,1)S(1)}, u32[]{:S(2)}, u32[]{:S(2)}) collective-permute-start(bf16[256,128]{1,0:T(8,128)(2,1)S(1)} %fusion.4), channel_id=1, source_target_pairs={{0,1},{1,0},{2,3},{3,2},{4,5},{5,4},{6,7},{7,6},{8,9},{9,8},{10,11... | collective-permute-start | bytes 196616 | tf_op jit(solution)/shard_map/ppermute | solution.py:41

commit v17 on v15

--- a/solution.py
+++ b/solution.py
@@ -90,8 +90,8 @@
     top = jnp.maximum(top_e, jnp.max(jnp.where(valid[None, :], coded, -jnp.inf), axis=1))
     alpha = jnp.exp(top_e - top)
     weights = jnp.exp(jnp.where(valid[None, :], coded - top[:, None], -jnp.inf))
-    numer = alpha[:, None] * numer_e + jnp.dot(weights, cache_v, precision=lax.Precision.HIGHEST)
-    denom = alpha * denom_e + jnp.dot(weights, cache_c, precision=lax.Precision.HIGHEST)
+    numer = alpha[:, None] * numer_e + jnp.dot(weights, cache_v, precision=lax.Precision.HIGH)
+    denom = alpha * denom_e + jnp.dot(weights, cache_c, precision=lax.Precision.HIGH)
     return (numer / denom[:, None]).astype(jnp.bfloat16)
 
 

time: 121 us -> 120 us (level)
  transfers between devices with their start and end apart: 7 -> 7, of which waited for: 5 -> 5; matrix products, arithmetic and copies ran while one was open for 15% -> 14% of each run, Pallas kernels for 0% -> 0%
where the time goes in v17:
time: 120 us
  starting transfers between devices  45.3 us (38%)
  waiting for transfers between devices  28.6 us (24%)
  blocking collectives  20.7 us (17%)
  matrix products  11.4 us (10%)
  local copies, waits for them, and re-layouts  7.36 us (6%)
  other arithmetic  5.26 us (4%)
    all_to_all x1, blocking collectives, reduce_out(): lax.all_to_all(chunks, HEAD_AXES, 0, 0, tiled=True).astype(jnp.float32)  20.7 us
    all_to_all x1, starting transfers between devices, code_prefix(): lax.all_to_all(_pack(sums, counts, span, n, head_dim), 'ctx', 0, 0, tiled...  12.4 us
    all_to_all x1, waiting for transfers between devices, project(): mine = lax.all_to_all(spread, HEAD_AXES, 0, 0, tiled=True)  11.9 us
    all_to_all x1, starting transfers between devices, project(): mine = lax.all_to_all(spread, HEAD_AXES, 0, 0, tiled=True)  11.1 us
    ppermute x3, starting transfers between devices, _send(): return lax.ppermute(value, HEAD_AXES, perm)  10.6 us
    all_to_all x1, waiting for transfers between devices, code_prefix(): lax.all_to_all(_pack(sums, counts, span, n, head_dim), 'ctx', 0, 0, tiled...  7.91 us
    all_to_all x1, waiting for transfers between devices, code_prefix(): back = lax.all_to_all(pre.astype(jnp.bfloat16), 'ctx', 0, 0, tiled=True)  7.64 us
    all_to_all x1, starting transfers between devices, code_prefix(): back = lax.all_to_all(pre.astype(jnp.bfloat16), 'ctx', 0, 0, tiled=True)  7.25 us
  transfers between devices with their start and end apart: 7, of which 5 were waited for; matrix products, arithmetic and copies ran while one was open for 14% of the time, Pallas kernels for 0%

profile of v17, /device:TPU:1, one launch (start us, length us, event | category | flops | bytes accessed | tf_op | source)
XLA Modules:
  0.0 119.6 jit_solution(3640700104513972743)
XLA Ops:
  0.0 0.0 copy-start
  0.0 0.0 copy-start.8
  0.0 2.3 %broadcast_in_dim.85 = bf16[16,2,128,128]{3,2,1,0:T(8,128)(2,1)} broadcast(bf16[2,128,128]{2,1,0:T(8,128)(2,1)} %bitcast.54), dimensions={1,2,3} | broadcast | bytes 1114112 | tf_op jit(solution)/shard_map/broadcast_in_dim | solution.py:204
  2.3 11.1 %all-to-all-start = ((bf16[32,128,128]{2,1,0:T(8,128)(2,1)}), bf16[32,128,128]{2,1,0:T(8,128)(2,1)}, u32[]{:S(2)}, u32[]{:S(2)}) async-start(bf16[32,128,128]{2,1,0:T(8,128)(2,1)} %bitcast.50), calls=%async_computation | async-start | bytes 2097152 | tf_op jit(solution)/shard_map/all_to_all | solution.py:207
  13.4 1.9 %dynamic-slice_bitcast_fusion = bf16[128,2048]{1,0:T(8,128)(2,1)} fusion(bf16[1,128,4096]{2,1,0:T(8,128)(2,1)} %param.8, s32[]{:T(128)S(6)} %select_n.70), kind=kLoop, calls=%fused_computation.15 | loop fusion | bytes 1048580 | tf_op jit(solution)/shard_map/dynamic_slice | solution.py:229
  15.3 2.3 %collective-permute-start.3 = (bf16[128,2048]{1,0:T(8,128)(2,1)}, bf16[128,2048]{1,0:T(8,128)(2,1)}, u32[]{:S(2)}, u32[]{:S(2)}) collective-permute-start(bf16[128,2048]{1,0:T(8,128)(2,1)} %dynamic-slice_bitcast_fusion), channel_id=1, source_target_pairs={{0,1},{1,0},{2,3},{3,2},{4,5},{5,4},{6,7},{7,6},{8,9},{9,8},{10,11... | collective-permute-start | bytes 1572872 | tf_op jit(solution)/shard_map/ppermute | solution.py:41
  18.3 0.0 copy-done.8
  18.3 0.1 convert_reduce_fusion.1
  18.4 0.1 reduce_sum.39
  18.6 11.9 %all-to-all-done = bf16[32,128,128]{2,1,0:T(8,128)(2,1)} async-done(((bf16[32,128,128]{2,1,0:T(8,128)(2,1)}), bf16[32,128,128]{2,1,0:T(8,128)(2,1)}, u32[]{:S(2)}, u32[]{:S(2)}) %all-to-all-start) | async-done | bytes 1048608 | tf_op jit(solution)/shard_map/all_to_all | solution.py:207
  30.4 2.0 %collective-permute-start = (bf16[32,128,128]{2,1,0:T(8,128)(2,1)}, bf16[32,128,128]{2,1,0:T(8,128)(2,1)}, u32[]{:S(2)}, u32[]{:S(2)}) collective-permute-start(bf16[32,128,128]{2,1,0:T(8,128)(2,1)} %all-to-all-done), channel_id=1, source_target_pairs={{0,1},{1,0},{2,3},{3,2},{4,5},{5,4},{6,7},{7,6},{8,9},{9,8},{10,11... | collective-permute-start | bytes 3145736 | tf_op jit(solution)/shard_map/ppermute | solution.py:41
  32.6 0.1 select_convert_fusion.1
  32.7 0.0 copy-done
  32.7 1.9 %convolution_bitcast_fusion.1 = bf16[128,384]{1,0:T(8,128)(2,1)S(1)} fusion(bf16[32,128,128]{2,1,0:T(8,128)(2,1)} %all-to-all-done, bf16[32,128,384]{2,1,0:T(8,128)(2,1)S(1)} %bitcast.48), kind=kOutput, calls=%fused_computation.8 | convolution fusion | flops 402653184 | bytes 4292608 | tf_op jit(solution)/shard_map/dot_general | solution.py:211
  34.6 0.7 collective-permute-done
  35.3 1.9 %convolution_bitcast_fusion = bf16[128,384]{1,0:T(8,128)(2,1)S(1)} fusion(bf16[32,128,128]{2,1,0:T(8,128)(2,1)} %collective-permute-done, bf16[32,128,384]{2,1,0:T(8,128)(2,1)S(1)} %bitcast.49), kind=kOutput, calls=%fused_computation.7 | convolution fusion | flops 402653184 | bytes 4292608 | tf_op jit(solution)/shard_map/dot_general | solution.py:212
  37.3 0.4 convolution_convert_fusion
  37.7 0.7 pad_maximum_fusion
  38.4 12.4 %all-to-all-start.1 = ((bf16[16,40,128]{2,1,0:T(8,128)(2,1)}), bf16[16,40,128]{2,1,0:T(8,128)(2,1)S(1)}, u32[]{:S(2)}, u32[]{:S(2)}) async-start(bf16[16,40,128]{2,1,0:T(8,128)(2,1)} %pad_maximum_fusion), calls=%async_computation.1 | async-start | bytes 327680 | tf_op jit(solution)/shard_map/all_to_all | solution.py:184
  50.8 0.1 pad.16.clone
  50.9 0.0 copy-start.4
  50.9 0.8 maximum_maximum_fusion
  51.7 0.0 copy-done.4
  51.7 3.9 %collective-permute-start.1 = (bf16[272,256]{1,0:T(8,128)(2,1)}, bf16[272,256]{1,0:T(8,128)(2,1)}, u32[]{:S(2)}, u32[]{:S(2)}) collective-permute-start(bf16[272,256]{1,0:T(8,128)(2,1)} %maximum_maximum_fusion), channel_id=1, source_target_pairs={{0,32},{32,64},{64,96},{96,128},{128,160},{160,192},{192,224},{224... | collective-permute-start | bytes 417800 | tf_op jit(solution)/shard_map/ppermute | solution.py:124
  55.6 7.9 %all-to-all-done.1 = bf16[16,40,128]{2,1,0:T(8,128)(2,1)S(1)} async-done(((bf16[16,40,128]{2,1,0:T(8,128)(2,1)}), bf16[16,40,128]{2,1,0:T(8,128)(2,1)S(1)}, u32[]{:S(2)}, u32[]{:S(2)}) %all-to-all-start.1) | async-done | bytes 163872 | tf_op jit(solution)/shard_map/all_to_all | solution.py:184
  63.5 0.2 fusion.34
  63.8 0.2 select_convert_fusion
  64.0 0.7 copy.13
  64.6 7.3 %all-to-all-start.2 = ((bf16[16,40,128]{2,1,0:T(8,128)(2,1)}), bf16[16,40,128]{2,1,0:T(8,128)(2,1)S(1)}, u32[]{:S(2)}, u32[]{:S(2)}) async-start(bf16[16,40,128]{2,1,0:T(8,128)(2,1)} %copy.13), calls=%async_computation.2 | async-start | bytes 327680 | tf_op jit(solution)/shard_map/all_to_all | solution.py:193
  71.9 0.0 collective-permute-done.1
  71.9 0.8 fusion.52
  72.7 0.9 slice.62
  73.6 0.0 copy-start.6
  73.6 0.2 convert_reduce_fusion
  73.8 0.5 copy-done.6
  74.2 1.2 select_reduce_fusion.1
  75.4 0.0 copy-start.2
  75.4 0.8 copy-done.2
  76.2 0.3 fusion.17
  76.5 7.6 %all-to-all-done.2 = bf16[16,40,128]{2,1,0:T(8,128)(2,1)S(1)} async-done(((bf16[16,40,128]{2,1,0:T(8,128)(2,1)}), bf16[16,40,128]{2,1,0:T(8,128)(2,1)S(1)}, u32[]{:S(2)}, u32[]{:S(2)}) %all-to-all-start.2) | async-done | bytes 163872 | tf_op jit(solution)/shard_map/all_to_all | solution.py:193
  84.2 0.1 add.74
  84.3 0.0 copy-start.3
  84.3 0.0 copy-start.5
  84.3 0.0 copy-start.7
  84.3 0.0 copy-start.1
  84.3 1.3 %select_reduce_fusion = (f32[256]{0:T(256)S(1)}, f32[256,512]{1,0:T(8,128)S(1)}) fusion(pred[512]{0:T(512)(128)(4,1)S(1)} %get-tuple-element.7, bf16[1,512,128]{2,1,0:T(8,128)(2,1)} %param.9, bf16[256,384]{1,0:T(8,128)(2,1)S(1)} %fusion.16), kind=kOutput, calls=%fused_computation.19 | convolution fusion | flops 33947392 | bytes 722432 | tf_op jit(solution)/shard_map/dot_general | solution.py:73
  85.7 1.3 %convolution_add_fusion.1 = f32[512,128]{1,0:T(8,128)S(1)} fusion(f32[512,128]{1,0:T(8,128)S(1)} %bitcast.52, s32[256]{0:T(256)S(1)} %bitcast.58, pred[256]{0:T(512)(128)(4,1)S(1)} %compare_and_fusion, bf16[272,256]{1,0:T(8,128)(2,1)} %collective-permute-done.1), kind=kOutput, calls=%fused_computation.5 | convolution fusion | flops 33882112 | bytes 591104 | tf_op jit(solution)/shard_map/dot_general | solution.py:141
  87.0 0.4 fusion.15
  87.4 0.4 fusion.14
  87.9 0.0 copy-done.3
  87.9 0.0 copy-done.5
  87.9 0.0 copy-done.7
  87.9 0.3 fusion.4
  88.2 6.3 %collective-permute-start.2 = (bf16[256,128]{1,0:T(8,128)(2,1)S(1)}, bf16[256,128]{1,0:T(8,128)(2,1)S(1)}, u32[]{:S(2)}, u32[]{:S(2)}) collective-permute-start(bf16[256,128]{1,0:T(8,128)(2,1)S(1)} %fusion.4), channel_id=1, source_target_pairs={{0,1},{1,0},{2,3},{3,2},{4,5},{5,4},{6,7},{7,6},{8,9},{9,8},{10,11... | collective-permute-start | bytes 196616 | tf_op jit(solution)/shard_map/ppermute | solution.py:41
  94.5 0.0 copy-done.1
  94.5 0.4 fusion.5
  95.0 0.0 collective-permute-done.3
  95.0 0.4 collective-permute-done.2
  95.4 1.5 %fusion.1 = bf16[32,8,2048]{2,1,0:T(8,128)(2,1)S(1)} fusion(f32[256,2048]{1,0:T(8,128)S(1)} %fusion.5, bf16[256,128]{1,0:T(8,128)(2,1)S(1)} %collective-permute-done.2, bf16[128,2048]{1,0:T(8,128)(2,1)} %collective-permute-done.3), kind=kOutput, calls=%fused_computation.2 | convolution fusion | flops 135266304 | bytes 3735552 | tf_op jit(solution)/shard_map/dot_general | solution.py:233
  96.9 20.7 %all_to_all.20 = bf16[32,8,2048]{2,1,0:T(8,128)(2,1)} all-to-all(bf16[32,8,2048]{2,1,0:T(8,128)(2,1)S(1)} %fusion.1), channel_id=1, replica_groups=mesh['ctx'=16,'hx'=4,'hy'=4,'hc'=2] {'hx','hy','hc'}, dimensions={0} | all-to-all | bytes 2097152 | tf_op jit(solution)/shard_map/all_to_all | solution.py:238
  117.6 2.0 %reduce = bf16[2,8,2048]{2,1,0:T(8,128)(2,1)} reduce(bf16[16,2,8,2048]{3,2,1,0:T(8,128)(2,1)} %bitcast.51, bf16[]{:T(256)} %constant.71.clone.1), dimensions={0}, to_apply=%region_5.6.clone | reduce | flops 491520 | bytes 1114114 | tf_op jit(solution)/shard_map/reduce_sum | solution.py:239
  (23 shorter events, 0.3 us)
Async XLA Ops:
  0.0 32.7 %copy-start = (bf16[4096,1,384]{2,0,1:T(8,128)(2,1)S(1)}, bf16[4096,1,384]{2,0,1:T(8,128)(2,1)}, u32[]{:S(2)}) copy-start(bf16[4096,1,384]{2,0,1:T(8,128)(2,1)} %param.7) | copy-start | bytes 9437188
  0.0 18.3 %copy-start.8 = (s32[1,256]{1,0:T(1,128)S(1)}, s32[1,256]{1,0:T(1,128)}, u32[]{:S(2)}) copy-start(s32[1,256]{1,0:T(1,128)} %param.10) | copy-start | bytes 3076
  2.3 28.2 %all-to-all-start = ((bf16[32,128,128]{2,1,0:T(8,128)(2,1)}), bf16[32,128,128]{2,1,0:T(8,128)(2,1)}, u32[]{:S(2)}, u32[]{:S(2)}) async-start(bf16[32,128,128]{2,1,0:T(8,128)(2,1)} %bitcast.50), calls=%async_computation | async-start | bytes 2097152 | tf_op jit(solution)/shard_map/all_to_all | solution.py:207
  15.3 79.7 %collective-permute-start.3 = (bf16[128,2048]{1,0:T(8,128)(2,1)}, bf16[128,2048]{1,0:T(8,128)(2,1)}, u32[]{:S(2)}, u32[]{:S(2)}) collective-permute-start(bf16[128,2048]{1,0:T(8,128)(2,1)} %dynamic-slice_bitcast_fusion), channel_id=1, source_target_pairs={{0,1},{1,0},{2,3},{3,2},{4,5},{5,4},{6,7},{7,6},{8,9},{9,8},{10,11... | collective-permute-start | bytes 1572872 | tf_op jit(solution)/shard_map/ppermute | solution.py:41
  30.4 4.9 %collective-permute-start = (bf16[32,128,128]{2,1,0:T(8,128)(2,1)}, bf16[32,128,128]{2,1,0:T(8,128)(2,1)}, u32[]{:S(2)}, u32[]{:S(2)}) collective-permute-start(bf16[32,128,128]{2,1,0:T(8,128)(2,1)} %all-to-all-done), channel_id=1, source_target_pairs={{0,1},{1,0},{2,3},{3,2},{4,5},{5,4},{6,7},{7,6},{8,9},{9,8},{10,11... | collective-permute-start | bytes 3145736 | tf_op jit(solution)/shard_map/ppermute | solution.py:41
  38.4 25.1 %all-to-all-start.1 = ((bf16[16,40,128]{2,1,0:T(8,128)(2,1)}), bf16[16,40,128]{2,1,0:T(8,128)(2,1)S(1)}, u32[]{:S(2)}, u32[]{:S(2)}) async-start(bf16[16,40,128]{2,1,0:T(8,128)(2,1)} %pad_maximum_fusion), calls=%async_computation.1 | async-start | bytes 327680 | tf_op jit(solution)/shard_map/all_to_all | solution.py:184
  50.9 0.8 copy-start.4
  51.7 20.2 %collective-permute-start.1 = (bf16[272,256]{1,0:T(8,128)(2,1)}, bf16[272,256]{1,0:T(8,128)(2,1)}, u32[]{:S(2)}, u32[]{:S(2)}) collective-permute-start(bf16[272,256]{1,0:T(8,128)(2,1)} %maximum_maximum_fusion), channel_id=1, source_target_pairs={{0,32},{32,64},{64,96},{96,128},{128,160},{160,192},{192,224},{224... | collective-permute-start | bytes 417800 | tf_op jit(solution)/shard_map/ppermute | solution.py:124
  64.6 19.5 %all-to-all-start.2 = ((bf16[16,40,128]{2,1,0:T(8,128)(2,1)}), bf16[16,40,128]{2,1,0:T(8,128)(2,1)S(1)}, u32[]{:S(2)}, u32[]{:S(2)}) async-start(bf16[16,40,128]{2,1,0:T(8,128)(2,1)} %copy.13), calls=%async_computation.2 | async-start | bytes 327680 | tf_op jit(solution)/shard_map/all_to_all | solution.py:193
  73.6 0.7 copy-start.6
  75.4 0.8 copy-start.2
  84.3 3.6 %copy-start.3 = (f32[256,512]{1,0:T(8,128)S(1)}, f32[256,512]{1,0:T(8,128)}, u32[]{:S(2)}) copy-start(f32[256,512]{1,0:T(8,128)} %copy-done.2) | copy-start | bytes 1572868
  84.3 3.6 %copy-start.5 = (bf16[256,256]{1,0:T(8,128)(2,1)S(1)}, bf16[256,256]{1,0:T(8,128)(2,1)}, u32[]{:S(2)}) copy-start(bf16[256,256]{1,0:T(8,128)(2,1)} %copy-done.4) | copy-start | bytes 393220
  84.3 3.6 %copy-start.7 = (bf16[256,256]{1,0:T(8,128)(2,1)S(1)}, bf16[256,256]{1,0:T(8,128)(2,1)}, u32[]{:S(2)}) copy-start(bf16[256,256]{1,0:T(8,128)(2,1)} %copy-done.6) | copy-start | bytes 393220
  84.3 10.3 %copy-start.1 = (bf16[1,128,4096]{2,1,0:T(8,128)(2,1)S(1)}, bf16[1,128,4096]{2,1,0:T(8,128)(2,1)}, u32[]{:S(2)}) copy-start(bf16[1,128,4096]{2,1,0:T(8,128)(2,1)} %param.8) | copy-start | bytes 3145732
  88.2 7.2 %collective-permute-start.2 = (bf16[256,128]{1,0:T(8,128)(2,1)S(1)}, bf16[256,128]{1,0:T(8,128)(2,1)S(1)}, u32[]{:S(2)}, u32[]{:S(2)}) collective-permute-start(bf16[256,128]{1,0:T(8,128)(2,1)S(1)} %fusion.4), channel_id=1, source_target_pairs={{0,1},{1,0},{2,3},{3,2},{4,5},{5,4},{6,7},{7,6},{8,9},{9,8},{10,11... | collective-permute-start | bytes 196616 | tf_op jit(solution)/shard_map/ppermute | solution.py:41
